TPU v7x, 512 devices: a whole 4x4x16 slice. The times are simulated.
512 devices in a mesh: patch: 16 (over y, x_hi, core), map: 32 (over x_lo, z).
Axes of the slice: x: 4 (x_hi: 2, x_lo: 2; x = x_hi * 2 + x_lo), y: 4, z: 16, core: 2. Of those that a mesh axis runs over, the one named last changes fastest.
Arguments:
- maps: bfloat16 [64, 32, 24576], P('map', None, 'patch'), may hold values from -6 to 6
- cotangent: bfloat16 [64, 32, 24576], P('map', None, 'patch'), may hold values from -6 to 6
- tiles: bfloat16 [96, 3, 256, 256], P('patch'), may hold values from -0.21875 to 0.21875
- columns: int32 [96, 3], P('patch'), may hold values from 0 to 95, as said below
- filters: bfloat16 [3, 32, 32], replicated, may hold values from -0.625 to 0.625
Outputs:
- output: bfloat16 [64, 32, 24576], P('map', None, 'patch')
- input_grad: bfloat16 [64, 32, 24576], P('map', None, 'patch')
- filter_grad: float32 [3, 32, 32], replicated
Inputs may be any that keep to these rules, and one draw needn't show every extreme that they name: `columns`: slot 0 of block row b names block b itself, slot 1 a block 1 to 2 before it and slot 2 a block 1 to 2 after it, counted cyclically over the 96 blocks; block row 0 reads exactly 2 blocks away on both sides.
All inputs are finite; a program needn't handle non-finite values.
Results may differ from a plain program's by a relative error of at most 0.0054.
Values may be sent and summed in bfloat16 or wider, within the bound.
No kernel may reach another device: no remote copies, remote signals or barrier semaphores. Data moves between devices by JAX's collectives and lax.ppermute only.
A program may use at most 64 MiB of HBM per device.

v0:
```python
import math

import jax
import jax.numpy as jnp
from jax import lax
from jax.sharding import PartitionSpec as P

REACH = 2


def extended_2(cells, sides, width):
    for axis, dim in sides:
        count = lax.axis_size(axis)
        head = lax.slice_in_dim(cells, 0, width, axis=dim)
        tail = lax.slice_in_dim(cells, cells.shape[dim] - width, cells.shape[dim], axis=dim)
        cells = jnp.concatenate(
            [
                lax.ppermute(tail, axis, [(i, (i + 1) % count) for i in range(count)]),
                cells,
                lax.ppermute(head, axis, [((i + 1) % count, i) for i in range(count)]),
            ],
            axis=dim,
        )
    return cells


def offset_sums(grad_blocks, tile_set, offset_mask):
    contrib = jnp.einsum(
        "nui,ujiq->nujq", grad_blocks, tile_set, preferred_element_type=jnp.float32
    )
    return jnp.einsum(
        "uje,nujq->nueq", offset_mask.astype(jnp.float32), contrib, precision=lax.Precision.HIGHEST
    )


def per_device(maps, cotangent, tiles, columns, filters):
    map_count = maps.shape[0]
    chan_count = maps.shape[1]
    pix_count = maps.shape[2]
    block_count = tiles.shape[0]
    block_size = tiles.shape[2]
    reach_blocks = REACH
    spread = 2 * reach_blocks + 1
    row_count = map_count * chan_count
    rim_cells = reach_blocks * block_size
    patch_count = lax.axis_size("patch")
    total_blocks = block_count * patch_count
    first_block = lax.axis_index("patch") * block_count
    row_ids = first_block + jnp.arange(block_count, dtype=jnp.int32)
    offset_ids = jnp.arange(spread, dtype=jnp.int32)
    own_offset = (columns - row_ids[:, None] + reach_blocks) % total_blocks
    own_mask = own_offset[:, :, None] == offset_ids[None, None, :]

    def forward_apply(field):
        extended = extended_2(field, (("patch", 2),), rim_cells)
        ext_blocks = extended.reshape(row_count, block_count + 2 * reach_blocks, block_size)
        shifted = jnp.stack(
            [ext_blocks[:, offset : offset + block_count] for offset in range(spread)], axis=2
        )
        picked = jnp.einsum(
            "rje,nreq->nrjq",
            own_mask.astype(jnp.bfloat16),
            shifted,
            preferred_element_type=jnp.bfloat16,
        )
        result = jnp.einsum("nrjq,rjiq->nri", picked, tiles, preferred_element_type=jnp.float32)
        return result.reshape(map_count, chan_count, pix_count)

    def adjoint_apply(grads):
        by_offset = offset_sums(grads.reshape(row_count, block_count, block_size), tiles, own_mask)
        window = jnp.pad(by_offset[:, :, 0], ((0, 0), (0, spread - 1), (0, 0)))
        for offset in range(1, spread):
            window = window + jnp.pad(
                by_offset[:, :, offset], ((0, 0), (offset, spread - 1 - offset), (0, 0))
            )
        own_part = window[:, reach_blocks : reach_blocks + block_count]
        outgoing = jnp.concatenate(
            [window[:, :reach_blocks], window[:, reach_blocks + block_count :]], axis=1
        )
        outgoing = outgoing.reshape(map_count, chan_count, 2 * rim_cells)
        incoming = extended_2(outgoing, (("patch", 2),), rim_cells)
        from_left = incoming[:, :, :rim_cells].reshape(row_count, reach_blocks, block_size)
        from_right = incoming[:, :, incoming.shape[2] - rim_cells :].reshape(
            row_count, reach_blocks, block_size
        )
        own_part = own_part.at[:, :reach_blocks].add(from_left)
        own_part = own_part.at[:, block_count - reach_blocks :].add(from_right)
        return own_part.reshape(map_count, chan_count, pix_count)

    x_one = forward_apply(maps).astype(jnp.bfloat16)
    x_two = (2.0 * forward_apply(x_one) - maps.astype(jnp.float32)).astype(jnp.bfloat16)
    terms = jnp.stack([maps, x_one, x_two])
    output = jnp.einsum("kco,kmcp->mop", filters, terms, preferred_element_type=jnp.float32).astype(
        jnp.bfloat16
    )
    grads = jnp.einsum("kco,mop->kmcp", filters, cotangent, preferred_element_type=jnp.float32)
    grad_two = grads[2].astype(jnp.bfloat16)
    update = (grads[1] + 2.0 * adjoint_apply(grad_two)).astype(jnp.bfloat16)
    input_grad = (grads[0] - grad_two.astype(jnp.float32) + adjoint_apply(update)).astype(
        jnp.bfloat16
    )
    scale = 1.0 / math.sqrt(map_count * lax.axis_size("map") * pix_count * patch_count)
    local_grad = jnp.einsum("kmcp,mop->kco", terms, cotangent, preferred_element_type=jnp.float32)
    filter_grad = lax.psum(local_grad, ("patch", "map")) * scale
    return (output, input_grad, filter_grad)


def solution(mesh):
    placed = (
        P("map", None, "patch"),
        P("map", None, "patch"),
        P("patch", None, None, None),
        P("patch", None),
        P(),
    )
    return jax.shard_map(
        per_device,
        mesh=mesh,
        in_specs=placed,
        out_specs=(P("map", None, "patch"), P("map", None, "patch"), P()),
        check_vma=False,
    )
```

profile of v0, /device:TPU:24, one launch (start us, length us, event | category | flops | bytes accessed | tf_op | source)
XLA Modules:
  0.0 219.5 jit_solution(9846326644404595408)
XLA Ops:
  4.6 2.3 %convolution_bitcast_fusion.3 = f32[64,6,5,256]{3,2,0,1:T(8,128)S(1)} fusion(f32[6,64,3,256]{3,1,2,0:T(8,128)S(1)} %fusion.38, s32[6,3]{1,0:T(8,128)S(1)} %copy.21), kind=kOutput, calls=%fused_computation.5 | convolution fusion | flops 17694810 | bytes 3145800 | tf_op jit(solution)/shard_map/uje,nujq->nueq/dot_general | solution.py:31
  6.9 1.8 fusion.56
  10.8 1.8 reshape.181
  12.6 1.8 fusion.58
  14.4 1.9 collective-permute-start.4
  16.3 6.0 %collective-permute-start.5 = (f32[2,32,512]{2,1,0:T(8,128)}, f32[2,32,512]{2,1,0:T(8,128)}, u32[]{:S(2)}, u32[]{:S(2)}) collective-permute-start(f32[2,32,512]{2,1,0:T(8,128)} %get-tuple-element.67), channel_id=1, source_target_pairs={{32,0},{64,32},{96,64},{128,96},{160,128},{192,160},{224,192},{256... | collective-permute-start | bytes 393224 | tf_op jit(solution)/shard_map/ppermute | solution.py:20
  23.9 1.9 collective-permute-start
  25.8 6.0 %collective-permute-start.1 = (bf16[2,32,512]{2,1,0:T(8,128)(2,1)}, bf16[2,32,512]{2,1,0:T(8,128)(2,1)}, u32[]{:S(2)}, u32[]{:S(2)}) collective-permute-start(bf16[2,32,512]{2,1,0:T(8,128)(2,1)} %get-tuple-element.72), channel_id=1, source_target_pairs={{32,0},{64,32},{96,64},{128,96},{160,128},{192,160},{224,192},{256... | collective-permute-start | bytes 196616 | tf_op jit(solution)/shard_map/ppermute | solution.py:20
  31.9 1.8 slice.264
  34.6 1.9 squeeze.35
  42.6 1.9 convert_element_type.73
  44.5 1.9 convert_element_type.72
  47.8 1.9 collective-permute-start.2
  49.8 6.2 %collective-permute-start.3 = (bf16[2,32,512]{2,1,0:T(8,128)(2,1)}, bf16[2,32,512]{2,1,0:T(8,128)(2,1)}, u32[]{:S(2)}, u32[]{:S(2)}) collective-permute-start(bf16[2,32,512]{2,1,0:T(8,128)(2,1)} %get-tuple-element.70), channel_id=1, source_target_pairs={{32,0},{64,32},{96,64},{128,96},{160,128},{192,160},{224,192},{256... | collective-permute-start | bytes 196616 | tf_op jit(solution)/shard_map/ppermute | solution.py:20
  63.6 2.3 %convolution_bitcast_fusion.2 = f32[64,6,5,256]{3,2,0,1:T(8,128)S(1)} fusion(f32[6,64,3,256]{3,1,2,0:T(8,128)S(1)} %fusion.34, s32[6,3]{1,0:T(8,128)S(1)} %copy.21), kind=kOutput, calls=%fused_computation.4 | convolution fusion | flops 17694810 | bytes 3145800 | tf_op jit(solution)/shard_map/uje,nujq->nueq/dot_general | solution.py:31
  65.9 1.8 fusion.55
  77.6 2.0 convolution_bitcast_fusion.6
  81.5 1.8 reshape.184
  84.9 1.9 collective-permute-start.6
  86.9 1.8 slice.279
  88.6 6.0 %collective-permute-start.7 = (f32[2,32,512]{2,1,0:T(8,128)}, f32[2,32,512]{2,1,0:T(8,128)}, u32[]{:S(2)}, u32[]{:S(2)}) collective-permute-start(f32[2,32,512]{2,1,0:T(8,128)} %get-tuple-element.65), channel_id=1, source_target_pairs={{32,0},{64,32},{96,64},{128,96},{160,128},{192,160},{224,192},{256... | collective-permute-start | bytes 393224 | tf_op jit(solution)/shard_map/ppermute | solution.py:20
  94.7 111.0 %psum.7 = f32[3,32,32]{2,1,0:T(8,128)} all-reduce(f32[3,32,32]{2,1,0:T(8,128)} %convolution_bitcast_fusion.6), channel_id=1, replica_groups=mesh['patch'=16,'map'=32] {'patch','map'}, use_global_device_ids=true, to_apply=%region_0.1 | all-reduce | flops 3072 | bytes 24576 | tf_op jit(solution)/shard_map/psum | solution.py:104
  213.8 2.0 copy.42
  215.8 1.9 reshape.187
  (117 shorter events, 46.7 us)
Async XLA Ops:
  0.6 3.5 %copy-start = (bf16[6,3,256,256]{3,2,1,0:T(8,128)(2,1)S(1)}, bf16[6,3,256,256]{3,2,1,0:T(8,128)(2,1)}, u32[]{:S(2)}) copy-start(bf16[6,3,256,256]{3,2,1,0:T(8,128)(2,1)} %param.15) | copy-start | bytes 7077892
  8.9 24.8 %copy-start.7 = (f32[64,6,256]{2,0,1:T(8,128)}, f32[64,6,256]{2,0,1:T(8,128)S(1)}, u32[]{:S(2)}) copy-start(f32[64,6,256]{2,0,1:T(8,128)S(1)} %get-tuple-element.73) | copy-start | bytes 1179652
  8.9 24.8 %copy-start.9 = (f32[64,6,256]{2,0,1:T(8,128)}, f32[64,6,256]{2,0,1:T(8,128)S(1)}, u32[]{:S(2)}) copy-start(f32[64,6,256]{2,0,1:T(8,128)S(1)} %get-tuple-element.74) | copy-start | bytes 1179652
  12.6 21.0 %copy-start.12 = (f32[64,6,256]{2,0,1:T(8,128)S(1)}, f32[64,6,256]{2,0,1:T(8,128)}, u32[]{:S(2)}) copy-start(f32[64,6,256]{2,0,1:T(8,128)} %copy-done.11) | copy-start | bytes 1179652
  12.6 21.0 %copy-start.14 = (f32[64,6,256]{2,0,1:T(8,128)S(1)}, f32[64,6,256]{2,0,1:T(8,128)}, u32[]{:S(2)}) copy-start(f32[64,6,256]{2,0,1:T(8,128)} %copy-done.13) | copy-start | bytes 1179652
  14.4 41.6 %collective-permute-start.4 = (f32[2,32,512]{2,1,0:T(8,128)}, f32[2,32,512]{2,1,0:T(8,128)}, u32[]{:S(2)}, u32[]{:S(2)}) collective-permute-start(f32[2,32,512]{2,1,0:T(8,128)} %get-tuple-element.68), channel_id=1, source_target_pairs={{0,32},{32,64},{64,96},{96,128},{128,160},{160,192},{192,224},{224... | collective-permute-start | bytes 393224 | tf_op jit(solution)/shard_map/ppermute | solution.py:18
  16.3 43.1 %collective-permute-start.5 = (f32[2,32,512]{2,1,0:T(8,128)}, f32[2,32,512]{2,1,0:T(8,128)}, u32[]{:S(2)}, u32[]{:S(2)}) collective-permute-start(f32[2,32,512]{2,1,0:T(8,128)} %get-tuple-element.67), channel_id=1, source_target_pairs={{32,0},{64,32},{96,64},{128,96},{160,128},{192,160},{224,192},{256... | collective-permute-start | bytes 393224 | tf_op jit(solution)/shard_map/ppermute | solution.py:20
  23.9 12.6 %collective-permute-start = (bf16[2,32,512]{2,1,0:T(8,128)(2,1)}, bf16[2,32,512]{2,1,0:T(8,128)(2,1)}, u32[]{:S(2)}, u32[]{:S(2)}) collective-permute-start(bf16[2,32,512]{2,1,0:T(8,128)(2,1)} %get-tuple-element.71), channel_id=1, source_target_pairs={{0,32},{32,64},{64,96},{96,128},{128,160},{160,192},{192,224},{224... | collective-permute-start | bytes 196616 | tf_op jit(solution)/shard_map/ppermute | solution.py:18
  25.8 10.7 %collective-permute-start.1 = (bf16[2,32,512]{2,1,0:T(8,128)(2,1)}, bf16[2,32,512]{2,1,0:T(8,128)(2,1)}, u32[]{:S(2)}, u32[]{:S(2)}) collective-permute-start(bf16[2,32,512]{2,1,0:T(8,128)(2,1)} %get-tuple-element.72), channel_id=1, source_target_pairs={{32,0},{64,32},{96,64},{128,96},{160,128},{192,160},{224,192},{256... | collective-permute-start | bytes 196616 | tf_op jit(solution)/shard_map/ppermute | solution.py:20
  33.8 2.7 %copy-start.18 = (bf16[2,32,1536]{2,1,0:T(8,128)(2,1)S(1)}, bf16[2,32,1536]{2,1,0:T(8,128)(2,1)}, u32[]{:S(2)}) copy-start(bf16[2,32,1536]{2,1,0:T(8,128)(2,1)} %param.13) | copy-start | bytes 589828
  41.8 15.9 %copy-start.8 = (f32[64,6,256]{2,0,1:T(8,128)S(1)}, f32[64,6,256]{2,0,1:T(8,128)}, u32[]{:S(2)}) copy-start(f32[64,6,256]{2,0,1:T(8,128)} %copy-done.7) | copy-start | bytes 1179652
  41.8 15.9 %copy-start.10 = (f32[64,6,256]{2,0,1:T(8,128)S(1)}, f32[64,6,256]{2,0,1:T(8,128)}, u32[]{:S(2)}) copy-start(f32[64,6,256]{2,0,1:T(8,128)} %copy-done.9) | copy-start | bytes 1179652
  47.8 22.0 %collective-permute-start.2 = (bf16[2,32,512]{2,1,0:T(8,128)(2,1)}, bf16[2,32,512]{2,1,0:T(8,128)(2,1)}, u32[]{:S(2)}, u32[]{:S(2)}) collective-permute-start(bf16[2,32,512]{2,1,0:T(8,128)(2,1)} %get-tuple-element.69), channel_id=1, source_target_pairs={{0,32},{32,64},{64,96},{96,128},{128,160},{160,192},{192,224},{224... | collective-permute-start | bytes 196616 | tf_op jit(solution)/shard_map/ppermute | solution.py:18
  49.8 20.1 %collective-permute-start.3 = (bf16[2,32,512]{2,1,0:T(8,128)(2,1)}, bf16[2,32,512]{2,1,0:T(8,128)(2,1)}, u32[]{:S(2)}, u32[]{:S(2)}) collective-permute-start(bf16[2,32,512]{2,1,0:T(8,128)(2,1)} %get-tuple-element.70), channel_id=1, source_target_pairs={{32,0},{64,32},{96,64},{128,96},{160,128},{192,160},{224,192},{256... | collective-permute-start | bytes 196616 | tf_op jit(solution)/shard_map/ppermute | solution.py:20
  67.7 1.3 copy-start.1
  76.5 3.1 %copy-start.22 = (bf16[1,2,32,1536]{3,2,1,0:T(8,128)(2,1)S(1)}, bf16[1,2,32,1536]{3,2,1,0:T(8,128)(2,1)}, u32[]{:S(2)}) copy-start(bf16[1,2,32,1536]{3,2,1,0:T(8,128)(2,1)} %convert_element_type.72) | copy-start | bytes 589828
  76.5 3.1 %copy-start.23 = (bf16[3,32,32]{2,1,0:T(8,128)(2,1)S(1)}, bf16[3,32,32]{2,1,0:T(8,128)(2,1)}, u32[]{:S(2)}) copy-start(bf16[3,32,32]{2,1,0:T(8,128)(2,1)} %param.17) | copy-start | bytes 18436
  77.6 3.0 %copy-start.20 = (f32[64,2,256]{2,0,1:T(8,128)S(1)}, f32[64,2,256]{2,0,1:T(8,128)}, u32[]{:S(2)}) copy-start(f32[64,2,256]{2,0,1:T(8,128)} %get-tuple-element.61) | copy-start | bytes 393220
  77.6 3.0 %copy-start.21 = (f32[64,2,256]{2,0,1:T(8,128)S(1)}, f32[64,2,256]{2,0,1:T(8,128)}, u32[]{:S(2)}) copy-start(f32[64,2,256]{2,0,1:T(8,128)} %get-tuple-element.62) | copy-start | bytes 393220
  80.6 128.2 %copy-start.2 = (f32[64,6,1,256]{3,0,1,2:T(8,128)S(1)}, f32[64,6,1,256]{3,0,1,2:T(8,128)}, u32[]{:S(2)}) copy-start(f32[64,6,1,256]{3,0,1,2:T(8,128)} %copy-done.1) | copy-start | bytes 1179652
  80.6 128.2 %copy-start.4 = (f32[64,6,1,256]{3,0,1,2:T(8,128)S(1)}, f32[64,6,1,256]{3,0,1,2:T(8,128)}, u32[]{:S(2)}) copy-start(f32[64,6,1,256]{3,0,1,2:T(8,128)} %copy-done.3) | copy-start | bytes 1179652
  84.9 122.2 %collective-permute-start.6 = (f32[2,32,512]{2,1,0:T(8,128)}, f32[2,32,512]{2,1,0:T(8,128)}, u32[]{:S(2)}, u32[]{:S(2)}) collective-permute-start(f32[2,32,512]{2,1,0:T(8,128)} %get-tuple-element.66), channel_id=1, source_target_pairs={{0,32},{32,64},{64,96},{96,128},{128,160},{160,192},{192,224},{224... | collective-permute-start | bytes 393224 | tf_op jit(solution)/shard_map/ppermute | solution.py:18
  88.6 121.8 %collective-permute-start.7 = (f32[2,32,512]{2,1,0:T(8,128)}, f32[2,32,512]{2,1,0:T(8,128)}, u32[]{:S(2)}, u32[]{:S(2)}) collective-permute-start(f32[2,32,512]{2,1,0:T(8,128)} %get-tuple-element.65), channel_id=1, source_target_pairs={{32,0},{64,32},{96,64},{128,96},{160,128},{192,160},{224,192},{256... | collective-permute-start | bytes 393224 | tf_op jit(solution)/shard_map/ppermute | solution.py:20
  210.4 7.3 %copy-start.16 = (f32[3,2,32,1536]{3,2,0,1:T(8,128)S(1)}, f32[3,2,32,1536]{3,2,0,1:T(8,128)}, u32[]{:S(2)}) copy-start(f32[3,2,32,1536]{3,2,0,1:T(8,128)} %copy-done.15) | copy-start | bytes 3538948
  (8 other events, 8.8 us)
where the time goes:
time: 223 us; the launch traced here: 219 us
  blocking collectives  111 us (50%)
  local copies, waits for them, and re-layouts  43.2 us (19%)
  starting transfers between devices  32 us (14%)
  other arithmetic  17 us (8%)
  matrix products  15.1 us (7%)
    psum x1, blocking collectives, per_device(): filter_grad = lax.psum(local_grad, ('patch', 'map')) * scale  111 us
    ppermute x4, starting transfers between devices, extended_2(): lax.ppermute(head, axis, [((i + 1) % count, i) for i in range(count)])  24.4 us
    ppermute x4, starting transfers between devices, extended_2(): lax.ppermute(tail, axis, [(i, (i + 1) % count) for i in range(count)])  7.64 us
    another operation x4, local copies, waits for them, and re-layouts  6 us
    dot_general x2, matrix products, offset_sums(): jnp.einsum('uje,nujq->nueq', offset_mask.astype(jnp.float32), contrib, pr...  4.57 us
    convert_element_type x3, local copies, waits for them, and re-layouts, per_device(): x_one = forward_apply(maps).astype(jnp.bfloat16)  4.53 us
  transfers between devices with their start and end apart: 8, of which 0 were waited for; matrix products, arithmetic and copies ran while one was open for 17% of the time, Pallas kernels for 0%

commit v1 on v0

v1 whole, which is shorter than its diff:
```python
import math

import jax
import jax.numpy as jnp
from jax import lax
from jax.sharding import PartitionSpec as P

REACH = 2


def butterfly_sum(x, axes):
    for axis in axes:
        count = lax.axis_size(axis)
        step = 1
        while step < count:
            x = x + lax.ppermute(x, axis, [(i, i ^ step) for i in range(count)])
            step *= 2
    return x


def per_device(maps, cotangent, tiles, columns, filters):
    map_count, chan_count, pix_count = maps.shape
    block_count = tiles.shape[0]
    block_size = tiles.shape[2]
    row_count = map_count * chan_count
    patch_count = lax.axis_size("patch")
    total_blocks = block_count * patch_count
    first_block = lax.axis_index("patch") * block_count
    row_ids = first_block + jnp.arange(block_count, dtype=jnp.int32)
    back_one = ((row_ids - columns[:, 1]) % total_blocks == 1)[None, :, None]
    next_one = ((columns[:, 2] - row_ids) % total_blocks == 1)[None, :, None]
    nb = block_count
    to_right = [(i, (i + 1) % patch_count) for i in range(patch_count)]
    to_left = [((i + 1) % patch_count, i) for i in range(patch_count)]

    def exchange(edge_left, edge_right):
        from_right = lax.ppermute(edge_left, "patch", to_left)
        from_left = lax.ppermute(edge_right, "patch", to_right)
        return from_left, from_right

    def forward_local(ext):
        s0 = ext[:, 2 : 2 + nb]
        s1 = jnp.where(back_one, ext[:, 1 : 1 + nb], ext[:, 0:nb])
        s2 = jnp.where(next_one, ext[:, 3 : 3 + nb], ext[:, 4 : 4 + nb])
        picked = jnp.stack([s0, s1, s2], axis=2).astype(jnp.bfloat16)
        return jnp.einsum("nrjq,rjiq->nri", picked, tiles, preferred_element_type=jnp.float32)

    def adjoint_window(grads):
        contrib = jnp.einsum("nri,rjiq->nrjq", grads, tiles, preferred_element_type=jnp.float32)
        c0, c1, c2 = contrib[:, :, 0], contrib[:, :, 1], contrib[:, :, 2]
        zero = jnp.zeros_like(c0)
        pad = lambda v, lo: jnp.pad(v, ((0, 0), (lo, 4 - lo), (0, 0)))
        return (
            pad(c0, 2)
            + pad(jnp.where(back_one, c1, zero), 1)
            + pad(jnp.where(back_one, zero, c1), 0)
            + pad(jnp.where(next_one, c2, zero), 3)
            + pad(jnp.where(next_one, zero, c2), 4)
        )

    x_zero = maps.reshape(row_count, nb, block_size)
    weights = filters
    grads = jnp.einsum("kco,mop->kmcp", weights, cotangent, preferred_element_type=jnp.float32)
    grads = grads.reshape(3, row_count, nb, block_size)
    grad_two = grads[2].astype(jnp.bfloat16)

    win1 = adjoint_window(grad_two)
    x0f = x_zero.astype(jnp.float32)
    send_left = jnp.stack([x0f[:, 0:2], win1[:, 0:2]])
    send_right = jnp.stack([x0f[:, nb - 2 : nb], win1[:, nb + 2 : nb + 4]])
    got_left, got_right = exchange(send_left, send_right)
    ext0 = jnp.concatenate([got_left[0], x0f, got_right[0]], axis=1)
    x_one = forward_local(ext0).astype(jnp.bfloat16)
    adj1 = win1[:, 2 : 2 + nb]
    adj1 = adj1.at[:, 0:2].add(got_left[1])
    adj1 = adj1.at[:, nb - 2 : nb].add(got_right[1])
    update = (grads[1] + 2.0 * adj1).astype(jnp.bfloat16)

    win2 = adjoint_window(update)
    x1f = x_one.astype(jnp.float32)
    send_left = jnp.stack([x1f[:, 0:2], win2[:, 0:2]])
    send_right = jnp.stack([x1f[:, nb - 2 : nb], win2[:, nb + 2 : nb + 4]])
    got_left, got_right = exchange(send_left, send_right)
    ext1 = jnp.concatenate([got_left[0], x1f, got_right[0]], axis=1)
    x_two = (2.0 * forward_local(ext1) - x0f).astype(jnp.bfloat16)
    adj2 = win2[:, 2 : 2 + nb]
    adj2 = adj2.at[:, 0:2].add(got_left[1])
    adj2 = adj2.at[:, nb - 2 : nb].add(got_right[1])
    input_grad = (grads[0] - grad_two.astype(jnp.float32) + adj2).astype(jnp.bfloat16)

    shape3 = (map_count, chan_count, pix_count)
    terms = jnp.stack([maps, x_one.reshape(shape3), x_two.reshape(shape3)])
    output = jnp.einsum("kco,kmcp->mop", filters, terms, preferred_element_type=jnp.float32).astype(
        jnp.bfloat16
    )
    scale = 1.0 / math.sqrt(map_count * lax.axis_size("map") * pix_count * patch_count)
    local_grad = jnp.einsum("kmcp,mop->kco", terms, cotangent, preferred_element_type=jnp.float32)
    filter_grad = butterfly_sum(local_grad, ("patch", "map")) * scale
    return (output, input_grad.reshape(shape3), filter_grad)


def solution(mesh):
    placed = (
        P("map", None, "patch"),
        P("map", None, "patch"),
        P("patch", None, None, None),
        P("patch", None),
        P(),
    )
    return jax.shard_map(
        per_device,
        mesh=mesh,
        in_specs=placed,
        out_specs=(P("map", None, "patch"), P("map", None, "patch"), P()),
        check_vma=False,
    )
```

time: 223 us -> 134 us (0.60)
  blocking collectives: 111 us -> 0 us
  waiting for transfers between devices: 0.02 us -> 48.6 us
  local copies, waits for them, and re-layouts: 43.2 us -> 18.7 us
  starting transfers between devices: 32 us -> 46.8 us
  other arithmetic: 17 us -> 7.97 us
  matrix products: 15.1 us -> 9.52 us
    psum x1 -> x0, blocking collectives: 111 us -> none  [per_device(): filter_grad = lax.psum(local_grad, ('patch', 'map')) * scale]
    ppermute x8 -> x13, waiting for transfers between devices: 0.02 us -> 48.6 us  [the longest x9 33.2 us: butterfly_sum(): x = x + lax.ppermute(x, axis, [(i, i ^ step) for i in range(count)])]
    ppermute x8 -> x13, starting transfers between devices: 32 us -> 46.8 us  [the longest x9 38.1 us: butterfly_sum(): x = x + lax.ppermute(x, axis, [(i, i ^ step) for i in range(count)])]
    slice x9 -> x3, local copies, waits for them, and re-layouts: 14.4 us -> 0.88 us  [the longest x1 0.82 us: per_device(): grads[0] - grad_two.astype(jnp.float32) + adj2]
    reshape x5 -> x1, local copies, waits for them, and re-layouts: 7.82 us -> 0.91 us  [per_device(): return (output, input_grad.reshape(shape3), filter_grad)]
    dot_general x9 -> x5, matrix products: 12.2 us -> 5.97 us  [the longest x2 2.6 us: forward_local(): jnp.einsum('nrjq,rjiq->nri', picked, tiles, preferred_element_type=jnp.fl...]
    scatter-add x4 -> x3, other arithmetic: 6.55 us -> 1.92 us  [the longest x1 0.94 us: per_device(): adj1 = adj1.at[:, nb - 2:nb].add(got_right[1])]
    another operation x6 -> x3, local copies, waits for them, and re-layouts: 6.16 us -> 2.11 us  [the longest x2 2.09 us: per_device(): terms = jnp.stack([maps, x_one.reshape(shape3), x_two.reshape(shape3)])]
  transfers between devices with their start and end apart: 8 -> 13, of which waited for: 0 -> 12; matrix products, arithmetic and copies ran while one was open for 17% -> 11% of each run, Pallas kernels for 0% -> 0%
where the time goes in v1:
time: 134 us; the launch traced here: 133 us
  waiting for transfers between devices  48.6 us (36%)
  starting transfers between devices  46.8 us (35%)
  local copies, waits for them, and re-layouts  18.7 us (14%)
  matrix products  9.52 us (7%)
  other arithmetic  7.97 us (6%)
    ppermute x9, starting transfers between devices, butterfly_sum(): x = x + lax.ppermute(x, axis, [(i, i ^ step) for i in range(count)])  38.1 us
    ppermute x9, waiting for transfers between devices, butterfly_sum(): x = x + lax.ppermute(x, axis, [(i, i ^ step) for i in range(count)])  33.2 us
    ppermute x2, waiting for transfers between devices, exchange(): from_left = lax.ppermute(edge_right, 'patch', to_right)  14.9 us
    convert_element_type x4, local copies, waits for them, and re-layouts, per_device(): x0f = x_zero.astype(jnp.float32)  5 us
    ppermute x2, starting transfers between devices, exchange(): from_left = lax.ppermute(edge_right, 'patch', to_right)  4.93 us
    ppermute x2, starting transfers between devices, exchange(): from_right = lax.ppermute(edge_left, 'patch', to_left)  3.82 us
    unnamed x24, local copies, waits for them, and re-layouts  2.77 us
  transfers between devices with their start and end apart: 13, of which 12 were waited for; matrix products, arithmetic and copies ran while one was open for 11% of the time, Pallas kernels for 0%

profile of v1, /device:TPU:24, one launch (start us, length us, event | category | flops | bytes accessed | tf_op | source)
XLA Modules:
  0.0 132.7 jit_solution(232271367629584991)
XLA Ops:
  9.2 1.9 %collective-permute-start = (f32[2,64,2,256]{3,1,2,0:T(8,128)S(1)}, f32[2,64,2,256]{3,1,2,0:T(8,128)S(1)}, u32[]{:S(2)}, u32[]{:S(2)}) collective-permute-start(f32[2,64,2,256]{3,1,2,0:T(8,128)S(1)} %pad_maximum_fusion.5), channel_id=1, source_target_pairs={{0,32},{32,64},{64,96},{96,128},{128,160},{160,192},{192,224},{224... | collective-permute-start | bytes 786440 | tf_op jit(solution)/shard_map/ppermute | solution.py:38
  11.3 8.0 %collective-permute-done = f32[2,64,2,256]{3,1,2,0:T(8,128)S(1)} collective-permute-done((f32[2,64,2,256]{3,1,2,0:T(8,128)S(1)}, f32[2,64,2,256]{3,1,2,0:T(8,128)S(1)}, u32[]{:S(2)}, u32[]{:S(2)}) %collective-permute-start) | collective-permute-done | bytes 262176 | tf_op jit(solution)/shard_map/ppermute | solution.py:38
  20.1 1.9 %collective-permute-start.1 = (f32[2,64,2,256]{3,1,2,0:T(8,128)}, f32[2,64,2,256]{3,1,2,0:T(8,128)}, u32[]{:S(2)}, u32[]{:S(2)}) collective-permute-start(f32[2,64,2,256]{3,1,2,0:T(8,128)} %pad_maximum_fusion.6), channel_id=1, source_target_pairs={{32,0},{64,32},{96,64},{128,96},{160,128},{192,160},{224,192},{256... | collective-permute-start | bytes 786440 | tf_op jit(solution)/shard_map/ppermute | solution.py:37
  32.2 3.0 %collective-permute-start.2 = (f32[2,64,2,256]{3,1,2,0:T(8,128)S(1)}, f32[2,64,2,256]{3,1,2,0:T(8,128)S(1)}, u32[]{:S(2)}, u32[]{:S(2)}) collective-permute-start(f32[2,64,2,256]{3,1,2,0:T(8,128)S(1)} %pad_maximum_fusion.7), channel_id=1, source_target_pairs={{0,32},{32,64},{64,96},{96,128},{128,160},{160,192},{192,224},{224... | collective-permute-start | bytes 786440 | tf_op jit(solution)/shard_map/ppermute | solution.py:38
  35.4 6.9 %collective-permute-done.2 = f32[2,64,2,256]{3,1,2,0:T(8,128)S(1)} collective-permute-done((f32[2,64,2,256]{3,1,2,0:T(8,128)S(1)}, f32[2,64,2,256]{3,1,2,0:T(8,128)S(1)}, u32[]{:S(2)}, u32[]{:S(2)}) %collective-permute-start.2) | collective-permute-done | bytes 262176 | tf_op jit(solution)/shard_map/ppermute | solution.py:38
  43.1 1.9 %collective-permute-start.3 = (f32[2,64,2,256]{3,1,2,0:T(8,128)}, f32[2,64,2,256]{3,1,2,0:T(8,128)}, u32[]{:S(2)}, u32[]{:S(2)}) collective-permute-start(f32[2,64,2,256]{3,1,2,0:T(8,128)} %pad_maximum_fusion.8), channel_id=1, source_target_pairs={{32,0},{64,32},{96,64},{128,96},{160,128},{192,160},{224,192},{256... | collective-permute-start | bytes 786440 | tf_op jit(solution)/shard_map/ppermute | solution.py:37
  45.9 1.9 %stack_reshape.6 = bf16[1,2,32,1536]{3,2,1,0:T(8,128)(2,1)} reshape(bf16[64,6,256]{2,1,0:T(8,128)(2,1)} %copy.28) | data formatting | bytes 393216 | tf_op jit(solution)/shard_map/stack;reshape | solution.py:92
  53.9 3.9 %collective-permute-start.4 = (f32[3,32,32]{2,1,0:T(8,128)S(1)}, f32[3,32,32]{2,1,0:T(8,128)S(1)}, u32[]{:S(2)}, u32[]{:S(2)}) collective-permute-start(f32[3,32,32]{2,1,0:T(8,128)S(1)} %convolution_bitcast_fusion.3), channel_id=1, source_target_pairs={{0,32},{32,0},{64,96},{96,64},{128,160},{160,128},{192,224},{224,1... | collective-permute-start | bytes 36872 | tf_op jit(solution)/shard_map/ppermute | solution.py:16
  58.6 11.2 %collective-permute-start.5 = (f32[3,32,32]{2,1,0:T(8,128)S(1)}, f32[3,32,32]{2,1,0:T(8,128)S(1)}, u32[]{:S(2)}, u32[]{:S(2)}) collective-permute-start(f32[3,32,32]{2,1,0:T(8,128)S(1)} %add.154), channel_id=1, source_target_pairs={{0,64},{32,96},{64,0},{96,32},{128,192},{160,224},{192,128},{224,1... | collective-permute-start | bytes 36872 | tf_op jit(solution)/shard_map/ppermute | solution.py:16
  69.8 2.2 %collective-permute-done.5 = f32[3,32,32]{2,1,0:T(8,128)S(1)} collective-permute-done((f32[3,32,32]{2,1,0:T(8,128)S(1)}, f32[3,32,32]{2,1,0:T(8,128)S(1)}, u32[]{:S(2)}, u32[]{:S(2)}) %collective-permute-start.5) | collective-permute-done | bytes 12320 | tf_op jit(solution)/shard_map/ppermute | solution.py:16
  72.1 1.9 %collective-permute-start.6 = (f32[3,32,32]{2,1,0:T(8,128)S(1)}, f32[3,32,32]{2,1,0:T(8,128)S(1)}, u32[]{:S(2)}, u32[]{:S(2)}) collective-permute-start(f32[3,32,32]{2,1,0:T(8,128)S(1)} %add.155), channel_id=1, source_target_pairs={{0,128},{32,160},{64,192},{96,224},{128,0},{160,32},{192,64},{224,... | collective-permute-start | bytes 36872 | tf_op jit(solution)/shard_map/ppermute | solution.py:16
  74.0 4.1 %collective-permute-done.6 = f32[3,32,32]{2,1,0:T(8,128)S(1)} collective-permute-done((f32[3,32,32]{2,1,0:T(8,128)S(1)}, f32[3,32,32]{2,1,0:T(8,128)S(1)}, u32[]{:S(2)}, u32[]{:S(2)}) %collective-permute-start.6) | collective-permute-done | bytes 12320 | tf_op jit(solution)/shard_map/ppermute | solution.py:16
  78.1 1.9 %collective-permute-start.7 = (f32[3,32,32]{2,1,0:T(8,128)S(1)}, f32[3,32,32]{2,1,0:T(8,128)S(1)}, u32[]{:S(2)}, u32[]{:S(2)}) collective-permute-start(f32[3,32,32]{2,1,0:T(8,128)S(1)} %add.156), channel_id=1, source_target_pairs={{0,256},{32,288},{64,320},{96,352},{128,384},{160,416},{192,448},{... | collective-permute-start | bytes 36872 | tf_op jit(solution)/shard_map/ppermute | solution.py:16
  80.0 5.6 %collective-permute-done.7 = f32[3,32,32]{2,1,0:T(8,128)S(1)} collective-permute-done((f32[3,32,32]{2,1,0:T(8,128)S(1)}, f32[3,32,32]{2,1,0:T(8,128)S(1)}, u32[]{:S(2)}, u32[]{:S(2)}) %collective-permute-start.7) | collective-permute-done | bytes 12320 | tf_op jit(solution)/shard_map/ppermute | solution.py:16
  85.6 1.9 %collective-permute-start.8 = (f32[3,32,32]{2,1,0:T(8,128)S(1)}, f32[3,32,32]{2,1,0:T(8,128)S(1)}, u32[]{:S(2)}, u32[]{:S(2)}) collective-permute-start(f32[3,32,32]{2,1,0:T(8,128)S(1)} %add.157), channel_id=1, source_target_pairs={{0,1},{1,0},{2,3},{3,2},{4,5},{5,4},{6,7},{7,6},{8,9},{9,8},{10,11... | collective-permute-start | bytes 36872 | tf_op jit(solution)/shard_map/ppermute | solution.py:16
  87.5 4.1 %collective-permute-done.8 = f32[3,32,32]{2,1,0:T(8,128)S(1)} collective-permute-done((f32[3,32,32]{2,1,0:T(8,128)S(1)}, f32[3,32,32]{2,1,0:T(8,128)S(1)}, u32[]{:S(2)}, u32[]{:S(2)}) %collective-permute-start.8) | collective-permute-done | bytes 12320 | tf_op jit(solution)/shard_map/ppermute | solution.py:16
  92.2 1.9 %collective-permute-start.9 = (f32[3,32,32]{2,1,0:T(8,128)}, f32[3,32,32]{2,1,0:T(8,128)}, u32[]{:S(2)}, u32[]{:S(2)}) collective-permute-start(f32[3,32,32]{2,1,0:T(8,128)} %add.158), channel_id=1, source_target_pairs={{0,2},{1,3},{2,0},{3,1},{4,6},{5,7},{6,4},{7,5},{8,10},{9,11},{10,... | collective-permute-start | bytes 36872 | tf_op jit(solution)/shard_map/ppermute | solution.py:16
  95.2 4.1 %collective-permute-done.9 = f32[3,32,32]{2,1,0:T(8,128)} collective-permute-done((f32[3,32,32]{2,1,0:T(8,128)}, f32[3,32,32]{2,1,0:T(8,128)}, u32[]{:S(2)}, u32[]{:S(2)}) %collective-permute-start.9) | collective-permute-done | bytes 12320 | tf_op jit(solution)/shard_map/ppermute | solution.py:16
  100.2 4.1 %collective-permute-start.10 = (f32[3,32,32]{2,1,0:T(8,128)S(1)}, f32[3,32,32]{2,1,0:T(8,128)S(1)}, u32[]{:S(2)}, u32[]{:S(2)}) collective-permute-start(f32[3,32,32]{2,1,0:T(8,128)S(1)} %add.159), channel_id=1, source_target_pairs={{0,4},{1,5},{2,6},{3,7},{4,0},{5,1},{6,2},{7,3},{8,12},{9,13},{10,... | collective-permute-start | bytes 36872 | tf_op jit(solution)/shard_map/ppermute | solution.py:16
  105.2 5.9 %collective-permute-done.10 = f32[3,32,32]{2,1,0:T(8,128)S(1)} collective-permute-done((f32[3,32,32]{2,1,0:T(8,128)S(1)}, f32[3,32,32]{2,1,0:T(8,128)S(1)}, u32[]{:S(2)}, u32[]{:S(2)}) %collective-permute-start.10) | collective-permute-done | bytes 12320 | tf_op jit(solution)/shard_map/ppermute | solution.py:16
  111.1 9.3 %collective-permute-start.11 = (f32[3,32,32]{2,1,0:T(8,128)S(1)}, f32[3,32,32]{2,1,0:T(8,128)S(1)}, u32[]{:S(2)}, u32[]{:S(2)}) collective-permute-start(f32[3,32,32]{2,1,0:T(8,128)S(1)} %add.160), channel_id=1, source_target_pairs={{0,8},{1,9},{2,10},{3,11},{4,12},{5,13},{6,14},{7,15},{8,0},{9,1},... | collective-permute-start | bytes 36872 | tf_op jit(solution)/shard_map/ppermute | solution.py:16
  120.7 5.4 %collective-permute-done.11 = f32[3,32,32]{2,1,0:T(8,128)S(1)} collective-permute-done((f32[3,32,32]{2,1,0:T(8,128)S(1)}, f32[3,32,32]{2,1,0:T(8,128)S(1)}, u32[]{:S(2)}, u32[]{:S(2)}) %collective-permute-start.11) | collective-permute-done | bytes 12320 | tf_op jit(solution)/shard_map/ppermute | solution.py:16
  126.1 1.9 %collective-permute-start.12 = (f32[3,32,32]{2,1,0:T(8,128)S(1)}, f32[3,32,32]{2,1,0:T(8,128)S(1)}, u32[]{:S(2)}, u32[]{:S(2)}) collective-permute-start(f32[3,32,32]{2,1,0:T(8,128)S(1)} %add.161), channel_id=1, source_target_pairs={{0,16},{1,17},{2,18},{3,19},{4,20},{5,21},{6,22},{7,23},{8,24},{9,... | collective-permute-start | bytes 36872 | tf_op jit(solution)/shard_map/ppermute | solution.py:16
  128.0 2.1 %fusion.1 = bf16[2,32,1536]{2,1,0:T(8,128)(2,1)} fusion(bf16[1,2,32,1536]{3,2,0,1:T(8,128)(2,1)} %bitcast.180, bf16[1,2,32,1536]{3,2,0,1:T(8,128)(2,1)} %bitcast.178, bf16[1,2,32,1536]{3,2,0,1:T(8,128)(2,1)} %bitcast.176, bf16[3,32,32]{2,1,0:T(8,128)(2,1)} %param.17), kind=kOutput, calls=%fused_computation.3 | convolution fusion | flops 19562496 | bytes 792576 | tf_op jit(solution)/shard_map/kco,kmcp->mop/dot_general | solution.py:93
  (84 shorter events, 34.6 us)
Async XLA Ops:
  0.6 3.4 %copy-start = (bf16[6,3,256,256]{3,2,1,0:T(8,128)(2,1)S(1)}, bf16[6,3,256,256]{3,2,1,0:T(8,128)(2,1)}, u32[]{:S(2)}) copy-start(bf16[6,3,256,256]{3,2,1,0:T(8,128)(2,1)} %param.15) | copy-start | bytes 7077892
  2.0 1.0 copy-start.2
  3.3 2.3 %copy-start.6 = (bf16[2,32,1536]{2,1,0:T(8,128)(2,1)S(1)}, bf16[2,32,1536]{2,1,0:T(8,128)(2,1)}, u32[]{:S(2)}) copy-start(bf16[2,32,1536]{2,1,0:T(8,128)(2,1)} %param.13) | copy-start | bytes 589828
  4.0 3.8 %copy-start.11 = (s32[6,3]{0,1:T(4,128)S(1)}, s32[6,3]{0,1:T(4,128)}, u32[]{:S(2)}) copy-start(s32[6,3]{0,1:T(4,128)} %param.16) | copy-start | bytes 220
  4.5 1.0 copy-start.1
  9.2 10.1 %collective-permute-start = (f32[2,64,2,256]{3,1,2,0:T(8,128)S(1)}, f32[2,64,2,256]{3,1,2,0:T(8,128)S(1)}, u32[]{:S(2)}, u32[]{:S(2)}) collective-permute-start(f32[2,64,2,256]{3,1,2,0:T(8,128)S(1)} %pad_maximum_fusion.5), channel_id=1, source_target_pairs={{0,32},{32,64},{64,96},{96,128},{128,160},{160,192},{192,224},{224... | collective-permute-start | bytes 786440 | tf_op jit(solution)/shard_map/ppermute | solution.py:38
  11.3 10.7 %copy-start.3 = (f32[3,2,32,1536]{3,2,0,1:T(8,128)S(1)}, f32[3,2,32,1536]{3,2,0,1:T(8,128)}, u32[]{:S(2)}) copy-start(f32[3,2,32,1536]{3,2,0,1:T(8,128)} %copy-done.2) | copy-start | bytes 3538948
  19.3 0.8 copy-start.9
  20.1 7.4 %collective-permute-start.1 = (f32[2,64,2,256]{3,1,2,0:T(8,128)}, f32[2,64,2,256]{3,1,2,0:T(8,128)}, u32[]{:S(2)}, u32[]{:S(2)}) collective-permute-start(f32[2,64,2,256]{3,1,2,0:T(8,128)} %pad_maximum_fusion.6), channel_id=1, source_target_pairs={{32,0},{64,32},{96,64},{128,96},{160,128},{192,160},{224,192},{256... | collective-permute-start | bytes 786440 | tf_op jit(solution)/shard_map/ppermute | solution.py:37
  32.1 12.9 %copy-start.8 = (bf16[6,64,256]{2,1,0:T(8,128)(2,1)}, bf16[6,64,256]{2,1,0:T(8,128)(2,1)S(1)}, u32[]{:S(2)}) copy-start(bf16[6,64,256]{2,1,0:T(8,128)(2,1)S(1)} %get-tuple-element.80) | copy-start | bytes 589828
  32.2 10.1 %collective-permute-start.2 = (f32[2,64,2,256]{3,1,2,0:T(8,128)S(1)}, f32[2,64,2,256]{3,1,2,0:T(8,128)S(1)}, u32[]{:S(2)}, u32[]{:S(2)}) collective-permute-start(f32[2,64,2,256]{3,1,2,0:T(8,128)S(1)} %pad_maximum_fusion.7), channel_id=1, source_target_pairs={{0,32},{32,64},{64,96},{96,128},{128,160},{160,192},{192,224},{224... | collective-permute-start | bytes 786440 | tf_op jit(solution)/shard_map/ppermute | solution.py:38
  42.3 0.8 copy-start.10
  43.1 6.1 %collective-permute-start.3 = (f32[2,64,2,256]{3,1,2,0:T(8,128)}, f32[2,64,2,256]{3,1,2,0:T(8,128)}, u32[]{:S(2)}, u32[]{:S(2)}) collective-permute-start(f32[2,64,2,256]{3,1,2,0:T(8,128)} %pad_maximum_fusion.8), channel_id=1, source_target_pairs={{32,0},{64,32},{96,64},{128,96},{160,128},{192,160},{224,192},{256... | collective-permute-start | bytes 786440 | tf_op jit(solution)/shard_map/ppermute | solution.py:37
  52.1 68.4 %copy-start.5 = (bf16[64,6,256]{2,1,0:T(8,128)(2,1)S(1)}, bf16[64,6,256]{2,1,0:T(8,128)(2,1)}, u32[]{:S(2)}) copy-start(bf16[64,6,256]{2,1,0:T(8,128)(2,1)} %copy-done.4) | copy-start | bytes 589828
  52.4 41.7 %copy-start.7 = (bf16[1,2,32,1536]{3,2,1,0:T(8,128)(2,1)}, bf16[1,2,32,1536]{3,2,1,0:T(8,128)(2,1)S(1)}, u32[]{:S(2)}) copy-start(bf16[1,2,32,1536]{3,2,1,0:T(8,128)(2,1)S(1)} %stack_reshape.7) | copy-start | bytes 589828
  53.9 4.8 %collective-permute-start.4 = (f32[3,32,32]{2,1,0:T(8,128)S(1)}, f32[3,32,32]{2,1,0:T(8,128)S(1)}, u32[]{:S(2)}, u32[]{:S(2)}) collective-permute-start(f32[3,32,32]{2,1,0:T(8,128)S(1)} %convolution_bitcast_fusion.3), channel_id=1, source_target_pairs={{0,32},{32,0},{64,96},{96,64},{128,160},{160,128},{192,224},{224,1... | collective-permute-start | bytes 36872 | tf_op jit(solution)/shard_map/ppermute | solution.py:16
  58.6 13.4 %collective-permute-start.5 = (f32[3,32,32]{2,1,0:T(8,128)S(1)}, f32[3,32,32]{2,1,0:T(8,128)S(1)}, u32[]{:S(2)}, u32[]{:S(2)}) collective-permute-start(f32[3,32,32]{2,1,0:T(8,128)S(1)} %add.154), channel_id=1, source_target_pairs={{0,64},{32,96},{64,0},{96,32},{128,192},{160,224},{192,128},{224,1... | collective-permute-start | bytes 36872 | tf_op jit(solution)/shard_map/ppermute | solution.py:16
  72.1 6.0 %collective-permute-start.6 = (f32[3,32,32]{2,1,0:T(8,128)S(1)}, f32[3,32,32]{2,1,0:T(8,128)S(1)}, u32[]{:S(2)}, u32[]{:S(2)}) collective-permute-start(f32[3,32,32]{2,1,0:T(8,128)S(1)} %add.155), channel_id=1, source_target_pairs={{0,128},{32,160},{64,192},{96,224},{128,0},{160,32},{192,64},{224,... | collective-permute-start | bytes 36872 | tf_op jit(solution)/shard_map/ppermute | solution.py:16
  78.1 7.5 %collective-permute-start.7 = (f32[3,32,32]{2,1,0:T(8,128)S(1)}, f32[3,32,32]{2,1,0:T(8,128)S(1)}, u32[]{:S(2)}, u32[]{:S(2)}) collective-permute-start(f32[3,32,32]{2,1,0:T(8,128)S(1)} %add.156), channel_id=1, source_target_pairs={{0,256},{32,288},{64,320},{96,352},{128,384},{160,416},{192,448},{... | collective-permute-start | bytes 36872 | tf_op jit(solution)/shard_map/ppermute | solution.py:16
  85.6 6.0 %collective-permute-start.8 = (f32[3,32,32]{2,1,0:T(8,128)S(1)}, f32[3,32,32]{2,1,0:T(8,128)S(1)}, u32[]{:S(2)}, u32[]{:S(2)}) collective-permute-start(f32[3,32,32]{2,1,0:T(8,128)S(1)} %add.157), channel_id=1, source_target_pairs={{0,1},{1,0},{2,3},{3,2},{4,5},{5,4},{6,7},{7,6},{8,9},{9,8},{10,11... | collective-permute-start | bytes 36872 | tf_op jit(solution)/shard_map/ppermute | solution.py:16
  92.2 7.2 %collective-permute-start.9 = (f32[3,32,32]{2,1,0:T(8,128)}, f32[3,32,32]{2,1,0:T(8,128)}, u32[]{:S(2)}, u32[]{:S(2)}) collective-permute-start(f32[3,32,32]{2,1,0:T(8,128)} %add.158), channel_id=1, source_target_pairs={{0,2},{1,3},{2,0},{3,1},{4,6},{5,7},{6,4},{7,5},{8,10},{9,11},{10,... | collective-permute-start | bytes 36872 | tf_op jit(solution)/shard_map/ppermute | solution.py:16
  100.2 10.9 %collective-permute-start.10 = (f32[3,32,32]{2,1,0:T(8,128)S(1)}, f32[3,32,32]{2,1,0:T(8,128)S(1)}, u32[]{:S(2)}, u32[]{:S(2)}) collective-permute-start(f32[3,32,32]{2,1,0:T(8,128)S(1)} %add.159), channel_id=1, source_target_pairs={{0,4},{1,5},{2,6},{3,7},{4,0},{5,1},{6,2},{7,3},{8,12},{9,13},{10,... | collective-permute-start | bytes 36872 | tf_op jit(solution)/shard_map/ppermute | solution.py:16
  111.1 14.9 %collective-permute-start.11 = (f32[3,32,32]{2,1,0:T(8,128)S(1)}, f32[3,32,32]{2,1,0:T(8,128)S(1)}, u32[]{:S(2)}, u32[]{:S(2)}) collective-permute-start(f32[3,32,32]{2,1,0:T(8,128)S(1)} %add.160), channel_id=1, source_target_pairs={{0,8},{1,9},{2,10},{3,11},{4,12},{5,13},{6,14},{7,15},{8,0},{9,1},... | collective-permute-start | bytes 36872 | tf_op jit(solution)/shard_map/ppermute | solution.py:16
  126.1 6.0 %collective-permute-start.12 = (f32[3,32,32]{2,1,0:T(8,128)S(1)}, f32[3,32,32]{2,1,0:T(8,128)S(1)}, u32[]{:S(2)}, u32[]{:S(2)}) collective-permute-start(f32[3,32,32]{2,1,0:T(8,128)S(1)} %add.161), channel_id=1, source_target_pairs={{0,16},{1,17},{2,18},{3,19},{4,20},{5,21},{6,22},{7,23},{8,24},{9,... | collective-permute-start | bytes 36872 | tf_op jit(solution)/shard_map/ppermute | solution.py:16
  (1 other events, 0.7 us)

commit v2 on v1

--- a/solution.py
+++ b/solution.py
@@ -8,7 +8,54 @@
 REACH = 2
 
 
+def ring_partner(coord, size, level):
+    if size == 4 and level == 1:
+        return (coord + 1) % size if coord % 2 else (coord - 1) % size
+    return coord ^ (1 << level)
+
+
+def torus_steps(patch_count, map_count):
+    def coords(p, m):
+        return dict(y=p // 4, x=((p // 2) % 2) * 2 + m // 16, z=m % 16, core=p % 2)
+
+    def linear(c):
+        p = c["y"] * 4 + (c["x"] // 2) * 2 + c["core"]
+        return p * map_count + (c["x"] % 2) * 16 + c["z"]
+
+    sizes = dict(core=2, x=4, y=4, z=16)
+    plan = [("core", 0), ("x", 0), ("x", 1), ("y", 0), ("y", 1), ("z", 0), ("z", 1)]
+    steps = []
+    for name, level in plan:
+        pairs = []
+        for p in range(patch_count):
+            for m in range(map_count):
+                c = coords(p, m)
+                d = dict(c)
+                d[name] = ring_partner(c[name], sizes[name], level)
+                pairs.append((linear(c), linear(d)))
+        steps.append(pairs)
+    for odd_up in (False, True):
+        pairs = []
+        for p in range(patch_count):
+            for m in range(map_count):
+                c = coords(p, m)
+                d = dict(c)
+                g = c["z"] // 4
+                if not odd_up:
+                    d["z"] = c["z"] ^ 4
+                else:
+                    d["z"] = (c["z"] + 4) % 16 if g % 2 else (c["z"] - 4) % 16
+                pairs.append((linear(c), linear(d)))
+        steps.append(pairs)
+    return steps
+
+
 def butterfly_sum(x, axes):
+    patch_count, map_count = (lax.axis_size(a) for a in axes)
+    if (patch_count, map_count) == (16, 32):
+        for pairs in torus_steps(patch_count, map_count):
+            x = x + lax.ppermute(x, axes, pairs)
+        return x
     for axis in axes:
         count = lax.axis_size(axis)
         step = 1

time: 134 us -> 129 us (0.963)
  waiting for transfers between devices: 48.6 us -> 41.5 us
  starting transfers between devices: 46.8 us -> 48.8 us
    ppermute x9, waiting for transfers between devices: 33.2 us -> 26.1 us  [butterfly_sum(): x = x + lax.ppermute(x, axes, pairs)]
    ppermute x9, starting transfers between devices: 38.1 us -> 40 us  [butterfly_sum(): x = x + lax.ppermute(x, axes, pairs)]
  transfers between devices with their start and end apart: 13 -> 13, of which waited for: 12 -> 11; matrix products, arithmetic and copies ran while one was open for 11% -> 12% of each run, Pallas kernels for 0% -> 0%
where the time goes in v2:
time: 129 us; the launch traced here: 128 us
  starting transfers between devices  48.8 us (38%)
  waiting for transfers between devices  41.5 us (32%)
  local copies, waits for them, and re-layouts  18.7 us (14%)
  matrix products  9.52 us (7%)
  other arithmetic  7.97 us (6%)
    ppermute x9, starting transfers between devices, butterfly_sum(): x = x + lax.ppermute(x, axes, pairs)  40 us
    ppermute x9, waiting for transfers between devices, butterfly_sum(): x = x + lax.ppermute(x, axes, pairs)  26.1 us
    ppermute x2, waiting for transfers between devices, exchange(): from_left = lax.ppermute(edge_right, 'patch', to_right)  14.9 us
    convert_element_type x4, local copies, waits for them, and re-layouts, per_device(): x0f = x_zero.astype(jnp.float32)  5 us
    ppermute x2, starting transfers between devices, exchange(): from_left = lax.ppermute(edge_right, 'patch', to_right)  4.93 us
    ppermute x2, starting transfers between devices, exchange(): from_right = lax.ppermute(edge_left, 'patch', to_left)  3.82 us
    unnamed x24, local copies, waits for them, and re-layouts  2.77 us
    dot_general x2, matrix products, forward_local(): jnp.einsum('nrjq,rjiq->nri', picked, tiles, preferred_element_type=jnp.fl...  2.6 us
  transfers between devices with their start and end apart: 13, of which 11 were waited for; matrix products, arithmetic and copies ran while one was open for 12% of the time, Pallas kernels for 0%

profile of v2, /device:TPU:24, one launch (start us, length us, event | category | flops | bytes accessed | tf_op | source)
XLA Modules:
  0.0 127.6 jit_solution(1478544434071113589)
XLA Ops:
  9.2 1.9 %collective-permute-start = (f32[2,64,2,256]{3,1,2,0:T(8,128)S(1)}, f32[2,64,2,256]{3,1,2,0:T(8,128)S(1)}, u32[]{:S(2)}, u32[]{:S(2)}) collective-permute-start(f32[2,64,2,256]{3,1,2,0:T(8,128)S(1)} %pad_maximum_fusion.5), channel_id=1, source_target_pairs={{0,32},{32,64},{64,96},{96,128},{128,160},{160,192},{192,224},{224... | collective-permute-start | bytes 786440 | tf_op jit(solution)/shard_map/ppermute | solution.py:85
  11.3 8.0 %collective-permute-done = f32[2,64,2,256]{3,1,2,0:T(8,128)S(1)} collective-permute-done((f32[2,64,2,256]{3,1,2,0:T(8,128)S(1)}, f32[2,64,2,256]{3,1,2,0:T(8,128)S(1)}, u32[]{:S(2)}, u32[]{:S(2)}) %collective-permute-start) | collective-permute-done | bytes 262176 | tf_op jit(solution)/shard_map/ppermute | solution.py:85
  20.1 1.9 %collective-permute-start.1 = (f32[2,64,2,256]{3,1,2,0:T(8,128)}, f32[2,64,2,256]{3,1,2,0:T(8,128)}, u32[]{:S(2)}, u32[]{:S(2)}) collective-permute-start(f32[2,64,2,256]{3,1,2,0:T(8,128)} %pad_maximum_fusion.6), channel_id=1, source_target_pairs={{32,0},{64,32},{96,64},{128,96},{160,128},{192,160},{224,192},{256... | collective-permute-start | bytes 786440 | tf_op jit(solution)/shard_map/ppermute | solution.py:84
  32.2 3.0 %collective-permute-start.2 = (f32[2,64,2,256]{3,1,2,0:T(8,128)S(1)}, f32[2,64,2,256]{3,1,2,0:T(8,128)S(1)}, u32[]{:S(2)}, u32[]{:S(2)}) collective-permute-start(f32[2,64,2,256]{3,1,2,0:T(8,128)S(1)} %pad_maximum_fusion.7), channel_id=1, source_target_pairs={{0,32},{32,64},{64,96},{96,128},{128,160},{160,192},{192,224},{224... | collective-permute-start | bytes 786440 | tf_op jit(solution)/shard_map/ppermute | solution.py:85
  35.4 6.9 %collective-permute-done.2 = f32[2,64,2,256]{3,1,2,0:T(8,128)S(1)} collective-permute-done((f32[2,64,2,256]{3,1,2,0:T(8,128)S(1)}, f32[2,64,2,256]{3,1,2,0:T(8,128)S(1)}, u32[]{:S(2)}, u32[]{:S(2)}) %collective-permute-start.2) | collective-permute-done | bytes 262176 | tf_op jit(solution)/shard_map/ppermute | solution.py:85
  43.1 1.9 %collective-permute-start.3 = (f32[2,64,2,256]{3,1,2,0:T(8,128)}, f32[2,64,2,256]{3,1,2,0:T(8,128)}, u32[]{:S(2)}, u32[]{:S(2)}) collective-permute-start(f32[2,64,2,256]{3,1,2,0:T(8,128)} %pad_maximum_fusion.8), channel_id=1, source_target_pairs={{32,0},{64,32},{96,64},{128,96},{160,128},{192,160},{224,192},{256... | collective-permute-start | bytes 786440 | tf_op jit(solution)/shard_map/ppermute | solution.py:84
  45.9 1.9 %stack_reshape.6 = bf16[1,2,32,1536]{3,2,1,0:T(8,128)(2,1)} reshape(bf16[64,6,256]{2,1,0:T(8,128)(2,1)} %copy.28) | data formatting | bytes 393216 | tf_op jit(solution)/shard_map/stack;reshape | solution.py:139
  53.9 3.9 %collective-permute-start.4 = (f32[3,32,32]{2,1,0:T(8,128)S(1)}, f32[3,32,32]{2,1,0:T(8,128)S(1)}, u32[]{:S(2)}, u32[]{:S(2)}) collective-permute-start(f32[3,32,32]{2,1,0:T(8,128)S(1)} %convolution_bitcast_fusion.3), channel_id=1, source_target_pairs={{0,32},{1,33},{2,34},{3,35},{4,36},{5,37},{6,38},{7,39},{8,40},{9,... | collective-permute-start | bytes 36872 | tf_op jit(solution)/shard_map/ppermute | solution.py:57
  58.6 2.0 %collective-permute-start.5 = (f32[3,32,32]{2,1,0:T(8,128)S(1)}, f32[3,32,32]{2,1,0:T(8,128)S(1)}, u32[]{:S(2)}, u32[]{:S(2)}) collective-permute-start(f32[3,32,32]{2,1,0:T(8,128)S(1)} %add.154), channel_id=1, source_target_pairs={{0,16},{1,17},{2,18},{3,19},{4,20},{5,21},{6,22},{7,23},{8,24},{9,... | collective-permute-start | bytes 36872 | tf_op jit(solution)/shard_map/ppermute | solution.py:57
  60.7 4.0 %collective-permute-done.5 = f32[3,32,32]{2,1,0:T(8,128)S(1)} collective-permute-done((f32[3,32,32]{2,1,0:T(8,128)S(1)}, f32[3,32,32]{2,1,0:T(8,128)S(1)}, u32[]{:S(2)}, u32[]{:S(2)}) %collective-permute-start.5) | collective-permute-done | bytes 12320 | tf_op jit(solution)/shard_map/ppermute | solution.py:57
  64.6 9.9 %collective-permute-start.6 = (f32[3,32,32]{2,1,0:T(8,128)S(1)}, f32[3,32,32]{2,1,0:T(8,128)S(1)}, u32[]{:S(2)}, u32[]{:S(2)}) collective-permute-start(f32[3,32,32]{2,1,0:T(8,128)S(1)} %add.155), channel_id=1, source_target_pairs={{0,80},{1,81},{2,82},{3,83},{4,84},{5,85},{6,86},{7,87},{8,88},{9,... | collective-permute-start | bytes 36872 | tf_op jit(solution)/shard_map/ppermute | solution.py:57
  74.6 2.1 %collective-permute-done.6 = f32[3,32,32]{2,1,0:T(8,128)S(1)} collective-permute-done((f32[3,32,32]{2,1,0:T(8,128)S(1)}, f32[3,32,32]{2,1,0:T(8,128)S(1)}, u32[]{:S(2)}, u32[]{:S(2)}) %collective-permute-start.6) | collective-permute-done | bytes 12320 | tf_op jit(solution)/shard_map/ppermute | solution.py:57
  76.6 1.9 %collective-permute-start.7 = (f32[3,32,32]{2,1,0:T(8,128)S(1)}, f32[3,32,32]{2,1,0:T(8,128)S(1)}, u32[]{:S(2)}, u32[]{:S(2)}) collective-permute-start(f32[3,32,32]{2,1,0:T(8,128)S(1)} %add.156), channel_id=1, source_target_pairs={{0,128},{1,129},{2,130},{3,131},{4,132},{5,133},{6,134},{7,135},{8... | collective-permute-start | bytes 36872 | tf_op jit(solution)/shard_map/ppermute | solution.py:57
  78.6 4.1 %collective-permute-done.7 = f32[3,32,32]{2,1,0:T(8,128)S(1)} collective-permute-done((f32[3,32,32]{2,1,0:T(8,128)S(1)}, f32[3,32,32]{2,1,0:T(8,128)S(1)}, u32[]{:S(2)}, u32[]{:S(2)}) %collective-permute-start.7) | collective-permute-done | bytes 12320 | tf_op jit(solution)/shard_map/ppermute | solution.py:57
  82.6 3.5 %collective-permute-start.8 = (f32[3,32,32]{2,1,0:T(8,128)S(1)}, f32[3,32,32]{2,1,0:T(8,128)S(1)}, u32[]{:S(2)}, u32[]{:S(2)}) collective-permute-start(f32[3,32,32]{2,1,0:T(8,128)S(1)} %add.157), channel_id=1, source_target_pairs={{0,384},{1,385},{2,386},{3,387},{4,388},{5,389},{6,390},{7,391},{8... | collective-permute-start | bytes 36872 | tf_op jit(solution)/shard_map/ppermute | solution.py:57
  86.1 3.7 %collective-permute-done.8 = f32[3,32,32]{2,1,0:T(8,128)S(1)} collective-permute-done((f32[3,32,32]{2,1,0:T(8,128)S(1)}, f32[3,32,32]{2,1,0:T(8,128)S(1)}, u32[]{:S(2)}, u32[]{:S(2)}) %collective-permute-start.8) | collective-permute-done | bytes 12320 | tf_op jit(solution)/shard_map/ppermute | solution.py:57
  90.4 1.9 %collective-permute-start.9 = (f32[3,32,32]{2,1,0:T(8,128)}, f32[3,32,32]{2,1,0:T(8,128)}, u32[]{:S(2)}, u32[]{:S(2)}) collective-permute-start(f32[3,32,32]{2,1,0:T(8,128)} %add.158), channel_id=1, source_target_pairs={{0,1},{1,0},{2,3},{3,2},{4,5},{5,4},{6,7},{7,6},{8,9},{9,8},{10,11... | collective-permute-start | bytes 36872 | tf_op jit(solution)/shard_map/ppermute | solution.py:57
  93.5 3.2 %collective-permute-done.9 = f32[3,32,32]{2,1,0:T(8,128)} collective-permute-done((f32[3,32,32]{2,1,0:T(8,128)}, f32[3,32,32]{2,1,0:T(8,128)}, u32[]{:S(2)}, u32[]{:S(2)}) %collective-permute-start.9) | collective-permute-done | bytes 12320 | tf_op jit(solution)/shard_map/ppermute | solution.py:57
  97.6 1.9 %collective-permute-start.10 = (f32[3,32,32]{2,1,0:T(8,128)S(1)}, f32[3,32,32]{2,1,0:T(8,128)S(1)}, u32[]{:S(2)}, u32[]{:S(2)}) collective-permute-start(f32[3,32,32]{2,1,0:T(8,128)S(1)} %add.159), channel_id=1, source_target_pairs={{0,2},{1,3},{2,0},{3,1},{4,6},{5,7},{6,4},{7,5},{8,10},{9,11},{10,... | collective-permute-start | bytes 36872 | tf_op jit(solution)/shard_map/ppermute | solution.py:57
  100.4 4.0 %collective-permute-done.10 = f32[3,32,32]{2,1,0:T(8,128)S(1)} collective-permute-done((f32[3,32,32]{2,1,0:T(8,128)S(1)}, f32[3,32,32]{2,1,0:T(8,128)S(1)}, u32[]{:S(2)}, u32[]{:S(2)}) %collective-permute-start.10) | collective-permute-done | bytes 12320 | tf_op jit(solution)/shard_map/ppermute | solution.py:57
  104.4 6.4 %collective-permute-start.11 = (f32[3,32,32]{2,1,0:T(8,128)S(1)}, f32[3,32,32]{2,1,0:T(8,128)S(1)}, u32[]{:S(2)}, u32[]{:S(2)}) collective-permute-start(f32[3,32,32]{2,1,0:T(8,128)S(1)} %add.160), channel_id=1, source_target_pairs={{0,4},{1,5},{2,6},{3,7},{4,0},{5,1},{6,2},{7,3},{8,12},{9,13},{10,... | collective-permute-start | bytes 36872 | tf_op jit(solution)/shard_map/ppermute | solution.py:57
  111.0 4.2 %collective-permute-done.11 = f32[3,32,32]{2,1,0:T(8,128)S(1)} collective-permute-done((f32[3,32,32]{2,1,0:T(8,128)S(1)}, f32[3,32,32]{2,1,0:T(8,128)S(1)}, u32[]{:S(2)}, u32[]{:S(2)}) %collective-permute-start.11) | collective-permute-done | bytes 12320 | tf_op jit(solution)/shard_map/ppermute | solution.py:57
  115.2 8.6 %collective-permute-start.12 = (f32[3,32,32]{2,1,0:T(8,128)S(1)}, f32[3,32,32]{2,1,0:T(8,128)S(1)}, u32[]{:S(2)}, u32[]{:S(2)}) collective-permute-start(f32[3,32,32]{2,1,0:T(8,128)S(1)} %add.161), channel_id=1, source_target_pairs={{0,12},{1,13},{2,14},{3,15},{4,8},{5,9},{6,10},{7,11},{8,4},{9,5},... | collective-permute-start | bytes 36872 | tf_op jit(solution)/shard_map/ppermute | solution.py:57
  123.8 2.1 %fusion.1 = bf16[2,32,1536]{2,1,0:T(8,128)(2,1)} fusion(bf16[1,2,32,1536]{3,2,0,1:T(8,128)(2,1)} %bitcast.180, bf16[1,2,32,1536]{3,2,0,1:T(8,128)(2,1)} %bitcast.178, bf16[1,2,32,1536]{3,2,0,1:T(8,128)(2,1)} %bitcast.176, bf16[3,32,32]{2,1,0:T(8,128)(2,1)} %param.17), kind=kOutput, calls=%fused_computation.3 | convolution fusion | flops 19562496 | bytes 792576 | tf_op jit(solution)/shard_map/kco,kmcp->mop/dot_general | solution.py:140
  (84 shorter events, 33.7 us)
Async XLA Ops:
  0.6 3.4 %copy-start = (bf16[6,3,256,256]{3,2,1,0:T(8,128)(2,1)S(1)}, bf16[6,3,256,256]{3,2,1,0:T(8,128)(2,1)}, u32[]{:S(2)}) copy-start(bf16[6,3,256,256]{3,2,1,0:T(8,128)(2,1)} %param.15) | copy-start | bytes 7077892
  2.0 1.0 copy-start.2
  3.3 2.3 %copy-start.6 = (bf16[2,32,1536]{2,1,0:T(8,128)(2,1)S(1)}, bf16[2,32,1536]{2,1,0:T(8,128)(2,1)}, u32[]{:S(2)}) copy-start(bf16[2,32,1536]{2,1,0:T(8,128)(2,1)} %param.13) | copy-start | bytes 589828
  4.0 3.8 %copy-start.11 = (s32[6,3]{0,1:T(4,128)S(1)}, s32[6,3]{0,1:T(4,128)}, u32[]{:S(2)}) copy-start(s32[6,3]{0,1:T(4,128)} %param.16) | copy-start | bytes 220
  4.5 1.0 copy-start.1
  9.2 10.1 %collective-permute-start = (f32[2,64,2,256]{3,1,2,0:T(8,128)S(1)}, f32[2,64,2,256]{3,1,2,0:T(8,128)S(1)}, u32[]{:S(2)}, u32[]{:S(2)}) collective-permute-start(f32[2,64,2,256]{3,1,2,0:T(8,128)S(1)} %pad_maximum_fusion.5), channel_id=1, source_target_pairs={{0,32},{32,64},{64,96},{96,128},{128,160},{160,192},{192,224},{224... | collective-permute-start | bytes 786440 | tf_op jit(solution)/shard_map/ppermute | solution.py:85
  11.3 10.7 %copy-start.3 = (f32[3,2,32,1536]{3,2,0,1:T(8,128)S(1)}, f32[3,2,32,1536]{3,2,0,1:T(8,128)}, u32[]{:S(2)}) copy-start(f32[3,2,32,1536]{3,2,0,1:T(8,128)} %copy-done.2) | copy-start | bytes 3538948
  19.3 0.8 copy-start.9
  20.1 7.4 %collective-permute-start.1 = (f32[2,64,2,256]{3,1,2,0:T(8,128)}, f32[2,64,2,256]{3,1,2,0:T(8,128)}, u32[]{:S(2)}, u32[]{:S(2)}) collective-permute-start(f32[2,64,2,256]{3,1,2,0:T(8,128)} %pad_maximum_fusion.6), channel_id=1, source_target_pairs={{32,0},{64,32},{96,64},{128,96},{160,128},{192,160},{224,192},{256... | collective-permute-start | bytes 786440 | tf_op jit(solution)/shard_map/ppermute | solution.py:84
  32.1 12.9 %copy-start.8 = (bf16[6,64,256]{2,1,0:T(8,128)(2,1)}, bf16[6,64,256]{2,1,0:T(8,128)(2,1)S(1)}, u32[]{:S(2)}) copy-start(bf16[6,64,256]{2,1,0:T(8,128)(2,1)S(1)} %get-tuple-element.80) | copy-start | bytes 589828
  32.2 10.1 %collective-permute-start.2 = (f32[2,64,2,256]{3,1,2,0:T(8,128)S(1)}, f32[2,64,2,256]{3,1,2,0:T(8,128)S(1)}, u32[]{:S(2)}, u32[]{:S(2)}) collective-permute-start(f32[2,64,2,256]{3,1,2,0:T(8,128)S(1)} %pad_maximum_fusion.7), channel_id=1, source_target_pairs={{0,32},{32,64},{64,96},{96,128},{128,160},{160,192},{192,224},{224... | collective-permute-start | bytes 786440 | tf_op jit(solution)/shard_map/ppermute | solution.py:85
  42.3 0.8 copy-start.10
  43.1 6.1 %collective-permute-start.3 = (f32[2,64,2,256]{3,1,2,0:T(8,128)}, f32[2,64,2,256]{3,1,2,0:T(8,128)}, u32[]{:S(2)}, u32[]{:S(2)}) collective-permute-start(f32[2,64,2,256]{3,1,2,0:T(8,128)} %pad_maximum_fusion.8), channel_id=1, source_target_pairs={{32,0},{64,32},{96,64},{128,96},{160,128},{192,160},{224,192},{256... | collective-permute-start | bytes 786440 | tf_op jit(solution)/shard_map/ppermute | solution.py:84
  52.1 58.7 %copy-start.5 = (bf16[64,6,256]{2,1,0:T(8,128)(2,1)S(1)}, bf16[64,6,256]{2,1,0:T(8,128)(2,1)}, u32[]{:S(2)}) copy-start(bf16[64,6,256]{2,1,0:T(8,128)(2,1)} %copy-done.4) | copy-start | bytes 589828
  52.4 40.0 %copy-start.7 = (bf16[1,2,32,1536]{3,2,1,0:T(8,128)(2,1)}, bf16[1,2,32,1536]{3,2,1,0:T(8,128)(2,1)S(1)}, u32[]{:S(2)}) copy-start(bf16[1,2,32,1536]{3,2,1,0:T(8,128)(2,1)S(1)} %stack_reshape.7) | copy-start | bytes 589828
  53.9 4.8 %collective-permute-start.4 = (f32[3,32,32]{2,1,0:T(8,128)S(1)}, f32[3,32,32]{2,1,0:T(8,128)S(1)}, u32[]{:S(2)}, u32[]{:S(2)}) collective-permute-start(f32[3,32,32]{2,1,0:T(8,128)S(1)} %convolution_bitcast_fusion.3), channel_id=1, source_target_pairs={{0,32},{1,33},{2,34},{3,35},{4,36},{5,37},{6,38},{7,39},{8,40},{9,... | collective-permute-start | bytes 36872 | tf_op jit(solution)/shard_map/ppermute | solution.py:57
  58.6 6.0 %collective-permute-start.5 = (f32[3,32,32]{2,1,0:T(8,128)S(1)}, f32[3,32,32]{2,1,0:T(8,128)S(1)}, u32[]{:S(2)}, u32[]{:S(2)}) collective-permute-start(f32[3,32,32]{2,1,0:T(8,128)S(1)} %add.154), channel_id=1, source_target_pairs={{0,16},{1,17},{2,18},{3,19},{4,20},{5,21},{6,22},{7,23},{8,24},{9,... | collective-permute-start | bytes 36872 | tf_op jit(solution)/shard_map/ppermute | solution.py:57
  64.6 12.0 %collective-permute-start.6 = (f32[3,32,32]{2,1,0:T(8,128)S(1)}, f32[3,32,32]{2,1,0:T(8,128)S(1)}, u32[]{:S(2)}, u32[]{:S(2)}) collective-permute-start(f32[3,32,32]{2,1,0:T(8,128)S(1)} %add.155), channel_id=1, source_target_pairs={{0,80},{1,81},{2,82},{3,83},{4,84},{5,85},{6,86},{7,87},{8,88},{9,... | collective-permute-start | bytes 36872 | tf_op jit(solution)/shard_map/ppermute | solution.py:57
  76.6 6.0 %collective-permute-start.7 = (f32[3,32,32]{2,1,0:T(8,128)S(1)}, f32[3,32,32]{2,1,0:T(8,128)S(1)}, u32[]{:S(2)}, u32[]{:S(2)}) collective-permute-start(f32[3,32,32]{2,1,0:T(8,128)S(1)} %add.156), channel_id=1, source_target_pairs={{0,128},{1,129},{2,130},{3,131},{4,132},{5,133},{6,134},{7,135},{8... | collective-permute-start | bytes 36872 | tf_op jit(solution)/shard_map/ppermute | solution.py:57
  82.6 7.2 %collective-permute-start.8 = (f32[3,32,32]{2,1,0:T(8,128)S(1)}, f32[3,32,32]{2,1,0:T(8,128)S(1)}, u32[]{:S(2)}, u32[]{:S(2)}) collective-permute-start(f32[3,32,32]{2,1,0:T(8,128)S(1)} %add.157), channel_id=1, source_target_pairs={{0,384},{1,385},{2,386},{3,387},{4,388},{5,389},{6,390},{7,391},{8... | collective-permute-start | bytes 36872 | tf_op jit(solution)/shard_map/ppermute | solution.py:57
  90.4 6.3 %collective-permute-start.9 = (f32[3,32,32]{2,1,0:T(8,128)}, f32[3,32,32]{2,1,0:T(8,128)}, u32[]{:S(2)}, u32[]{:S(2)}) collective-permute-start(f32[3,32,32]{2,1,0:T(8,128)} %add.158), channel_id=1, source_target_pairs={{0,1},{1,0},{2,3},{3,2},{4,5},{5,4},{6,7},{7,6},{8,9},{9,8},{10,11... | collective-permute-start | bytes 36872 | tf_op jit(solution)/shard_map/ppermute | solution.py:57
  97.6 6.9 %collective-permute-start.10 = (f32[3,32,32]{2,1,0:T(8,128)S(1)}, f32[3,32,32]{2,1,0:T(8,128)S(1)}, u32[]{:S(2)}, u32[]{:S(2)}) collective-permute-start(f32[3,32,32]{2,1,0:T(8,128)S(1)} %add.159), channel_id=1, source_target_pairs={{0,2},{1,3},{2,0},{3,1},{4,6},{5,7},{6,4},{7,5},{8,10},{9,11},{10,... | collective-permute-start | bytes 36872 | tf_op jit(solution)/shard_map/ppermute | solution.py:57
  104.4 10.8 %collective-permute-start.11 = (f32[3,32,32]{2,1,0:T(8,128)S(1)}, f32[3,32,32]{2,1,0:T(8,128)S(1)}, u32[]{:S(2)}, u32[]{:S(2)}) collective-permute-start(f32[3,32,32]{2,1,0:T(8,128)S(1)} %add.160), channel_id=1, source_target_pairs={{0,4},{1,5},{2,6},{3,7},{4,0},{5,1},{6,2},{7,3},{8,12},{9,13},{10,... | collective-permute-start | bytes 36872 | tf_op jit(solution)/shard_map/ppermute | solution.py:57
  115.2 11.7 %collective-permute-start.12 = (f32[3,32,32]{2,1,0:T(8,128)S(1)}, f32[3,32,32]{2,1,0:T(8,128)S(1)}, u32[]{:S(2)}, u32[]{:S(2)}) collective-permute-start(f32[3,32,32]{2,1,0:T(8,128)S(1)} %add.161), channel_id=1, source_target_pairs={{0,12},{1,13},{2,14},{3,15},{4,8},{5,9},{6,10},{7,11},{8,4},{9,5},... | collective-permute-start | bytes 36872 | tf_op jit(solution)/shard_map/ppermute | solution.py:57
  (1 other events, 0.7 us)

commit v3 on v2

--- a/solution.py
+++ b/solution.py
@@ -112,9 +112,13 @@
     grad_two = grads[2].astype(jnp.bfloat16)
 
     win1 = adjoint_window(grad_two)
+    cot_rows = cotangent.reshape(row_count, nb, block_size)
+    winc = adjoint_window(cot_rows)
     x0f = x_zero.astype(jnp.float32)
-    send_left = jnp.stack([x0f[:, 0:2], win1[:, 0:2]])
-    send_right = jnp.stack([x0f[:, nb - 2 : nb], win1[:, nb + 2 : nb + 4]])
+    send_left = jnp.stack([x0f[:, 0:2], win1[:, 0:2], winc[:, 0:2]])
+    send_right = jnp.stack(
+        [x0f[:, nb - 2 : nb], win1[:, nb + 2 : nb + 4], winc[:, nb + 2 : nb + 4]]
+    )
     got_left, got_right = exchange(send_left, send_right)
     ext0 = jnp.concatenate([got_left[0], x0f, got_right[0]], axis=1)
     x_one = forward_local(ext0).astype(jnp.bfloat16)
@@ -122,6 +126,24 @@
     adj1 = adj1.at[:, 0:2].add(got_left[1])
     adj1 = adj1.at[:, nb - 2 : nb].add(got_right[1])
     update = (grads[1] + 2.0 * adj1).astype(jnp.bfloat16)
+    lt_cot = winc[:, 2 : 2 + nb]
+    lt_cot = lt_cot.at[:, 0:2].add(got_left[2])
+    lt_cot = lt_cot.at[:, nb - 2 : nb].add(got_right[2])
+
+    shape3 = (map_count, chan_count, pix_count)
+    x_one3 = x_one.reshape(shape3)
+    g_zero = jnp.einsum("mcp,mop->co", maps, cotangent, preferred_element_type=jnp.float32)
+    g_one = jnp.einsum("mcp,mop->co", x_one3, cotangent, preferred_element_type=jnp.float32)
+    g_cross = jnp.einsum(
+        "mcp,mop->co",
+        x_one3.astype(jnp.float32),
+        lt_cot.reshape(shape3),
+        preferred_element_type=jnp.float32,
+        precision=lax.Precision.HIGHEST,
+    )
+    local_grad = jnp.stack([g_zero, g_one, 2.0 * g_cross - g_zero])
+    scale = 1.0 / math.sqrt(map_count * lax.axis_size("map") * pix_count * patch_count)
+    filter_grad = butterfly_sum(local_grad, ("patch", "map")) * scale
 
     win2 = adjoint_window(update)
     x1f = x_one.astype(jnp.float32)
@@ -135,14 +157,10 @@
     adj2 = adj2.at[:, nb - 2 : nb].add(got_right[1])
     input_grad = (grads[0] - grad_two.astype(jnp.float32) + adj2).astype(jnp.bfloat16)
 
-    shape3 = (map_count, chan_count, pix_count)
-    terms = jnp.stack([maps, x_one.reshape(shape3), x_two.reshape(shape3)])
+    terms = jnp.stack([maps, x_one3, x_two.reshape(shape3)])
     output = jnp.einsum("kco,kmcp->mop", filters, terms, preferred_element_type=jnp.float32).astype(
         jnp.bfloat16
     )
-    scale = 1.0 / math.sqrt(map_count * lax.axis_size("map") * pix_count * patch_count)
-    local_grad = jnp.einsum("kmcp,mop->kco", terms, cotangent, preferred_element_type=jnp.float32)
-    filter_grad = butterfly_sum(local_grad, ("patch", "map")) * scale
     return (output, input_grad.reshape(shape3), filter_grad)
 
 

time: 129 us -> 152 us (1.18)
  the two profiles are of different devices: /device:TPU:24 before, /device:TPU:1 now
where the time goes in v3:
time: 152 us; the launch traced here: 150 us
  starting transfers between devices  56.8 us (37%)
  local copies, waits for them, and re-layouts  38.9 us (26%)
  waiting for transfers between devices  24 us (16%)
  other arithmetic  18.2 us (12%)
  matrix products  10.8 us (7%)
    ppermute x9, starting transfers between devices, butterfly_sum(): x = x + lax.ppermute(x, axes, pairs)  37.8 us
    ppermute x9, waiting for transfers between devices, butterfly_sum(): x = x + lax.ppermute(x, axes, pairs)  14.7 us
    ppermute x2, starting transfers between devices, exchange(): from_right = lax.ppermute(edge_left, 'patch', to_left)  11.1 us
    ppermute x2, waiting for transfers between devices, exchange(): from_right = lax.ppermute(edge_left, 'patch', to_left)  9.31 us
    ppermute x2, starting transfers between devices, exchange(): from_left = lax.ppermute(edge_right, 'patch', to_right)  7.94 us
    unnamed x86, local copies, waits for them, and re-layouts  6.45 us
    convert_element_type x4, local copies, waits for them, and re-layouts, per_device(): x0f = x_zero.astype(jnp.float32)  5.72 us
    dot_general x2, matrix products, forward_local(): jnp.einsum('nrjq,rjiq->nri', picked, tiles, preferred_element_type=jnp.fl...  4.33 us
  transfers between devices with their start and end apart: 13, of which 8 were waited for; matrix products, arithmetic and copies ran while one was open for 19% of the time, Pallas kernels for 0%

profile of v3, /device:TPU:1, one launch (start us, length us, event | category | flops | bytes accessed | tf_op | source)
XLA Modules:
  0.0 150.2 jit_solution(9703683420577065512)
XLA Ops:
  14.5 6.0 %collective-permute-start = (f32[3,64,2,256]{3,1,2,0:T(8,128)}, f32[3,64,2,256]{3,1,2,0:T(8,128)}, u32[]{:S(2)}, u32[]{:S(2)}) collective-permute-start(f32[3,64,2,256]{3,1,2,0:T(8,128)} %pad_maximum_fusion.4), channel_id=1, source_target_pairs={{0,32},{32,64},{64,96},{96,128},{128,160},{160,192},{192,224},{224... | collective-permute-start | bytes 1179656 | tf_op jit(solution)/shard_map/ppermute | solution.py:85
  30.2 1.9 %squeeze.68 = f32[64,6,256]{2,1,0:T(8,128)} reshape(f32[1,2,32,1536]{3,2,0,1:T(8,128)} %get-tuple-element.94) | data formatting | bytes 786432 | tf_op jit(solution)/shard_map/squeeze | solution.py:128
  32.1 2.0 %add_bitcast_fusion.3 = (f32[1,64,2,256]{3,1,2,0:T(8,128)S(1)}, f32[64,6,256]{2,0,1:T(8,128)}) fusion(f32[64,6,256]{2,0,1:T(8,128)} %copy-done.9, f32[64,6,256]{2,0,1:T(8,128)} %copy-done.10, f32[64,6,256]{2,0,1:T(8,128)} %copy-done.8, f32[64,6,256]{2,0,1:T(8,128)} %copy-done.7, f32[64,6,256]{2,0,1:T(8,128)S(1)} %slice_bitcast_fusion.8, ...), kind=kLoop, calls=%fused_computation.136 | loop fusion | flops 294912 | bytes 2359296 | tf_op jit(solution)/shard_map/stack | solution.py:118
  35.2 4.7 %collective-permute-start.1 = (f32[3,64,2,256]{3,1,2,0:T(8,128)S(1)}, f32[3,64,2,256]{3,1,2,0:T(8,128)S(1)}, u32[]{:S(2)}, u32[]{:S(2)}) collective-permute-start(f32[3,64,2,256]{3,1,2,0:T(8,128)S(1)} %pad_maximum_fusion.5), channel_id=1, source_target_pairs={{32,0},{64,32},{96,64},{128,96},{160,128},{192,160},{224,192},{256... | collective-permute-start | bytes 1179656 | tf_op jit(solution)/shard_map/ppermute | solution.py:84
  41.7 4.2 %collective-permute-done.1 = f32[3,64,2,256]{3,1,2,0:T(8,128)S(1)} collective-permute-done((f32[3,64,2,256]{3,1,2,0:T(8,128)S(1)}, f32[3,64,2,256]{3,1,2,0:T(8,128)S(1)}, u32[]{:S(2)}, u32[]{:S(2)}) %collective-permute-start.1) | collective-permute-done | bytes 393248 | tf_op jit(solution)/shard_map/ppermute | solution.py:84
  49.5 1.9 %reshape.264 = f32[2,32,1536]{2,1,0:T(8,128)} reshape(f32[64,6,256]{2,1,0:T(8,128)} %copy.44) | data formatting | bytes 786432 | tf_op jit(solution)/shard_map/reshape | solution.py:140
  53.7 2.5 %bitcast_convert_fusion = (f32[64,6,256]{2,0,1:T(8,128)}, bf16[6,64,256]{2,1,0:T(8,128)(2,1)S(1)}) fusion(bf16[6,3,256,256]{3,2,1,0:T(8,128)(2,1)S(1)} %copy-done, bf16[64,6,1,256]{3,0,1,2:T(8,128)(2,1)S(1)} %get-tuple-element.108, bf16[64,6,1,256]{3,0,1,2:T(8,128)(2,1)S(1)} %get-tuple-element.107, bf16[64,6,1,256]{3,0,1,2:T(8,128)(2,1)} %copy.29), kind=kOutput, calls=%fused_computation.158 | convolution fusion | flops 151781376 | bytes 3538944 | tf_op jit(solution)/shard_map/nrjq,rjiq->nri/dot_general | solution.py:93
  62.3 6.6 %collective-permute-start.4 = (f32[3,32,32]{2,1,0:T(8,128)S(1)}, f32[3,32,32]{2,1,0:T(8,128)S(1)}, u32[]{:S(2)}, u32[]{:S(2)}) collective-permute-start(f32[3,32,32]{2,1,0:T(8,128)S(1)} %pad_maximum_fusion.8), channel_id=1, source_target_pairs={{0,32},{1,33},{2,34},{3,35},{4,36},{5,37},{6,38},{7,39},{8,40},{9,... | collective-permute-start | bytes 36872 | tf_op jit(solution)/shard_map/ppermute | solution.py:57
  71.5 1.9 %collective-permute-start.5 = (f32[3,32,32]{2,1,0:T(8,128)S(1)}, f32[3,32,32]{2,1,0:T(8,128)S(1)}, u32[]{:S(2)}, u32[]{:S(2)}) collective-permute-start(f32[3,32,32]{2,1,0:T(8,128)S(1)} %fusion.115), channel_id=1, source_target_pairs={{0,16},{1,17},{2,18},{3,19},{4,20},{5,21},{6,22},{7,23},{8,24},{9,... | collective-permute-start | bytes 36872 | tf_op jit(solution)/shard_map/ppermute | solution.py:57
  74.1 1.9 %collective-permute-start.2 = (f32[2,64,2,256]{3,1,2,0:T(8,128)}, f32[2,64,2,256]{3,1,2,0:T(8,128)}, u32[]{:S(2)}, u32[]{:S(2)}) collective-permute-start(f32[2,64,2,256]{3,1,2,0:T(8,128)} %pad_maximum_fusion.6), channel_id=1, source_target_pairs={{0,32},{32,64},{64,96},{96,128},{128,160},{160,192},{192,224},{224... | collective-permute-start | bytes 786440 | tf_op jit(solution)/shard_map/ppermute | solution.py:85
  76.7 2.1 %collective-permute-start.6 = (f32[3,32,32]{2,1,0:T(8,128)S(1)}, f32[3,32,32]{2,1,0:T(8,128)S(1)}, u32[]{:S(2)}, u32[]{:S(2)}) collective-permute-start(f32[3,32,32]{2,1,0:T(8,128)S(1)} %fusion.125), channel_id=1, source_target_pairs={{0,80},{1,81},{2,82},{3,83},{4,84},{5,85},{6,86},{7,87},{8,88},{9,... | collective-permute-start | bytes 36872 | tf_op jit(solution)/shard_map/ppermute | solution.py:57
  78.8 4.4 %collective-permute-done.6 = f32[3,32,32]{2,1,0:T(8,128)S(1)} collective-permute-done((f32[3,32,32]{2,1,0:T(8,128)S(1)}, f32[3,32,32]{2,1,0:T(8,128)S(1)}, u32[]{:S(2)}, u32[]{:S(2)}) %collective-permute-start.6) | collective-permute-done | bytes 12320 | tf_op jit(solution)/shard_map/ppermute | solution.py:57
  83.2 2.0 %collective-permute-start.7 = (f32[3,32,32]{2,1,0:T(8,128)S(1)}, f32[3,32,32]{2,1,0:T(8,128)S(1)}, u32[]{:S(2)}, u32[]{:S(2)}) collective-permute-start(f32[3,32,32]{2,1,0:T(8,128)S(1)} %add.198), channel_id=1, source_target_pairs={{0,128},{1,129},{2,130},{3,131},{4,132},{5,133},{6,134},{7,135},{8... | collective-permute-start | bytes 36872 | tf_op jit(solution)/shard_map/ppermute | solution.py:57
  85.2 2.8 %collective-permute-done.7 = f32[3,32,32]{2,1,0:T(8,128)S(1)} collective-permute-done((f32[3,32,32]{2,1,0:T(8,128)S(1)}, f32[3,32,32]{2,1,0:T(8,128)S(1)}, u32[]{:S(2)}, u32[]{:S(2)}) %collective-permute-start.7) | collective-permute-done | bytes 12320 | tf_op jit(solution)/shard_map/ppermute | solution.py:57
  88.0 7.2 %collective-permute-start.8 = (f32[3,32,32]{2,1,0:T(8,128)S(1)}, f32[3,32,32]{2,1,0:T(8,128)S(1)}, u32[]{:S(2)}, u32[]{:S(2)}) collective-permute-start(f32[3,32,32]{2,1,0:T(8,128)S(1)} %add.199), channel_id=1, source_target_pairs={{0,384},{1,385},{2,386},{3,387},{4,388},{5,389},{6,390},{7,391},{8... | collective-permute-start | bytes 36872 | tf_op jit(solution)/shard_map/ppermute | solution.py:57
  96.8 1.9 %collective-permute-start.9 = (f32[3,32,32]{2,1,0:T(8,128)S(1)}, f32[3,32,32]{2,1,0:T(8,128)S(1)}, u32[]{:S(2)}, u32[]{:S(2)}) collective-permute-start(f32[3,32,32]{2,1,0:T(8,128)S(1)} %add.200), channel_id=1, source_target_pairs={{0,1},{1,0},{2,3},{3,2},{4,5},{5,4},{6,7},{7,6},{8,9},{9,8},{10,11... | collective-permute-start | bytes 36872 | tf_op jit(solution)/shard_map/ppermute | solution.py:57
  98.7 2.9 %collective-permute-done.9 = f32[3,32,32]{2,1,0:T(8,128)S(1)} collective-permute-done((f32[3,32,32]{2,1,0:T(8,128)S(1)}, f32[3,32,32]{2,1,0:T(8,128)S(1)}, u32[]{:S(2)}, u32[]{:S(2)}) %collective-permute-start.9) | collective-permute-done | bytes 12320 | tf_op jit(solution)/shard_map/ppermute | solution.py:57
  102.2 1.9 %collective-permute-start.10 = (f32[3,32,32]{2,1,0:T(8,128)}, f32[3,32,32]{2,1,0:T(8,128)}, u32[]{:S(2)}, u32[]{:S(2)}) collective-permute-start(f32[3,32,32]{2,1,0:T(8,128)} %add.201), channel_id=1, source_target_pairs={{0,2},{1,3},{2,0},{3,1},{4,6},{5,7},{6,4},{7,5},{8,10},{9,11},{10,... | collective-permute-start | bytes 36872 | tf_op jit(solution)/shard_map/ppermute | solution.py:57
  106.0 2.5 %collective-permute-done.10 = f32[3,32,32]{2,1,0:T(8,128)} collective-permute-done((f32[3,32,32]{2,1,0:T(8,128)}, f32[3,32,32]{2,1,0:T(8,128)}, u32[]{:S(2)}, u32[]{:S(2)}) %collective-permute-start.10) | collective-permute-done | bytes 12320 | tf_op jit(solution)/shard_map/ppermute | solution.py:57
  110.0 6.3 %collective-permute-start.11 = (f32[3,32,32]{2,1,0:T(8,128)}, f32[3,32,32]{2,1,0:T(8,128)}, u32[]{:S(2)}, u32[]{:S(2)}) collective-permute-start(f32[3,32,32]{2,1,0:T(8,128)} %add.202), channel_id=1, source_target_pairs={{0,4},{1,5},{2,6},{3,7},{4,0},{5,1},{6,2},{7,3},{8,12},{9,13},{10,... | collective-permute-start | bytes 36872 | tf_op jit(solution)/shard_map/ppermute | solution.py:57
  116.2 2.1 %pad_add_fusion = f32[64,10,256]{2,0,1:T(8,128)} fusion(f32[64,6,256]{2,0,1:T(8,128)} %get-tuple-element.95, f32[64,6,256]{2,0,1:T(8,128)} %get-tuple-element.96, f32[64,6,256]{2,0,1:T(8,128)S(1)} %get-tuple-element.82, f32[64,6,256]{2,0,1:T(8,128)S(1)} %get-tuple-element.81, f32[64,6,256]{2,0,1:T(8,128)S(1)} %slice_bitcast_fusion.2), kind=kLoop, calls=%fused_computation.27 | loop fusion | flops 655360 | bytes 2621440 | tf_op jit(solution)/shard_map/add | solution.py:101
  122.2 7.8 %collective-permute-start.12 = (f32[3,32,32]{2,1,0:T(8,128)S(1)}, f32[3,32,32]{2,1,0:T(8,128)S(1)}, u32[]{:S(2)}, u32[]{:S(2)}) collective-permute-start(f32[3,32,32]{2,1,0:T(8,128)S(1)} %add.203), channel_id=1, source_target_pairs={{0,12},{1,13},{2,14},{3,15},{4,8},{5,9},{6,10},{7,11},{8,4},{9,5},... | collective-permute-start | bytes 36872 | tf_op jit(solution)/shard_map/ppermute | solution.py:57
  131.1 6.4 %collective-permute-start.3 = (f32[2,64,2,256]{3,1,2,0:T(8,128)S(1)}, f32[2,64,2,256]{3,1,2,0:T(8,128)S(1)}, u32[]{:S(2)}, u32[]{:S(2)}) collective-permute-start(f32[2,64,2,256]{3,1,2,0:T(8,128)S(1)} %pad_maximum_fusion.7), channel_id=1, source_target_pairs={{32,0},{64,32},{96,64},{128,96},{160,128},{192,160},{224,192},{256... | collective-permute-start | bytes 786440 | tf_op jit(solution)/shard_map/ppermute | solution.py:84
  139.1 5.1 %collective-permute-done.3 = f32[2,64,2,256]{3,1,2,0:T(8,128)S(1)} collective-permute-done((f32[2,64,2,256]{3,1,2,0:T(8,128)S(1)}, f32[2,64,2,256]{3,1,2,0:T(8,128)S(1)}, u32[]{:S(2)}, u32[]{:S(2)}) %collective-permute-start.3) | collective-permute-done | bytes 262176 | tf_op jit(solution)/shard_map/ppermute | solution.py:84
  (158 shorter events, 59.6 us)
Async XLA Ops:
  12.6 7.9 %copy-start.1 = (f32[64,6,256]{2,0,1:T(8,128)}, f32[64,6,256]{2,0,1:T(8,128)S(1)}, u32[]{:S(2)}) copy-start(f32[64,6,256]{2,0,1:T(8,128)S(1)} %get-tuple-element.114) | copy-start | bytes 1179652
  12.6 7.9 %copy-start.3 = (f32[64,6,256]{2,0,1:T(8,128)}, f32[64,6,256]{2,0,1:T(8,128)S(1)}, u32[]{:S(2)}) copy-start(f32[64,6,256]{2,0,1:T(8,128)S(1)} %get-tuple-element.115) | copy-start | bytes 1179652
  14.5 17.6 %collective-permute-start = (f32[3,64,2,256]{3,1,2,0:T(8,128)}, f32[3,64,2,256]{3,1,2,0:T(8,128)}, u32[]{:S(2)}, u32[]{:S(2)}) collective-permute-start(f32[3,64,2,256]{3,1,2,0:T(8,128)} %pad_maximum_fusion.4), channel_id=1, source_target_pairs={{0,32},{32,64},{64,96},{96,128},{128,160},{160,192},{192,224},{224... | collective-permute-start | bytes 1179656 | tf_op jit(solution)/shard_map/ppermute | solution.py:85
  34.1 11.7 %copy-start.19 = (f32[64,6,256]{2,0,1:T(8,128)S(1)}, f32[64,6,256]{2,0,1:T(8,128)}, u32[]{:S(2)}) copy-start(f32[64,6,256]{2,0,1:T(8,128)} %get-tuple-element.80) | copy-start | bytes 1179652
  34.1 12.5 %copy-start.26 = (f32[64,6,256]{2,1,0:T(8,128)S(1)}, f32[64,6,256]{2,1,0:T(8,128)}, u32[]{:S(2)}) copy-start(f32[64,6,256]{2,1,0:T(8,128)} %squeeze.68) | copy-start | bytes 1179652
  35.2 10.6 %collective-permute-start.1 = (f32[3,64,2,256]{3,1,2,0:T(8,128)S(1)}, f32[3,64,2,256]{3,1,2,0:T(8,128)S(1)}, u32[]{:S(2)}, u32[]{:S(2)}) collective-permute-start(f32[3,64,2,256]{3,1,2,0:T(8,128)S(1)} %pad_maximum_fusion.5), channel_id=1, source_target_pairs={{32,0},{64,32},{96,64},{128,96},{160,128},{192,160},{224,192},{256... | collective-permute-start | bytes 1179656 | tf_op jit(solution)/shard_map/ppermute | solution.py:84
  62.3 9.2 %collective-permute-start.4 = (f32[3,32,32]{2,1,0:T(8,128)S(1)}, f32[3,32,32]{2,1,0:T(8,128)S(1)}, u32[]{:S(2)}, u32[]{:S(2)}) collective-permute-start(f32[3,32,32]{2,1,0:T(8,128)S(1)} %pad_maximum_fusion.8), channel_id=1, source_target_pairs={{0,32},{1,33},{2,34},{3,35},{4,36},{5,37},{6,38},{7,39},{8,40},{9,... | collective-permute-start | bytes 36872 | tf_op jit(solution)/shard_map/ppermute | solution.py:57
  71.5 5.3 %collective-permute-start.5 = (f32[3,32,32]{2,1,0:T(8,128)S(1)}, f32[3,32,32]{2,1,0:T(8,128)S(1)}, u32[]{:S(2)}, u32[]{:S(2)}) collective-permute-start(f32[3,32,32]{2,1,0:T(8,128)S(1)} %fusion.115), channel_id=1, source_target_pairs={{0,16},{1,17},{2,18},{3,19},{4,20},{5,21},{6,22},{7,23},{8,24},{9,... | collective-permute-start | bytes 36872 | tf_op jit(solution)/shard_map/ppermute | solution.py:57
  74.1 55.9 %collective-permute-start.2 = (f32[2,64,2,256]{3,1,2,0:T(8,128)}, f32[2,64,2,256]{3,1,2,0:T(8,128)}, u32[]{:S(2)}, u32[]{:S(2)}) collective-permute-start(f32[2,64,2,256]{3,1,2,0:T(8,128)} %pad_maximum_fusion.6), channel_id=1, source_target_pairs={{0,32},{32,64},{64,96},{96,128},{128,160},{160,192},{192,224},{224... | collective-permute-start | bytes 786440 | tf_op jit(solution)/shard_map/ppermute | solution.py:85
  76.7 6.4 %collective-permute-start.6 = (f32[3,32,32]{2,1,0:T(8,128)S(1)}, f32[3,32,32]{2,1,0:T(8,128)S(1)}, u32[]{:S(2)}, u32[]{:S(2)}) collective-permute-start(f32[3,32,32]{2,1,0:T(8,128)S(1)} %fusion.125), channel_id=1, source_target_pairs={{0,80},{1,81},{2,82},{3,83},{4,84},{5,85},{6,86},{7,87},{8,88},{9,... | collective-permute-start | bytes 36872 | tf_op jit(solution)/shard_map/ppermute | solution.py:57
  83.2 4.8 %collective-permute-start.7 = (f32[3,32,32]{2,1,0:T(8,128)S(1)}, f32[3,32,32]{2,1,0:T(8,128)S(1)}, u32[]{:S(2)}, u32[]{:S(2)}) collective-permute-start(f32[3,32,32]{2,1,0:T(8,128)S(1)} %add.198), channel_id=1, source_target_pairs={{0,128},{1,129},{2,130},{3,131},{4,132},{5,133},{6,134},{7,135},{8... | collective-permute-start | bytes 36872 | tf_op jit(solution)/shard_map/ppermute | solution.py:57
  88.0 8.7 %collective-permute-start.8 = (f32[3,32,32]{2,1,0:T(8,128)S(1)}, f32[3,32,32]{2,1,0:T(8,128)S(1)}, u32[]{:S(2)}, u32[]{:S(2)}) collective-permute-start(f32[3,32,32]{2,1,0:T(8,128)S(1)} %add.199), channel_id=1, source_target_pairs={{0,384},{1,385},{2,386},{3,387},{4,388},{5,389},{6,390},{7,391},{8... | collective-permute-start | bytes 36872 | tf_op jit(solution)/shard_map/ppermute | solution.py:57
  96.8 4.8 %collective-permute-start.9 = (f32[3,32,32]{2,1,0:T(8,128)S(1)}, f32[3,32,32]{2,1,0:T(8,128)S(1)}, u32[]{:S(2)}, u32[]{:S(2)}) collective-permute-start(f32[3,32,32]{2,1,0:T(8,128)S(1)} %add.200), channel_id=1, source_target_pairs={{0,1},{1,0},{2,3},{3,2},{4,5},{5,4},{6,7},{7,6},{8,9},{9,8},{10,11... | collective-permute-start | bytes 36872 | tf_op jit(solution)/shard_map/ppermute | solution.py:57
  102.2 6.3 %collective-permute-start.10 = (f32[3,32,32]{2,1,0:T(8,128)}, f32[3,32,32]{2,1,0:T(8,128)}, u32[]{:S(2)}, u32[]{:S(2)}) collective-permute-start(f32[3,32,32]{2,1,0:T(8,128)} %add.201), channel_id=1, source_target_pairs={{0,2},{1,3},{2,0},{3,1},{4,6},{5,7},{6,4},{7,5},{8,10},{9,11},{10,... | collective-permute-start | bytes 36872 | tf_op jit(solution)/shard_map/ppermute | solution.py:57
  110.0 11.4 %collective-permute-start.11 = (f32[3,32,32]{2,1,0:T(8,128)}, f32[3,32,32]{2,1,0:T(8,128)}, u32[]{:S(2)}, u32[]{:S(2)}) collective-permute-start(f32[3,32,32]{2,1,0:T(8,128)} %add.202), channel_id=1, source_target_pairs={{0,4},{1,5},{2,6},{3,7},{4,0},{5,1},{6,2},{7,3},{8,12},{9,13},{10,... | collective-permute-start | bytes 36872 | tf_op jit(solution)/shard_map/ppermute | solution.py:57
  120.2 10.8 %copy-start.28 = (f32[1,64,2,256]{3,1,2,0:T(8,128)S(1)}, f32[1,64,2,256]{3,1,2,0:T(8,128)}, u32[]{:S(2)}) copy-start(f32[1,64,2,256]{3,1,2,0:T(8,128)} %get-tuple-element.106) | copy-start | bytes 393220
  120.2 24.0 %copy-start.20 = (f32[64,6,256]{2,1,0:T(8,128)S(1)}, f32[64,6,256]{2,1,0:T(8,128)}, u32[]{:S(2)}) copy-start(f32[64,6,256]{2,1,0:T(8,128)} %squeeze.74) | copy-start | bytes 1179652
  120.2 24.1 %copy-start.22 = (bf16[64,6,256]{2,1,0:T(8,128)(2,1)S(1)}, bf16[64,6,256]{2,1,0:T(8,128)(2,1)}, u32[]{:S(2)}) copy-start(bf16[64,6,256]{2,1,0:T(8,128)(2,1)} %copy-done.21) | copy-start | bytes 589828
  122.2 15.4 %collective-permute-start.12 = (f32[3,32,32]{2,1,0:T(8,128)S(1)}, f32[3,32,32]{2,1,0:T(8,128)S(1)}, u32[]{:S(2)}, u32[]{:S(2)}) collective-permute-start(f32[3,32,32]{2,1,0:T(8,128)S(1)} %add.203), channel_id=1, source_target_pairs={{0,12},{1,13},{2,14},{3,15},{4,8},{5,9},{6,10},{7,11},{8,4},{9,5},... | collective-permute-start | bytes 36872 | tf_op jit(solution)/shard_map/ppermute | solution.py:57
  131.0 15.9 %copy-start.27 = (f32[64,6,256]{2,0,1:T(8,128)S(1)}, f32[64,6,256]{2,0,1:T(8,128)}, u32[]{:S(2)}) copy-start(f32[64,6,256]{2,0,1:T(8,128)} %get-tuple-element.117) | copy-start | bytes 1179652
  131.0 15.9 %copy-start.38 = (pred[6]{0:T(512)(128)(4,1)S(1)}, pred[6]{0:T(512)(128)(4,1)}, u32[]{:S(2)}) copy-start(pred[6]{0:T(512)(128)(4,1)} %copy-done.36) | copy-start | bytes 22
  131.1 15.9 %copy-start.41 = (pred[6]{0:T(512)(128)(4,1)S(1)}, pred[6]{0:T(512)(128)(4,1)}, u32[]{:S(2)}) copy-start(pred[6]{0:T(512)(128)(4,1)} %copy-done.39) | copy-start | bytes 22
  131.1 16.0 %copy-start.17 = (f32[64,6,256]{2,0,1:T(8,128)S(1)}, f32[64,6,256]{2,0,1:T(8,128)}, u32[]{:S(2)}) copy-start(f32[64,6,256]{2,0,1:T(8,128)} %copy-done.16) | copy-start | bytes 1179652
  131.1 13.2 %collective-permute-start.3 = (f32[2,64,2,256]{3,1,2,0:T(8,128)S(1)}, f32[2,64,2,256]{3,1,2,0:T(8,128)S(1)}, u32[]{:S(2)}, u32[]{:S(2)}) collective-permute-start(f32[2,64,2,256]{3,1,2,0:T(8,128)S(1)} %pad_maximum_fusion.7), channel_id=1, source_target_pairs={{32,0},{64,32},{96,64},{128,96},{160,128},{192,160},{224,192},{256... | collective-permute-start | bytes 786440 | tf_op jit(solution)/shard_map/ppermute | solution.py:84
  (32 other events, 102.4 us)

commit v4 on v2

--- a/solution.py
+++ b/solution.py
@@ -74,8 +74,8 @@
     total_blocks = block_count * patch_count
     first_block = lax.axis_index("patch") * block_count
     row_ids = first_block + jnp.arange(block_count, dtype=jnp.int32)
-    back_one = ((row_ids - columns[:, 1]) % total_blocks == 1)[None, :, None]
-    next_one = ((columns[:, 2] - row_ids) % total_blocks == 1)[None, :, None]
+    back_one = ((row_ids - columns[:, 1]) % total_blocks == 1)[:, None, None]
+    next_one = ((columns[:, 2] - row_ids) % total_blocks == 1)[:, None, None]
     nb = block_count
     to_right = [(i, (i + 1) % patch_count) for i in range(patch_count)]
     to_left = [((i + 1) % patch_count, i) for i in range(patch_count)]
@@ -85,18 +85,24 @@
         from_left = lax.ppermute(edge_right, "patch", to_right)
         return from_left, from_right
 
+    def to_blocks(field):
+        return field.reshape(row_count, nb, block_size).transpose(1, 0, 2)
+
+    def from_blocks(field):
+        return field.transpose(1, 0, 2).reshape(map_count, chan_count, pix_count)
+
     def forward_local(ext):
-        s0 = ext[:, 2 : 2 + nb]
-        s1 = jnp.where(back_one, ext[:, 1 : 1 + nb], ext[:, 0:nb])
-        s2 = jnp.where(next_one, ext[:, 3 : 3 + nb], ext[:, 4 : 4 + nb])
-        picked = jnp.stack([s0, s1, s2], axis=2).astype(jnp.bfloat16)
-        return jnp.einsum("nrjq,rjiq->nri", picked, tiles, preferred_element_type=jnp.float32)
+        s0 = ext[2 : 2 + nb]
+        s1 = jnp.where(back_one, ext[1 : 1 + nb], ext[0:nb])
+        s2 = jnp.where(next_one, ext[3 : 3 + nb], ext[4 : 4 + nb])
+        picked = jnp.stack([s0, s1, s2], axis=1).astype(jnp.bfloat16)
+        return jnp.einsum("rjnq,rjiq->rni", picked, tiles, preferred_element_type=jnp.float32)
 
     def adjoint_window(grads):
-        contrib = jnp.einsum("nri,rjiq->nrjq", grads, tiles, preferred_element_type=jnp.float32)
-        c0, c1, c2 = contrib[:, :, 0], contrib[:, :, 1], contrib[:, :, 2]
+        contrib = jnp.einsum("rni,rjiq->rjnq", grads, tiles, preferred_element_type=jnp.float32)
+        c0, c1, c2 = contrib[:, 0], contrib[:, 1], contrib[:, 2]
         zero = jnp.zeros_like(c0)
-        pad = lambda v, lo: jnp.pad(v, ((0, 0), (lo, 4 - lo), (0, 0)))
+        pad = lambda v, lo: jnp.pad(v, ((lo, 4 - lo), (0, 0), (0, 0)))
         return (
             pad(c0, 2)
             + pad(jnp.where(back_one, c1, zero), 1)
@@ -105,45 +111,44 @@
             + pad(jnp.where(next_one, zero, c2), 4)
         )
 
-    x_zero = maps.reshape(row_count, nb, block_size)
-    weights = filters
-    grads = jnp.einsum("kco,mop->kmcp", weights, cotangent, preferred_element_type=jnp.float32)
-    grads = grads.reshape(3, row_count, nb, block_size)
+    x_zero = to_blocks(maps)
+    cot_b = to_blocks(cotangent).reshape(nb, map_count, chan_count, block_size)
+    grads = jnp.einsum("kco,rmop->krmcp", filters, cot_b, preferred_element_type=jnp.float32)
+    grads = grads.reshape(3, nb, row_count, block_size)
     grad_two = grads[2].astype(jnp.bfloat16)
 
     win1 = adjoint_window(grad_two)
     x0f = x_zero.astype(jnp.float32)
-    send_left = jnp.stack([x0f[:, 0:2], win1[:, 0:2]])
-    send_right = jnp.stack([x0f[:, nb - 2 : nb], win1[:, nb + 2 : nb + 4]])
+    send_left = jnp.stack([x0f[0:2], win1[0:2]])
+    send_right = jnp.stack([x0f[nb - 2 : nb], win1[nb + 2 : nb + 4]])
     got_left, got_right = exchange(send_left, send_right)
-    ext0 = jnp.concatenate([got_left[0], x0f, got_right[0]], axis=1)
+    ext0 = jnp.concatenate([got_left[0], x0f, got_right[0]], axis=0)
     x_one = forward_local(ext0).astype(jnp.bfloat16)
-    adj1 = win1[:, 2 : 2 + nb]
-    adj1 = adj1.at[:, 0:2].add(got_left[1])
-    adj1 = adj1.at[:, nb - 2 : nb].add(got_right[1])
+    adj1 = win1[2 : 2 + nb]
+    adj1 = adj1.at[0:2].add(got_left[1])
+    adj1 = adj1.at[nb - 2 : nb].add(got_right[1])
     update = (grads[1] + 2.0 * adj1).astype(jnp.bfloat16)
 
     win2 = adjoint_window(update)
     x1f = x_one.astype(jnp.float32)
-    send_left = jnp.stack([x1f[:, 0:2], win2[:, 0:2]])
-    send_right = jnp.stack([x1f[:, nb - 2 : nb], win2[:, nb + 2 : nb + 4]])
+    send_left = jnp.stack([x1f[0:2], win2[0:2]])
+    send_right = jnp.stack([x1f[nb - 2 : nb], win2[nb + 2 : nb + 4]])
     got_left, got_right = exchange(send_left, send_right)
-    ext1 = jnp.concatenate([got_left[0], x1f, got_right[0]], axis=1)
+    ext1 = jnp.concatenate([got_left[0], x1f, got_right[0]], axis=0)
     x_two = (2.0 * forward_local(ext1) - x0f).astype(jnp.bfloat16)
-    adj2 = win2[:, 2 : 2 + nb]
-    adj2 = adj2.at[:, 0:2].add(got_left[1])
-    adj2 = adj2.at[:, nb - 2 : nb].add(got_right[1])
+    adj2 = win2[2 : 2 + nb]
+    adj2 = adj2.at[0:2].add(got_left[1])
+    adj2 = adj2.at[nb - 2 : nb].add(got_right[1])
     input_grad = (grads[0] - grad_two.astype(jnp.float32) + adj2).astype(jnp.bfloat16)
 
-    shape3 = (map_count, chan_count, pix_count)
-    terms = jnp.stack([maps, x_one.reshape(shape3), x_two.reshape(shape3)])
-    output = jnp.einsum("kco,kmcp->mop", filters, terms, preferred_element_type=jnp.float32).astype(
-        jnp.bfloat16
-    )
+    split = (nb, map_count, chan_count, block_size)
+    terms = jnp.stack([x_zero.reshape(split), x_one.reshape(split), x_two.reshape(split)])
+    out_b = jnp.einsum("kco,krmcp->rmop", filters, terms, preferred_element_type=jnp.float32)
+    output = from_blocks(out_b.astype(jnp.bfloat16).reshape(nb, row_count, block_size))
     scale = 1.0 / math.sqrt(map_count * lax.axis_size("map") * pix_count * patch_count)
-    local_grad = jnp.einsum("kmcp,mop->kco", terms, cotangent, preferred_element_type=jnp.float32)
+    local_grad = jnp.einsum("krmcp,rmop->kco", terms, cot_b, preferred_element_type=jnp.float32)
     filter_grad = butterfly_sum(local_grad, ("patch", "map")) * scale
-    return (output, input_grad.reshape(shape3), filter_grad)
+    return (output, from_blocks(input_grad), filter_grad)
 
 
 def solution(mesh):

time: 129 us -> 118 us (0.915)
  local copies, waits for them, and re-layouts: 18.7 us -> 7.59 us
  waiting for transfers between devices: 41.5 us -> 48.5 us
  matrix products: 9.52 us -> 4.34 us
  other arithmetic: 7.97 us -> 3.92 us
  starting transfers between devices: 48.8 us -> 50.8 us
    ppermute x2, waiting for transfers between devices: 0.59 us -> 7.63 us  [exchange(): from_right = lax.ppermute(edge_left, 'patch', to_left)]
    convert_element_type x8 -> x0, local copies, waits for them, and re-layouts: 6.28 us -> none  [the longest x4 5 us: per_device(): x0f = x_zero.astype(jnp.float32)]
    squeeze x8 -> x6, local copies, waits for them, and re-layouts: 5.71 us -> 0.09 us  [the longest x2 0.05 us: adjoint_window(): c0, c1, c2 = (contrib[:, 0], contrib[:, 1], contrib[:, 2])]
    dot_general x7, matrix products: 9.52 us -> 4.34 us  [the longest x2 1.67 us: forward_local(): jnp.einsum('rjnq,rjiq->rni', picked, tiles, preferred_element_type=jnp.fl...]
    reshape x1 -> x5, local copies, waits for them, and re-layouts: 0.91 us -> 4.44 us  [the longest x2 2.51 us: to_blocks(): return field.reshape(row_count, nb, block_size).transpose(1, 0, 2)]
    another operation x3 -> x1, local copies, waits for them, and re-layouts: 2.11 us -> 0.02 us  [per_device(): send_right = jnp.stack([x1f[nb - 2:nb], win2[nb + 2:nb + 4]])]
    scatter-add x3, other arithmetic: 1.92 us -> 0.11 us  [the longest x1 0.05 us: per_device(): adj2 = adj2.at[0:2].add(got_left[1])]
    add x8, other arithmetic: 1.51 us -> 0.07 us  [butterfly_sum(): x = x + lax.ppermute(x, axes, pairs)]
  transfers between devices with their start and end apart: 13 -> 13, of which waited for: 11 -> 12; matrix products, arithmetic and copies ran while one was open for 12% -> 2% of each run, Pallas kernels for 0% -> 0%
where the time goes in v4:
time: 118 us; the launch traced here: 116 us
  starting transfers between devices  50.8 us (43%)
  waiting for transfers between devices  48.5 us (41%)
  local copies, waits for them, and re-layouts  7.59 us (6%)
  matrix products  4.34 us (4%)
  other arithmetic  3.92 us (3%)
    ppermute x9, starting transfers between devices, butterfly_sum(): x = x + lax.ppermute(x, axes, pairs)  40.7 us
    ppermute x9, waiting for transfers between devices, butterfly_sum(): x = x + lax.ppermute(x, axes, pairs)  27.1 us
    ppermute x2, waiting for transfers between devices, exchange(): from_left = lax.ppermute(edge_right, 'patch', to_right)  13.7 us
    ppermute x2, waiting for transfers between devices, exchange(): from_right = lax.ppermute(edge_left, 'patch', to_left)  7.63 us
    ppermute x2, starting transfers between devices, exchange(): from_left = lax.ppermute(edge_right, 'patch', to_right)  6.24 us
    ppermute x2, starting transfers between devices, exchange(): from_right = lax.ppermute(edge_left, 'patch', to_left)  3.84 us
    unnamed x18, local copies, waits for them, and re-layouts  2.75 us
    reshape x2, local copies, waits for them, and re-layouts, to_blocks(): return field.reshape(row_count, nb, block_size).transpose(1, 0, 2)  2.51 us
  transfers between devices with their start and end apart: 13, of which 12 were waited for; matrix products, arithmetic and copies ran while one was open for 2% of the time, Pallas kernels for 0%

profile of v4, /device:TPU:24, one launch (start us, length us, event | category | flops | bytes accessed | tf_op | source)
XLA Modules:
  0.0 116.2 jit_solution(18094294421055997995)
XLA Ops:
  9.1 1.9 %collective-permute-start = (f32[2,2,64,256]{3,2,1,0:T(8,128)S(1)}, f32[2,2,64,256]{3,2,1,0:T(8,128)S(1)}, u32[]{:S(2)}, u32[]{:S(2)}) collective-permute-start(f32[2,2,64,256]{3,2,1,0:T(8,128)S(1)} %pad_maximum_fusion.5), channel_id=1, source_target_pairs={{0,32},{32,64},{64,96},{96,128},{128,160},{160,192},{192,224},{224... | collective-permute-start | bytes 786440 | tf_op jit(solution)/shard_map/ppermute | solution.py:85
  11.2 8.0 %collective-permute-done = f32[2,2,64,256]{3,2,1,0:T(8,128)S(1)} collective-permute-done((f32[2,2,64,256]{3,2,1,0:T(8,128)S(1)}, f32[2,2,64,256]{3,2,1,0:T(8,128)S(1)}, u32[]{:S(2)}, u32[]{:S(2)}) %collective-permute-start) | collective-permute-done | bytes 262176 | tf_op jit(solution)/shard_map/ppermute | solution.py:85
  19.3 1.9 %collective-permute-start.1 = (f32[2,2,64,256]{3,2,1,0:T(8,128)S(1)}, f32[2,2,64,256]{3,2,1,0:T(8,128)S(1)}, u32[]{:S(2)}, u32[]{:S(2)}) collective-permute-start(f32[2,2,64,256]{3,2,1,0:T(8,128)S(1)} %pad_maximum_fusion.6), channel_id=1, source_target_pairs={{32,0},{64,32},{96,64},{128,96},{160,128},{192,160},{224,192},{256... | collective-permute-start | bytes 786440 | tf_op jit(solution)/shard_map/ppermute | solution.py:84
  21.3 3.8 %collective-permute-done.1 = f32[2,2,64,256]{3,2,1,0:T(8,128)S(1)} collective-permute-done((f32[2,2,64,256]{3,2,1,0:T(8,128)S(1)}, f32[2,2,64,256]{3,2,1,0:T(8,128)S(1)}, u32[]{:S(2)}, u32[]{:S(2)}) %collective-permute-start.1) | collective-permute-done | bytes 262176 | tf_op jit(solution)/shard_map/ppermute | solution.py:84
  27.6 4.3 %collective-permute-start.2 = (f32[2,2,64,256]{3,2,1,0:T(8,128)S(1)}, f32[2,2,64,256]{3,2,1,0:T(8,128)S(1)}, u32[]{:S(2)}, u32[]{:S(2)}) collective-permute-start(f32[2,2,64,256]{3,2,1,0:T(8,128)S(1)} %pad_maximum_fusion.7), channel_id=1, source_target_pairs={{0,32},{32,64},{64,96},{96,128},{128,160},{160,192},{192,224},{224... | collective-permute-start | bytes 786440 | tf_op jit(solution)/shard_map/ppermute | solution.py:85
  32.1 5.8 %collective-permute-done.2 = f32[2,2,64,256]{3,2,1,0:T(8,128)S(1)} collective-permute-done((f32[2,2,64,256]{3,2,1,0:T(8,128)S(1)}, f32[2,2,64,256]{3,2,1,0:T(8,128)S(1)}, u32[]{:S(2)}, u32[]{:S(2)}) %collective-permute-start.2) | collective-permute-done | bytes 262176 | tf_op jit(solution)/shard_map/ppermute | solution.py:85
  37.9 1.9 %collective-permute-start.3 = (f32[2,2,64,256]{3,2,1,0:T(8,128)S(1)}, f32[2,2,64,256]{3,2,1,0:T(8,128)S(1)}, u32[]{:S(2)}, u32[]{:S(2)}) collective-permute-start(f32[2,2,64,256]{3,2,1,0:T(8,128)S(1)} %pad_maximum_fusion.8), channel_id=1, source_target_pairs={{32,0},{64,32},{96,64},{128,96},{160,128},{192,160},{224,192},{256... | collective-permute-start | bytes 786440 | tf_op jit(solution)/shard_map/ppermute | solution.py:84
  39.8 3.9 %collective-permute-done.3 = f32[2,2,64,256]{3,2,1,0:T(8,128)S(1)} collective-permute-done((f32[2,2,64,256]{3,2,1,0:T(8,128)S(1)}, f32[2,2,64,256]{3,2,1,0:T(8,128)S(1)}, u32[]{:S(2)}, u32[]{:S(2)}) %collective-permute-start.3) | collective-permute-done | bytes 262176 | tf_op jit(solution)/shard_map/ppermute | solution.py:84
  45.1 5.0 %collective-permute-start.4 = (f32[3,32,32]{2,1,0:T(8,128)S(1)}, f32[3,32,32]{2,1,0:T(8,128)S(1)}, u32[]{:S(2)}, u32[]{:S(2)}) collective-permute-start(f32[3,32,32]{2,1,0:T(8,128)S(1)} %convolution_bitcast_fusion.2), channel_id=1, source_target_pairs={{0,32},{1,33},{2,34},{3,35},{4,36},{5,37},{6,38},{7,39},{8,40},{9,... | collective-permute-start | bytes 36872 | tf_op jit(solution)/shard_map/ppermute | solution.py:57
  51.0 1.9 %collective-permute-start.5 = (f32[3,32,32]{2,1,0:T(8,128)S(1)}, f32[3,32,32]{2,1,0:T(8,128)S(1)}, u32[]{:S(2)}, u32[]{:S(2)}) collective-permute-start(f32[3,32,32]{2,1,0:T(8,128)S(1)} %add.154), channel_id=1, source_target_pairs={{0,16},{1,17},{2,18},{3,19},{4,20},{5,21},{6,22},{7,23},{8,24},{9,... | collective-permute-start | bytes 36872 | tf_op jit(solution)/shard_map/ppermute | solution.py:57
  52.9 4.1 %collective-permute-done.5 = f32[3,32,32]{2,1,0:T(8,128)S(1)} collective-permute-done((f32[3,32,32]{2,1,0:T(8,128)S(1)}, f32[3,32,32]{2,1,0:T(8,128)S(1)}, u32[]{:S(2)}, u32[]{:S(2)}) %collective-permute-start.5) | collective-permute-done | bytes 12320 | tf_op jit(solution)/shard_map/ppermute | solution.py:57
  57.0 8.8 %collective-permute-start.6 = (f32[3,32,32]{2,1,0:T(8,128)S(1)}, f32[3,32,32]{2,1,0:T(8,128)S(1)}, u32[]{:S(2)}, u32[]{:S(2)}) collective-permute-start(f32[3,32,32]{2,1,0:T(8,128)S(1)} %add.155), channel_id=1, source_target_pairs={{0,80},{1,81},{2,82},{3,83},{4,84},{5,85},{6,86},{7,87},{8,88},{9,... | collective-permute-start | bytes 36872 | tf_op jit(solution)/shard_map/ppermute | solution.py:57
  65.8 2.1 %collective-permute-done.6 = f32[3,32,32]{2,1,0:T(8,128)S(1)} collective-permute-done((f32[3,32,32]{2,1,0:T(8,128)S(1)}, f32[3,32,32]{2,1,0:T(8,128)S(1)}, u32[]{:S(2)}, u32[]{:S(2)}) %collective-permute-start.6) | collective-permute-done | bytes 12320 | tf_op jit(solution)/shard_map/ppermute | solution.py:57
  67.8 1.9 %collective-permute-start.7 = (f32[3,32,32]{2,1,0:T(8,128)S(1)}, f32[3,32,32]{2,1,0:T(8,128)S(1)}, u32[]{:S(2)}, u32[]{:S(2)}) collective-permute-start(f32[3,32,32]{2,1,0:T(8,128)S(1)} %add.156), channel_id=1, source_target_pairs={{0,128},{1,129},{2,130},{3,131},{4,132},{5,133},{6,134},{7,135},{8... | collective-permute-start | bytes 36872 | tf_op jit(solution)/shard_map/ppermute | solution.py:57
  69.8 4.1 %collective-permute-done.7 = f32[3,32,32]{2,1,0:T(8,128)S(1)} collective-permute-done((f32[3,32,32]{2,1,0:T(8,128)S(1)}, f32[3,32,32]{2,1,0:T(8,128)S(1)}, u32[]{:S(2)}, u32[]{:S(2)}) %collective-permute-start.7) | collective-permute-done | bytes 12320 | tf_op jit(solution)/shard_map/ppermute | solution.py:57
  73.8 3.5 %collective-permute-start.8 = (f32[3,32,32]{2,1,0:T(8,128)S(1)}, f32[3,32,32]{2,1,0:T(8,128)S(1)}, u32[]{:S(2)}, u32[]{:S(2)}) collective-permute-start(f32[3,32,32]{2,1,0:T(8,128)S(1)} %add.157), channel_id=1, source_target_pairs={{0,384},{1,385},{2,386},{3,387},{4,388},{5,389},{6,390},{7,391},{8... | collective-permute-start | bytes 36872 | tf_op jit(solution)/shard_map/ppermute | solution.py:57
  77.4 3.7 %collective-permute-done.8 = f32[3,32,32]{2,1,0:T(8,128)S(1)} collective-permute-done((f32[3,32,32]{2,1,0:T(8,128)S(1)}, f32[3,32,32]{2,1,0:T(8,128)S(1)}, u32[]{:S(2)}, u32[]{:S(2)}) %collective-permute-start.8) | collective-permute-done | bytes 12320 | tf_op jit(solution)/shard_map/ppermute | solution.py:57
  81.0 1.9 %collective-permute-start.9 = (f32[3,32,32]{2,1,0:T(8,128)S(1)}, f32[3,32,32]{2,1,0:T(8,128)S(1)}, u32[]{:S(2)}, u32[]{:S(2)}) collective-permute-start(f32[3,32,32]{2,1,0:T(8,128)S(1)} %add.158), channel_id=1, source_target_pairs={{0,1},{1,0},{2,3},{3,2},{4,5},{5,4},{6,7},{7,6},{8,9},{9,8},{10,11... | collective-permute-start | bytes 36872 | tf_op jit(solution)/shard_map/ppermute | solution.py:57
  83.0 4.1 %collective-permute-done.9 = f32[3,32,32]{2,1,0:T(8,128)S(1)} collective-permute-done((f32[3,32,32]{2,1,0:T(8,128)S(1)}, f32[3,32,32]{2,1,0:T(8,128)S(1)}, u32[]{:S(2)}, u32[]{:S(2)}) %collective-permute-start.9) | collective-permute-done | bytes 12320 | tf_op jit(solution)/shard_map/ppermute | solution.py:57
  87.0 1.9 %collective-permute-start.10 = (f32[3,32,32]{2,1,0:T(8,128)S(1)}, f32[3,32,32]{2,1,0:T(8,128)S(1)}, u32[]{:S(2)}, u32[]{:S(2)}) collective-permute-start(f32[3,32,32]{2,1,0:T(8,128)S(1)} %add.159), channel_id=1, source_target_pairs={{0,2},{1,3},{2,0},{3,1},{4,6},{5,7},{6,4},{7,5},{8,10},{9,11},{10,... | collective-permute-start | bytes 36872 | tf_op jit(solution)/shard_map/ppermute | solution.py:57
  89.0 4.9 %collective-permute-done.10 = f32[3,32,32]{2,1,0:T(8,128)S(1)} collective-permute-done((f32[3,32,32]{2,1,0:T(8,128)S(1)}, f32[3,32,32]{2,1,0:T(8,128)S(1)}, u32[]{:S(2)}, u32[]{:S(2)}) %collective-permute-start.10) | collective-permute-done | bytes 12320 | tf_op jit(solution)/shard_map/ppermute | solution.py:57
  93.9 6.7 %collective-permute-start.11 = (f32[3,32,32]{2,1,0:T(8,128)S(1)}, f32[3,32,32]{2,1,0:T(8,128)S(1)}, u32[]{:S(2)}, u32[]{:S(2)}) collective-permute-start(f32[3,32,32]{2,1,0:T(8,128)S(1)} %add.160), channel_id=1, source_target_pairs={{0,4},{1,5},{2,6},{3,7},{4,0},{5,1},{6,2},{7,3},{8,12},{9,13},{10,... | collective-permute-start | bytes 36872 | tf_op jit(solution)/shard_map/ppermute | solution.py:57
  100.7 3.5 %collective-permute-done.11 = f32[3,32,32]{2,1,0:T(8,128)S(1)} collective-permute-done((f32[3,32,32]{2,1,0:T(8,128)S(1)}, f32[3,32,32]{2,1,0:T(8,128)S(1)}, u32[]{:S(2)}, u32[]{:S(2)}) %collective-permute-start.11) | collective-permute-done | bytes 12320 | tf_op jit(solution)/shard_map/ppermute | solution.py:57
  104.2 9.0 %collective-permute-start.12 = (f32[3,32,32]{2,1,0:T(8,128)S(1)}, f32[3,32,32]{2,1,0:T(8,128)S(1)}, u32[]{:S(2)}, u32[]{:S(2)}) collective-permute-start(f32[3,32,32]{2,1,0:T(8,128)S(1)} %add.161), channel_id=1, source_target_pairs={{0,12},{1,13},{2,14},{3,15},{4,8},{5,9},{6,10},{7,11},{8,4},{9,5},... | collective-permute-start | bytes 36872 | tf_op jit(solution)/shard_map/ppermute | solution.py:57
  (74 shorter events, 16.7 us)
Async XLA Ops:
  0.6 5.4 %copy-start = (bf16[6,3,256,256]{3,2,1,0:T(8,128)(2,1)S(1)}, bf16[6,3,256,256]{3,2,1,0:T(8,128)(2,1)}, u32[]{:S(2)}) copy-start(bf16[6,3,256,256]{3,2,1,0:T(8,128)(2,1)} %param.15) | copy-start | bytes 7077892
  2.0 4.1 %copy-start.4 = (bf16[64,6,256]{2,1,0:T(8,128)(2,1)}, bf16[64,6,256]{2,1,0:T(8,128)(2,1)S(1)}, u32[]{:S(2)}) copy-start(bf16[64,6,256]{2,1,0:T(8,128)(2,1)S(1)} %reshape.187) | copy-start | bytes 589828
  5.0 1.0 copy-start.2
  6.0 1.6 %copy-start.8 = (s32[6,3]{0,1:T(4,128)S(1)}, s32[6,3]{0,1:T(4,128)}, u32[]{:S(2)}) copy-start(s32[6,3]{0,1:T(4,128)} %param.16) | copy-start | bytes 220
  6.6 1.0 copy-start.1
  9.1 10.1 %collective-permute-start = (f32[2,2,64,256]{3,2,1,0:T(8,128)S(1)}, f32[2,2,64,256]{3,2,1,0:T(8,128)S(1)}, u32[]{:S(2)}, u32[]{:S(2)}) collective-permute-start(f32[2,2,64,256]{3,2,1,0:T(8,128)S(1)} %pad_maximum_fusion.5), channel_id=1, source_target_pairs={{0,32},{32,64},{64,96},{96,128},{128,160},{160,192},{192,224},{224... | collective-permute-start | bytes 786440 | tf_op jit(solution)/shard_map/ppermute | solution.py:85
  11.1 10.0 %copy-start.3 = (f32[3,6,2,32,256]{4,3,0,2,1:T(8,128)S(1)}, f32[3,6,2,32,256]{4,3,0,2,1:T(8,128)}, u32[]{:S(2)}) copy-start(f32[3,6,2,32,256]{4,3,0,2,1:T(8,128)} %copy-done.2) | copy-start | bytes 3538948
  19.3 5.8 %collective-permute-start.1 = (f32[2,2,64,256]{3,2,1,0:T(8,128)S(1)}, f32[2,2,64,256]{3,2,1,0:T(8,128)S(1)}, u32[]{:S(2)}, u32[]{:S(2)}) collective-permute-start(f32[2,2,64,256]{3,2,1,0:T(8,128)S(1)} %pad_maximum_fusion.6), channel_id=1, source_target_pairs={{32,0},{64,32},{96,64},{128,96},{160,128},{192,160},{224,192},{256... | collective-permute-start | bytes 786440 | tf_op jit(solution)/shard_map/ppermute | solution.py:84
  25.7 0.9 copy-start.6
  27.6 10.3 %collective-permute-start.2 = (f32[2,2,64,256]{3,2,1,0:T(8,128)S(1)}, f32[2,2,64,256]{3,2,1,0:T(8,128)S(1)}, u32[]{:S(2)}, u32[]{:S(2)}) collective-permute-start(f32[2,2,64,256]{3,2,1,0:T(8,128)S(1)} %pad_maximum_fusion.7), channel_id=1, source_target_pairs={{0,32},{32,64},{64,96},{96,128},{128,160},{160,192},{192,224},{224... | collective-permute-start | bytes 786440 | tf_op jit(solution)/shard_map/ppermute | solution.py:85
  37.9 5.8 %collective-permute-start.3 = (f32[2,2,64,256]{3,2,1,0:T(8,128)S(1)}, f32[2,2,64,256]{3,2,1,0:T(8,128)S(1)}, u32[]{:S(2)}, u32[]{:S(2)}) collective-permute-start(f32[2,2,64,256]{3,2,1,0:T(8,128)S(1)} %pad_maximum_fusion.8), channel_id=1, source_target_pairs={{32,0},{64,32},{96,64},{128,96},{160,128},{192,160},{224,192},{256... | collective-permute-start | bytes 786440 | tf_op jit(solution)/shard_map/ppermute | solution.py:84
  43.8 1.0 copy-start.5
  44.8 68.4 %copy-start.7 = (bf16[3,32,32]{2,1,0:T(8,128)(2,1)S(1)}, bf16[3,32,32]{2,1,0:T(8,128)(2,1)}, u32[]{:S(2)}) copy-start(bf16[3,32,32]{2,1,0:T(8,128)(2,1)} %param.17) | copy-start | bytes 18436
  45.1 5.9 %collective-permute-start.4 = (f32[3,32,32]{2,1,0:T(8,128)S(1)}, f32[3,32,32]{2,1,0:T(8,128)S(1)}, u32[]{:S(2)}, u32[]{:S(2)}) collective-permute-start(f32[3,32,32]{2,1,0:T(8,128)S(1)} %convolution_bitcast_fusion.2), channel_id=1, source_target_pairs={{0,32},{1,33},{2,34},{3,35},{4,36},{5,37},{6,38},{7,39},{8,40},{9,... | collective-permute-start | bytes 36872 | tf_op jit(solution)/shard_map/ppermute | solution.py:57
  51.0 6.0 %collective-permute-start.5 = (f32[3,32,32]{2,1,0:T(8,128)S(1)}, f32[3,32,32]{2,1,0:T(8,128)S(1)}, u32[]{:S(2)}, u32[]{:S(2)}) collective-permute-start(f32[3,32,32]{2,1,0:T(8,128)S(1)} %add.154), channel_id=1, source_target_pairs={{0,16},{1,17},{2,18},{3,19},{4,20},{5,21},{6,22},{7,23},{8,24},{9,... | collective-permute-start | bytes 36872 | tf_op jit(solution)/shard_map/ppermute | solution.py:57
  57.0 10.8 %collective-permute-start.6 = (f32[3,32,32]{2,1,0:T(8,128)S(1)}, f32[3,32,32]{2,1,0:T(8,128)S(1)}, u32[]{:S(2)}, u32[]{:S(2)}) collective-permute-start(f32[3,32,32]{2,1,0:T(8,128)S(1)} %add.155), channel_id=1, source_target_pairs={{0,80},{1,81},{2,82},{3,83},{4,84},{5,85},{6,86},{7,87},{8,88},{9,... | collective-permute-start | bytes 36872 | tf_op jit(solution)/shard_map/ppermute | solution.py:57
  67.8 6.0 %collective-permute-start.7 = (f32[3,32,32]{2,1,0:T(8,128)S(1)}, f32[3,32,32]{2,1,0:T(8,128)S(1)}, u32[]{:S(2)}, u32[]{:S(2)}) collective-permute-start(f32[3,32,32]{2,1,0:T(8,128)S(1)} %add.156), channel_id=1, source_target_pairs={{0,128},{1,129},{2,130},{3,131},{4,132},{5,133},{6,134},{7,135},{8... | collective-permute-start | bytes 36872 | tf_op jit(solution)/shard_map/ppermute | solution.py:57
  73.8 7.2 %collective-permute-start.8 = (f32[3,32,32]{2,1,0:T(8,128)S(1)}, f32[3,32,32]{2,1,0:T(8,128)S(1)}, u32[]{:S(2)}, u32[]{:S(2)}) collective-permute-start(f32[3,32,32]{2,1,0:T(8,128)S(1)} %add.157), channel_id=1, source_target_pairs={{0,384},{1,385},{2,386},{3,387},{4,388},{5,389},{6,390},{7,391},{8... | collective-permute-start | bytes 36872 | tf_op jit(solution)/shard_map/ppermute | solution.py:57
  81.0 6.0 %collective-permute-start.9 = (f32[3,32,32]{2,1,0:T(8,128)S(1)}, f32[3,32,32]{2,1,0:T(8,128)S(1)}, u32[]{:S(2)}, u32[]{:S(2)}) collective-permute-start(f32[3,32,32]{2,1,0:T(8,128)S(1)} %add.158), channel_id=1, source_target_pairs={{0,1},{1,0},{2,3},{3,2},{4,5},{5,4},{6,7},{7,6},{8,9},{9,8},{10,11... | collective-permute-start | bytes 36872 | tf_op jit(solution)/shard_map/ppermute | solution.py:57
  87.0 6.9 %collective-permute-start.10 = (f32[3,32,32]{2,1,0:T(8,128)S(1)}, f32[3,32,32]{2,1,0:T(8,128)S(1)}, u32[]{:S(2)}, u32[]{:S(2)}) collective-permute-start(f32[3,32,32]{2,1,0:T(8,128)S(1)} %add.159), channel_id=1, source_target_pairs={{0,2},{1,3},{2,0},{3,1},{4,6},{5,7},{6,4},{7,5},{8,10},{9,11},{10,... | collective-permute-start | bytes 36872 | tf_op jit(solution)/shard_map/ppermute | solution.py:57
  93.9 10.3 %collective-permute-start.11 = (f32[3,32,32]{2,1,0:T(8,128)S(1)}, f32[3,32,32]{2,1,0:T(8,128)S(1)}, u32[]{:S(2)}, u32[]{:S(2)}) collective-permute-start(f32[3,32,32]{2,1,0:T(8,128)S(1)} %add.160), channel_id=1, source_target_pairs={{0,4},{1,5},{2,6},{3,7},{4,0},{5,1},{6,2},{7,3},{8,12},{9,13},{10,... | collective-permute-start | bytes 36872 | tf_op jit(solution)/shard_map/ppermute | solution.py:57
  104.2 11.3 %collective-permute-start.12 = (f32[3,32,32]{2,1,0:T(8,128)S(1)}, f32[3,32,32]{2,1,0:T(8,128)S(1)}, u32[]{:S(2)}, u32[]{:S(2)}) collective-permute-start(f32[3,32,32]{2,1,0:T(8,128)S(1)} %add.161), channel_id=1, source_target_pairs={{0,12},{1,13},{2,14},{3,15},{4,8},{5,9},{6,10},{7,11},{8,4},{9,5},... | collective-permute-start | bytes 36872 | tf_op jit(solution)/shard_map/ppermute | solution.py:57

commit v5 on v4

--- a/solution.py
+++ b/solution.py
@@ -147,7 +147,8 @@
     output = from_blocks(out_b.astype(jnp.bfloat16).reshape(nb, row_count, block_size))
     scale = 1.0 / math.sqrt(map_count * lax.axis_size("map") * pix_count * patch_count)
     local_grad = jnp.einsum("krmcp,rmop->kco", terms, cot_b, preferred_element_type=jnp.float32)
-    filter_grad = butterfly_sum(local_grad, ("patch", "map")) * scale
+    flat = local_grad.reshape(-1, 128)
+    filter_grad = butterfly_sum(flat, ("patch", "map")).reshape(local_grad.shape) * scale
     return (output, from_blocks(input_grad), filter_grad)
 
 

time: 118 us -> 118 us (level)
  waiting for transfers between devices: 48.5 us -> 44 us
  local copies, waits for them, and re-layouts: 7.59 us -> 11 us
  matrix products: 4.34 us -> 5.98 us
    ppermute x9, waiting for transfers between devices: 27.1 us -> 23.4 us  [butterfly_sum(): x = x + lax.ppermute(x, axes, pairs)]
    unnamed x18 -> x24, local copies, waits for them, and re-layouts: 2.75 us -> 3.83 us
  transfers between devices with their start and end apart: 13 -> 13, of which waited for: 12 -> 12; matrix products, arithmetic and copies ran while one was open for 2% -> 5% of each run, Pallas kernels for 0% -> 0%
where the time goes in v5:
time: 118 us; the launch traced here: 117 us
  starting transfers between devices  50.6 us (43%)
  waiting for transfers between devices  44 us (37%)
  local copies, waits for them, and re-layouts  11 us (9%)
  matrix products  5.98 us (5%)
  other arithmetic  4.18 us (4%)
    ppermute x9, starting transfers between devices, butterfly_sum(): x = x + lax.ppermute(x, axes, pairs)  40.5 us
    ppermute x9, waiting for transfers between devices, butterfly_sum(): x = x + lax.ppermute(x, axes, pairs)  23.4 us
    ppermute x2, waiting for transfers between devices, exchange(): from_left = lax.ppermute(edge_right, 'patch', to_right)  13.7 us
    ppermute x2, waiting for transfers between devices, exchange(): from_right = lax.ppermute(edge_left, 'patch', to_left)  6.9 us
    ppermute x2, starting transfers between devices, exchange(): from_left = lax.ppermute(edge_right, 'patch', to_right)  6.24 us
    ppermute x2, starting transfers between devices, exchange(): from_right = lax.ppermute(edge_left, 'patch', to_left)  3.84 us
    unnamed x24, local copies, waits for them, and re-layouts  3.83 us
    reshape x2, local copies, waits for them, and re-layouts, to_blocks(): return field.reshape(row_count, nb, block_size).transpose(1, 0, 2)  2.51 us
  transfers between devices with their start and end apart: 13, of which 12 were waited for; matrix products, arithmetic and copies ran while one was open for 5% of the time, Pallas kernels for 0%

profile of v5, /device:TPU:24, one launch (start us, length us, event | category | flops | bytes accessed | tf_op | source)
XLA Modules:
  0.0 116.8 jit_solution(14299480598198539000)
XLA Ops:
  9.1 1.9 %collective-permute-start = (f32[2,2,64,256]{3,2,1,0:T(8,128)S(1)}, f32[2,2,64,256]{3,2,1,0:T(8,128)S(1)}, u32[]{:S(2)}, u32[]{:S(2)}) collective-permute-start(f32[2,2,64,256]{3,2,1,0:T(8,128)S(1)} %pad_maximum_fusion.5), channel_id=1, source_target_pairs={{0,32},{32,64},{64,96},{96,128},{128,160},{160,192},{192,224},{224... | collective-permute-start | bytes 786440 | tf_op jit(solution)/shard_map/ppermute | solution.py:85
  11.2 8.0 %collective-permute-done = f32[2,2,64,256]{3,2,1,0:T(8,128)S(1)} collective-permute-done((f32[2,2,64,256]{3,2,1,0:T(8,128)S(1)}, f32[2,2,64,256]{3,2,1,0:T(8,128)S(1)}, u32[]{:S(2)}, u32[]{:S(2)}) %collective-permute-start) | collective-permute-done | bytes 262176 | tf_op jit(solution)/shard_map/ppermute | solution.py:85
  19.2 1.9 %collective-permute-start.1 = (f32[2,2,64,256]{3,2,1,0:T(8,128)S(1)}, f32[2,2,64,256]{3,2,1,0:T(8,128)S(1)}, u32[]{:S(2)}, u32[]{:S(2)}) collective-permute-start(f32[2,2,64,256]{3,2,1,0:T(8,128)S(1)} %pad_maximum_fusion.6), channel_id=1, source_target_pairs={{32,0},{64,32},{96,64},{128,96},{160,128},{192,160},{224,192},{256... | collective-permute-start | bytes 786440 | tf_op jit(solution)/shard_map/ppermute | solution.py:84
  22.0 3.0 %collective-permute-done.1 = f32[2,2,64,256]{3,2,1,0:T(8,128)S(1)} collective-permute-done((f32[2,2,64,256]{3,2,1,0:T(8,128)S(1)}, f32[2,2,64,256]{3,2,1,0:T(8,128)S(1)}, u32[]{:S(2)}, u32[]{:S(2)}) %collective-permute-start.1) | collective-permute-done | bytes 262176 | tf_op jit(solution)/shard_map/ppermute | solution.py:84
  27.5 4.3 %collective-permute-start.2 = (f32[2,2,64,256]{3,2,1,0:T(8,128)S(1)}, f32[2,2,64,256]{3,2,1,0:T(8,128)S(1)}, u32[]{:S(2)}, u32[]{:S(2)}) collective-permute-start(f32[2,2,64,256]{3,2,1,0:T(8,128)S(1)} %pad_maximum_fusion.7), channel_id=1, source_target_pairs={{0,32},{32,64},{64,96},{96,128},{128,160},{160,192},{192,224},{224... | collective-permute-start | bytes 786440 | tf_op jit(solution)/shard_map/ppermute | solution.py:85
  32.0 5.7 %collective-permute-done.2 = f32[2,2,64,256]{3,2,1,0:T(8,128)S(1)} collective-permute-done((f32[2,2,64,256]{3,2,1,0:T(8,128)S(1)}, f32[2,2,64,256]{3,2,1,0:T(8,128)S(1)}, u32[]{:S(2)}, u32[]{:S(2)}) %collective-permute-start.2) | collective-permute-done | bytes 262176 | tf_op jit(solution)/shard_map/ppermute | solution.py:85
  37.9 1.9 %collective-permute-start.3 = (f32[2,2,64,256]{3,2,1,0:T(8,128)S(1)}, f32[2,2,64,256]{3,2,1,0:T(8,128)S(1)}, u32[]{:S(2)}, u32[]{:S(2)}) collective-permute-start(f32[2,2,64,256]{3,2,1,0:T(8,128)S(1)} %pad_maximum_fusion.8), channel_id=1, source_target_pairs={{32,0},{64,32},{96,64},{128,96},{160,128},{192,160},{224,192},{256... | collective-permute-start | bytes 786440 | tf_op jit(solution)/shard_map/ppermute | solution.py:84
  39.8 3.9 %collective-permute-done.3 = f32[2,2,64,256]{3,2,1,0:T(8,128)S(1)} collective-permute-done((f32[2,2,64,256]{3,2,1,0:T(8,128)S(1)}, f32[2,2,64,256]{3,2,1,0:T(8,128)S(1)}, u32[]{:S(2)}, u32[]{:S(2)}) %collective-permute-start.3) | collective-permute-done | bytes 262176 | tf_op jit(solution)/shard_map/ppermute | solution.py:84
  47.7 5.0 %collective-permute-start.4 = (f32[24,128]{1,0:T(8,128)S(1)}, f32[24,128]{1,0:T(8,128)S(1)}, u32[]{:S(2)}, u32[]{:S(2)}) collective-permute-start(f32[24,128]{1,0:T(8,128)S(1)} %reshape.202), channel_id=1, source_target_pairs={{0,32},{1,33},{2,34},{3,35},{4,36},{5,37},{6,38},{7,39},{8,40},{9,... | collective-permute-start | bytes 36872 | tf_op jit(solution)/shard_map/ppermute | solution.py:57
  53.6 1.9 %collective-permute-start.5 = (f32[24,128]{1,0:T(8,128)S(1)}, f32[24,128]{1,0:T(8,128)S(1)}, u32[]{:S(2)}, u32[]{:S(2)}) collective-permute-start(f32[24,128]{1,0:T(8,128)S(1)} %add.154), channel_id=1, source_target_pairs={{0,16},{1,17},{2,18},{3,19},{4,20},{5,21},{6,22},{7,23},{8,24},{9,... | collective-permute-start | bytes 36872 | tf_op jit(solution)/shard_map/ppermute | solution.py:57
  55.5 3.7 %collective-permute-done.5 = f32[24,128]{1,0:T(8,128)S(1)} collective-permute-done((f32[24,128]{1,0:T(8,128)S(1)}, f32[24,128]{1,0:T(8,128)S(1)}, u32[]{:S(2)}, u32[]{:S(2)}) %collective-permute-start.5) | collective-permute-done | bytes 12320 | tf_op jit(solution)/shard_map/ppermute | solution.py:57
  59.1 8.6 %collective-permute-start.6 = (f32[24,128]{1,0:T(8,128)S(1)}, f32[24,128]{1,0:T(8,128)S(1)}, u32[]{:S(2)}, u32[]{:S(2)}) collective-permute-start(f32[24,128]{1,0:T(8,128)S(1)} %add.155), channel_id=1, source_target_pairs={{0,80},{1,81},{2,82},{3,83},{4,84},{5,85},{6,86},{7,87},{8,88},{9,... | collective-permute-start | bytes 36872 | tf_op jit(solution)/shard_map/ppermute | solution.py:57
  67.7 1.7 %collective-permute-done.6 = f32[24,128]{1,0:T(8,128)S(1)} collective-permute-done((f32[24,128]{1,0:T(8,128)S(1)}, f32[24,128]{1,0:T(8,128)S(1)}, u32[]{:S(2)}, u32[]{:S(2)}) %collective-permute-start.6) | collective-permute-done | bytes 12320 | tf_op jit(solution)/shard_map/ppermute | solution.py:57
  69.4 1.9 %collective-permute-start.7 = (f32[24,128]{1,0:T(8,128)S(1)}, f32[24,128]{1,0:T(8,128)S(1)}, u32[]{:S(2)}, u32[]{:S(2)}) collective-permute-start(f32[24,128]{1,0:T(8,128)S(1)} %add.156), channel_id=1, source_target_pairs={{0,128},{1,129},{2,130},{3,131},{4,132},{5,133},{6,134},{7,135},{8... | collective-permute-start | bytes 36872 | tf_op jit(solution)/shard_map/ppermute | solution.py:57
  71.3 3.7 %collective-permute-done.7 = f32[24,128]{1,0:T(8,128)S(1)} collective-permute-done((f32[24,128]{1,0:T(8,128)S(1)}, f32[24,128]{1,0:T(8,128)S(1)}, u32[]{:S(2)}, u32[]{:S(2)}) %collective-permute-start.7) | collective-permute-done | bytes 12320 | tf_op jit(solution)/shard_map/ppermute | solution.py:57
  75.0 3.7 %collective-permute-start.8 = (f32[24,128]{1,0:T(8,128)S(1)}, f32[24,128]{1,0:T(8,128)S(1)}, u32[]{:S(2)}, u32[]{:S(2)}) collective-permute-start(f32[24,128]{1,0:T(8,128)S(1)} %add.157), channel_id=1, source_target_pairs={{0,384},{1,385},{2,386},{3,387},{4,388},{5,389},{6,390},{7,391},{8... | collective-permute-start | bytes 36872 | tf_op jit(solution)/shard_map/ppermute | solution.py:57
  78.7 3.1 %collective-permute-done.8 = f32[24,128]{1,0:T(8,128)S(1)} collective-permute-done((f32[24,128]{1,0:T(8,128)S(1)}, f32[24,128]{1,0:T(8,128)S(1)}, u32[]{:S(2)}, u32[]{:S(2)}) %collective-permute-start.8) | collective-permute-done | bytes 12320 | tf_op jit(solution)/shard_map/ppermute | solution.py:57
  81.8 1.9 %collective-permute-start.9 = (f32[24,128]{1,0:T(8,128)S(1)}, f32[24,128]{1,0:T(8,128)S(1)}, u32[]{:S(2)}, u32[]{:S(2)}) collective-permute-start(f32[24,128]{1,0:T(8,128)S(1)} %add.158), channel_id=1, source_target_pairs={{0,1},{1,0},{2,3},{3,2},{4,5},{5,4},{6,7},{7,6},{8,9},{9,8},{10,11... | collective-permute-start | bytes 36872 | tf_op jit(solution)/shard_map/ppermute | solution.py:57
  83.7 3.7 %collective-permute-done.9 = f32[24,128]{1,0:T(8,128)S(1)} collective-permute-done((f32[24,128]{1,0:T(8,128)S(1)}, f32[24,128]{1,0:T(8,128)S(1)}, u32[]{:S(2)}, u32[]{:S(2)}) %collective-permute-start.9) | collective-permute-done | bytes 12320 | tf_op jit(solution)/shard_map/ppermute | solution.py:57
  87.4 1.9 %collective-permute-start.10 = (f32[24,128]{1,0:T(8,128)S(1)}, f32[24,128]{1,0:T(8,128)S(1)}, u32[]{:S(2)}, u32[]{:S(2)}) collective-permute-start(f32[24,128]{1,0:T(8,128)S(1)} %add.159), channel_id=1, source_target_pairs={{0,2},{1,3},{2,0},{3,1},{4,6},{5,7},{6,4},{7,5},{8,10},{9,11},{10,... | collective-permute-start | bytes 36872 | tf_op jit(solution)/shard_map/ppermute | solution.py:57
  90.2 3.6 %collective-permute-done.10 = f32[24,128]{1,0:T(8,128)S(1)} collective-permute-done((f32[24,128]{1,0:T(8,128)S(1)}, f32[24,128]{1,0:T(8,128)S(1)}, u32[]{:S(2)}, u32[]{:S(2)}) %collective-permute-start.10) | collective-permute-done | bytes 12320 | tf_op jit(solution)/shard_map/ppermute | solution.py:57
  93.8 6.1 %collective-permute-start.11 = (f32[24,128]{1,0:T(8,128)S(1)}, f32[24,128]{1,0:T(8,128)S(1)}, u32[]{:S(2)}, u32[]{:S(2)}) collective-permute-start(f32[24,128]{1,0:T(8,128)S(1)} %add.160), channel_id=1, source_target_pairs={{0,4},{1,5},{2,6},{3,7},{4,0},{5,1},{6,2},{7,3},{8,12},{9,13},{10,... | collective-permute-start | bytes 36872 | tf_op jit(solution)/shard_map/ppermute | solution.py:57
  100.1 3.2 %collective-permute-done.11 = f32[24,128]{1,0:T(8,128)S(1)} collective-permute-done((f32[24,128]{1,0:T(8,128)S(1)}, f32[24,128]{1,0:T(8,128)S(1)}, u32[]{:S(2)}, u32[]{:S(2)}) %collective-permute-start.11) | collective-permute-done | bytes 12320 | tf_op jit(solution)/shard_map/ppermute | solution.py:57
  103.3 9.4 %collective-permute-start.12 = (f32[24,128]{1,0:T(8,128)S(1)}, f32[24,128]{1,0:T(8,128)S(1)}, u32[]{:S(2)}, u32[]{:S(2)}) collective-permute-start(f32[24,128]{1,0:T(8,128)S(1)} %add.161), channel_id=1, source_target_pairs={{0,12},{1,13},{2,14},{3,15},{4,8},{5,9},{6,10},{7,11},{8,4},{9,5},... | collective-permute-start | bytes 36872 | tf_op jit(solution)/shard_map/ppermute | solution.py:57
  (82 shorter events, 22.0 us)
Async XLA Ops:
  0.6 5.4 %copy-start = (bf16[6,3,256,256]{3,2,1,0:T(8,128)(2,1)S(1)}, bf16[6,3,256,256]{3,2,1,0:T(8,128)(2,1)}, u32[]{:S(2)}) copy-start(bf16[6,3,256,256]{3,2,1,0:T(8,128)(2,1)} %param.15) | copy-start | bytes 7077892
  2.0 4.1 %copy-start.5 = (bf16[64,6,256]{2,1,0:T(8,128)(2,1)}, bf16[64,6,256]{2,1,0:T(8,128)(2,1)S(1)}, u32[]{:S(2)}) copy-start(bf16[64,6,256]{2,1,0:T(8,128)(2,1)S(1)} %reshape.193) | copy-start | bytes 589828
  5.0 1.0 copy-start.2
  6.0 1.6 %copy-start.9 = (s32[6,3]{0,1:T(4,128)S(1)}, s32[6,3]{0,1:T(4,128)}, u32[]{:S(2)}) copy-start(s32[6,3]{0,1:T(4,128)} %param.16) | copy-start | bytes 220
  6.6 1.0 copy-start.1
  9.1 10.1 %collective-permute-start = (f32[2,2,64,256]{3,2,1,0:T(8,128)S(1)}, f32[2,2,64,256]{3,2,1,0:T(8,128)S(1)}, u32[]{:S(2)}, u32[]{:S(2)}) collective-permute-start(f32[2,2,64,256]{3,2,1,0:T(8,128)S(1)} %pad_maximum_fusion.5), channel_id=1, source_target_pairs={{0,32},{32,64},{64,96},{96,128},{128,160},{160,192},{192,224},{224... | collective-permute-start | bytes 786440 | tf_op jit(solution)/shard_map/ppermute | solution.py:85
  11.1 10.0 %copy-start.3 = (f32[3,6,2,32,256]{4,3,0,2,1:T(8,128)S(1)}, f32[3,6,2,32,256]{4,3,0,2,1:T(8,128)}, u32[]{:S(2)}) copy-start(f32[3,6,2,32,256]{4,3,0,2,1:T(8,128)} %copy-done.2) | copy-start | bytes 3538948
  19.2 5.8 %collective-permute-start.1 = (f32[2,2,64,256]{3,2,1,0:T(8,128)S(1)}, f32[2,2,64,256]{3,2,1,0:T(8,128)S(1)}, u32[]{:S(2)}, u32[]{:S(2)}) collective-permute-start(f32[2,2,64,256]{3,2,1,0:T(8,128)S(1)} %pad_maximum_fusion.6), channel_id=1, source_target_pairs={{32,0},{64,32},{96,64},{128,96},{160,128},{192,160},{224,192},{256... | collective-permute-start | bytes 786440 | tf_op jit(solution)/shard_map/ppermute | solution.py:84
  25.7 0.9 copy-start.7
  27.4 17.8 %copy-start.10 = (bf16[6,64,256]{2,1,0:T(8,128)(2,1)}, bf16[6,64,256]{2,1,0:T(8,128)(2,1)S(1)}, u32[]{:S(2)}) copy-start(bf16[6,64,256]{2,1,0:T(8,128)(2,1)S(1)} %get-tuple-element.82) | copy-start | bytes 589828
  27.5 10.3 %collective-permute-start.2 = (f32[2,2,64,256]{3,2,1,0:T(8,128)S(1)}, f32[2,2,64,256]{3,2,1,0:T(8,128)S(1)}, u32[]{:S(2)}, u32[]{:S(2)}) collective-permute-start(f32[2,2,64,256]{3,2,1,0:T(8,128)S(1)} %pad_maximum_fusion.7), channel_id=1, source_target_pairs={{0,32},{32,64},{64,96},{96,128},{128,160},{160,192},{192,224},{224... | collective-permute-start | bytes 786440 | tf_op jit(solution)/shard_map/ppermute | solution.py:85
  37.9 5.8 %collective-permute-start.3 = (f32[2,2,64,256]{3,2,1,0:T(8,128)S(1)}, f32[2,2,64,256]{3,2,1,0:T(8,128)S(1)}, u32[]{:S(2)}, u32[]{:S(2)}) collective-permute-start(f32[2,2,64,256]{3,2,1,0:T(8,128)S(1)} %pad_maximum_fusion.8), channel_id=1, source_target_pairs={{32,0},{64,32},{96,64},{128,96},{160,128},{192,160},{224,192},{256... | collective-permute-start | bytes 786440 | tf_op jit(solution)/shard_map/ppermute | solution.py:84
  43.7 0.7 copy-start.8
  44.4 1.5 %copy-start.6 = (bf16[64,6,256]{2,1,0:T(8,128)(2,1)S(1)}, bf16[64,6,256]{2,1,0:T(8,128)(2,1)}, u32[]{:S(2)}) copy-start(bf16[64,6,256]{2,1,0:T(8,128)(2,1)} %copy-done.5) | copy-start | bytes 589828
  45.2 54.8 %copy-start.4 = (f32[1,6,2,32,256]{4,3,0,2,1:T(8,128)S(1)}, f32[1,6,2,32,256]{4,3,0,2,1:T(8,128)}, u32[]{:S(2)}) copy-start(f32[1,6,2,32,256]{4,3,0,2,1:T(8,128)} %get-tuple-element.65) | copy-start | bytes 1179652
  47.7 5.8 %collective-permute-start.4 = (f32[24,128]{1,0:T(8,128)S(1)}, f32[24,128]{1,0:T(8,128)S(1)}, u32[]{:S(2)}, u32[]{:S(2)}) collective-permute-start(f32[24,128]{1,0:T(8,128)S(1)} %reshape.202), channel_id=1, source_target_pairs={{0,32},{1,33},{2,34},{3,35},{4,36},{5,37},{6,38},{7,39},{8,40},{9,... | collective-permute-start | bytes 36872 | tf_op jit(solution)/shard_map/ppermute | solution.py:57
  53.6 5.6 %collective-permute-start.5 = (f32[24,128]{1,0:T(8,128)S(1)}, f32[24,128]{1,0:T(8,128)S(1)}, u32[]{:S(2)}, u32[]{:S(2)}) collective-permute-start(f32[24,128]{1,0:T(8,128)S(1)} %add.154), channel_id=1, source_target_pairs={{0,16},{1,17},{2,18},{3,19},{4,20},{5,21},{6,22},{7,23},{8,24},{9,... | collective-permute-start | bytes 36872 | tf_op jit(solution)/shard_map/ppermute | solution.py:57
  59.1 10.3 %collective-permute-start.6 = (f32[24,128]{1,0:T(8,128)S(1)}, f32[24,128]{1,0:T(8,128)S(1)}, u32[]{:S(2)}, u32[]{:S(2)}) collective-permute-start(f32[24,128]{1,0:T(8,128)S(1)} %add.155), channel_id=1, source_target_pairs={{0,80},{1,81},{2,82},{3,83},{4,84},{5,85},{6,86},{7,87},{8,88},{9,... | collective-permute-start | bytes 36872 | tf_op jit(solution)/shard_map/ppermute | solution.py:57
  69.4 5.6 %collective-permute-start.7 = (f32[24,128]{1,0:T(8,128)S(1)}, f32[24,128]{1,0:T(8,128)S(1)}, u32[]{:S(2)}, u32[]{:S(2)}) collective-permute-start(f32[24,128]{1,0:T(8,128)S(1)} %add.156), channel_id=1, source_target_pairs={{0,128},{1,129},{2,130},{3,131},{4,132},{5,133},{6,134},{7,135},{8... | collective-permute-start | bytes 36872 | tf_op jit(solution)/shard_map/ppermute | solution.py:57
  75.0 6.8 %collective-permute-start.8 = (f32[24,128]{1,0:T(8,128)S(1)}, f32[24,128]{1,0:T(8,128)S(1)}, u32[]{:S(2)}, u32[]{:S(2)}) collective-permute-start(f32[24,128]{1,0:T(8,128)S(1)} %add.157), channel_id=1, source_target_pairs={{0,384},{1,385},{2,386},{3,387},{4,388},{5,389},{6,390},{7,391},{8... | collective-permute-start | bytes 36872 | tf_op jit(solution)/shard_map/ppermute | solution.py:57
  81.8 5.6 %collective-permute-start.9 = (f32[24,128]{1,0:T(8,128)S(1)}, f32[24,128]{1,0:T(8,128)S(1)}, u32[]{:S(2)}, u32[]{:S(2)}) collective-permute-start(f32[24,128]{1,0:T(8,128)S(1)} %add.158), channel_id=1, source_target_pairs={{0,1},{1,0},{2,3},{3,2},{4,5},{5,4},{6,7},{7,6},{8,9},{9,8},{10,11... | collective-permute-start | bytes 36872 | tf_op jit(solution)/shard_map/ppermute | solution.py:57
  87.4 6.5 %collective-permute-start.10 = (f32[24,128]{1,0:T(8,128)S(1)}, f32[24,128]{1,0:T(8,128)S(1)}, u32[]{:S(2)}, u32[]{:S(2)}) collective-permute-start(f32[24,128]{1,0:T(8,128)S(1)} %add.159), channel_id=1, source_target_pairs={{0,2},{1,3},{2,0},{3,1},{4,6},{5,7},{6,4},{7,5},{8,10},{9,11},{10,... | collective-permute-start | bytes 36872 | tf_op jit(solution)/shard_map/ppermute | solution.py:57
  93.8 9.5 %collective-permute-start.11 = (f32[24,128]{1,0:T(8,128)S(1)}, f32[24,128]{1,0:T(8,128)S(1)}, u32[]{:S(2)}, u32[]{:S(2)}) collective-permute-start(f32[24,128]{1,0:T(8,128)S(1)} %add.160), channel_id=1, source_target_pairs={{0,4},{1,5},{2,6},{3,7},{4,0},{5,1},{6,2},{7,3},{8,12},{9,13},{10,... | collective-permute-start | bytes 36872 | tf_op jit(solution)/shard_map/ppermute | solution.py:57
  103.3 12.8 %collective-permute-start.12 = (f32[24,128]{1,0:T(8,128)S(1)}, f32[24,128]{1,0:T(8,128)S(1)}, u32[]{:S(2)}, u32[]{:S(2)}) collective-permute-start(f32[24,128]{1,0:T(8,128)S(1)} %add.161), channel_id=1, source_target_pairs={{0,12},{1,13},{2,14},{3,15},{4,8},{5,9},{6,10},{7,11},{8,4},{9,5},... | collective-permute-start | bytes 36872 | tf_op jit(solution)/shard_map/ppermute | solution.py:57
  (1 other events, 0.7 us)

commit v6 on v5

--- a/solution.py
+++ b/solution.py
@@ -81,6 +81,7 @@
     to_left = [((i + 1) % patch_count, i) for i in range(patch_count)]
 
     def exchange(edge_left, edge_right):
+        edge_left, edge_right = lax.optimization_barrier((edge_left, edge_right))
         from_right = lax.ppermute(edge_left, "patch", to_left)
         from_left = lax.ppermute(edge_right, "patch", to_right)
         return from_left, from_right

time: 118 us -> 111 us (0.941)
  waiting for transfers between devices: 44 us -> 30.5 us
  starting transfers between devices: 50.6 us -> 55.9 us
  local copies, waits for them, and re-layouts: 11 us -> 12.7 us
    ppermute x2, waiting for transfers between devices: 13.7 us -> 2.53 us  [exchange(): from_left = lax.ppermute(edge_right, 'patch', to_right)]
    ppermute x2, starting transfers between devices: 3.84 us -> 7.97 us  [exchange(): from_right = lax.ppermute(edge_left, 'patch', to_left)]
    ppermute x2, starting transfers between devices: 6.24 us -> 8.83 us  [exchange(): from_left = lax.ppermute(edge_right, 'patch', to_right)]
    ppermute x2, waiting for transfers between devices: 6.9 us -> 4.35 us  [exchange(): from_right = lax.ppermute(edge_left, 'patch', to_left)]
    unnamed x24 -> x54, local copies, waits for them, and re-layouts: 3.83 us -> 5.43 us
    ppermute x9, starting transfers between devices: 40.5 us -> 39.1 us  [butterfly_sum(): x = x + lax.ppermute(x, axes, pairs)]
  transfers between devices with their start and end apart: 13 -> 13, of which waited for: 12 -> 12; matrix products, arithmetic and copies ran while one was open for 5% -> 4% of each run, Pallas kernels for 0% -> 0%
where the time goes in v6:
time: 111 us; the launch traced here: 110 us
  starting transfers between devices  55.9 us (50%)
  waiting for transfers between devices  30.5 us (27%)
  local copies, waits for them, and re-layouts  12.7 us (11%)
  matrix products  4.96 us (4%)
  other arithmetic  4.44 us (4%)
  between operations  1.26 us (1%)
    ppermute x9, starting transfers between devices, butterfly_sum(): x = x + lax.ppermute(x, axes, pairs)  39.1 us
    ppermute x9, waiting for transfers between devices, butterfly_sum(): x = x + lax.ppermute(x, axes, pairs)  23.7 us
    ppermute x2, starting transfers between devices, exchange(): from_left = lax.ppermute(edge_right, 'patch', to_right)  8.83 us
    ppermute x2, starting transfers between devices, exchange(): from_right = lax.ppermute(edge_left, 'patch', to_left)  7.97 us
    unnamed x54, local copies, waits for them, and re-layouts  5.43 us
    ppermute x2, waiting for transfers between devices, exchange(): from_right = lax.ppermute(edge_left, 'patch', to_left)  4.35 us
    reshape x2, local copies, waits for them, and re-layouts, to_blocks(): return field.reshape(row_count, nb, block_size).transpose(1, 0, 2)  2.6 us
    ppermute x2, waiting for transfers between devices, exchange(): from_left = lax.ppermute(edge_right, 'patch', to_right)  2.53 us
  transfers between devices with their start and end apart: 13, of which 12 were waited for; matrix products, arithmetic and copies ran while one was open for 4% of the time, Pallas kernels for 0%

profile of v6, /device:TPU:24, one launch (start us, length us, event | category | flops | bytes accessed | tf_op | source)
XLA Modules:
  0.0 109.8 jit_solution(3307021427413712889)
XLA Ops:
  9.2 1.4 %fusion.60 = (f32[6,64,256]{2,1,0:T(8,128)S(1)}, f32[6,64,256]{2,1,0:T(8,128)S(1)}, f32[6,64,256]{2,1,0:T(8,128)S(1)}, f32[6,64,256]{2,1,0:T(8,128)S(1)}) fusion(f32[6,3,64,256]{3,2,0,1:T(8,128)} %copy-done.5, pred[6]{0:T(512)(128)(4,1)S(1)} %get-tuple-element.87, pred[6]{0:T(512)(128)(4,1)S(1)} %get-tuple-element.88), kind=kLoop, calls=%fused_computation.71 | loop fusion | flops 393216 | bytes 2359308 | tf_op jit(solution)/shard_map/jit(_where)/select_n | solution.py:109
  10.7 1.9 %collective-permute-start = (f32[2,2,64,256]{3,2,1,0:T(8,128)S(1)}, f32[2,2,64,256]{3,2,1,0:T(8,128)S(1)}, u32[]{:S(2)}, u32[]{:S(2)}) collective-permute-start(f32[2,2,64,256]{3,2,1,0:T(8,128)S(1)} %get-tuple-element.55), channel_id=1, source_target_pairs={{0,32},{32,64},{64,96},{96,128},{128,160},{160,192},{192,224},{224... | collective-permute-start | bytes 786440 | tf_op jit(solution)/shard_map/ppermute | solution.py:86
  12.6 6.0 %collective-permute-start.1 = (f32[2,2,64,256]{3,2,1,0:T(8,128)S(1)}, f32[2,2,64,256]{3,2,1,0:T(8,128)S(1)}, u32[]{:S(2)}, u32[]{:S(2)}) collective-permute-start(f32[2,2,64,256]{3,2,1,0:T(8,128)S(1)} %get-tuple-element.56), channel_id=1, source_target_pairs={{32,0},{64,32},{96,64},{128,96},{160,128},{192,160},{224,192},{256... | collective-permute-start | bytes 786440 | tf_op jit(solution)/shard_map/ppermute | solution.py:85
  20.8 1.7 %collective-permute-done.1 = f32[2,2,64,256]{3,2,1,0:T(8,128)S(1)} collective-permute-done((f32[2,2,64,256]{3,2,1,0:T(8,128)S(1)}, f32[2,2,64,256]{3,2,1,0:T(8,128)S(1)}, u32[]{:S(2)}, u32[]{:S(2)}) %collective-permute-start.1) | collective-permute-done | bytes 262176 | tf_op jit(solution)/shard_map/ppermute | solution.py:85
  25.3 6.9 %collective-permute-start.2 = (f32[2,2,64,256]{3,2,1,0:T(8,128)S(1)}, f32[2,2,64,256]{3,2,1,0:T(8,128)S(1)}, u32[]{:S(2)}, u32[]{:S(2)}) collective-permute-start(f32[2,2,64,256]{3,2,1,0:T(8,128)S(1)} %pad_maximum_fusion.8), channel_id=1, source_target_pairs={{0,32},{32,64},{64,96},{96,128},{128,160},{160,192},{192,224},{224... | collective-permute-start | bytes 786440 | tf_op jit(solution)/shard_map/ppermute | solution.py:86
  32.2 1.9 %collective-permute-start.3 = (f32[2,2,64,256]{3,2,1,0:T(8,128)S(1)}, f32[2,2,64,256]{3,2,1,0:T(8,128)S(1)}, u32[]{:S(2)}, u32[]{:S(2)}) collective-permute-start(f32[2,2,64,256]{3,2,1,0:T(8,128)S(1)} %pad_maximum_fusion.7), channel_id=1, source_target_pairs={{32,0},{64,32},{96,64},{128,96},{160,128},{192,160},{224,192},{256... | collective-permute-start | bytes 786440 | tf_op jit(solution)/shard_map/ppermute | solution.py:85
  34.1 1.4 %collective-permute-done.2 = f32[2,2,64,256]{3,2,1,0:T(8,128)S(1)} collective-permute-done((f32[2,2,64,256]{3,2,1,0:T(8,128)S(1)}, f32[2,2,64,256]{3,2,1,0:T(8,128)S(1)}, u32[]{:S(2)}, u32[]{:S(2)}) %collective-permute-start.2) | collective-permute-done | bytes 262176 | tf_op jit(solution)/shard_map/ppermute | solution.py:86
  35.6 2.6 %collective-permute-done.3 = f32[2,2,64,256]{3,2,1,0:T(8,128)S(1)} collective-permute-done((f32[2,2,64,256]{3,2,1,0:T(8,128)S(1)}, f32[2,2,64,256]{3,2,1,0:T(8,128)S(1)}, u32[]{:S(2)}, u32[]{:S(2)}) %collective-permute-start.3) | collective-permute-done | bytes 262176 | tf_op jit(solution)/shard_map/ppermute | solution.py:85
  42.3 8.1 %collective-permute-start.4 = (f32[24,128]{1,0:T(8,128)S(1)}, f32[24,128]{1,0:T(8,128)S(1)}, u32[]{:S(2)}, u32[]{:S(2)}) collective-permute-start(f32[24,128]{1,0:T(8,128)S(1)} %reshape.202), channel_id=1, source_target_pairs={{0,32},{1,33},{2,34},{3,35},{4,36},{5,37},{6,38},{7,39},{8,40},{9,... | collective-permute-start | bytes 36872 | tf_op jit(solution)/shard_map/ppermute | solution.py:57
  51.2 1.9 %collective-permute-start.5 = (f32[24,128]{1,0:T(8,128)S(1)}, f32[24,128]{1,0:T(8,128)S(1)}, u32[]{:S(2)}, u32[]{:S(2)}) collective-permute-start(f32[24,128]{1,0:T(8,128)S(1)} %add.154), channel_id=1, source_target_pairs={{0,16},{1,17},{2,18},{3,19},{4,20},{5,21},{6,22},{7,23},{8,24},{9,... | collective-permute-start | bytes 36872 | tf_op jit(solution)/shard_map/ppermute | solution.py:57
  53.1 3.7 %collective-permute-done.5 = f32[24,128]{1,0:T(8,128)S(1)} collective-permute-done((f32[24,128]{1,0:T(8,128)S(1)}, f32[24,128]{1,0:T(8,128)S(1)}, u32[]{:S(2)}, u32[]{:S(2)}) %collective-permute-start.5) | collective-permute-done | bytes 12320 | tf_op jit(solution)/shard_map/ppermute | solution.py:57
  56.8 5.5 %collective-permute-start.6 = (f32[24,128]{1,0:T(8,128)S(1)}, f32[24,128]{1,0:T(8,128)S(1)}, u32[]{:S(2)}, u32[]{:S(2)}) collective-permute-start(f32[24,128]{1,0:T(8,128)S(1)} %add.155), channel_id=1, source_target_pairs={{0,80},{1,81},{2,82},{3,83},{4,84},{5,85},{6,86},{7,87},{8,88},{9,... | collective-permute-start | bytes 36872 | tf_op jit(solution)/shard_map/ppermute | solution.py:57
  62.3 1.7 %collective-permute-done.6 = f32[24,128]{1,0:T(8,128)S(1)} collective-permute-done((f32[24,128]{1,0:T(8,128)S(1)}, f32[24,128]{1,0:T(8,128)S(1)}, u32[]{:S(2)}, u32[]{:S(2)}) %collective-permute-start.6) | collective-permute-done | bytes 12320 | tf_op jit(solution)/shard_map/ppermute | solution.py:57
  63.9 1.9 %collective-permute-start.7 = (f32[24,128]{1,0:T(8,128)S(1)}, f32[24,128]{1,0:T(8,128)S(1)}, u32[]{:S(2)}, u32[]{:S(2)}) collective-permute-start(f32[24,128]{1,0:T(8,128)S(1)} %add.156), channel_id=1, source_target_pairs={{0,128},{1,129},{2,130},{3,131},{4,132},{5,133},{6,134},{7,135},{8... | collective-permute-start | bytes 36872 | tf_op jit(solution)/shard_map/ppermute | solution.py:57
  65.8 3.7 %collective-permute-done.7 = f32[24,128]{1,0:T(8,128)S(1)} collective-permute-done((f32[24,128]{1,0:T(8,128)S(1)}, f32[24,128]{1,0:T(8,128)S(1)}, u32[]{:S(2)}, u32[]{:S(2)}) %collective-permute-start.7) | collective-permute-done | bytes 12320 | tf_op jit(solution)/shard_map/ppermute | solution.py:57
  69.5 3.8 %collective-permute-start.8 = (f32[24,128]{1,0:T(8,128)S(1)}, f32[24,128]{1,0:T(8,128)S(1)}, u32[]{:S(2)}, u32[]{:S(2)}) collective-permute-start(f32[24,128]{1,0:T(8,128)S(1)} %add.157), channel_id=1, source_target_pairs={{0,384},{1,385},{2,386},{3,387},{4,388},{5,389},{6,390},{7,391},{8... | collective-permute-start | bytes 36872 | tf_op jit(solution)/shard_map/ppermute | solution.py:57
  74.7 1.8 %collective-permute-done.8 = f32[24,128]{1,0:T(8,128)S(1)} collective-permute-done((f32[24,128]{1,0:T(8,128)S(1)}, f32[24,128]{1,0:T(8,128)S(1)}, u32[]{:S(2)}, u32[]{:S(2)}) %collective-permute-start.8) | collective-permute-done | bytes 12320 | tf_op jit(solution)/shard_map/ppermute | solution.py:57
  76.4 1.9 %collective-permute-start.9 = (f32[24,128]{1,0:T(8,128)S(1)}, f32[24,128]{1,0:T(8,128)S(1)}, u32[]{:S(2)}, u32[]{:S(2)}) collective-permute-start(f32[24,128]{1,0:T(8,128)S(1)} %add.158), channel_id=1, source_target_pairs={{0,1},{1,0},{2,3},{3,2},{4,5},{5,4},{6,7},{7,6},{8,9},{9,8},{10,11... | collective-permute-start | bytes 36872 | tf_op jit(solution)/shard_map/ppermute | solution.py:57
  78.4 3.6 %collective-permute-done.9 = f32[24,128]{1,0:T(8,128)S(1)} collective-permute-done((f32[24,128]{1,0:T(8,128)S(1)}, f32[24,128]{1,0:T(8,128)S(1)}, u32[]{:S(2)}, u32[]{:S(2)}) %collective-permute-start.9) | collective-permute-done | bytes 12320 | tf_op jit(solution)/shard_map/ppermute | solution.py:57
  82.0 1.9 %collective-permute-start.10 = (f32[24,128]{1,0:T(8,128)S(1)}, f32[24,128]{1,0:T(8,128)S(1)}, u32[]{:S(2)}, u32[]{:S(2)}) collective-permute-start(f32[24,128]{1,0:T(8,128)S(1)} %add.159), channel_id=1, source_target_pairs={{0,2},{1,3},{2,0},{3,1},{4,6},{5,7},{6,4},{7,5},{8,10},{9,11},{10,... | collective-permute-start | bytes 36872 | tf_op jit(solution)/shard_map/ppermute | solution.py:57
  84.0 4.5 %collective-permute-done.10 = f32[24,128]{1,0:T(8,128)S(1)} collective-permute-done((f32[24,128]{1,0:T(8,128)S(1)}, f32[24,128]{1,0:T(8,128)S(1)}, u32[]{:S(2)}, u32[]{:S(2)}) %collective-permute-start.10) | collective-permute-done | bytes 12320 | tf_op jit(solution)/shard_map/ppermute | solution.py:57
  88.5 5.4 %collective-permute-start.11 = (f32[24,128]{1,0:T(8,128)S(1)}, f32[24,128]{1,0:T(8,128)S(1)}, u32[]{:S(2)}, u32[]{:S(2)}) collective-permute-start(f32[24,128]{1,0:T(8,128)S(1)} %add.160), channel_id=1, source_target_pairs={{0,4},{1,5},{2,6},{3,7},{4,0},{5,1},{6,2},{7,3},{8,12},{9,13},{10,... | collective-permute-start | bytes 36872 | tf_op jit(solution)/shard_map/ppermute | solution.py:57
  94.0 4.0 %collective-permute-done.11 = f32[24,128]{1,0:T(8,128)S(1)} collective-permute-done((f32[24,128]{1,0:T(8,128)S(1)}, f32[24,128]{1,0:T(8,128)S(1)}, u32[]{:S(2)}, u32[]{:S(2)}) %collective-permute-start.11) | collective-permute-done | bytes 12320 | tf_op jit(solution)/shard_map/ppermute | solution.py:57
  98.1 8.6 %collective-permute-start.12 = (f32[24,128]{1,0:T(8,128)S(1)}, f32[24,128]{1,0:T(8,128)S(1)}, u32[]{:S(2)}, u32[]{:S(2)}) collective-permute-start(f32[24,128]{1,0:T(8,128)S(1)} %add.161), channel_id=1, source_target_pairs={{0,12},{1,13},{2,14},{3,15},{4,8},{5,9},{6,10},{7,11},{8,4},{9,5},... | collective-permute-start | bytes 36872 | tf_op jit(solution)/shard_map/ppermute | solution.py:57
  (112 shorter events, 22.6 us)
Async XLA Ops:
  10.7 10.1 %collective-permute-start = (f32[2,2,64,256]{3,2,1,0:T(8,128)S(1)}, f32[2,2,64,256]{3,2,1,0:T(8,128)S(1)}, u32[]{:S(2)}, u32[]{:S(2)}) collective-permute-start(f32[2,2,64,256]{3,2,1,0:T(8,128)S(1)} %get-tuple-element.55), channel_id=1, source_target_pairs={{0,32},{32,64},{64,96},{96,128},{128,160},{160,192},{192,224},{224... | collective-permute-start | bytes 786440 | tf_op jit(solution)/shard_map/ppermute | solution.py:86
  12.6 9.9 %collective-permute-start.1 = (f32[2,2,64,256]{3,2,1,0:T(8,128)S(1)}, f32[2,2,64,256]{3,2,1,0:T(8,128)S(1)}, u32[]{:S(2)}, u32[]{:S(2)}) collective-permute-start(f32[2,2,64,256]{3,2,1,0:T(8,128)S(1)} %get-tuple-element.56), channel_id=1, source_target_pairs={{32,0},{64,32},{96,64},{128,96},{160,128},{192,160},{224,192},{256... | collective-permute-start | bytes 786440 | tf_op jit(solution)/shard_map/ppermute | solution.py:85
  25.1 14.6 %copy-start.23 = (bf16[6,64,256]{2,1,0:T(8,128)(2,1)}, bf16[6,64,256]{2,1,0:T(8,128)(2,1)S(1)}, u32[]{:S(2)}) copy-start(bf16[6,64,256]{2,1,0:T(8,128)(2,1)S(1)} %get-tuple-element.90) | copy-start | bytes 589828
  25.3 10.3 %collective-permute-start.2 = (f32[2,2,64,256]{3,2,1,0:T(8,128)S(1)}, f32[2,2,64,256]{3,2,1,0:T(8,128)S(1)}, u32[]{:S(2)}, u32[]{:S(2)}) collective-permute-start(f32[2,2,64,256]{3,2,1,0:T(8,128)S(1)} %pad_maximum_fusion.8), channel_id=1, source_target_pairs={{0,32},{32,64},{64,96},{96,128},{128,160},{160,192},{192,224},{224... | collective-permute-start | bytes 786440 | tf_op jit(solution)/shard_map/ppermute | solution.py:86
  32.2 6.0 %collective-permute-start.3 = (f32[2,2,64,256]{3,2,1,0:T(8,128)S(1)}, f32[2,2,64,256]{3,2,1,0:T(8,128)S(1)}, u32[]{:S(2)}, u32[]{:S(2)}) collective-permute-start(f32[2,2,64,256]{3,2,1,0:T(8,128)S(1)} %pad_maximum_fusion.7), channel_id=1, source_target_pairs={{32,0},{64,32},{96,64},{128,96},{160,128},{192,160},{224,192},{256... | collective-permute-start | bytes 786440 | tf_op jit(solution)/shard_map/ppermute | solution.py:85
  42.2 36.1 %copy-start.2 = (f32[6,64,256]{2,1,0:T(8,128)S(1)}, f32[6,64,256]{2,1,0:T(8,128)}, u32[]{:S(2)}) copy-start(f32[6,64,256]{2,1,0:T(8,128)} %copy-done.1) | copy-start | bytes 1179652
  42.2 36.1 %copy-start.4 = (f32[6,64,256]{2,1,0:T(8,128)S(1)}, f32[6,64,256]{2,1,0:T(8,128)}, u32[]{:S(2)}) copy-start(f32[6,64,256]{2,1,0:T(8,128)} %copy-done.3) | copy-start | bytes 1179652
  42.2 36.1 %copy-start.20 = (f32[2,2,64,256]{3,2,1,0:T(8,128)S(1)}, f32[2,2,64,256]{3,2,1,0:T(8,128)}, u32[]{:S(2)}) copy-start(f32[2,2,64,256]{3,2,1,0:T(8,128)} %copy-done.19) | copy-start | bytes 786436
  42.3 8.9 %collective-permute-start.4 = (f32[24,128]{1,0:T(8,128)S(1)}, f32[24,128]{1,0:T(8,128)S(1)}, u32[]{:S(2)}, u32[]{:S(2)}) collective-permute-start(f32[24,128]{1,0:T(8,128)S(1)} %reshape.202), channel_id=1, source_target_pairs={{0,32},{1,33},{2,34},{3,35},{4,36},{5,37},{6,38},{7,39},{8,40},{9,... | collective-permute-start | bytes 36872 | tf_op jit(solution)/shard_map/ppermute | solution.py:57
  51.2 5.6 %collective-permute-start.5 = (f32[24,128]{1,0:T(8,128)S(1)}, f32[24,128]{1,0:T(8,128)S(1)}, u32[]{:S(2)}, u32[]{:S(2)}) collective-permute-start(f32[24,128]{1,0:T(8,128)S(1)} %add.154), channel_id=1, source_target_pairs={{0,16},{1,17},{2,18},{3,19},{4,20},{5,21},{6,22},{7,23},{8,24},{9,... | collective-permute-start | bytes 36872 | tf_op jit(solution)/shard_map/ppermute | solution.py:57
  56.8 7.2 %collective-permute-start.6 = (f32[24,128]{1,0:T(8,128)S(1)}, f32[24,128]{1,0:T(8,128)S(1)}, u32[]{:S(2)}, u32[]{:S(2)}) collective-permute-start(f32[24,128]{1,0:T(8,128)S(1)} %add.155), channel_id=1, source_target_pairs={{0,80},{1,81},{2,82},{3,83},{4,84},{5,85},{6,86},{7,87},{8,88},{9,... | collective-permute-start | bytes 36872 | tf_op jit(solution)/shard_map/ppermute | solution.py:57
  63.9 5.6 %collective-permute-start.7 = (f32[24,128]{1,0:T(8,128)S(1)}, f32[24,128]{1,0:T(8,128)S(1)}, u32[]{:S(2)}, u32[]{:S(2)}) collective-permute-start(f32[24,128]{1,0:T(8,128)S(1)} %add.156), channel_id=1, source_target_pairs={{0,128},{1,129},{2,130},{3,131},{4,132},{5,133},{6,134},{7,135},{8... | collective-permute-start | bytes 36872 | tf_op jit(solution)/shard_map/ppermute | solution.py:57
  69.5 14.4 %copy-start.18 = (f32[2,2,64,256]{3,2,1,0:T(8,128)S(1)}, f32[2,2,64,256]{3,2,1,0:T(8,128)}, u32[]{:S(2)}) copy-start(f32[2,2,64,256]{3,2,1,0:T(8,128)} %copy-done.17) | copy-start | bytes 786436
  69.5 6.9 %collective-permute-start.8 = (f32[24,128]{1,0:T(8,128)S(1)}, f32[24,128]{1,0:T(8,128)S(1)}, u32[]{:S(2)}, u32[]{:S(2)}) collective-permute-start(f32[24,128]{1,0:T(8,128)S(1)} %add.157), channel_id=1, source_target_pairs={{0,384},{1,385},{2,386},{3,387},{4,388},{5,389},{6,390},{7,391},{8... | collective-permute-start | bytes 36872 | tf_op jit(solution)/shard_map/ppermute | solution.py:57
  74.6 19.4 %copy-start.11 = (bf16[1,6,2,32,256]{4,3,0,2,1:T(8,128)(2,1)S(1)}, bf16[1,6,2,32,256]{4,3,0,2,1:T(8,128)(2,1)}, u32[]{:S(2)}) copy-start(bf16[1,6,2,32,256]{4,3,0,2,1:T(8,128)(2,1)} %copy-done.10) | copy-start | bytes 589828
  74.6 19.4 %copy-start.12 = (f32[1,6,2,32,256]{4,3,0,2,1:T(8,128)S(1)}, f32[1,6,2,32,256]{4,3,0,2,1:T(8,128)}, u32[]{:S(2)}) copy-start(f32[1,6,2,32,256]{4,3,0,2,1:T(8,128)} %get-tuple-element.73) | copy-start | bytes 1179652
  74.6 32.1 %copy-start.16 = (bf16[64,6,256]{2,0,1:T(8,128)(2,1)S(1)}, bf16[64,6,256]{2,0,1:T(8,128)(2,1)}, u32[]{:S(2)}) copy-start(bf16[64,6,256]{2,0,1:T(8,128)(2,1)} %get-tuple-element.60) | copy-start | bytes 589828
  74.6 32.1 %copy-start.21 = (bf16[3,32,32]{2,1,0:T(8,128)(2,1)S(1)}, bf16[3,32,32]{2,1,0:T(8,128)(2,1)}, u32[]{:S(2)}) copy-start(bf16[3,32,32]{2,1,0:T(8,128)(2,1)} %param.17) | copy-start | bytes 18436
  74.6 32.1 %copy-start.24 = (bf16[6,64,256]{2,1,0:T(8,128)(2,1)S(1)}, bf16[6,64,256]{2,1,0:T(8,128)(2,1)}, u32[]{:S(2)}) copy-start(bf16[6,64,256]{2,1,0:T(8,128)(2,1)} %copy-done.23) | copy-start | bytes 589828
  74.6 32.1 %copy-start.26 = (bf16[6,64,256]{2,1,0:T(8,128)(2,1)S(1)}, bf16[6,64,256]{2,1,0:T(8,128)(2,1)}, u32[]{:S(2)}) copy-start(bf16[6,64,256]{2,1,0:T(8,128)(2,1)} %copy-done.25) | copy-start | bytes 589828
  76.4 5.6 %collective-permute-start.9 = (f32[24,128]{1,0:T(8,128)S(1)}, f32[24,128]{1,0:T(8,128)S(1)}, u32[]{:S(2)}, u32[]{:S(2)}) collective-permute-start(f32[24,128]{1,0:T(8,128)S(1)} %add.158), channel_id=1, source_target_pairs={{0,1},{1,0},{2,3},{3,2},{4,5},{5,4},{6,7},{7,6},{8,9},{9,8},{10,11... | collective-permute-start | bytes 36872 | tf_op jit(solution)/shard_map/ppermute | solution.py:57
  82.0 6.5 %collective-permute-start.10 = (f32[24,128]{1,0:T(8,128)S(1)}, f32[24,128]{1,0:T(8,128)S(1)}, u32[]{:S(2)}, u32[]{:S(2)}) collective-permute-start(f32[24,128]{1,0:T(8,128)S(1)} %add.159), channel_id=1, source_target_pairs={{0,2},{1,3},{2,0},{3,1},{4,6},{5,7},{6,4},{7,5},{8,10},{9,11},{10,... | collective-permute-start | bytes 36872 | tf_op jit(solution)/shard_map/ppermute | solution.py:57
  88.5 9.6 %collective-permute-start.11 = (f32[24,128]{1,0:T(8,128)S(1)}, f32[24,128]{1,0:T(8,128)S(1)}, u32[]{:S(2)}, u32[]{:S(2)}) collective-permute-start(f32[24,128]{1,0:T(8,128)S(1)} %add.160), channel_id=1, source_target_pairs={{0,4},{1,5},{2,6},{3,7},{4,0},{5,1},{6,2},{7,3},{8,12},{9,13},{10,... | collective-permute-start | bytes 36872 | tf_op jit(solution)/shard_map/ppermute | solution.py:57
  98.1 11.0 %collective-permute-start.12 = (f32[24,128]{1,0:T(8,128)S(1)}, f32[24,128]{1,0:T(8,128)S(1)}, u32[]{:S(2)}, u32[]{:S(2)}) collective-permute-start(f32[24,128]{1,0:T(8,128)S(1)} %add.161), channel_id=1, source_target_pairs={{0,12},{1,13},{2,14},{3,15},{4,8},{5,9},{6,10},{7,11},{8,4},{9,5},... | collective-permute-start | bytes 36872 | tf_op jit(solution)/shard_map/ppermute | solution.py:57
  (16 other events, 39.3 us)

commit v7 on v4

--- a/solution.py
+++ b/solution.py
@@ -81,6 +81,7 @@
     to_left = [((i + 1) % patch_count, i) for i in range(patch_count)]
 
     def exchange(edge_left, edge_right):
+        edge_left, edge_right = lax.optimization_barrier((edge_left, edge_right))
         from_right = lax.ppermute(edge_left, "patch", to_left)
         from_left = lax.ppermute(edge_right, "patch", to_right)
         return from_left, from_right
@@ -117,10 +118,39 @@
     grads = grads.reshape(3, nb, row_count, block_size)
     grad_two = grads[2].astype(jnp.bfloat16)
 
+    by_block = cotangent.reshape(map_count, chan_count, nb, block_size)
+    map_blocks = maps.reshape(row_count, nb, block_size)
+
+    def edge_out(lo, slot):
+        cot_edge = by_block[:, :, lo : lo + 2].transpose(2, 0, 1, 3)
+        g_edge = jnp.einsum(
+            "co,rmoq->rmcq", filters[2], cot_edge, preferred_element_type=jnp.float32
+        ).astype(jnp.bfloat16).reshape(2, row_count, block_size)
+        return jnp.einsum(
+            "rni,riq->rnq", g_edge, tiles[lo : lo + 2, slot], preferred_element_type=jnp.float32
+        )
+
+    cl = edge_out(0, 1)
+    cr = edge_out(nb - 2, 2)
+    zero = jnp.zeros_like(cl[0])
+    out_left = jnp.stack(
+        [
+            jnp.where(back_one[0], zero, cl[0]),
+            jnp.where(back_one[0], cl[0], zero) + jnp.where(back_one[1], zero, cl[1]),
+        ]
+    )
+    out_right = jnp.stack(
+        [
+            jnp.where(next_one[nb - 2], zero, cr[0]) + jnp.where(next_one[nb - 1], cr[1], zero),
+            jnp.where(next_one[nb - 1], zero, cr[1]),
+        ]
+    )
+    halo_left = map_blocks[:, 0:2].transpose(1, 0, 2).astype(jnp.float32)
+    halo_right = map_blocks[:, nb - 2 : nb].transpose(1, 0, 2).astype(jnp.float32)
+    send_left = jnp.stack([halo_left, out_left])
+    send_right = jnp.stack([halo_right, out_right])
     win1 = adjoint_window(grad_two)
     x0f = x_zero.astype(jnp.float32)
-    send_left = jnp.stack([x0f[0:2], win1[0:2]])
-    send_right = jnp.stack([x0f[nb - 2 : nb], win1[nb + 2 : nb + 4]])
     got_left, got_right = exchange(send_left, send_right)
     ext0 = jnp.concatenate([got_left[0], x0f, got_right[0]], axis=0)
     x_one = forward_local(ext0).astype(jnp.bfloat16)

time: 118 us -> 116 us (0.983)
  waiting for transfers between devices: 48.5 us -> 34.9 us
  other arithmetic: 3.92 us -> 8.13 us
  matrix products: 4.34 us -> 7.98 us
  starting transfers between devices: 50.8 us -> 54.4 us
    ppermute x2, waiting for transfers between devices: 13.7 us -> 1.22 us  [exchange(): from_left = lax.ppermute(edge_right, 'patch', to_right)]
    ppermute x2, waiting for transfers between devices: 7.63 us -> 3.26 us  [exchange(): from_right = lax.ppermute(edge_left, 'patch', to_left)]
    ppermute x2, starting transfers between devices: 3.84 us -> 7.97 us  [exchange(): from_right = lax.ppermute(edge_left, 'patch', to_left)]
    dot_general x0 -> x4, matrix products: none -> 3.64 us  [the longest x2 1.95 us: edge_out(): jnp.einsum('rni,riq->rnq', g_edge, tiles[lo:lo + 2, slot], preferred_elem...]
    ppermute x9, starting transfers between devices: 40.7 us -> 37.3 us  [butterfly_sum(): x = x + lax.ppermute(x, axes, pairs)]
    ppermute x9, waiting for transfers between devices: 27.1 us -> 30.4 us  [butterfly_sum(): x = x + lax.ppermute(x, axes, pairs)]
    ppermute x2, starting transfers between devices: 6.24 us -> 9.13 us  [exchange(): from_left = lax.ppermute(edge_right, 'patch', to_right)]
    unnamed x18 -> x8, local copies, waits for them, and re-layouts: 2.75 us -> 0.02 us
  transfers between devices with their start and end apart: 13 -> 13, of which waited for: 12 -> 12; matrix products, arithmetic and copies ran while one was open for 2% -> 5% of each run, Pallas kernels for 0% -> 0%
where the time goes in v7:
time: 116 us; the launch traced here: 114 us
  starting transfers between devices  54.4 us (47%)
  waiting for transfers between devices  34.9 us (30%)
  other arithmetic  8.13 us (7%)
  matrix products  7.98 us (7%)
  local copies, waits for them, and re-layouts  7.74 us (7%)
    ppermute x9, starting transfers between devices, butterfly_sum(): x = x + lax.ppermute(x, axes, pairs)  37.3 us
    ppermute x9, waiting for transfers between devices, butterfly_sum(): x = x + lax.ppermute(x, axes, pairs)  30.4 us
    ppermute x2, starting transfers between devices, exchange(): from_left = lax.ppermute(edge_right, 'patch', to_right)  9.13 us
    ppermute x2, starting transfers between devices, exchange(): from_right = lax.ppermute(edge_left, 'patch', to_left)  7.97 us
    ppermute x2, waiting for transfers between devices, exchange(): from_right = lax.ppermute(edge_left, 'patch', to_left)  3.26 us
  transfers between devices with their start and end apart: 13, of which 12 were waited for; matrix products, arithmetic and copies ran while one was open for 5% of the time, Pallas kernels for 0%

profile of v7, /device:TPU:24, one launch (start us, length us, event | category | flops | bytes accessed | tf_op | source)
XLA Modules:
  0.0 114.3 jit_solution(17663649208957715672)
XLA Ops:
  0.7 1.3 %reshape.208 = bf16[64,6,256]{2,1,0:T(8,128)(2,1)S(1)} reshape(bf16[2,32,1536]{2,1,0:T(8,128)(2,1)} %param.13) | data formatting | bytes 393216 | tf_op jit(solution)/shard_map/reshape | solution.py:90
  7.7 1.3 %slice_select_fusion.3 = (f32[1,64,256]{2,1,0:T(8,128)S(1)}, f32[1,64,256]{2,1,0:T(8,128)S(1)}) fusion(f32[2,64,256]{2,1,0:T(8,128)S(1)} %fusion.40, pred[]{:T(512)} %bitcast.7, pred[]{:T(512)} %bitcast.15), kind=kLoop, calls=%fused_computation.119 | loop fusion | flops 65536 | bytes 262146 | tf_op jit(solution)/shard_map/jit(_where)/select_n | solution.py:138
  9.0 2.2 %fusion.55 = (f32[1,64,256]{2,1,0:T(8,128)S(1)}, f32[1,64,256]{2,1,0:T(8,128)S(1)}) fusion(f32[2,64,256]{2,1,0:T(8,128)} %fusion.39, pred[]{:T(512)} %bitcast.27, pred[]{:T(512)} %bitcast.20), kind=kLoop, calls=%fused_computation.113 | loop fusion | flops 65536 | bytes 262146 | tf_op jit(solution)/shard_map/add | solution.py:144
  12.0 1.9 %collective-permute-start = (f32[2,2,64,256]{3,2,1,0:T(8,128)}, f32[2,2,64,256]{3,2,1,0:T(8,128)}, u32[]{:S(2)}, u32[]{:S(2)}) collective-permute-start(f32[2,2,64,256]{3,2,1,0:T(8,128)} %pad_maximum_fusion.6), channel_id=1, source_target_pairs={{0,32},{32,64},{64,96},{96,128},{128,160},{160,192},{192,224},{224... | collective-permute-start | bytes 786440 | tf_op jit(solution)/shard_map/ppermute | solution.py:86
  13.9 6.0 %collective-permute-start.1 = (f32[2,2,64,256]{3,2,1,0:T(8,128)S(1)}, f32[2,2,64,256]{3,2,1,0:T(8,128)}, u32[]{:S(2)}, u32[]{:S(2)}) collective-permute-start(f32[2,2,64,256]{3,2,1,0:T(8,128)S(1)} %pad_maximum_fusion.5), channel_id=1, source_target_pairs={{32,0},{64,32},{96,64},{128,96},{160,128},{192,160},{224,192},{256... | collective-permute-start | bytes 786440 | tf_op jit(solution)/shard_map/ppermute | solution.py:85
  28.5 7.2 %collective-permute-start.2 = (f32[2,2,64,256]{3,2,1,0:T(8,128)S(1)}, f32[2,2,64,256]{3,2,1,0:T(8,128)S(1)}, u32[]{:S(2)}, u32[]{:S(2)}) collective-permute-start(f32[2,2,64,256]{3,2,1,0:T(8,128)S(1)} %pad_maximum_fusion.8), channel_id=1, source_target_pairs={{0,32},{32,64},{64,96},{96,128},{128,160},{160,192},{192,224},{224... | collective-permute-start | bytes 786440 | tf_op jit(solution)/shard_map/ppermute | solution.py:86
  35.7 1.9 %collective-permute-start.3 = (f32[2,2,64,256]{3,2,1,0:T(8,128)S(1)}, f32[2,2,64,256]{3,2,1,0:T(8,128)S(1)}, u32[]{:S(2)}, u32[]{:S(2)}) collective-permute-start(f32[2,2,64,256]{3,2,1,0:T(8,128)S(1)} %pad_maximum_fusion.7), channel_id=1, source_target_pairs={{32,0},{64,32},{96,64},{128,96},{160,128},{192,160},{224,192},{256... | collective-permute-start | bytes 786440 | tf_op jit(solution)/shard_map/ppermute | solution.py:85
  38.9 2.8 %collective-permute-done.3 = f32[2,2,64,256]{3,2,1,0:T(8,128)S(1)} collective-permute-done((f32[2,2,64,256]{3,2,1,0:T(8,128)S(1)}, f32[2,2,64,256]{3,2,1,0:T(8,128)S(1)}, u32[]{:S(2)}, u32[]{:S(2)}) %collective-permute-start.3) | collective-permute-done | bytes 262176 | tf_op jit(solution)/shard_map/ppermute | solution.py:85
  43.0 9.1 %collective-permute-start.4 = (f32[3,32,32]{2,1,0:T(8,128)S(1)}, f32[3,32,32]{2,1,0:T(8,128)S(1)}, u32[]{:S(2)}, u32[]{:S(2)}) collective-permute-start(f32[3,32,32]{2,1,0:T(8,128)S(1)} %convolution_bitcast_fusion.6), channel_id=1, source_target_pairs={{0,32},{1,33},{2,34},{3,35},{4,36},{5,37},{6,38},{7,39},{8,40},{9,... | collective-permute-start | bytes 36872 | tf_op jit(solution)/shard_map/ppermute | solution.py:57
  53.0 1.9 %collective-permute-start.5 = (f32[3,32,32]{2,1,0:T(8,128)S(1)}, f32[3,32,32]{2,1,0:T(8,128)S(1)}, u32[]{:S(2)}, u32[]{:S(2)}) collective-permute-start(f32[3,32,32]{2,1,0:T(8,128)S(1)} %add.164), channel_id=1, source_target_pairs={{0,16},{1,17},{2,18},{3,19},{4,20},{5,21},{6,22},{7,23},{8,24},{9,... | collective-permute-start | bytes 36872 | tf_op jit(solution)/shard_map/ppermute | solution.py:57
  54.9 4.1 %collective-permute-done.5 = f32[3,32,32]{2,1,0:T(8,128)S(1)} collective-permute-done((f32[3,32,32]{2,1,0:T(8,128)S(1)}, f32[3,32,32]{2,1,0:T(8,128)S(1)}, u32[]{:S(2)}, u32[]{:S(2)}) %collective-permute-start.5) | collective-permute-done | bytes 12320 | tf_op jit(solution)/shard_map/ppermute | solution.py:57
  59.0 5.7 %collective-permute-start.6 = (f32[3,32,32]{2,1,0:T(8,128)S(1)}, f32[3,32,32]{2,1,0:T(8,128)S(1)}, u32[]{:S(2)}, u32[]{:S(2)}) collective-permute-start(f32[3,32,32]{2,1,0:T(8,128)S(1)} %add.165), channel_id=1, source_target_pairs={{0,80},{1,81},{2,82},{3,83},{4,84},{5,85},{6,86},{7,87},{8,88},{9,... | collective-permute-start | bytes 36872 | tf_op jit(solution)/shard_map/ppermute | solution.py:57
  64.7 2.1 %collective-permute-done.6 = f32[3,32,32]{2,1,0:T(8,128)S(1)} collective-permute-done((f32[3,32,32]{2,1,0:T(8,128)S(1)}, f32[3,32,32]{2,1,0:T(8,128)S(1)}, u32[]{:S(2)}, u32[]{:S(2)}) %collective-permute-start.6) | collective-permute-done | bytes 12320 | tf_op jit(solution)/shard_map/ppermute | solution.py:57
  66.7 1.9 %collective-permute-start.7 = (f32[3,32,32]{2,1,0:T(8,128)S(1)}, f32[3,32,32]{2,1,0:T(8,128)S(1)}, u32[]{:S(2)}, u32[]{:S(2)}) collective-permute-start(f32[3,32,32]{2,1,0:T(8,128)S(1)} %add.166), channel_id=1, source_target_pairs={{0,128},{1,129},{2,130},{3,131},{4,132},{5,133},{6,134},{7,135},{8... | collective-permute-start | bytes 36872 | tf_op jit(solution)/shard_map/ppermute | solution.py:57
  68.6 4.1 %collective-permute-done.7 = f32[3,32,32]{2,1,0:T(8,128)S(1)} collective-permute-done((f32[3,32,32]{2,1,0:T(8,128)S(1)}, f32[3,32,32]{2,1,0:T(8,128)S(1)}, u32[]{:S(2)}, u32[]{:S(2)}) %collective-permute-start.7) | collective-permute-done | bytes 12320 | tf_op jit(solution)/shard_map/ppermute | solution.py:57
  72.7 4.1 %collective-permute-start.8 = (f32[3,32,32]{2,1,0:T(8,128)S(1)}, f32[3,32,32]{2,1,0:T(8,128)S(1)}, u32[]{:S(2)}, u32[]{:S(2)}) collective-permute-start(f32[3,32,32]{2,1,0:T(8,128)S(1)} %add.167), channel_id=1, source_target_pairs={{0,384},{1,385},{2,386},{3,387},{4,388},{5,389},{6,390},{7,391},{8... | collective-permute-start | bytes 36872 | tf_op jit(solution)/shard_map/ppermute | solution.py:57
  77.0 2.9 %collective-permute-done.8 = f32[3,32,32]{2,1,0:T(8,128)S(1)} collective-permute-done((f32[3,32,32]{2,1,0:T(8,128)S(1)}, f32[3,32,32]{2,1,0:T(8,128)S(1)}, u32[]{:S(2)}, u32[]{:S(2)}) %collective-permute-start.8) | collective-permute-done | bytes 12320 | tf_op jit(solution)/shard_map/ppermute | solution.py:57
  79.9 1.9 %collective-permute-start.9 = (f32[3,32,32]{2,1,0:T(8,128)S(1)}, f32[3,32,32]{2,1,0:T(8,128)S(1)}, u32[]{:S(2)}, u32[]{:S(2)}) collective-permute-start(f32[3,32,32]{2,1,0:T(8,128)S(1)} %add.168), channel_id=1, source_target_pairs={{0,1},{1,0},{2,3},{3,2},{4,5},{5,4},{6,7},{7,6},{8,9},{9,8},{10,11... | collective-permute-start | bytes 36872 | tf_op jit(solution)/shard_map/ppermute | solution.py:57
  81.9 4.0 %collective-permute-done.9 = f32[3,32,32]{2,1,0:T(8,128)S(1)} collective-permute-done((f32[3,32,32]{2,1,0:T(8,128)S(1)}, f32[3,32,32]{2,1,0:T(8,128)S(1)}, u32[]{:S(2)}, u32[]{:S(2)}) %collective-permute-start.9) | collective-permute-done | bytes 12320 | tf_op jit(solution)/shard_map/ppermute | solution.py:57
  85.9 1.9 %collective-permute-start.10 = (f32[3,32,32]{2,1,0:T(8,128)S(1)}, f32[3,32,32]{2,1,0:T(8,128)S(1)}, u32[]{:S(2)}, u32[]{:S(2)}) collective-permute-start(f32[3,32,32]{2,1,0:T(8,128)S(1)} %add.169), channel_id=1, source_target_pairs={{0,2},{1,3},{2,0},{3,1},{4,6},{5,7},{6,4},{7,5},{8,10},{9,11},{10,... | collective-permute-start | bytes 36872 | tf_op jit(solution)/shard_map/ppermute | solution.py:57
  87.9 4.9 %collective-permute-done.10 = f32[3,32,32]{2,1,0:T(8,128)S(1)} collective-permute-done((f32[3,32,32]{2,1,0:T(8,128)S(1)}, f32[3,32,32]{2,1,0:T(8,128)S(1)}, u32[]{:S(2)}, u32[]{:S(2)}) %collective-permute-start.10) | collective-permute-done | bytes 12320 | tf_op jit(solution)/shard_map/ppermute | solution.py:57
  92.8 4.4 %collective-permute-start.11 = (f32[3,32,32]{2,1,0:T(8,128)S(1)}, f32[3,32,32]{2,1,0:T(8,128)S(1)}, u32[]{:S(2)}, u32[]{:S(2)}) collective-permute-start(f32[3,32,32]{2,1,0:T(8,128)S(1)} %add.170), channel_id=1, source_target_pairs={{0,4},{1,5},{2,6},{3,7},{4,0},{5,1},{6,2},{7,3},{8,12},{9,13},{10,... | collective-permute-start | bytes 36872 | tf_op jit(solution)/shard_map/ppermute | solution.py:57
  97.3 6.4 %collective-permute-done.11 = f32[3,32,32]{2,1,0:T(8,128)S(1)} collective-permute-done((f32[3,32,32]{2,1,0:T(8,128)S(1)}, f32[3,32,32]{2,1,0:T(8,128)S(1)}, u32[]{:S(2)}, u32[]{:S(2)}) %collective-permute-start.11) | collective-permute-done | bytes 12320 | tf_op jit(solution)/shard_map/ppermute | solution.py:57
  103.7 6.4 %collective-permute-start.12 = (f32[3,32,32]{2,1,0:T(8,128)S(1)}, f32[3,32,32]{2,1,0:T(8,128)S(1)}, u32[]{:S(2)}, u32[]{:S(2)}) collective-permute-start(f32[3,32,32]{2,1,0:T(8,128)S(1)} %add.171), channel_id=1, source_target_pairs={{0,12},{1,13},{2,14},{3,15},{4,8},{5,9},{6,10},{7,11},{8,4},{9,5},... | collective-permute-start | bytes 36872 | tf_op jit(solution)/shard_map/ppermute | solution.py:57
  (77 shorter events, 22.7 us)
Async XLA Ops:
  0.6 5.6 %copy-start = (bf16[6,3,256,256]{3,2,1,0:T(8,128)(2,1)S(1)}, bf16[6,3,256,256]{3,2,1,0:T(8,128)(2,1)}, u32[]{:S(2)}) copy-start(bf16[6,3,256,256]{3,2,1,0:T(8,128)(2,1)} %param.15) | copy-start | bytes 7077892
  0.6 6.4 %copy-start.3 = (s32[6,3]{0,1:T(4,128)S(1)}, s32[6,3]{0,1:T(4,128)}, u32[]{:S(2)}) copy-start(s32[6,3]{0,1:T(4,128)} %param.16) | copy-start | bytes 220
  2.0 18.0 %copy-start.1 = (bf16[2,32,1536]{2,1,0:T(8,128)(2,1)S(1)}, bf16[2,32,1536]{2,1,0:T(8,128)(2,1)}, u32[]{:S(2)}) copy-start(bf16[2,32,1536]{2,1,0:T(8,128)(2,1)} %param.14) | copy-start | bytes 589828
  12.0 10.5 %collective-permute-start = (f32[2,2,64,256]{3,2,1,0:T(8,128)}, f32[2,2,64,256]{3,2,1,0:T(8,128)}, u32[]{:S(2)}, u32[]{:S(2)}) collective-permute-start(f32[2,2,64,256]{3,2,1,0:T(8,128)} %pad_maximum_fusion.6), channel_id=1, source_target_pairs={{0,32},{32,64},{64,96},{96,128},{128,160},{160,192},{192,224},{224... | collective-permute-start | bytes 786440 | tf_op jit(solution)/shard_map/ppermute | solution.py:86
  13.9 9.9 %collective-permute-start.1 = (f32[2,2,64,256]{3,2,1,0:T(8,128)S(1)}, f32[2,2,64,256]{3,2,1,0:T(8,128)}, u32[]{:S(2)}, u32[]{:S(2)}) collective-permute-start(f32[2,2,64,256]{3,2,1,0:T(8,128)S(1)} %pad_maximum_fusion.5), channel_id=1, source_target_pairs={{32,0},{64,32},{96,64},{128,96},{160,128},{192,160},{224,192},{256... | collective-permute-start | bytes 786440 | tf_op jit(solution)/shard_map/ppermute | solution.py:85
  28.5 10.4 %collective-permute-start.2 = (f32[2,2,64,256]{3,2,1,0:T(8,128)S(1)}, f32[2,2,64,256]{3,2,1,0:T(8,128)S(1)}, u32[]{:S(2)}, u32[]{:S(2)}) collective-permute-start(f32[2,2,64,256]{3,2,1,0:T(8,128)S(1)} %pad_maximum_fusion.8), channel_id=1, source_target_pairs={{0,32},{32,64},{64,96},{96,128},{128,160},{160,192},{192,224},{224... | collective-permute-start | bytes 786440 | tf_op jit(solution)/shard_map/ppermute | solution.py:86
  35.7 6.0 %collective-permute-start.3 = (f32[2,2,64,256]{3,2,1,0:T(8,128)S(1)}, f32[2,2,64,256]{3,2,1,0:T(8,128)S(1)}, u32[]{:S(2)}, u32[]{:S(2)}) collective-permute-start(f32[2,2,64,256]{3,2,1,0:T(8,128)S(1)} %pad_maximum_fusion.7), channel_id=1, source_target_pairs={{32,0},{64,32},{96,64},{128,96},{160,128},{192,160},{224,192},{256... | collective-permute-start | bytes 786440 | tf_op jit(solution)/shard_map/ppermute | solution.py:85
  43.0 9.9 %collective-permute-start.4 = (f32[3,32,32]{2,1,0:T(8,128)S(1)}, f32[3,32,32]{2,1,0:T(8,128)S(1)}, u32[]{:S(2)}, u32[]{:S(2)}) collective-permute-start(f32[3,32,32]{2,1,0:T(8,128)S(1)} %convolution_bitcast_fusion.6), channel_id=1, source_target_pairs={{0,32},{1,33},{2,34},{3,35},{4,36},{5,37},{6,38},{7,39},{8,40},{9,... | collective-permute-start | bytes 36872 | tf_op jit(solution)/shard_map/ppermute | solution.py:57
  53.0 6.0 %collective-permute-start.5 = (f32[3,32,32]{2,1,0:T(8,128)S(1)}, f32[3,32,32]{2,1,0:T(8,128)S(1)}, u32[]{:S(2)}, u32[]{:S(2)}) collective-permute-start(f32[3,32,32]{2,1,0:T(8,128)S(1)} %add.164), channel_id=1, source_target_pairs={{0,16},{1,17},{2,18},{3,19},{4,20},{5,21},{6,22},{7,23},{8,24},{9,... | collective-permute-start | bytes 36872 | tf_op jit(solution)/shard_map/ppermute | solution.py:57
  59.0 7.7 %collective-permute-start.6 = (f32[3,32,32]{2,1,0:T(8,128)S(1)}, f32[3,32,32]{2,1,0:T(8,128)S(1)}, u32[]{:S(2)}, u32[]{:S(2)}) collective-permute-start(f32[3,32,32]{2,1,0:T(8,128)S(1)} %add.165), channel_id=1, source_target_pairs={{0,80},{1,81},{2,82},{3,83},{4,84},{5,85},{6,86},{7,87},{8,88},{9,... | collective-permute-start | bytes 36872 | tf_op jit(solution)/shard_map/ppermute | solution.py:57
  66.7 6.0 %collective-permute-start.7 = (f32[3,32,32]{2,1,0:T(8,128)S(1)}, f32[3,32,32]{2,1,0:T(8,128)S(1)}, u32[]{:S(2)}, u32[]{:S(2)}) collective-permute-start(f32[3,32,32]{2,1,0:T(8,128)S(1)} %add.166), channel_id=1, source_target_pairs={{0,128},{1,129},{2,130},{3,131},{4,132},{5,133},{6,134},{7,135},{8... | collective-permute-start | bytes 36872 | tf_op jit(solution)/shard_map/ppermute | solution.py:57
  72.7 7.2 %collective-permute-start.8 = (f32[3,32,32]{2,1,0:T(8,128)S(1)}, f32[3,32,32]{2,1,0:T(8,128)S(1)}, u32[]{:S(2)}, u32[]{:S(2)}) collective-permute-start(f32[3,32,32]{2,1,0:T(8,128)S(1)} %add.167), channel_id=1, source_target_pairs={{0,384},{1,385},{2,386},{3,387},{4,388},{5,389},{6,390},{7,391},{8... | collective-permute-start | bytes 36872 | tf_op jit(solution)/shard_map/ppermute | solution.py:57
  77.0 33.1 %copy-start.2 = (bf16[3,32,32]{2,1,0:T(8,128)(2,1)S(1)}, bf16[3,32,32]{2,1,0:T(8,128)(2,1)}, u32[]{:S(2)}) copy-start(bf16[3,32,32]{2,1,0:T(8,128)(2,1)} %param.17) | copy-start | bytes 18436
  79.9 6.0 %collective-permute-start.9 = (f32[3,32,32]{2,1,0:T(8,128)S(1)}, f32[3,32,32]{2,1,0:T(8,128)S(1)}, u32[]{:S(2)}, u32[]{:S(2)}) collective-permute-start(f32[3,32,32]{2,1,0:T(8,128)S(1)} %add.168), channel_id=1, source_target_pairs={{0,1},{1,0},{2,3},{3,2},{4,5},{5,4},{6,7},{7,6},{8,9},{9,8},{10,11... | collective-permute-start | bytes 36872 | tf_op jit(solution)/shard_map/ppermute | solution.py:57
  85.9 6.9 %collective-permute-start.10 = (f32[3,32,32]{2,1,0:T(8,128)S(1)}, f32[3,32,32]{2,1,0:T(8,128)S(1)}, u32[]{:S(2)}, u32[]{:S(2)}) collective-permute-start(f32[3,32,32]{2,1,0:T(8,128)S(1)} %add.169), channel_id=1, source_target_pairs={{0,2},{1,3},{2,0},{3,1},{4,6},{5,7},{6,4},{7,5},{8,10},{9,11},{10,... | collective-permute-start | bytes 36872 | tf_op jit(solution)/shard_map/ppermute | solution.py:57
  92.8 10.9 %collective-permute-start.11 = (f32[3,32,32]{2,1,0:T(8,128)S(1)}, f32[3,32,32]{2,1,0:T(8,128)S(1)}, u32[]{:S(2)}, u32[]{:S(2)}) collective-permute-start(f32[3,32,32]{2,1,0:T(8,128)S(1)} %add.170), channel_id=1, source_target_pairs={{0,4},{1,5},{2,6},{3,7},{4,0},{5,1},{6,2},{7,3},{8,12},{9,13},{10,... | collective-permute-start | bytes 36872 | tf_op jit(solution)/shard_map/ppermute | solution.py:57
  103.7 9.9 %collective-permute-start.12 = (f32[3,32,32]{2,1,0:T(8,128)S(1)}, f32[3,32,32]{2,1,0:T(8,128)S(1)}, u32[]{:S(2)}, u32[]{:S(2)}) collective-permute-start(f32[3,32,32]{2,1,0:T(8,128)S(1)} %add.171), channel_id=1, source_target_pairs={{0,12},{1,13},{2,14},{3,15},{4,8},{5,9},{6,10},{7,11},{8,4},{9,5},... | collective-permute-start | bytes 36872 | tf_op jit(solution)/shard_map/ppermute | solution.py:57

commit v8 on v4

--- a/solution.py
+++ b/solution.py
@@ -81,6 +81,7 @@
     to_left = [((i + 1) % patch_count, i) for i in range(patch_count)]
 
     def exchange(edge_left, edge_right):
+        edge_left, edge_right = lax.optimization_barrier((edge_left, edge_right))
         from_right = lax.ppermute(edge_left, "patch", to_left)
         from_left = lax.ppermute(edge_right, "patch", to_right)
         return from_left, from_right
@@ -146,7 +147,9 @@
     out_b = jnp.einsum("kco,krmcp->rmop", filters, terms, preferred_element_type=jnp.float32)
     output = from_blocks(out_b.astype(jnp.bfloat16).reshape(nb, row_count, block_size))
     scale = 1.0 / math.sqrt(map_count * lax.axis_size("map") * pix_count * patch_count)
-    local_grad = jnp.einsum("krmcp,rmop->kco", terms, cot_b, preferred_element_type=jnp.float32)
+    early = jnp.einsum("krmcp,rmop->kco", terms[:2], cot_b, preferred_element_type=jnp.float32)
+    late = jnp.einsum("rmcp,rmop->co", terms[2], cot_b, preferred_element_type=jnp.float32)
+    local_grad = jnp.concatenate([early, late[None]])
     filter_grad = butterfly_sum(local_grad, ("patch", "map")) * scale
     return (output, from_blocks(input_grad), filter_grad)
 

time: 118 us -> 111 us (0.941)
  waiting for transfers between devices: 48.5 us -> 35 us
  starting transfers between devices: 50.8 us -> 55.9 us
  matrix products: 4.34 us -> 5.54 us
    ppermute x2, waiting for transfers between devices: 13.7 us -> 3.02 us  [exchange(): from_left = lax.ppermute(edge_right, 'patch', to_right)]
    ppermute x2, starting transfers between devices: 3.84 us -> 7.97 us  [exchange(): from_right = lax.ppermute(edge_left, 'patch', to_left)]
    ppermute x2, waiting for transfers between devices: 7.63 us -> 4.34 us  [exchange(): from_right = lax.ppermute(edge_left, 'patch', to_left)]
    ppermute x2, starting transfers between devices: 6.24 us -> 8.83 us  [exchange(): from_left = lax.ppermute(edge_right, 'patch', to_right)]
    ppermute x9, starting transfers between devices: 40.7 us -> 39.1 us  [butterfly_sum(): x = x + lax.ppermute(x, axes, pairs)]
  transfers between devices with their start and end apart: 13 -> 13, of which waited for: 12 -> 12; matrix products, arithmetic and copies ran while one was open for 2% -> 3% of each run, Pallas kernels for 0% -> 0%
where the time goes in v8:
time: 111 us; the launch traced here: 110 us
  starting transfers between devices  55.9 us (50%)
  waiting for transfers between devices  35 us (32%)
  local copies, waits for them, and re-layouts  8.04 us (7%)
  matrix products  5.54 us (5%)
  other arithmetic  4.08 us (4%)
    ppermute x9, starting transfers between devices, butterfly_sum(): x = x + lax.ppermute(x, axes, pairs)  39.1 us
    ppermute x9, waiting for transfers between devices, butterfly_sum(): x = x + lax.ppermute(x, axes, pairs)  27.7 us
    ppermute x2, starting transfers between devices, exchange(): from_left = lax.ppermute(edge_right, 'patch', to_right)  8.83 us
    ppermute x2, starting transfers between devices, exchange(): from_right = lax.ppermute(edge_left, 'patch', to_left)  7.97 us
    ppermute x2, waiting for transfers between devices, exchange(): from_right = lax.ppermute(edge_left, 'patch', to_left)  4.34 us
    ppermute x2, waiting for transfers between devices, exchange(): from_left = lax.ppermute(edge_right, 'patch', to_right)  3.02 us
    reshape x2, local copies, waits for them, and re-layouts, to_blocks(): return field.reshape(row_count, nb, block_size).transpose(1, 0, 2)  2.46 us
  transfers between devices with their start and end apart: 13, of which 12 were waited for; matrix products, arithmetic and copies ran while one was open for 3% of the time, Pallas kernels for 0%

profile of v8, /device:TPU:24, one launch (start us, length us, event | category | flops | bytes accessed | tf_op | source)
XLA Modules:
  0.0 109.7 jit_solution(13514511657914042817)
XLA Ops:
  6.1 1.6 %fusion.8 = f32[6,3,64,256]{3,2,0,1:T(8,128)} fusion(bf16[6,64,256,1]{2,1,0,3:T(8,128)(2,1)S(1)} %bitcast.192, bf16[6,3,256,256]{3,2,1,0:T(8,128)(2,1)S(1)} %copy-done), kind=kOutput, calls=%fused_computation.9 | convolution fusion | flops 150994944 | bytes 3735552 | tf_op jit(solution)/shard_map/rni,rjiq->rjnq/dot_general | solution.py:103
  10.9 1.9 %collective-permute-start = (f32[2,2,64,256]{3,2,1,0:T(8,128)S(1)}, f32[2,2,64,256]{3,2,1,0:T(8,128)S(1)}, u32[]{:S(2)}, u32[]{:S(2)}) collective-permute-start(f32[2,2,64,256]{3,2,1,0:T(8,128)S(1)} %get-tuple-element.55), channel_id=1, source_target_pairs={{0,32},{32,64},{64,96},{96,128},{128,160},{160,192},{192,224},{224... | collective-permute-start | bytes 786440 | tf_op jit(solution)/shard_map/ppermute | solution.py:86
  12.8 6.0 %collective-permute-start.1 = (f32[2,2,64,256]{3,2,1,0:T(8,128)S(1)}, f32[2,2,64,256]{3,2,1,0:T(8,128)S(1)}, u32[]{:S(2)}, u32[]{:S(2)}) collective-permute-start(f32[2,2,64,256]{3,2,1,0:T(8,128)S(1)} %get-tuple-element.56), channel_id=1, source_target_pairs={{32,0},{64,32},{96,64},{128,96},{160,128},{192,160},{224,192},{256... | collective-permute-start | bytes 786440 | tf_op jit(solution)/shard_map/ppermute | solution.py:85
  19.1 1.9 %collective-permute-done = f32[2,2,64,256]{3,2,1,0:T(8,128)S(1)} collective-permute-done((f32[2,2,64,256]{3,2,1,0:T(8,128)S(1)}, f32[2,2,64,256]{3,2,1,0:T(8,128)S(1)}, u32[]{:S(2)}, u32[]{:S(2)}) %collective-permute-start) | collective-permute-done | bytes 262176 | tf_op jit(solution)/shard_map/ppermute | solution.py:86
  21.1 1.7 %collective-permute-done.1 = f32[2,2,64,256]{3,2,1,0:T(8,128)S(1)} collective-permute-done((f32[2,2,64,256]{3,2,1,0:T(8,128)S(1)}, f32[2,2,64,256]{3,2,1,0:T(8,128)S(1)}, u32[]{:S(2)}, u32[]{:S(2)}) %collective-permute-start.1) | collective-permute-done | bytes 262176 | tf_op jit(solution)/shard_map/ppermute | solution.py:85
  25.3 6.9 %collective-permute-start.2 = (f32[2,2,64,256]{3,2,1,0:T(8,128)S(1)}, f32[2,2,64,256]{3,2,1,0:T(8,128)S(1)}, u32[]{:S(2)}, u32[]{:S(2)}) collective-permute-start(f32[2,2,64,256]{3,2,1,0:T(8,128)S(1)} %pad_maximum_fusion.8), channel_id=1, source_target_pairs={{0,32},{32,64},{64,96},{96,128},{128,160},{160,192},{192,224},{224... | collective-permute-start | bytes 786440 | tf_op jit(solution)/shard_map/ppermute | solution.py:86
  32.2 1.9 %collective-permute-start.3 = (f32[2,2,64,256]{3,2,1,0:T(8,128)S(1)}, f32[2,2,64,256]{3,2,1,0:T(8,128)S(1)}, u32[]{:S(2)}, u32[]{:S(2)}) collective-permute-start(f32[2,2,64,256]{3,2,1,0:T(8,128)S(1)} %pad_maximum_fusion.7), channel_id=1, source_target_pairs={{32,0},{64,32},{96,64},{128,96},{160,128},{192,160},{224,192},{256... | collective-permute-start | bytes 786440 | tf_op jit(solution)/shard_map/ppermute | solution.py:85
  35.6 2.6 %collective-permute-done.3 = f32[2,2,64,256]{3,2,1,0:T(8,128)S(1)} collective-permute-done((f32[2,2,64,256]{3,2,1,0:T(8,128)S(1)}, f32[2,2,64,256]{3,2,1,0:T(8,128)S(1)}, u32[]{:S(2)}, u32[]{:S(2)}) %collective-permute-start.3) | collective-permute-done | bytes 262176 | tf_op jit(solution)/shard_map/ppermute | solution.py:85
  39.4 8.0 %collective-permute-start.4 = (f32[3,32,32]{2,1,0:T(8,128)S(1)}, f32[3,32,32]{2,1,0:T(8,128)S(1)}, u32[]{:S(2)}, u32[]{:S(2)}) collective-permute-start(f32[3,32,32]{2,1,0:T(8,128)S(1)} %pad_maximum_fusion.9), channel_id=1, source_target_pairs={{0,32},{1,33},{2,34},{3,35},{4,36},{5,37},{6,38},{7,39},{8,40},{9,... | collective-permute-start | bytes 36872 | tf_op jit(solution)/shard_map/ppermute | solution.py:57
  48.2 1.9 %collective-permute-start.5 = (f32[3,32,32]{2,1,0:T(8,128)S(1)}, f32[3,32,32]{2,1,0:T(8,128)S(1)}, u32[]{:S(2)}, u32[]{:S(2)}) collective-permute-start(f32[3,32,32]{2,1,0:T(8,128)S(1)} %fusion.97), channel_id=1, source_target_pairs={{0,16},{1,17},{2,18},{3,19},{4,20},{5,21},{6,22},{7,23},{8,24},{9,... | collective-permute-start | bytes 36872 | tf_op jit(solution)/shard_map/ppermute | solution.py:57
  50.2 4.1 %collective-permute-done.5 = f32[3,32,32]{2,1,0:T(8,128)S(1)} collective-permute-done((f32[3,32,32]{2,1,0:T(8,128)S(1)}, f32[3,32,32]{2,1,0:T(8,128)S(1)}, u32[]{:S(2)}, u32[]{:S(2)}) %collective-permute-start.5) | collective-permute-done | bytes 12320 | tf_op jit(solution)/shard_map/ppermute | solution.py:57
  54.2 5.7 %collective-permute-start.6 = (f32[3,32,32]{2,1,0:T(8,128)S(1)}, f32[3,32,32]{2,1,0:T(8,128)S(1)}, u32[]{:S(2)}, u32[]{:S(2)}) collective-permute-start(f32[3,32,32]{2,1,0:T(8,128)S(1)} %add.155), channel_id=1, source_target_pairs={{0,80},{1,81},{2,82},{3,83},{4,84},{5,85},{6,86},{7,87},{8,88},{9,... | collective-permute-start | bytes 36872 | tf_op jit(solution)/shard_map/ppermute | solution.py:57
  59.9 2.1 %collective-permute-done.6 = f32[3,32,32]{2,1,0:T(8,128)S(1)} collective-permute-done((f32[3,32,32]{2,1,0:T(8,128)S(1)}, f32[3,32,32]{2,1,0:T(8,128)S(1)}, u32[]{:S(2)}, u32[]{:S(2)}) %collective-permute-start.6) | collective-permute-done | bytes 12320 | tf_op jit(solution)/shard_map/ppermute | solution.py:57
  62.0 1.9 %collective-permute-start.7 = (f32[3,32,32]{2,1,0:T(8,128)S(1)}, f32[3,32,32]{2,1,0:T(8,128)S(1)}, u32[]{:S(2)}, u32[]{:S(2)}) collective-permute-start(f32[3,32,32]{2,1,0:T(8,128)S(1)} %add.156), channel_id=1, source_target_pairs={{0,128},{1,129},{2,130},{3,131},{4,132},{5,133},{6,134},{7,135},{8... | collective-permute-start | bytes 36872 | tf_op jit(solution)/shard_map/ppermute | solution.py:57
  63.9 4.1 %collective-permute-done.7 = f32[3,32,32]{2,1,0:T(8,128)S(1)} collective-permute-done((f32[3,32,32]{2,1,0:T(8,128)S(1)}, f32[3,32,32]{2,1,0:T(8,128)S(1)}, u32[]{:S(2)}, u32[]{:S(2)}) %collective-permute-start.7) | collective-permute-done | bytes 12320 | tf_op jit(solution)/shard_map/ppermute | solution.py:57
  68.0 3.5 %collective-permute-start.8 = (f32[3,32,32]{2,1,0:T(8,128)S(1)}, f32[3,32,32]{2,1,0:T(8,128)S(1)}, u32[]{:S(2)}, u32[]{:S(2)}) collective-permute-start(f32[3,32,32]{2,1,0:T(8,128)S(1)} %add.157), channel_id=1, source_target_pairs={{0,384},{1,385},{2,386},{3,387},{4,388},{5,389},{6,390},{7,391},{8... | collective-permute-start | bytes 36872 | tf_op jit(solution)/shard_map/ppermute | solution.py:57
  71.7 3.5 %collective-permute-done.8 = f32[3,32,32]{2,1,0:T(8,128)S(1)} collective-permute-done((f32[3,32,32]{2,1,0:T(8,128)S(1)}, f32[3,32,32]{2,1,0:T(8,128)S(1)}, u32[]{:S(2)}, u32[]{:S(2)}) %collective-permute-start.8) | collective-permute-done | bytes 12320 | tf_op jit(solution)/shard_map/ppermute | solution.py:57
  75.2 1.9 %collective-permute-start.9 = (f32[3,32,32]{2,1,0:T(8,128)S(1)}, f32[3,32,32]{2,1,0:T(8,128)S(1)}, u32[]{:S(2)}, u32[]{:S(2)}) collective-permute-start(f32[3,32,32]{2,1,0:T(8,128)S(1)} %add.158), channel_id=1, source_target_pairs={{0,1},{1,0},{2,3},{3,2},{4,5},{5,4},{6,7},{7,6},{8,9},{9,8},{10,11... | collective-permute-start | bytes 36872 | tf_op jit(solution)/shard_map/ppermute | solution.py:57
  77.2 4.0 %collective-permute-done.9 = f32[3,32,32]{2,1,0:T(8,128)S(1)} collective-permute-done((f32[3,32,32]{2,1,0:T(8,128)S(1)}, f32[3,32,32]{2,1,0:T(8,128)S(1)}, u32[]{:S(2)}, u32[]{:S(2)}) %collective-permute-start.9) | collective-permute-done | bytes 12320 | tf_op jit(solution)/shard_map/ppermute | solution.py:57
  81.2 1.9 %collective-permute-start.10 = (f32[3,32,32]{2,1,0:T(8,128)S(1)}, f32[3,32,32]{2,1,0:T(8,128)S(1)}, u32[]{:S(2)}, u32[]{:S(2)}) collective-permute-start(f32[3,32,32]{2,1,0:T(8,128)S(1)} %add.159), channel_id=1, source_target_pairs={{0,2},{1,3},{2,0},{3,1},{4,6},{5,7},{6,4},{7,5},{8,10},{9,11},{10,... | collective-permute-start | bytes 36872 | tf_op jit(solution)/shard_map/ppermute | solution.py:57
  83.2 4.9 %collective-permute-done.10 = f32[3,32,32]{2,1,0:T(8,128)S(1)} collective-permute-done((f32[3,32,32]{2,1,0:T(8,128)S(1)}, f32[3,32,32]{2,1,0:T(8,128)S(1)}, u32[]{:S(2)}, u32[]{:S(2)}) %collective-permute-start.10) | collective-permute-done | bytes 12320 | tf_op jit(solution)/shard_map/ppermute | solution.py:57
  88.1 6.1 %collective-permute-start.11 = (f32[3,32,32]{2,1,0:T(8,128)S(1)}, f32[3,32,32]{2,1,0:T(8,128)S(1)}, u32[]{:S(2)}, u32[]{:S(2)}) collective-permute-start(f32[3,32,32]{2,1,0:T(8,128)S(1)} %add.160), channel_id=1, source_target_pairs={{0,4},{1,5},{2,6},{3,7},{4,0},{5,1},{6,2},{7,3},{8,12},{9,13},{10,... | collective-permute-start | bytes 36872 | tf_op jit(solution)/shard_map/ppermute | solution.py:57
  94.3 4.2 %collective-permute-done.11 = f32[3,32,32]{2,1,0:T(8,128)S(1)} collective-permute-done((f32[3,32,32]{2,1,0:T(8,128)S(1)}, f32[3,32,32]{2,1,0:T(8,128)S(1)}, u32[]{:S(2)}, u32[]{:S(2)}) %collective-permute-start.11) | collective-permute-done | bytes 12320 | tf_op jit(solution)/shard_map/ppermute | solution.py:57
  98.5 8.2 %collective-permute-start.12 = (f32[3,32,32]{2,1,0:T(8,128)S(1)}, f32[3,32,32]{2,1,0:T(8,128)S(1)}, u32[]{:S(2)}, u32[]{:S(2)}) collective-permute-start(f32[3,32,32]{2,1,0:T(8,128)S(1)} %add.161), channel_id=1, source_target_pairs={{0,12},{1,13},{2,14},{3,15},{4,8},{5,9},{6,10},{7,11},{8,4},{9,5},... | collective-permute-start | bytes 36872 | tf_op jit(solution)/shard_map/ppermute | solution.py:57
  (76 shorter events, 18.1 us)
Async XLA Ops:
  0.6 5.4 %copy-start = (bf16[6,3,256,256]{3,2,1,0:T(8,128)(2,1)S(1)}, bf16[6,3,256,256]{3,2,1,0:T(8,128)(2,1)}, u32[]{:S(2)}) copy-start(bf16[6,3,256,256]{3,2,1,0:T(8,128)(2,1)} %param.15) | copy-start | bytes 7077892
  3.8 2.2 %copy-start.3 = (bf16[64,6,256]{2,1,0:T(8,128)(2,1)}, bf16[64,6,256]{2,1,0:T(8,128)(2,1)S(1)}, u32[]{:S(2)}) copy-start(bf16[64,6,256]{2,1,0:T(8,128)(2,1)S(1)} %reshape.187) | copy-start | bytes 589828
  5.0 1.0 copy-start.1
  6.1 3.3 %copy-start.8 = (s32[6,3]{0,1:T(4,128)S(1)}, s32[6,3]{0,1:T(4,128)}, u32[]{:S(2)}) copy-start(s32[6,3]{0,1:T(4,128)} %param.16) | copy-start | bytes 220
  9.3 1.5 %copy-start.5 = (f32[1,2,64,256]{3,2,1,0:T(8,128)S(1)}, f32[1,2,64,256]{3,2,1,0:T(8,128)}, u32[]{:S(2)}) copy-start(f32[1,2,64,256]{3,2,1,0:T(8,128)} %get-tuple-element.86) | copy-start | bytes 393220
  9.4 9.5 %copy-start.2 = (f32[3,6,2,32,256]{4,3,0,2,1:T(8,128)S(1)}, f32[3,6,2,32,256]{4,3,0,2,1:T(8,128)}, u32[]{:S(2)}) copy-start(f32[3,6,2,32,256]{4,3,0,2,1:T(8,128)} %copy-done.1) | copy-start | bytes 3538948
  10.9 10.1 %collective-permute-start = (f32[2,2,64,256]{3,2,1,0:T(8,128)S(1)}, f32[2,2,64,256]{3,2,1,0:T(8,128)S(1)}, u32[]{:S(2)}, u32[]{:S(2)}) collective-permute-start(f32[2,2,64,256]{3,2,1,0:T(8,128)S(1)} %get-tuple-element.55), channel_id=1, source_target_pairs={{0,32},{32,64},{64,96},{96,128},{128,160},{160,192},{192,224},{224... | collective-permute-start | bytes 786440 | tf_op jit(solution)/shard_map/ppermute | solution.py:86
  12.8 9.9 %collective-permute-start.1 = (f32[2,2,64,256]{3,2,1,0:T(8,128)S(1)}, f32[2,2,64,256]{3,2,1,0:T(8,128)S(1)}, u32[]{:S(2)}, u32[]{:S(2)}) collective-permute-start(f32[2,2,64,256]{3,2,1,0:T(8,128)S(1)} %get-tuple-element.56), channel_id=1, source_target_pairs={{32,0},{64,32},{96,64},{128,96},{160,128},{192,160},{224,192},{256... | collective-permute-start | bytes 786440 | tf_op jit(solution)/shard_map/ppermute | solution.py:85
  23.4 0.9 copy-start.6
  25.2 9.0 %copy-start.4 = (bf16[64,6,256]{2,1,0:T(8,128)(2,1)S(1)}, bf16[64,6,256]{2,1,0:T(8,128)(2,1)}, u32[]{:S(2)}) copy-start(bf16[64,6,256]{2,1,0:T(8,128)(2,1)} %copy-done.3) | copy-start | bytes 589828
  25.3 10.3 %collective-permute-start.2 = (f32[2,2,64,256]{3,2,1,0:T(8,128)S(1)}, f32[2,2,64,256]{3,2,1,0:T(8,128)S(1)}, u32[]{:S(2)}, u32[]{:S(2)}) collective-permute-start(f32[2,2,64,256]{3,2,1,0:T(8,128)S(1)} %pad_maximum_fusion.8), channel_id=1, source_target_pairs={{0,32},{32,64},{64,96},{96,128},{128,160},{160,192},{192,224},{224... | collective-permute-start | bytes 786440 | tf_op jit(solution)/shard_map/ppermute | solution.py:86
  32.2 6.0 %collective-permute-start.3 = (f32[2,2,64,256]{3,2,1,0:T(8,128)S(1)}, f32[2,2,64,256]{3,2,1,0:T(8,128)S(1)}, u32[]{:S(2)}, u32[]{:S(2)}) collective-permute-start(f32[2,2,64,256]{3,2,1,0:T(8,128)S(1)} %pad_maximum_fusion.7), channel_id=1, source_target_pairs={{32,0},{64,32},{96,64},{128,96},{160,128},{192,160},{224,192},{256... | collective-permute-start | bytes 786440 | tf_op jit(solution)/shard_map/ppermute | solution.py:85
  39.4 8.8 %collective-permute-start.4 = (f32[3,32,32]{2,1,0:T(8,128)S(1)}, f32[3,32,32]{2,1,0:T(8,128)S(1)}, u32[]{:S(2)}, u32[]{:S(2)}) collective-permute-start(f32[3,32,32]{2,1,0:T(8,128)S(1)} %pad_maximum_fusion.9), channel_id=1, source_target_pairs={{0,32},{1,33},{2,34},{3,35},{4,36},{5,37},{6,38},{7,39},{8,40},{9,... | collective-permute-start | bytes 36872 | tf_op jit(solution)/shard_map/ppermute | solution.py:57
  48.2 6.0 %collective-permute-start.5 = (f32[3,32,32]{2,1,0:T(8,128)S(1)}, f32[3,32,32]{2,1,0:T(8,128)S(1)}, u32[]{:S(2)}, u32[]{:S(2)}) collective-permute-start(f32[3,32,32]{2,1,0:T(8,128)S(1)} %fusion.97), channel_id=1, source_target_pairs={{0,16},{1,17},{2,18},{3,19},{4,20},{5,21},{6,22},{7,23},{8,24},{9,... | collective-permute-start | bytes 36872 | tf_op jit(solution)/shard_map/ppermute | solution.py:57
  54.2 7.7 %collective-permute-start.6 = (f32[3,32,32]{2,1,0:T(8,128)S(1)}, f32[3,32,32]{2,1,0:T(8,128)S(1)}, u32[]{:S(2)}, u32[]{:S(2)}) collective-permute-start(f32[3,32,32]{2,1,0:T(8,128)S(1)} %add.155), channel_id=1, source_target_pairs={{0,80},{1,81},{2,82},{3,83},{4,84},{5,85},{6,86},{7,87},{8,88},{9,... | collective-permute-start | bytes 36872 | tf_op jit(solution)/shard_map/ppermute | solution.py:57
  62.0 6.0 %collective-permute-start.7 = (f32[3,32,32]{2,1,0:T(8,128)S(1)}, f32[3,32,32]{2,1,0:T(8,128)S(1)}, u32[]{:S(2)}, u32[]{:S(2)}) collective-permute-start(f32[3,32,32]{2,1,0:T(8,128)S(1)} %add.156), channel_id=1, source_target_pairs={{0,128},{1,129},{2,130},{3,131},{4,132},{5,133},{6,134},{7,135},{8... | collective-permute-start | bytes 36872 | tf_op jit(solution)/shard_map/ppermute | solution.py:57
  68.0 7.2 %collective-permute-start.8 = (f32[3,32,32]{2,1,0:T(8,128)S(1)}, f32[3,32,32]{2,1,0:T(8,128)S(1)}, u32[]{:S(2)}, u32[]{:S(2)}) collective-permute-start(f32[3,32,32]{2,1,0:T(8,128)S(1)} %add.157), channel_id=1, source_target_pairs={{0,384},{1,385},{2,386},{3,387},{4,388},{5,389},{6,390},{7,391},{8... | collective-permute-start | bytes 36872 | tf_op jit(solution)/shard_map/ppermute | solution.py:57
  71.7 35.0 %copy-start.7 = (bf16[3,32,32]{2,1,0:T(8,128)(2,1)S(1)}, bf16[3,32,32]{2,1,0:T(8,128)(2,1)}, u32[]{:S(2)}) copy-start(bf16[3,32,32]{2,1,0:T(8,128)(2,1)} %param.17) | copy-start | bytes 18436
  75.2 6.0 %collective-permute-start.9 = (f32[3,32,32]{2,1,0:T(8,128)S(1)}, f32[3,32,32]{2,1,0:T(8,128)S(1)}, u32[]{:S(2)}, u32[]{:S(2)}) collective-permute-start(f32[3,32,32]{2,1,0:T(8,128)S(1)} %add.158), channel_id=1, source_target_pairs={{0,1},{1,0},{2,3},{3,2},{4,5},{5,4},{6,7},{7,6},{8,9},{9,8},{10,11... | collective-permute-start | bytes 36872 | tf_op jit(solution)/shard_map/ppermute | solution.py:57
  81.2 6.9 %collective-permute-start.10 = (f32[3,32,32]{2,1,0:T(8,128)S(1)}, f32[3,32,32]{2,1,0:T(8,128)S(1)}, u32[]{:S(2)}, u32[]{:S(2)}) collective-permute-start(f32[3,32,32]{2,1,0:T(8,128)S(1)} %add.159), channel_id=1, source_target_pairs={{0,2},{1,3},{2,0},{3,1},{4,6},{5,7},{6,4},{7,5},{8,10},{9,11},{10,... | collective-permute-start | bytes 36872 | tf_op jit(solution)/shard_map/ppermute | solution.py:57
  88.1 10.4 %collective-permute-start.11 = (f32[3,32,32]{2,1,0:T(8,128)S(1)}, f32[3,32,32]{2,1,0:T(8,128)S(1)}, u32[]{:S(2)}, u32[]{:S(2)}) collective-permute-start(f32[3,32,32]{2,1,0:T(8,128)S(1)} %add.160), channel_id=1, source_target_pairs={{0,4},{1,5},{2,6},{3,7},{4,0},{5,1},{6,2},{7,3},{8,12},{9,13},{10,... | collective-permute-start | bytes 36872 | tf_op jit(solution)/shard_map/ppermute | solution.py:57
  98.5 10.6 %collective-permute-start.12 = (f32[3,32,32]{2,1,0:T(8,128)S(1)}, f32[3,32,32]{2,1,0:T(8,128)S(1)}, u32[]{:S(2)}, u32[]{:S(2)}) collective-permute-start(f32[3,32,32]{2,1,0:T(8,128)S(1)} %add.161), channel_id=1, source_target_pairs={{0,12},{1,13},{2,14},{3,15},{4,8},{5,9},{6,10},{7,11},{8,4},{9,5},... | collective-permute-start | bytes 36872 | tf_op jit(solution)/shard_map/ppermute | solution.py:57

commit v9 on v8

--- a/solution.py
+++ b/solution.py
@@ -114,14 +114,18 @@
 
     x_zero = to_blocks(maps)
     cot_b = to_blocks(cotangent).reshape(nb, map_count, chan_count, block_size)
-    grads = jnp.einsum("kco,rmop->krmcp", filters, cot_b, preferred_element_type=jnp.float32)
+    cot_split = cotangent.reshape(map_count, chan_count, nb, block_size)
+    grads = jnp.einsum("kco,morp->krmcp", filters, cot_split, preferred_element_type=jnp.float32)
     grads = grads.reshape(3, nb, row_count, block_size)
     grad_two = grads[2].astype(jnp.bfloat16)
 
     win1 = adjoint_window(grad_two)
     x0f = x_zero.astype(jnp.float32)
-    send_left = jnp.stack([x0f[0:2], win1[0:2]])
-    send_right = jnp.stack([x0f[nb - 2 : nb], win1[nb + 2 : nb + 4]])
+    map_blocks = maps.reshape(row_count, nb, block_size)
+    halo_left = map_blocks[:, 0:2].transpose(1, 0, 2).astype(jnp.float32)
+    halo_right = map_blocks[:, nb - 2 : nb].transpose(1, 0, 2).astype(jnp.float32)
+    send_left = jnp.stack([halo_left, win1[0:2]])
+    send_right = jnp.stack([halo_right, win1[nb + 2 : nb + 4]])
     got_left, got_right = exchange(send_left, send_right)
     ext0 = jnp.concatenate([got_left[0], x0f, got_right[0]], axis=0)
     x_one = forward_local(ext0).astype(jnp.bfloat16)

time: 111 us -> 121 us (1.090)
  the two profiles are of different devices: /device:TPU:24 before, /device:TPU:2 now
where the time goes in v9:
time: 121 us; the launch traced here: 120 us
  starting transfers between devices  52.3 us (43%)
  waiting for transfers between devices  40.2 us (33%)
  local copies, waits for them, and re-layouts  12 us (10%)
  other arithmetic  7.62 us (6%)
  matrix products  6.47 us (5%)
  between operations  1.24 us (1%)
    ppermute x9, starting transfers between devices, butterfly_sum(): x = x + lax.ppermute(x, axes, pairs)  33.5 us
    ppermute x9, waiting for transfers between devices, butterfly_sum(): x = x + lax.ppermute(x, axes, pairs)  30.3 us
    ppermute x2, starting transfers between devices, exchange(): from_right = lax.ppermute(edge_left, 'patch', to_left)  14.7 us
    ppermute x2, waiting for transfers between devices, exchange(): from_left = lax.ppermute(edge_right, 'patch', to_right)  7.85 us
    ppermute x2, starting transfers between devices, exchange(): from_left = lax.ppermute(edge_right, 'patch', to_right)  4.09 us
    reshape x5, local copies, waits for them, and re-layouts, to_blocks(): return field.reshape(row_count, nb, block_size).transpose(1, 0, 2)  3.12 us
    unnamed x44, local copies, waits for them, and re-layouts  2.82 us
  transfers between devices with their start and end apart: 13, of which 13 were waited for; matrix products, arithmetic and copies ran while one was open for 7% of the time, Pallas kernels for 0%

profile of v9, /device:TPU:2, one launch (start us, length us, event | category | flops | bytes accessed | tf_op | source)
XLA Modules:
  0.0 119.8 jit_solution(3239518785107906684)
XLA Ops:
  0.6 2.0 %reshape.191 = bf16[2,32,6,256]{3,2,1,0:T(8,128)(2,1)} reshape(bf16[2,32,1536]{2,1,0:T(8,128)(2,1)} %param.14) | data formatting | bytes 393216 | tf_op jit(solution)/shard_map/reshape | solution.py:117
  10.1 2.1 %collective-permute-start = (f32[2,2,64,256]{3,2,1,0:T(8,128)S(1)}, f32[2,2,64,256]{3,2,1,0:T(8,128)S(1)}, u32[]{:S(2)}, u32[]{:S(2)}) collective-permute-start(f32[2,2,64,256]{3,2,1,0:T(8,128)S(1)} %get-tuple-element.55), channel_id=1, source_target_pairs={{0,32},{32,64},{64,96},{96,128},{128,160},{160,192},{192,224},{224... | collective-permute-start | bytes 786440 | tf_op jit(solution)/shard_map/ppermute | solution.py:86
  12.2 7.3 %collective-permute-start.1 = (f32[2,2,64,256]{3,2,1,0:T(8,128)S(1)}, f32[2,2,64,256]{3,2,1,0:T(8,128)S(1)}, u32[]{:S(2)}, u32[]{:S(2)}) collective-permute-start(f32[2,2,64,256]{3,2,1,0:T(8,128)S(1)} %get-tuple-element.56), channel_id=1, source_target_pairs={{32,0},{64,32},{96,64},{128,96},{160,128},{192,160},{224,192},{256... | collective-permute-start | bytes 786440 | tf_op jit(solution)/shard_map/ppermute | solution.py:85
  21.6 1.7 %collective-permute-done.1 = f32[2,2,64,256]{3,2,1,0:T(8,128)S(1)} collective-permute-done((f32[2,2,64,256]{3,2,1,0:T(8,128)S(1)}, f32[2,2,64,256]{3,2,1,0:T(8,128)S(1)}, u32[]{:S(2)}, u32[]{:S(2)}) %collective-permute-start.1) | collective-permute-done | bytes 262176 | tf_op jit(solution)/shard_map/ppermute | solution.py:85
  28.0 7.4 %collective-permute-start.3 = (f32[2,2,64,256]{3,2,1,0:T(8,128)}, f32[2,2,64,256]{3,2,1,0:T(8,128)}, u32[]{:S(2)}, u32[]{:S(2)}) collective-permute-start(f32[2,2,64,256]{3,2,1,0:T(8,128)} %pad_maximum_fusion.7), channel_id=1, source_target_pairs={{32,0},{64,32},{96,64},{128,96},{160,128},{192,160},{224,192},{256... | collective-permute-start | bytes 786440 | tf_op jit(solution)/shard_map/ppermute | solution.py:85
  35.4 1.9 %reshape.199 = bf16[64,6,256]{2,1,0:T(8,128)(2,1)} reshape(bf16[2,32,1536]{2,1,0:T(8,128)(2,1)} %param.14) | data formatting | bytes 393216 | tf_op jit(solution)/shard_map/reshape | solution.py:90
  37.3 2.0 %collective-permute-start.2 = (f32[2,2,64,256]{3,2,1,0:T(8,128)}, f32[2,2,64,256]{3,2,1,0:T(8,128)S(1)}, u32[]{:S(2)}, u32[]{:S(2)}) collective-permute-start(f32[2,2,64,256]{3,2,1,0:T(8,128)} %pad_maximum_fusion.8), channel_id=1, source_target_pairs={{0,32},{32,64},{64,96},{96,128},{128,160},{160,192},{192,224},{224... | collective-permute-start | bytes 786440 | tf_op jit(solution)/shard_map/ppermute | solution.py:86
  42.1 6.9 %collective-permute-done.2 = f32[2,2,64,256]{3,2,1,0:T(8,128)S(1)} collective-permute-done((f32[2,2,64,256]{3,2,1,0:T(8,128)}, f32[2,2,64,256]{3,2,1,0:T(8,128)S(1)}, u32[]{:S(2)}, u32[]{:S(2)}) %collective-permute-start.2) | collective-permute-done | bytes 262176 | tf_op jit(solution)/shard_map/ppermute | solution.py:86
  51.5 1.9 %collective-permute-start.4 = (f32[3,32,32]{2,1,0:T(8,128)S(1)}, f32[3,32,32]{2,1,0:T(8,128)S(1)}, u32[]{:S(2)}, u32[]{:S(2)}) collective-permute-start(f32[3,32,32]{2,1,0:T(8,128)S(1)} %pad_maximum_fusion.9), channel_id=1, source_target_pairs={{0,32},{1,33},{2,34},{3,35},{4,36},{5,37},{6,38},{7,39},{8,40},{9,... | collective-permute-start | bytes 36872 | tf_op jit(solution)/shard_map/ppermute | solution.py:57
  54.7 7.8 %collective-permute-start.5 = (f32[3,32,32]{2,1,0:T(8,128)S(1)}, f32[3,32,32]{2,1,0:T(8,128)S(1)}, u32[]{:S(2)}, u32[]{:S(2)}) collective-permute-start(f32[3,32,32]{2,1,0:T(8,128)S(1)} %fusion.94), channel_id=1, source_target_pairs={{0,16},{1,17},{2,18},{3,19},{4,20},{5,21},{6,22},{7,23},{8,24},{9,... | collective-permute-start | bytes 36872 | tf_op jit(solution)/shard_map/ppermute | solution.py:57
  62.5 2.1 %collective-permute-done.5 = f32[3,32,32]{2,1,0:T(8,128)S(1)} collective-permute-done((f32[3,32,32]{2,1,0:T(8,128)S(1)}, f32[3,32,32]{2,1,0:T(8,128)S(1)}, u32[]{:S(2)}, u32[]{:S(2)}) %collective-permute-start.5) | collective-permute-done | bytes 12320 | tf_op jit(solution)/shard_map/ppermute | solution.py:57
  64.6 1.9 %collective-permute-start.6 = (f32[3,32,32]{2,1,0:T(8,128)S(1)}, f32[3,32,32]{2,1,0:T(8,128)S(1)}, u32[]{:S(2)}, u32[]{:S(2)}) collective-permute-start(f32[3,32,32]{2,1,0:T(8,128)S(1)} %add.155), channel_id=1, source_target_pairs={{0,80},{1,81},{2,82},{3,83},{4,84},{5,85},{6,86},{7,87},{8,88},{9,... | collective-permute-start | bytes 36872 | tf_op jit(solution)/shard_map/ppermute | solution.py:57
  66.5 4.1 %collective-permute-done.6 = f32[3,32,32]{2,1,0:T(8,128)S(1)} collective-permute-done((f32[3,32,32]{2,1,0:T(8,128)S(1)}, f32[3,32,32]{2,1,0:T(8,128)S(1)}, u32[]{:S(2)}, u32[]{:S(2)}) %collective-permute-start.6) | collective-permute-done | bytes 12320 | tf_op jit(solution)/shard_map/ppermute | solution.py:57
  70.6 1.9 %collective-permute-start.7 = (f32[3,32,32]{2,1,0:T(8,128)S(1)}, f32[3,32,32]{2,1,0:T(8,128)S(1)}, u32[]{:S(2)}, u32[]{:S(2)}) collective-permute-start(f32[3,32,32]{2,1,0:T(8,128)S(1)} %add.156), channel_id=1, source_target_pairs={{0,128},{1,129},{2,130},{3,131},{4,132},{5,133},{6,134},{7,135},{8... | collective-permute-start | bytes 36872 | tf_op jit(solution)/shard_map/ppermute | solution.py:57
  72.5 4.0 %collective-permute-done.7 = f32[3,32,32]{2,1,0:T(8,128)S(1)} collective-permute-done((f32[3,32,32]{2,1,0:T(8,128)S(1)}, f32[3,32,32]{2,1,0:T(8,128)S(1)}, u32[]{:S(2)}, u32[]{:S(2)}) %collective-permute-start.7) | collective-permute-done | bytes 12320 | tf_op jit(solution)/shard_map/ppermute | solution.py:57
  76.6 1.9 %collective-permute-start.8 = (f32[3,32,32]{2,1,0:T(8,128)S(1)}, f32[3,32,32]{2,1,0:T(8,128)S(1)}, u32[]{:S(2)}, u32[]{:S(2)}) collective-permute-start(f32[3,32,32]{2,1,0:T(8,128)S(1)} %add.157), channel_id=1, source_target_pairs={{0,384},{1,385},{2,386},{3,387},{4,388},{5,389},{6,390},{7,391},{8... | collective-permute-start | bytes 36872 | tf_op jit(solution)/shard_map/ppermute | solution.py:57
  78.7 5.0 %collective-permute-done.8 = f32[3,32,32]{2,1,0:T(8,128)S(1)} collective-permute-done((f32[3,32,32]{2,1,0:T(8,128)S(1)}, f32[3,32,32]{2,1,0:T(8,128)S(1)}, u32[]{:S(2)}, u32[]{:S(2)}) %collective-permute-start.8) | collective-permute-done | bytes 12320 | tf_op jit(solution)/shard_map/ppermute | solution.py:57
  83.8 1.9 %collective-permute-start.9 = (f32[3,32,32]{2,1,0:T(8,128)S(1)}, f32[3,32,32]{2,1,0:T(8,128)S(1)}, u32[]{:S(2)}, u32[]{:S(2)}) collective-permute-start(f32[3,32,32]{2,1,0:T(8,128)S(1)} %add.158), channel_id=1, source_target_pairs={{0,1},{1,0},{2,3},{3,2},{4,5},{5,4},{6,7},{7,6},{8,9},{9,8},{10,11... | collective-permute-start | bytes 36872 | tf_op jit(solution)/shard_map/ppermute | solution.py:57
  85.7 4.0 %collective-permute-done.9 = f32[3,32,32]{2,1,0:T(8,128)S(1)} collective-permute-done((f32[3,32,32]{2,1,0:T(8,128)S(1)}, f32[3,32,32]{2,1,0:T(8,128)S(1)}, u32[]{:S(2)}, u32[]{:S(2)}) %collective-permute-start.9) | collective-permute-done | bytes 12320 | tf_op jit(solution)/shard_map/ppermute | solution.py:57
  89.8 1.9 %collective-permute-start.10 = (f32[3,32,32]{2,1,0:T(8,128)S(1)}, f32[3,32,32]{2,1,0:T(8,128)S(1)}, u32[]{:S(2)}, u32[]{:S(2)}) collective-permute-start(f32[3,32,32]{2,1,0:T(8,128)S(1)} %add.159), channel_id=1, source_target_pairs={{0,2},{1,3},{2,0},{3,1},{4,6},{5,7},{6,4},{7,5},{8,10},{9,11},{10,... | collective-permute-start | bytes 36872 | tf_op jit(solution)/shard_map/ppermute | solution.py:57
  92.6 4.5 %collective-permute-done.10 = f32[3,32,32]{2,1,0:T(8,128)S(1)} collective-permute-done((f32[3,32,32]{2,1,0:T(8,128)S(1)}, f32[3,32,32]{2,1,0:T(8,128)S(1)}, u32[]{:S(2)}, u32[]{:S(2)}) %collective-permute-start.10) | collective-permute-done | bytes 12320 | tf_op jit(solution)/shard_map/ppermute | solution.py:57
  97.2 5.3 %collective-permute-start.11 = (f32[3,32,32]{2,1,0:T(8,128)S(1)}, f32[3,32,32]{2,1,0:T(8,128)S(1)}, u32[]{:S(2)}, u32[]{:S(2)}) collective-permute-start(f32[3,32,32]{2,1,0:T(8,128)S(1)} %add.160), channel_id=1, source_target_pairs={{0,4},{1,5},{2,6},{3,7},{4,0},{5,1},{6,2},{7,3},{8,12},{9,13},{10,... | collective-permute-start | bytes 36872 | tf_op jit(solution)/shard_map/ppermute | solution.py:57
  102.5 5.1 %collective-permute-done.11 = f32[3,32,32]{2,1,0:T(8,128)S(1)} collective-permute-done((f32[3,32,32]{2,1,0:T(8,128)S(1)}, f32[3,32,32]{2,1,0:T(8,128)S(1)}, u32[]{:S(2)}, u32[]{:S(2)}) %collective-permute-start.11) | collective-permute-done | bytes 12320 | tf_op jit(solution)/shard_map/ppermute | solution.py:57
  107.6 8.9 %collective-permute-start.12 = (f32[3,32,32]{2,1,0:T(8,128)S(1)}, f32[3,32,32]{2,1,0:T(8,128)S(1)}, u32[]{:S(2)}, u32[]{:S(2)}) collective-permute-start(f32[3,32,32]{2,1,0:T(8,128)S(1)} %add.161), channel_id=1, source_target_pairs={{0,12},{1,13},{2,14},{3,15},{4,8},{5,9},{6,10},{7,11},{8,4},{9,5},... | collective-permute-start | bytes 36872 | tf_op jit(solution)/shard_map/ppermute | solution.py:57
  (106 shorter events, 25.1 us)
Async XLA Ops:
  0.6 4.3 %copy-start = (bf16[6,3,256,256]{3,2,1,0:T(8,128)(2,1)S(1)}, bf16[6,3,256,256]{3,2,1,0:T(8,128)(2,1)}, u32[]{:S(2)}) copy-start(bf16[6,3,256,256]{3,2,1,0:T(8,128)(2,1)} %param.15) | copy-start | bytes 7077892
  5.0 3.6 %copy-start.20 = (s32[6,3]{0,1:T(4,128)S(1)}, s32[6,3]{0,1:T(4,128)}, u32[]{:S(2)}) copy-start(s32[6,3]{0,1:T(4,128)} %param.16) | copy-start | bytes 220
  8.6 10.9 %copy-start.9 = (f32[3,6,2,32,256]{4,3,0,1,2:T(8,128)S(1)}, f32[3,6,2,32,256]{4,3,0,1,2:T(8,128)}, u32[]{:S(2)}) copy-start(f32[3,6,2,32,256]{4,3,0,1,2:T(8,128)} %copy-done.8) | copy-start | bytes 3538948
  10.1 10.3 %copy-start.7 = (bf16[64,6,256]{2,1,0:T(8,128)(2,1)S(1)}, bf16[64,6,256]{2,1,0:T(8,128)(2,1)}, u32[]{:S(2)}) copy-start(bf16[64,6,256]{2,1,0:T(8,128)(2,1)} %copy-done.6) | copy-start | bytes 589828
  10.1 11.4 %collective-permute-start = (f32[2,2,64,256]{3,2,1,0:T(8,128)S(1)}, f32[2,2,64,256]{3,2,1,0:T(8,128)S(1)}, u32[]{:S(2)}, u32[]{:S(2)}) collective-permute-start(f32[2,2,64,256]{3,2,1,0:T(8,128)S(1)} %get-tuple-element.55), channel_id=1, source_target_pairs={{0,32},{32,64},{64,96},{96,128},{128,160},{160,192},{192,224},{224... | collective-permute-start | bytes 786440 | tf_op jit(solution)/shard_map/ppermute | solution.py:86
  12.2 11.1 %collective-permute-start.1 = (f32[2,2,64,256]{3,2,1,0:T(8,128)S(1)}, f32[2,2,64,256]{3,2,1,0:T(8,128)S(1)}, u32[]{:S(2)}, u32[]{:S(2)}) collective-permute-start(f32[2,2,64,256]{3,2,1,0:T(8,128)S(1)} %get-tuple-element.56), channel_id=1, source_target_pairs={{32,0},{64,32},{96,64},{128,96},{160,128},{192,160},{224,192},{256... | collective-permute-start | bytes 786440 | tf_op jit(solution)/shard_map/ppermute | solution.py:85
  28.0 13.1 %collective-permute-start.3 = (f32[2,2,64,256]{3,2,1,0:T(8,128)}, f32[2,2,64,256]{3,2,1,0:T(8,128)}, u32[]{:S(2)}, u32[]{:S(2)}) collective-permute-start(f32[2,2,64,256]{3,2,1,0:T(8,128)} %pad_maximum_fusion.7), channel_id=1, source_target_pairs={{32,0},{64,32},{96,64},{128,96},{160,128},{192,160},{224,192},{256... | collective-permute-start | bytes 786440 | tf_op jit(solution)/shard_map/ppermute | solution.py:85
  37.3 13.1 %copy-start.15 = (bf16[64,6,256]{2,0,1:T(8,128)(2,1)S(1)}, bf16[64,6,256]{2,0,1:T(8,128)(2,1)}, u32[]{:S(2)}) copy-start(bf16[64,6,256]{2,0,1:T(8,128)(2,1)} %copy-done.14) | copy-start | bytes 589828
  37.3 13.1 %copy-start.21 = (bf16[6,64,256]{2,1,0:T(8,128)(2,1)S(1)}, bf16[6,64,256]{2,1,0:T(8,128)(2,1)}, u32[]{:S(2)}) copy-start(bf16[6,64,256]{2,1,0:T(8,128)(2,1)} %get-tuple-element.88) | copy-start | bytes 589828
  37.3 11.6 %collective-permute-start.2 = (f32[2,2,64,256]{3,2,1,0:T(8,128)}, f32[2,2,64,256]{3,2,1,0:T(8,128)S(1)}, u32[]{:S(2)}, u32[]{:S(2)}) collective-permute-start(f32[2,2,64,256]{3,2,1,0:T(8,128)} %pad_maximum_fusion.8), channel_id=1, source_target_pairs={{0,32},{32,64},{64,96},{96,128},{128,160},{160,192},{192,224},{224... | collective-permute-start | bytes 786440 | tf_op jit(solution)/shard_map/ppermute | solution.py:86
  50.4 22.1 %copy-start.12 = (f32[1,6,2,32,256]{4,3,0,1,2:T(8,128)S(1)}, f32[1,6,2,32,256]{4,3,0,1,2:T(8,128)}, u32[]{:S(2)}) copy-start(f32[1,6,2,32,256]{4,3,0,1,2:T(8,128)} %get-tuple-element.71) | copy-start | bytes 1179652
  50.4 28.1 %copy-start.2 = (f32[6,64,256]{2,1,0:T(8,128)S(1)}, f32[6,64,256]{2,1,0:T(8,128)}, u32[]{:S(2)}) copy-start(f32[6,64,256]{2,1,0:T(8,128)} %copy-done.1) | copy-start | bytes 1179652
  50.4 28.1 %copy-start.4 = (f32[6,64,256]{2,1,0:T(8,128)S(1)}, f32[6,64,256]{2,1,0:T(8,128)}, u32[]{:S(2)}) copy-start(f32[6,64,256]{2,1,0:T(8,128)} %copy-done.3) | copy-start | bytes 1179652
  51.5 3.1 %collective-permute-start.4 = (f32[3,32,32]{2,1,0:T(8,128)S(1)}, f32[3,32,32]{2,1,0:T(8,128)S(1)}, u32[]{:S(2)}, u32[]{:S(2)}) collective-permute-start(f32[3,32,32]{2,1,0:T(8,128)S(1)} %pad_maximum_fusion.9), channel_id=1, source_target_pairs={{0,32},{1,33},{2,34},{3,35},{4,36},{5,37},{6,38},{7,39},{8,40},{9,... | collective-permute-start | bytes 36872 | tf_op jit(solution)/shard_map/ppermute | solution.py:57
  54.7 9.9 %collective-permute-start.5 = (f32[3,32,32]{2,1,0:T(8,128)S(1)}, f32[3,32,32]{2,1,0:T(8,128)S(1)}, u32[]{:S(2)}, u32[]{:S(2)}) collective-permute-start(f32[3,32,32]{2,1,0:T(8,128)S(1)} %fusion.94), channel_id=1, source_target_pairs={{0,16},{1,17},{2,18},{3,19},{4,20},{5,21},{6,22},{7,23},{8,24},{9,... | collective-permute-start | bytes 36872 | tf_op jit(solution)/shard_map/ppermute | solution.py:57
  64.6 6.0 %collective-permute-start.6 = (f32[3,32,32]{2,1,0:T(8,128)S(1)}, f32[3,32,32]{2,1,0:T(8,128)S(1)}, u32[]{:S(2)}, u32[]{:S(2)}) collective-permute-start(f32[3,32,32]{2,1,0:T(8,128)S(1)} %add.155), channel_id=1, source_target_pairs={{0,80},{1,81},{2,82},{3,83},{4,84},{5,85},{6,86},{7,87},{8,88},{9,... | collective-permute-start | bytes 36872 | tf_op jit(solution)/shard_map/ppermute | solution.py:57
  70.6 6.0 %collective-permute-start.7 = (f32[3,32,32]{2,1,0:T(8,128)S(1)}, f32[3,32,32]{2,1,0:T(8,128)S(1)}, u32[]{:S(2)}, u32[]{:S(2)}) collective-permute-start(f32[3,32,32]{2,1,0:T(8,128)S(1)} %add.156), channel_id=1, source_target_pairs={{0,128},{1,129},{2,130},{3,131},{4,132},{5,133},{6,134},{7,135},{8... | collective-permute-start | bytes 36872 | tf_op jit(solution)/shard_map/ppermute | solution.py:57
  76.6 7.2 %collective-permute-start.8 = (f32[3,32,32]{2,1,0:T(8,128)S(1)}, f32[3,32,32]{2,1,0:T(8,128)S(1)}, u32[]{:S(2)}, u32[]{:S(2)}) collective-permute-start(f32[3,32,32]{2,1,0:T(8,128)S(1)} %add.157), channel_id=1, source_target_pairs={{0,384},{1,385},{2,386},{3,387},{4,388},{5,389},{6,390},{7,391},{8... | collective-permute-start | bytes 36872 | tf_op jit(solution)/shard_map/ppermute | solution.py:57
  78.7 23.7 %copy-start.11 = (bf16[1,6,2,32,256]{4,3,2,1,0:T(8,128)(2,1)S(1)}, bf16[1,6,2,32,256]{4,3,2,1,0:T(8,128)(2,1)}, u32[]{:S(2)}) copy-start(bf16[1,6,2,32,256]{4,3,2,1,0:T(8,128)(2,1)} %copy-done.10) | copy-start | bytes 589828
  78.7 37.8 %copy-start.19 = (bf16[3,32,32]{2,1,0:T(8,128)(2,1)S(1)}, bf16[3,32,32]{2,1,0:T(8,128)(2,1)}, u32[]{:S(2)}) copy-start(bf16[3,32,32]{2,1,0:T(8,128)(2,1)} %param.17) | copy-start | bytes 18436
  83.8 6.0 %collective-permute-start.9 = (f32[3,32,32]{2,1,0:T(8,128)S(1)}, f32[3,32,32]{2,1,0:T(8,128)S(1)}, u32[]{:S(2)}, u32[]{:S(2)}) collective-permute-start(f32[3,32,32]{2,1,0:T(8,128)S(1)} %add.158), channel_id=1, source_target_pairs={{0,1},{1,0},{2,3},{3,2},{4,5},{5,4},{6,7},{7,6},{8,9},{9,8},{10,11... | collective-permute-start | bytes 36872 | tf_op jit(solution)/shard_map/ppermute | solution.py:57
  89.8 7.4 %collective-permute-start.10 = (f32[3,32,32]{2,1,0:T(8,128)S(1)}, f32[3,32,32]{2,1,0:T(8,128)S(1)}, u32[]{:S(2)}, u32[]{:S(2)}) collective-permute-start(f32[3,32,32]{2,1,0:T(8,128)S(1)} %add.159), channel_id=1, source_target_pairs={{0,2},{1,3},{2,0},{3,1},{4,6},{5,7},{6,4},{7,5},{8,10},{9,11},{10,... | collective-permute-start | bytes 36872 | tf_op jit(solution)/shard_map/ppermute | solution.py:57
  97.2 10.5 %collective-permute-start.11 = (f32[3,32,32]{2,1,0:T(8,128)S(1)}, f32[3,32,32]{2,1,0:T(8,128)S(1)}, u32[]{:S(2)}, u32[]{:S(2)}) collective-permute-start(f32[3,32,32]{2,1,0:T(8,128)S(1)} %add.160), channel_id=1, source_target_pairs={{0,4},{1,5},{2,6},{3,7},{4,0},{5,1},{6,2},{7,3},{8,12},{9,13},{10,... | collective-permute-start | bytes 36872 | tf_op jit(solution)/shard_map/ppermute | solution.py:57
  107.6 11.6 %collective-permute-start.12 = (f32[3,32,32]{2,1,0:T(8,128)S(1)}, f32[3,32,32]{2,1,0:T(8,128)S(1)}, u32[]{:S(2)}, u32[]{:S(2)}) collective-permute-start(f32[3,32,32]{2,1,0:T(8,128)S(1)} %add.161), channel_id=1, source_target_pairs={{0,12},{1,13},{2,14},{3,15},{4,8},{5,9},{6,10},{7,11},{8,4},{9,5},... | collective-permute-start | bytes 36872 | tf_op jit(solution)/shard_map/ppermute | solution.py:57
  (11 other events, 13.5 us)

commit v10 on v8

--- a/solution.py
+++ b/solution.py
@@ -3,6 +3,8 @@
 import jax
 import jax.numpy as jnp
 from jax import lax
+from jax.experimental import pallas as pl
+from jax.experimental.pallas import tpu as pltpu
 from jax.sharding import PartitionSpec as P
 
 REACH = 2
@@ -65,6 +67,32 @@
     return x
 
 
+def window_kernel(flags_ref, cot_ref, f_ref, tiles_ref, win_ref):
+    nb = tiles_ref.shape[0]
+    bs = tiles_ref.shape[2]
+    win_ref[...] = jnp.zeros(win_ref.shape, win_ref.dtype)
+    f = f_ref[...]
+    for r in range(nb):
+        rows = [
+            jnp.dot(f, cot_ref[m, :, r * bs : (r + 1) * bs], preferred_element_type=jnp.float32)
+            for m in range(cot_ref.shape[0])
+        ]
+        g = jnp.concatenate(rows, axis=0).astype(jnp.bfloat16)
+        win_ref[r + 2] += jnp.dot(g, tiles_ref[r, 0], preferred_element_type=jnp.float32)
+        win_ref[r + flags_ref[r, 0]] += jnp.dot(g, tiles_ref[r, 1], preferred_element_type=jnp.float32)
+        win_ref[r + 4 - flags_ref[r, 1]] += jnp.dot(g, tiles_ref[r, 2], preferred_element_type=jnp.float32)
+
+def first_window(flags, cot, f2, tiles):
+    nb, bs = tiles.shape[0], tiles.shape[2]
+    rows = cot.shape[0] * f2.shape[0]
+    return pl.pallas_call(
+        window_kernel,
+        out_shape=jax.ShapeDtypeStruct((nb + 4, rows, bs), jnp.float32),
+        in_specs=[pl.BlockSpec(memory_space=pltpu.SMEM)] + [pl.BlockSpec(memory_space=pltpu.VMEM)] * 3,
+        out_specs=pl.BlockSpec(memory_space=pltpu.VMEM),
+    )(flags, cot, f2, tiles)
+
+
 def per_device(maps, cotangent, tiles, columns, filters):
     map_count, chan_count, pix_count = maps.shape
     block_count = tiles.shape[0]
@@ -118,7 +146,8 @@
     grads = grads.reshape(3, nb, row_count, block_size)
     grad_two = grads[2].astype(jnp.bfloat16)
 
-    win1 = adjoint_window(grad_two)
+    flags = jnp.stack([back_one[:, 0, 0], next_one[:, 0, 0]], axis=1).astype(jnp.int32)
+    win1 = first_window(flags, cotangent, filters[2], tiles)
     x0f = x_zero.astype(jnp.float32)
     send_left = jnp.stack([x0f[0:2], win1[0:2]])
     send_right = jnp.stack([x0f[nb - 2 : nb], win1[nb + 2 : nb + 4]])

time: 111 us -> 109 us (0.982)
  Pallas kernels: 0 us -> 3.73 us
  matrix products: 5.54 us -> 3.21 us
  other arithmetic: 4.08 us -> 2.49 us
  local copies, waits for them, and re-layouts: 8.04 us -> 6.85 us
    pallas_call x0 -> x1, Pallas kernels: none -> 3.73 us  [first_window(): pl.pallas_call(window_kernel, out_shape=jax.ShapeDtypeStruct((nb + 4, row...]
    dot_general x2 -> x1, matrix products: 2.1 us -> 0.54 us  [adjoint_window(): jnp.einsum('rni,rjiq->rjnq', grads, tiles, preferred_element_type=jnp.flo...]
    select_n x2 -> x1, other arithmetic: 1.66 us -> 0.22 us  [adjoint_window(): jnp.where(back_one, c1, zero)]
    unnamed x18 -> x12, local copies, waits for them, and re-layouts: 1.59 us -> 0.21 us
    squeeze x0 -> x1, local copies, waits for them, and re-layouts: none -> 1.29 us  [per_device(): win1 = first_window(flags, cotangent, filters[2], tiles)]
where the time goes in v10:
time: 109 us; the launch traced here: 108 us
  starting transfers between devices  55.9 us (51%)
  waiting for transfers between devices  34.6 us (32%)
  local copies, waits for them, and re-layouts  6.85 us (6%)
  Pallas kernels  3.73 us (3%)
  matrix products  3.21 us (3%)
  other arithmetic  2.49 us (2%)
    ppermute x9, starting transfers between devices, butterfly_sum(): x = x + lax.ppermute(x, axes, pairs)  39.1 us
    ppermute x9, waiting for transfers between devices, butterfly_sum(): x = x + lax.ppermute(x, axes, pairs)  27.7 us
    ppermute x2, starting transfers between devices, exchange(): from_left = lax.ppermute(edge_right, 'patch', to_right)  8.84 us
    ppermute x2, starting transfers between devices, exchange(): from_right = lax.ppermute(edge_left, 'patch', to_left)  7.97 us
    ppermute x2, waiting for transfers between devices, exchange(): from_right = lax.ppermute(edge_left, 'patch', to_left)  4.37 us
    pallas_call x1, Pallas kernels, first_window(): pl.pallas_call(window_kernel, out_shape=jax.ShapeDtypeStruct((nb + 4, row...  3.73 us
    ppermute x2, waiting for transfers between devices, exchange(): from_left = lax.ppermute(edge_right, 'patch', to_right)  2.5 us
  transfers between devices with their start and end apart: 13, of which 12 were waited for; matrix products, arithmetic and copies ran while one was open for 3% of the time, Pallas kernels for 0%

profile of v10, /device:TPU:24, one launch (start us, length us, event | category | flops | bytes accessed | tf_op | source)
XLA Modules:
  0.0 107.8 jit_solution(12059840853206955355)
XLA Ops:
  4.8 3.7 %shard_map.76 = f32[10,64,256]{2,1,0:T(8,128)} custom-call(s32[6,2]{1,0:T(8,128)} %add_convert_fusion.flags_ref, bf16[2,32,1536]{2,1,0:T(8,128)(2,1)} %cot_ref.1, bf16[32,32]{1,0:T(8,128)(2,1)} %slice_bitcast_fusion.17.f_ref, bf16[6,3,256,256]{3,2,1,0:T(8,128)(2,1)} %tiles_ref.1), custom_call_target="tpu_custom_call" | custom-call | tf_op jit(solution)/shard_map/pallas_call | solution.py:88
  9.6 1.9 %collective-permute-start = (f32[2,2,64,256]{3,2,1,0:T(8,128)S(1)}, f32[2,2,64,256]{3,2,1,0:T(8,128)S(1)}, u32[]{:S(2)}, u32[]{:S(2)}) collective-permute-start(f32[2,2,64,256]{3,2,1,0:T(8,128)S(1)} %pad_maximum_fusion.6), channel_id=1, source_target_pairs={{0,32},{32,64},{64,96},{96,128},{128,160},{160,192},{192,224},{224... | collective-permute-start | bytes 786440 | tf_op jit(solution)/shard_map/ppermute | solution.py:114
  11.5 6.0 %collective-permute-start.1 = (f32[2,2,64,256]{3,2,1,0:T(8,128)S(1)}, f32[2,2,64,256]{3,2,1,0:T(8,128)S(1)}, u32[]{:S(2)}, u32[]{:S(2)}) collective-permute-start(f32[2,2,64,256]{3,2,1,0:T(8,128)S(1)} %pad_maximum_fusion.5), channel_id=1, source_target_pairs={{32,0},{64,32},{96,64},{128,96},{160,128},{192,160},{224,192},{256... | collective-permute-start | bytes 786440 | tf_op jit(solution)/shard_map/ppermute | solution.py:113
  18.4 1.3 %collective-permute-done = f32[2,2,64,256]{3,2,1,0:T(8,128)S(1)} collective-permute-done((f32[2,2,64,256]{3,2,1,0:T(8,128)S(1)}, f32[2,2,64,256]{3,2,1,0:T(8,128)S(1)}, u32[]{:S(2)}, u32[]{:S(2)}) %collective-permute-start) | collective-permute-done | bytes 262176 | tf_op jit(solution)/shard_map/ppermute | solution.py:114
  19.7 1.7 %collective-permute-done.1 = f32[2,2,64,256]{3,2,1,0:T(8,128)S(1)} collective-permute-done((f32[2,2,64,256]{3,2,1,0:T(8,128)S(1)}, f32[2,2,64,256]{3,2,1,0:T(8,128)S(1)}, u32[]{:S(2)}, u32[]{:S(2)}) %collective-permute-start.1) | collective-permute-done | bytes 262176 | tf_op jit(solution)/shard_map/ppermute | solution.py:113
  23.5 6.9 %collective-permute-start.2 = (f32[2,2,64,256]{3,2,1,0:T(8,128)S(1)}, f32[2,2,64,256]{3,2,1,0:T(8,128)S(1)}, u32[]{:S(2)}, u32[]{:S(2)}) collective-permute-start(f32[2,2,64,256]{3,2,1,0:T(8,128)S(1)} %pad_maximum_fusion.8), channel_id=1, source_target_pairs={{0,32},{32,64},{64,96},{96,128},{128,160},{160,192},{192,224},{224... | collective-permute-start | bytes 786440 | tf_op jit(solution)/shard_map/ppermute | solution.py:114
  30.4 1.9 %collective-permute-start.3 = (f32[2,2,64,256]{3,2,1,0:T(8,128)S(1)}, f32[2,2,64,256]{3,2,1,0:T(8,128)S(1)}, u32[]{:S(2)}, u32[]{:S(2)}) collective-permute-start(f32[2,2,64,256]{3,2,1,0:T(8,128)S(1)} %pad_maximum_fusion.7), channel_id=1, source_target_pairs={{32,0},{64,32},{96,64},{128,96},{160,128},{192,160},{224,192},{256... | collective-permute-start | bytes 786440 | tf_op jit(solution)/shard_map/ppermute | solution.py:113
  33.7 2.6 %collective-permute-done.3 = f32[2,2,64,256]{3,2,1,0:T(8,128)S(1)} collective-permute-done((f32[2,2,64,256]{3,2,1,0:T(8,128)S(1)}, f32[2,2,64,256]{3,2,1,0:T(8,128)S(1)}, u32[]{:S(2)}, u32[]{:S(2)}) %collective-permute-start.3) | collective-permute-done | bytes 262176 | tf_op jit(solution)/shard_map/ppermute | solution.py:113
  37.6 7.9 %collective-permute-start.4 = (f32[3,32,32]{2,1,0:T(8,128)S(1)}, f32[3,32,32]{2,1,0:T(8,128)S(1)}, u32[]{:S(2)}, u32[]{:S(2)}) collective-permute-start(f32[3,32,32]{2,1,0:T(8,128)S(1)} %pad_maximum_fusion.9), channel_id=1, source_target_pairs={{0,32},{1,33},{2,34},{3,35},{4,36},{5,37},{6,38},{7,39},{8,40},{9,... | collective-permute-start | bytes 36872 | tf_op jit(solution)/shard_map/ppermute | solution.py:59
  46.4 1.9 %collective-permute-start.5 = (f32[3,32,32]{2,1,0:T(8,128)S(1)}, f32[3,32,32]{2,1,0:T(8,128)S(1)}, u32[]{:S(2)}, u32[]{:S(2)}) collective-permute-start(f32[3,32,32]{2,1,0:T(8,128)S(1)} %fusion.89), channel_id=1, source_target_pairs={{0,16},{1,17},{2,18},{3,19},{4,20},{5,21},{6,22},{7,23},{8,24},{9,... | collective-permute-start | bytes 36872 | tf_op jit(solution)/shard_map/ppermute | solution.py:59
  48.3 4.1 %collective-permute-done.5 = f32[3,32,32]{2,1,0:T(8,128)S(1)} collective-permute-done((f32[3,32,32]{2,1,0:T(8,128)S(1)}, f32[3,32,32]{2,1,0:T(8,128)S(1)}, u32[]{:S(2)}, u32[]{:S(2)}) %collective-permute-start.5) | collective-permute-done | bytes 12320 | tf_op jit(solution)/shard_map/ppermute | solution.py:59
  52.4 5.7 %collective-permute-start.6 = (f32[3,32,32]{2,1,0:T(8,128)S(1)}, f32[3,32,32]{2,1,0:T(8,128)S(1)}, u32[]{:S(2)}, u32[]{:S(2)}) collective-permute-start(f32[3,32,32]{2,1,0:T(8,128)S(1)} %add.151), channel_id=1, source_target_pairs={{0,80},{1,81},{2,82},{3,83},{4,84},{5,85},{6,86},{7,87},{8,88},{9,... | collective-permute-start | bytes 36872 | tf_op jit(solution)/shard_map/ppermute | solution.py:59
  58.1 2.1 %collective-permute-done.6 = f32[3,32,32]{2,1,0:T(8,128)S(1)} collective-permute-done((f32[3,32,32]{2,1,0:T(8,128)S(1)}, f32[3,32,32]{2,1,0:T(8,128)S(1)}, u32[]{:S(2)}, u32[]{:S(2)}) %collective-permute-start.6) | collective-permute-done | bytes 12320 | tf_op jit(solution)/shard_map/ppermute | solution.py:59
  60.1 1.9 %collective-permute-start.7 = (f32[3,32,32]{2,1,0:T(8,128)S(1)}, f32[3,32,32]{2,1,0:T(8,128)S(1)}, u32[]{:S(2)}, u32[]{:S(2)}) collective-permute-start(f32[3,32,32]{2,1,0:T(8,128)S(1)} %add.152), channel_id=1, source_target_pairs={{0,128},{1,129},{2,130},{3,131},{4,132},{5,133},{6,134},{7,135},{8... | collective-permute-start | bytes 36872 | tf_op jit(solution)/shard_map/ppermute | solution.py:59
  62.1 4.1 %collective-permute-done.7 = f32[3,32,32]{2,1,0:T(8,128)S(1)} collective-permute-done((f32[3,32,32]{2,1,0:T(8,128)S(1)}, f32[3,32,32]{2,1,0:T(8,128)S(1)}, u32[]{:S(2)}, u32[]{:S(2)}) %collective-permute-start.7) | collective-permute-done | bytes 12320 | tf_op jit(solution)/shard_map/ppermute | solution.py:59
  66.1 3.5 %collective-permute-start.8 = (f32[3,32,32]{2,1,0:T(8,128)S(1)}, f32[3,32,32]{2,1,0:T(8,128)S(1)}, u32[]{:S(2)}, u32[]{:S(2)}) collective-permute-start(f32[3,32,32]{2,1,0:T(8,128)S(1)} %add.153), channel_id=1, source_target_pairs={{0,384},{1,385},{2,386},{3,387},{4,388},{5,389},{6,390},{7,391},{8... | collective-permute-start | bytes 36872 | tf_op jit(solution)/shard_map/ppermute | solution.py:59
  69.8 3.5 %collective-permute-done.8 = f32[3,32,32]{2,1,0:T(8,128)S(1)} collective-permute-done((f32[3,32,32]{2,1,0:T(8,128)S(1)}, f32[3,32,32]{2,1,0:T(8,128)S(1)}, u32[]{:S(2)}, u32[]{:S(2)}) %collective-permute-start.8) | collective-permute-done | bytes 12320 | tf_op jit(solution)/shard_map/ppermute | solution.py:59
  73.3 1.9 %collective-permute-start.9 = (f32[3,32,32]{2,1,0:T(8,128)S(1)}, f32[3,32,32]{2,1,0:T(8,128)S(1)}, u32[]{:S(2)}, u32[]{:S(2)}) collective-permute-start(f32[3,32,32]{2,1,0:T(8,128)S(1)} %add.154), channel_id=1, source_target_pairs={{0,1},{1,0},{2,3},{3,2},{4,5},{5,4},{6,7},{7,6},{8,9},{9,8},{10,11... | collective-permute-start | bytes 36872 | tf_op jit(solution)/shard_map/ppermute | solution.py:59
  75.3 4.0 %collective-permute-done.9 = f32[3,32,32]{2,1,0:T(8,128)S(1)} collective-permute-done((f32[3,32,32]{2,1,0:T(8,128)S(1)}, f32[3,32,32]{2,1,0:T(8,128)S(1)}, u32[]{:S(2)}, u32[]{:S(2)}) %collective-permute-start.9) | collective-permute-done | bytes 12320 | tf_op jit(solution)/shard_map/ppermute | solution.py:59
  79.3 1.9 %collective-permute-start.10 = (f32[3,32,32]{2,1,0:T(8,128)S(1)}, f32[3,32,32]{2,1,0:T(8,128)S(1)}, u32[]{:S(2)}, u32[]{:S(2)}) collective-permute-start(f32[3,32,32]{2,1,0:T(8,128)S(1)} %add.155), channel_id=1, source_target_pairs={{0,2},{1,3},{2,0},{3,1},{4,6},{5,7},{6,4},{7,5},{8,10},{9,11},{10,... | collective-permute-start | bytes 36872 | tf_op jit(solution)/shard_map/ppermute | solution.py:59
  81.3 4.9 %collective-permute-done.10 = f32[3,32,32]{2,1,0:T(8,128)S(1)} collective-permute-done((f32[3,32,32]{2,1,0:T(8,128)S(1)}, f32[3,32,32]{2,1,0:T(8,128)S(1)}, u32[]{:S(2)}, u32[]{:S(2)}) %collective-permute-start.10) | collective-permute-done | bytes 12320 | tf_op jit(solution)/shard_map/ppermute | solution.py:59
  86.2 6.1 %collective-permute-start.11 = (f32[3,32,32]{2,1,0:T(8,128)S(1)}, f32[3,32,32]{2,1,0:T(8,128)S(1)}, u32[]{:S(2)}, u32[]{:S(2)}) collective-permute-start(f32[3,32,32]{2,1,0:T(8,128)S(1)} %add.156), channel_id=1, source_target_pairs={{0,4},{1,5},{2,6},{3,7},{4,0},{5,1},{6,2},{7,3},{8,12},{9,13},{10,... | collective-permute-start | bytes 36872 | tf_op jit(solution)/shard_map/ppermute | solution.py:59
  92.4 4.3 %collective-permute-done.11 = f32[3,32,32]{2,1,0:T(8,128)S(1)} collective-permute-done((f32[3,32,32]{2,1,0:T(8,128)S(1)}, f32[3,32,32]{2,1,0:T(8,128)S(1)}, u32[]{:S(2)}, u32[]{:S(2)}) %collective-permute-start.11) | collective-permute-done | bytes 12320 | tf_op jit(solution)/shard_map/ppermute | solution.py:59
  96.7 8.2 %collective-permute-start.12 = (f32[3,32,32]{2,1,0:T(8,128)S(1)}, f32[3,32,32]{2,1,0:T(8,128)S(1)}, u32[]{:S(2)}, u32[]{:S(2)}) collective-permute-start(f32[3,32,32]{2,1,0:T(8,128)S(1)} %add.157), channel_id=1, source_target_pairs={{0,12},{1,13},{2,14},{3,15},{4,8},{5,9},{6,10},{7,11},{8,4},{9,5},... | collective-permute-start | bytes 36872 | tf_op jit(solution)/shard_map/ppermute | solution.py:59
  (72 shorter events, 14.6 us)
Async XLA Ops:
  4.8 12.8 %copy-start.2 = (bf16[2,32,1536]{2,1,0:T(8,128)(2,1)S(1)}, bf16[2,32,1536]{2,1,0:T(8,128)(2,1)}, u32[]{:S(2)}) copy-start(bf16[2,32,1536]{2,1,0:T(8,128)(2,1)} %cot_ref.1) | copy-start | bytes 589828
  4.8 13.1 %copy-start.3 = (bf16[3,32,32]{2,1,0:T(8,128)(2,1)S(1)}, bf16[3,32,32]{2,1,0:T(8,128)(2,1)}, u32[]{:S(2)}) copy-start(bf16[3,32,32]{2,1,0:T(8,128)(2,1)} %param.17) | copy-start | bytes 18436
  9.6 8.8 %copy-start.4 = (s32[6,3]{0,1:T(4,128)S(1)}, s32[6,3]{0,1:T(4,128)}, u32[]{:S(2)}) copy-start(s32[6,3]{0,1:T(4,128)} %param.16) | copy-start | bytes 220
  9.6 10.1 %collective-permute-start = (f32[2,2,64,256]{3,2,1,0:T(8,128)S(1)}, f32[2,2,64,256]{3,2,1,0:T(8,128)S(1)}, u32[]{:S(2)}, u32[]{:S(2)}) collective-permute-start(f32[2,2,64,256]{3,2,1,0:T(8,128)S(1)} %pad_maximum_fusion.6), channel_id=1, source_target_pairs={{0,32},{32,64},{64,96},{96,128},{128,160},{160,192},{192,224},{224... | collective-permute-start | bytes 786440 | tf_op jit(solution)/shard_map/ppermute | solution.py:114
  11.5 9.9 %collective-permute-start.1 = (f32[2,2,64,256]{3,2,1,0:T(8,128)S(1)}, f32[2,2,64,256]{3,2,1,0:T(8,128)S(1)}, u32[]{:S(2)}, u32[]{:S(2)}) collective-permute-start(f32[2,2,64,256]{3,2,1,0:T(8,128)S(1)} %pad_maximum_fusion.5), channel_id=1, source_target_pairs={{32,0},{64,32},{96,64},{128,96},{160,128},{192,160},{224,192},{256... | collective-permute-start | bytes 786440 | tf_op jit(solution)/shard_map/ppermute | solution.py:113
  17.8 1.9 %copy-start.1 = (f32[10,64,256]{2,1,0:T(8,128)S(1)}, f32[10,64,256]{2,1,0:T(8,128)}, u32[]{:S(2)}) copy-start(f32[10,64,256]{2,1,0:T(8,128)} %shard_map.76) | copy-start | bytes 1966084
  17.8 1.9 %slice-start = ((f32[10,64,256]{2,1,0:T(8,128)}), f32[6,64,256]{2,1,0:T(8,128)S(1)}, s32[]{:S(2)}) async-start(f32[10,64,256]{2,1,0:T(8,128)} %shard_map.76), calls=%async_computation | async-start | bytes 786432 | tf_op jit(solution)/shard_map/slice | solution.py:157
  18.2 3.3 %copy-start = (bf16[6,3,256,256]{3,2,1,0:T(8,128)(2,1)S(1)}, bf16[6,3,256,256]{3,2,1,0:T(8,128)(2,1)}, u32[]{:S(2)}) copy-start(bf16[6,3,256,256]{3,2,1,0:T(8,128)(2,1)} %tiles_ref.1) | copy-start | bytes 7077892
  23.5 10.3 %collective-permute-start.2 = (f32[2,2,64,256]{3,2,1,0:T(8,128)S(1)}, f32[2,2,64,256]{3,2,1,0:T(8,128)S(1)}, u32[]{:S(2)}, u32[]{:S(2)}) collective-permute-start(f32[2,2,64,256]{3,2,1,0:T(8,128)S(1)} %pad_maximum_fusion.8), channel_id=1, source_target_pairs={{0,32},{32,64},{64,96},{96,128},{128,160},{160,192},{192,224},{224... | collective-permute-start | bytes 786440 | tf_op jit(solution)/shard_map/ppermute | solution.py:114
  30.4 6.0 %collective-permute-start.3 = (f32[2,2,64,256]{3,2,1,0:T(8,128)S(1)}, f32[2,2,64,256]{3,2,1,0:T(8,128)S(1)}, u32[]{:S(2)}, u32[]{:S(2)}) collective-permute-start(f32[2,2,64,256]{3,2,1,0:T(8,128)S(1)} %pad_maximum_fusion.7), channel_id=1, source_target_pairs={{32,0},{64,32},{96,64},{128,96},{160,128},{192,160},{224,192},{256... | collective-permute-start | bytes 786440 | tf_op jit(solution)/shard_map/ppermute | solution.py:113
  37.6 8.8 %collective-permute-start.4 = (f32[3,32,32]{2,1,0:T(8,128)S(1)}, f32[3,32,32]{2,1,0:T(8,128)S(1)}, u32[]{:S(2)}, u32[]{:S(2)}) collective-permute-start(f32[3,32,32]{2,1,0:T(8,128)S(1)} %pad_maximum_fusion.9), channel_id=1, source_target_pairs={{0,32},{1,33},{2,34},{3,35},{4,36},{5,37},{6,38},{7,39},{8,40},{9,... | collective-permute-start | bytes 36872 | tf_op jit(solution)/shard_map/ppermute | solution.py:59
  46.4 6.0 %collective-permute-start.5 = (f32[3,32,32]{2,1,0:T(8,128)S(1)}, f32[3,32,32]{2,1,0:T(8,128)S(1)}, u32[]{:S(2)}, u32[]{:S(2)}) collective-permute-start(f32[3,32,32]{2,1,0:T(8,128)S(1)} %fusion.89), channel_id=1, source_target_pairs={{0,16},{1,17},{2,18},{3,19},{4,20},{5,21},{6,22},{7,23},{8,24},{9,... | collective-permute-start | bytes 36872 | tf_op jit(solution)/shard_map/ppermute | solution.py:59
  52.4 7.8 %collective-permute-start.6 = (f32[3,32,32]{2,1,0:T(8,128)S(1)}, f32[3,32,32]{2,1,0:T(8,128)S(1)}, u32[]{:S(2)}, u32[]{:S(2)}) collective-permute-start(f32[3,32,32]{2,1,0:T(8,128)S(1)} %add.151), channel_id=1, source_target_pairs={{0,80},{1,81},{2,82},{3,83},{4,84},{5,85},{6,86},{7,87},{8,88},{9,... | collective-permute-start | bytes 36872 | tf_op jit(solution)/shard_map/ppermute | solution.py:59
  60.1 6.0 %collective-permute-start.7 = (f32[3,32,32]{2,1,0:T(8,128)S(1)}, f32[3,32,32]{2,1,0:T(8,128)S(1)}, u32[]{:S(2)}, u32[]{:S(2)}) collective-permute-start(f32[3,32,32]{2,1,0:T(8,128)S(1)} %add.152), channel_id=1, source_target_pairs={{0,128},{1,129},{2,130},{3,131},{4,132},{5,133},{6,134},{7,135},{8... | collective-permute-start | bytes 36872 | tf_op jit(solution)/shard_map/ppermute | solution.py:59
  66.1 7.2 %collective-permute-start.8 = (f32[3,32,32]{2,1,0:T(8,128)S(1)}, f32[3,32,32]{2,1,0:T(8,128)S(1)}, u32[]{:S(2)}, u32[]{:S(2)}) collective-permute-start(f32[3,32,32]{2,1,0:T(8,128)S(1)} %add.153), channel_id=1, source_target_pairs={{0,384},{1,385},{2,386},{3,387},{4,388},{5,389},{6,390},{7,391},{8... | collective-permute-start | bytes 36872 | tf_op jit(solution)/shard_map/ppermute | solution.py:59
  73.3 6.0 %collective-permute-start.9 = (f32[3,32,32]{2,1,0:T(8,128)S(1)}, f32[3,32,32]{2,1,0:T(8,128)S(1)}, u32[]{:S(2)}, u32[]{:S(2)}) collective-permute-start(f32[3,32,32]{2,1,0:T(8,128)S(1)} %add.154), channel_id=1, source_target_pairs={{0,1},{1,0},{2,3},{3,2},{4,5},{5,4},{6,7},{7,6},{8,9},{9,8},{10,11... | collective-permute-start | bytes 36872 | tf_op jit(solution)/shard_map/ppermute | solution.py:59
  79.3 6.9 %collective-permute-start.10 = (f32[3,32,32]{2,1,0:T(8,128)S(1)}, f32[3,32,32]{2,1,0:T(8,128)S(1)}, u32[]{:S(2)}, u32[]{:S(2)}) collective-permute-start(f32[3,32,32]{2,1,0:T(8,128)S(1)} %add.155), channel_id=1, source_target_pairs={{0,2},{1,3},{2,0},{3,1},{4,6},{5,7},{6,4},{7,5},{8,10},{9,11},{10,... | collective-permute-start | bytes 36872 | tf_op jit(solution)/shard_map/ppermute | solution.py:59
  86.2 10.4 %collective-permute-start.11 = (f32[3,32,32]{2,1,0:T(8,128)S(1)}, f32[3,32,32]{2,1,0:T(8,128)S(1)}, u32[]{:S(2)}, u32[]{:S(2)}) collective-permute-start(f32[3,32,32]{2,1,0:T(8,128)S(1)} %add.156), channel_id=1, source_target_pairs={{0,4},{1,5},{2,6},{3,7},{4,0},{5,1},{6,2},{7,3},{8,12},{9,13},{10,... | collective-permute-start | bytes 36872 | tf_op jit(solution)/shard_map/ppermute | solution.py:59
  96.7 10.5 %collective-permute-start.12 = (f32[3,32,32]{2,1,0:T(8,128)S(1)}, f32[3,32,32]{2,1,0:T(8,128)S(1)}, u32[]{:S(2)}, u32[]{:S(2)}) collective-permute-start(f32[3,32,32]{2,1,0:T(8,128)S(1)} %add.157), channel_id=1, source_target_pairs={{0,12},{1,13},{2,14},{3,15},{4,8},{5,9},{6,10},{7,11},{8,4},{9,5},... | collective-permute-start | bytes 36872 | tf_op jit(solution)/shard_map/ppermute | solution.py:59

commit v11 on v10

--- a/solution.py
+++ b/solution.py
@@ -67,30 +67,45 @@
     return x
 
 
-def window_kernel(flags_ref, cot_ref, f_ref, tiles_ref, win_ref):
+def window_kernel(flags_ref, cot_ref, maps_ref, f_ref, tiles_ref, win_ref, left_ref, right_ref):
     nb = tiles_ref.shape[0]
     bs = tiles_ref.shape[2]
+    maps_per = cot_ref.shape[0]
     win_ref[...] = jnp.zeros(win_ref.shape, win_ref.dtype)
-    f = f_ref[...]
+    f = f_ref[2]
     for r in range(nb):
         rows = [
             jnp.dot(f, cot_ref[m, :, r * bs : (r + 1) * bs], preferred_element_type=jnp.float32)
-            for m in range(cot_ref.shape[0])
+            for m in range(maps_per)
         ]
         g = jnp.concatenate(rows, axis=0).astype(jnp.bfloat16)
         win_ref[r + 2] += jnp.dot(g, tiles_ref[r, 0], preferred_element_type=jnp.float32)
         win_ref[r + flags_ref[r, 0]] += jnp.dot(g, tiles_ref[r, 1], preferred_element_type=jnp.float32)
         win_ref[r + 4 - flags_ref[r, 1]] += jnp.dot(g, tiles_ref[r, 2], preferred_element_type=jnp.float32)
 
-def first_window(flags, cot, f2, tiles):
+    def map_block(r):
+        return jnp.concatenate(
+            [maps_ref[m, :, r * bs : (r + 1) * bs] for m in range(maps_per)], axis=0
+        ).astype(jnp.float32)
+
+    for i in range(2):
+        left_ref[0, i] = map_block(i)
+        left_ref[1, i] = win_ref[i]
+        right_ref[0, i] = map_block(nb - 2 + i)
+        right_ref[1, i] = win_ref[nb + 2 + i]
+
+
+def first_window(flags, cot, maps, filters, tiles):
     nb, bs = tiles.shape[0], tiles.shape[2]
-    rows = cot.shape[0] * f2.shape[0]
+    rows = cot.shape[0] * cot.shape[1]
+    edge = jax.ShapeDtypeStruct((2, 2, rows, bs), jnp.float32)
+    vmem = pl.BlockSpec(memory_space=pltpu.VMEM)
     return pl.pallas_call(
         window_kernel,
-        out_shape=jax.ShapeDtypeStruct((nb + 4, rows, bs), jnp.float32),
-        in_specs=[pl.BlockSpec(memory_space=pltpu.SMEM)] + [pl.BlockSpec(memory_space=pltpu.VMEM)] * 3,
-        out_specs=pl.BlockSpec(memory_space=pltpu.VMEM),
-    )(flags, cot, f2, tiles)
+        out_shape=(jax.ShapeDtypeStruct((nb + 4, rows, bs), jnp.float32), edge, edge),
+        in_specs=[pl.BlockSpec(memory_space=pltpu.SMEM)] + [vmem] * 4,
+        out_specs=(vmem, vmem, vmem),
+    )(flags, cot, maps, filters, tiles)
 
 
 def per_device(maps, cotangent, tiles, columns, filters):
@@ -147,10 +162,8 @@
     grad_two = grads[2].astype(jnp.bfloat16)
 
     flags = jnp.stack([back_one[:, 0, 0], next_one[:, 0, 0]], axis=1).astype(jnp.int32)
-    win1 = first_window(flags, cotangent, filters[2], tiles)
+    win1, send_left, send_right = first_window(flags, cotangent, maps, filters, tiles)
     x0f = x_zero.astype(jnp.float32)
-    send_left = jnp.stack([x0f[0:2], win1[0:2]])
-    send_right = jnp.stack([x0f[nb - 2 : nb], win1[nb + 2 : nb + 4]])
     got_left, got_right = exchange(send_left, send_right)
     ext0 = jnp.concatenate([got_left[0], x0f, got_right[0]], axis=0)
     x_one = forward_local(ext0).astype(jnp.bfloat16)

time: 109 us -> 113 us (1.037)
  the two profiles are of different devices: /device:TPU:24 before, /device:TPU:2 now
where the time goes in v11:
time: 113 us
  starting transfers between devices  51.8 us (46%)
  waiting for transfers between devices  40.4 us (36%)
  local copies, waits for them, and re-layouts  7.98 us (7%)
  other arithmetic  4.29 us (4%)
  Pallas kernels  4 us (4%)
  matrix products  3.2 us (3%)
    ppermute x9, starting transfers between devices, butterfly_sum(): x = x + lax.ppermute(x, axes, pairs)  33.5 us
    ppermute x9, waiting for transfers between devices, butterfly_sum(): x = x + lax.ppermute(x, axes, pairs)  31.3 us
    ppermute x2, starting transfers between devices, exchange(): from_right = lax.ppermute(edge_left, 'patch', to_left)  14.3 us
    ppermute x2, waiting for transfers between devices, exchange(): from_left = lax.ppermute(edge_right, 'patch', to_right)  5.37 us
    pallas_call x1, Pallas kernels, first_window(): pl.pallas_call(window_kernel, out_shape=(jax.ShapeDtypeStruct((nb + 4, ro...  4 us
    ppermute x2, starting transfers between devices, exchange(): from_left = lax.ppermute(edge_right, 'patch', to_right)  3.96 us
    ppermute x2, waiting for transfers between devices, exchange(): from_right = lax.ppermute(edge_left, 'patch', to_left)  3.73 us
  transfers between devices with their start and end apart: 13, of which 11 were waited for; matrix products, arithmetic and copies ran while one was open for 6% of the time, Pallas kernels for 0%

profile of v11, /device:TPU:2, one launch (start us, length us, event | category | flops | bytes accessed | tf_op | source)
XLA Modules:
  0.0 112.8 jit_solution(579742048535694341)
XLA Ops:
  2.3 4.0 %shard_map.76 = (f32[10,64,256]{2,1,0:T(8,128)}, f32[2,2,64,256]{3,2,1,0:T(8,128)}, f32[2,2,64,256]{3,2,1,0:T(8,128)}) custom-call(s32[6,2]{1,0:T(8,128)} %add_convert_fusion.flags_ref, bf16[2,32,1536]{2,1,0:T(8,128)(2,1)} %cot_ref.1, bf16[2,32,1536]{2,1,0:T(8,128)(2,1)} %maps_ref.1, bf16[3,32,32]{2,1,0:T(8,128)(2,1)} %f_ref.1, ...), custom_call_target="tpu_custom_call" | custom-call | tf_op jit(solution)/shard_map/pallas_call | solution.py:103
  6.3 2.0 %collective-permute-start = (f32[2,2,64,256]{3,2,1,0:T(8,128)}, f32[2,2,64,256]{3,2,1,0:T(8,128)}, u32[]{:S(2)}, u32[]{:S(2)}) collective-permute-start(f32[2,2,64,256]{3,2,1,0:T(8,128)} %get-tuple-element.60), channel_id=1, source_target_pairs={{0,32},{32,64},{64,96},{96,128},{128,160},{160,192},{192,224},{224... | collective-permute-start | bytes 786440 | tf_op jit(solution)/shard_map/ppermute | solution.py:129
  8.3 7.3 %collective-permute-start.1 = (f32[2,2,64,256]{3,2,1,0:T(8,128)}, f32[2,2,64,256]{3,2,1,0:T(8,128)}, u32[]{:S(2)}, u32[]{:S(2)}) collective-permute-start(f32[2,2,64,256]{3,2,1,0:T(8,128)} %get-tuple-element.61), channel_id=1, source_target_pairs={{32,0},{64,32},{96,64},{128,96},{160,128},{192,160},{224,192},{256... | collective-permute-start | bytes 786440 | tf_op jit(solution)/shard_map/ppermute | solution.py:128
  16.7 1.3 %reshape.196 = bf16[64,6,256]{2,1,0:T(8,128)(2,1)S(1)} reshape(bf16[2,32,1536]{2,1,0:T(8,128)(2,1)} %maps_ref.1) | data formatting | bytes 393216 | tf_op jit(solution)/shard_map/reshape | solution.py:133
  24.9 7.1 %collective-permute-start.3 = (f32[2,2,64,256]{3,2,1,0:T(8,128)S(1)}, f32[2,2,64,256]{3,2,1,0:T(8,128)S(1)}, u32[]{:S(2)}, u32[]{:S(2)}) collective-permute-start(f32[2,2,64,256]{3,2,1,0:T(8,128)S(1)} %pad_maximum_fusion.5), channel_id=1, source_target_pairs={{32,0},{64,32},{96,64},{128,96},{160,128},{192,160},{224,192},{256... | collective-permute-start | bytes 786440 | tf_op jit(solution)/shard_map/ppermute | solution.py:128
  32.0 1.9 %collective-permute-start.2 = (f32[2,2,64,256]{3,2,1,0:T(8,128)S(1)}, f32[2,2,64,256]{3,2,1,0:T(8,128)S(1)}, u32[]{:S(2)}, u32[]{:S(2)}) collective-permute-start(f32[2,2,64,256]{3,2,1,0:T(8,128)S(1)} %pad_maximum_fusion.6), channel_id=1, source_target_pairs={{0,32},{32,64},{64,96},{96,128},{128,160},{160,192},{192,224},{224... | collective-permute-start | bytes 786440 | tf_op jit(solution)/shard_map/ppermute | solution.py:129
  34.2 3.7 %collective-permute-done.3 = f32[2,2,64,256]{3,2,1,0:T(8,128)S(1)} collective-permute-done((f32[2,2,64,256]{3,2,1,0:T(8,128)S(1)}, f32[2,2,64,256]{3,2,1,0:T(8,128)S(1)}, u32[]{:S(2)}, u32[]{:S(2)}) %collective-permute-start.3) | collective-permute-done | bytes 262176 | tf_op jit(solution)/shard_map/ppermute | solution.py:128
  37.9 5.4 %collective-permute-done.2 = f32[2,2,64,256]{3,2,1,0:T(8,128)S(1)} collective-permute-done((f32[2,2,64,256]{3,2,1,0:T(8,128)S(1)}, f32[2,2,64,256]{3,2,1,0:T(8,128)S(1)}, u32[]{:S(2)}, u32[]{:S(2)}) %collective-permute-start.2) | collective-permute-done | bytes 262176 | tf_op jit(solution)/shard_map/ppermute | solution.py:129
  44.5 1.9 %collective-permute-start.4 = (f32[3,32,32]{2,1,0:T(8,128)S(1)}, f32[3,32,32]{2,1,0:T(8,128)S(1)}, u32[]{:S(2)}, u32[]{:S(2)}) collective-permute-start(f32[3,32,32]{2,1,0:T(8,128)S(1)} %pad_maximum_fusion.7), channel_id=1, source_target_pairs={{0,32},{1,33},{2,34},{3,35},{4,36},{5,37},{6,38},{7,39},{8,40},{9,... | collective-permute-start | bytes 36872 | tf_op jit(solution)/shard_map/ppermute | solution.py:59
  47.6 7.8 %collective-permute-start.5 = (f32[3,32,32]{2,1,0:T(8,128)S(1)}, f32[3,32,32]{2,1,0:T(8,128)S(1)}, u32[]{:S(2)}, u32[]{:S(2)}) collective-permute-start(f32[3,32,32]{2,1,0:T(8,128)S(1)} %fusion.89), channel_id=1, source_target_pairs={{0,16},{1,17},{2,18},{3,19},{4,20},{5,21},{6,22},{7,23},{8,24},{9,... | collective-permute-start | bytes 36872 | tf_op jit(solution)/shard_map/ppermute | solution.py:59
  55.4 2.1 %collective-permute-done.5 = f32[3,32,32]{2,1,0:T(8,128)S(1)} collective-permute-done((f32[3,32,32]{2,1,0:T(8,128)S(1)}, f32[3,32,32]{2,1,0:T(8,128)S(1)}, u32[]{:S(2)}, u32[]{:S(2)}) %collective-permute-start.5) | collective-permute-done | bytes 12320 | tf_op jit(solution)/shard_map/ppermute | solution.py:59
  57.5 1.9 %collective-permute-start.6 = (f32[3,32,32]{2,1,0:T(8,128)S(1)}, f32[3,32,32]{2,1,0:T(8,128)S(1)}, u32[]{:S(2)}, u32[]{:S(2)}) collective-permute-start(f32[3,32,32]{2,1,0:T(8,128)S(1)} %add.151), channel_id=1, source_target_pairs={{0,80},{1,81},{2,82},{3,83},{4,84},{5,85},{6,86},{7,87},{8,88},{9,... | collective-permute-start | bytes 36872 | tf_op jit(solution)/shard_map/ppermute | solution.py:59
  59.4 4.1 %collective-permute-done.6 = f32[3,32,32]{2,1,0:T(8,128)S(1)} collective-permute-done((f32[3,32,32]{2,1,0:T(8,128)S(1)}, f32[3,32,32]{2,1,0:T(8,128)S(1)}, u32[]{:S(2)}, u32[]{:S(2)}) %collective-permute-start.6) | collective-permute-done | bytes 12320 | tf_op jit(solution)/shard_map/ppermute | solution.py:59
  63.5 1.9 %collective-permute-start.7 = (f32[3,32,32]{2,1,0:T(8,128)S(1)}, f32[3,32,32]{2,1,0:T(8,128)S(1)}, u32[]{:S(2)}, u32[]{:S(2)}) collective-permute-start(f32[3,32,32]{2,1,0:T(8,128)S(1)} %add.152), channel_id=1, source_target_pairs={{0,128},{1,129},{2,130},{3,131},{4,132},{5,133},{6,134},{7,135},{8... | collective-permute-start | bytes 36872 | tf_op jit(solution)/shard_map/ppermute | solution.py:59
  65.4 4.1 %collective-permute-done.7 = f32[3,32,32]{2,1,0:T(8,128)S(1)} collective-permute-done((f32[3,32,32]{2,1,0:T(8,128)S(1)}, f32[3,32,32]{2,1,0:T(8,128)S(1)}, u32[]{:S(2)}, u32[]{:S(2)}) %collective-permute-start.7) | collective-permute-done | bytes 12320 | tf_op jit(solution)/shard_map/ppermute | solution.py:59
  69.5 1.9 %collective-permute-start.8 = (f32[3,32,32]{2,1,0:T(8,128)S(1)}, f32[3,32,32]{2,1,0:T(8,128)S(1)}, u32[]{:S(2)}, u32[]{:S(2)}) collective-permute-start(f32[3,32,32]{2,1,0:T(8,128)S(1)} %add.153), channel_id=1, source_target_pairs={{0,384},{1,385},{2,386},{3,387},{4,388},{5,389},{6,390},{7,391},{8... | collective-permute-start | bytes 36872 | tf_op jit(solution)/shard_map/ppermute | solution.py:59
  71.6 5.1 %collective-permute-done.8 = f32[3,32,32]{2,1,0:T(8,128)S(1)} collective-permute-done((f32[3,32,32]{2,1,0:T(8,128)S(1)}, f32[3,32,32]{2,1,0:T(8,128)S(1)}, u32[]{:S(2)}, u32[]{:S(2)}) %collective-permute-start.8) | collective-permute-done | bytes 12320 | tf_op jit(solution)/shard_map/ppermute | solution.py:59
  76.7 1.9 %collective-permute-start.9 = (f32[3,32,32]{2,1,0:T(8,128)S(1)}, f32[3,32,32]{2,1,0:T(8,128)S(1)}, u32[]{:S(2)}, u32[]{:S(2)}) collective-permute-start(f32[3,32,32]{2,1,0:T(8,128)S(1)} %add.154), channel_id=1, source_target_pairs={{0,1},{1,0},{2,3},{3,2},{4,5},{5,4},{6,7},{7,6},{8,9},{9,8},{10,11... | collective-permute-start | bytes 36872 | tf_op jit(solution)/shard_map/ppermute | solution.py:59
  78.7 4.0 %collective-permute-done.9 = f32[3,32,32]{2,1,0:T(8,128)S(1)} collective-permute-done((f32[3,32,32]{2,1,0:T(8,128)S(1)}, f32[3,32,32]{2,1,0:T(8,128)S(1)}, u32[]{:S(2)}, u32[]{:S(2)}) %collective-permute-start.9) | collective-permute-done | bytes 12320 | tf_op jit(solution)/shard_map/ppermute | solution.py:59
  82.7 1.9 %collective-permute-start.10 = (f32[3,32,32]{2,1,0:T(8,128)S(1)}, f32[3,32,32]{2,1,0:T(8,128)S(1)}, u32[]{:S(2)}, u32[]{:S(2)}) collective-permute-start(f32[3,32,32]{2,1,0:T(8,128)S(1)} %add.155), channel_id=1, source_target_pairs={{0,2},{1,3},{2,0},{3,1},{4,6},{5,7},{6,4},{7,5},{8,10},{9,11},{10,... | collective-permute-start | bytes 36872 | tf_op jit(solution)/shard_map/ppermute | solution.py:59
  84.7 5.4 %collective-permute-done.10 = f32[3,32,32]{2,1,0:T(8,128)S(1)} collective-permute-done((f32[3,32,32]{2,1,0:T(8,128)S(1)}, f32[3,32,32]{2,1,0:T(8,128)S(1)}, u32[]{:S(2)}, u32[]{:S(2)}) %collective-permute-start.10) | collective-permute-done | bytes 12320 | tf_op jit(solution)/shard_map/ppermute | solution.py:59
  90.1 5.3 %collective-permute-start.11 = (f32[3,32,32]{2,1,0:T(8,128)S(1)}, f32[3,32,32]{2,1,0:T(8,128)S(1)}, u32[]{:S(2)}, u32[]{:S(2)}) collective-permute-start(f32[3,32,32]{2,1,0:T(8,128)S(1)} %add.156), channel_id=1, source_target_pairs={{0,4},{1,5},{2,6},{3,7},{4,0},{5,1},{6,2},{7,3},{8,12},{9,13},{10,... | collective-permute-start | bytes 36872 | tf_op jit(solution)/shard_map/ppermute | solution.py:59
  95.4 5.1 %collective-permute-done.11 = f32[3,32,32]{2,1,0:T(8,128)S(1)} collective-permute-done((f32[3,32,32]{2,1,0:T(8,128)S(1)}, f32[3,32,32]{2,1,0:T(8,128)S(1)}, u32[]{:S(2)}, u32[]{:S(2)}) %collective-permute-start.11) | collective-permute-done | bytes 12320 | tf_op jit(solution)/shard_map/ppermute | solution.py:59
  100.6 8.9 %collective-permute-start.12 = (f32[3,32,32]{2,1,0:T(8,128)S(1)}, f32[3,32,32]{2,1,0:T(8,128)S(1)}, u32[]{:S(2)}, u32[]{:S(2)}) collective-permute-start(f32[3,32,32]{2,1,0:T(8,128)S(1)} %add.157), channel_id=1, source_target_pairs={{0,12},{1,13},{2,14},{3,15},{4,8},{5,9},{6,10},{7,11},{8,4},{9,5},... | collective-permute-start | bytes 36872 | tf_op jit(solution)/shard_map/ppermute | solution.py:59
  (70 shorter events, 15.7 us)
Async XLA Ops:
  0.6 15.0 %copy-start.3 = (bf16[2,32,1536]{2,1,0:T(8,128)(2,1)S(1)}, bf16[2,32,1536]{2,1,0:T(8,128)(2,1)}, u32[]{:S(2)}) copy-start(bf16[2,32,1536]{2,1,0:T(8,128)(2,1)} %cot_ref.1) | copy-start | bytes 589828
  0.6 15.3 %copy-start.4 = (bf16[3,32,32]{2,1,0:T(8,128)(2,1)S(1)}, bf16[3,32,32]{2,1,0:T(8,128)(2,1)}, u32[]{:S(2)}) copy-start(bf16[3,32,32]{2,1,0:T(8,128)(2,1)} %f_ref.1) | copy-start | bytes 18436
  6.3 10.4 %copy-start.5 = (s32[6,3]{0,1:T(4,128)S(1)}, s32[6,3]{0,1:T(4,128)}, u32[]{:S(2)}) copy-start(s32[6,3]{0,1:T(4,128)} %param.16) | copy-start | bytes 220
  6.3 12.8 %collective-permute-start = (f32[2,2,64,256]{3,2,1,0:T(8,128)}, f32[2,2,64,256]{3,2,1,0:T(8,128)}, u32[]{:S(2)}, u32[]{:S(2)}) collective-permute-start(f32[2,2,64,256]{3,2,1,0:T(8,128)} %get-tuple-element.60), channel_id=1, source_target_pairs={{0,32},{32,64},{64,96},{96,128},{128,160},{160,192},{192,224},{224... | collective-permute-start | bytes 786440 | tf_op jit(solution)/shard_map/ppermute | solution.py:129
  8.3 11.8 %collective-permute-start.1 = (f32[2,2,64,256]{3,2,1,0:T(8,128)}, f32[2,2,64,256]{3,2,1,0:T(8,128)}, u32[]{:S(2)}, u32[]{:S(2)}) collective-permute-start(f32[2,2,64,256]{3,2,1,0:T(8,128)} %get-tuple-element.61), channel_id=1, source_target_pairs={{32,0},{64,32},{96,64},{128,96},{160,128},{192,160},{224,192},{256... | collective-permute-start | bytes 786440 | tf_op jit(solution)/shard_map/ppermute | solution.py:128
  15.9 0.7 copy-start.1
  16.7 4.5 %copy-start = (bf16[6,3,256,256]{3,2,1,0:T(8,128)(2,1)S(1)}, bf16[6,3,256,256]{3,2,1,0:T(8,128)(2,1)}, u32[]{:S(2)}) copy-start(bf16[6,3,256,256]{3,2,1,0:T(8,128)(2,1)} %tiles_ref.1) | copy-start | bytes 7077892
  24.7 9.2 %copy-start.2 = (bf16[64,6,256]{2,1,0:T(8,128)(2,1)S(1)}, bf16[64,6,256]{2,1,0:T(8,128)(2,1)}, u32[]{:S(2)}) copy-start(bf16[64,6,256]{2,1,0:T(8,128)(2,1)} %copy-done.1) | copy-start | bytes 589828
  24.9 13.1 %collective-permute-start.3 = (f32[2,2,64,256]{3,2,1,0:T(8,128)S(1)}, f32[2,2,64,256]{3,2,1,0:T(8,128)S(1)}, u32[]{:S(2)}, u32[]{:S(2)}) collective-permute-start(f32[2,2,64,256]{3,2,1,0:T(8,128)S(1)} %pad_maximum_fusion.5), channel_id=1, source_target_pairs={{32,0},{64,32},{96,64},{128,96},{160,128},{192,160},{224,192},{256... | collective-permute-start | bytes 786440 | tf_op jit(solution)/shard_map/ppermute | solution.py:128
  32.0 11.3 %collective-permute-start.2 = (f32[2,2,64,256]{3,2,1,0:T(8,128)S(1)}, f32[2,2,64,256]{3,2,1,0:T(8,128)S(1)}, u32[]{:S(2)}, u32[]{:S(2)}) collective-permute-start(f32[2,2,64,256]{3,2,1,0:T(8,128)S(1)} %pad_maximum_fusion.6), channel_id=1, source_target_pairs={{0,32},{32,64},{64,96},{96,128},{128,160},{160,192},{192,224},{224... | collective-permute-start | bytes 786440 | tf_op jit(solution)/shard_map/ppermute | solution.py:129
  44.5 3.1 %collective-permute-start.4 = (f32[3,32,32]{2,1,0:T(8,128)S(1)}, f32[3,32,32]{2,1,0:T(8,128)S(1)}, u32[]{:S(2)}, u32[]{:S(2)}) collective-permute-start(f32[3,32,32]{2,1,0:T(8,128)S(1)} %pad_maximum_fusion.7), channel_id=1, source_target_pairs={{0,32},{1,33},{2,34},{3,35},{4,36},{5,37},{6,38},{7,39},{8,40},{9,... | collective-permute-start | bytes 36872 | tf_op jit(solution)/shard_map/ppermute | solution.py:59
  47.6 9.9 %collective-permute-start.5 = (f32[3,32,32]{2,1,0:T(8,128)S(1)}, f32[3,32,32]{2,1,0:T(8,128)S(1)}, u32[]{:S(2)}, u32[]{:S(2)}) collective-permute-start(f32[3,32,32]{2,1,0:T(8,128)S(1)} %fusion.89), channel_id=1, source_target_pairs={{0,16},{1,17},{2,18},{3,19},{4,20},{5,21},{6,22},{7,23},{8,24},{9,... | collective-permute-start | bytes 36872 | tf_op jit(solution)/shard_map/ppermute | solution.py:59
  57.5 6.0 %collective-permute-start.6 = (f32[3,32,32]{2,1,0:T(8,128)S(1)}, f32[3,32,32]{2,1,0:T(8,128)S(1)}, u32[]{:S(2)}, u32[]{:S(2)}) collective-permute-start(f32[3,32,32]{2,1,0:T(8,128)S(1)} %add.151), channel_id=1, source_target_pairs={{0,80},{1,81},{2,82},{3,83},{4,84},{5,85},{6,86},{7,87},{8,88},{9,... | collective-permute-start | bytes 36872 | tf_op jit(solution)/shard_map/ppermute | solution.py:59
  63.5 6.0 %collective-permute-start.7 = (f32[3,32,32]{2,1,0:T(8,128)S(1)}, f32[3,32,32]{2,1,0:T(8,128)S(1)}, u32[]{:S(2)}, u32[]{:S(2)}) collective-permute-start(f32[3,32,32]{2,1,0:T(8,128)S(1)} %add.152), channel_id=1, source_target_pairs={{0,128},{1,129},{2,130},{3,131},{4,132},{5,133},{6,134},{7,135},{8... | collective-permute-start | bytes 36872 | tf_op jit(solution)/shard_map/ppermute | solution.py:59
  69.5 7.2 %collective-permute-start.8 = (f32[3,32,32]{2,1,0:T(8,128)S(1)}, f32[3,32,32]{2,1,0:T(8,128)S(1)}, u32[]{:S(2)}, u32[]{:S(2)}) collective-permute-start(f32[3,32,32]{2,1,0:T(8,128)S(1)} %add.153), channel_id=1, source_target_pairs={{0,384},{1,385},{2,386},{3,387},{4,388},{5,389},{6,390},{7,391},{8... | collective-permute-start | bytes 36872 | tf_op jit(solution)/shard_map/ppermute | solution.py:59
  76.7 6.0 %collective-permute-start.9 = (f32[3,32,32]{2,1,0:T(8,128)S(1)}, f32[3,32,32]{2,1,0:T(8,128)S(1)}, u32[]{:S(2)}, u32[]{:S(2)}) collective-permute-start(f32[3,32,32]{2,1,0:T(8,128)S(1)} %add.154), channel_id=1, source_target_pairs={{0,1},{1,0},{2,3},{3,2},{4,5},{5,4},{6,7},{7,6},{8,9},{9,8},{10,11... | collective-permute-start | bytes 36872 | tf_op jit(solution)/shard_map/ppermute | solution.py:59
  82.7 7.4 %collective-permute-start.10 = (f32[3,32,32]{2,1,0:T(8,128)S(1)}, f32[3,32,32]{2,1,0:T(8,128)S(1)}, u32[]{:S(2)}, u32[]{:S(2)}) collective-permute-start(f32[3,32,32]{2,1,0:T(8,128)S(1)} %add.155), channel_id=1, source_target_pairs={{0,2},{1,3},{2,0},{3,1},{4,6},{5,7},{6,4},{7,5},{8,10},{9,11},{10,... | collective-permute-start | bytes 36872 | tf_op jit(solution)/shard_map/ppermute | solution.py:59
  90.1 10.5 %collective-permute-start.11 = (f32[3,32,32]{2,1,0:T(8,128)S(1)}, f32[3,32,32]{2,1,0:T(8,128)S(1)}, u32[]{:S(2)}, u32[]{:S(2)}) collective-permute-start(f32[3,32,32]{2,1,0:T(8,128)S(1)} %add.156), channel_id=1, source_target_pairs={{0,4},{1,5},{2,6},{3,7},{4,0},{5,1},{6,2},{7,3},{8,12},{9,13},{10,... | collective-permute-start | bytes 36872 | tf_op jit(solution)/shard_map/ppermute | solution.py:59
  100.6 11.6 %collective-permute-start.12 = (f32[3,32,32]{2,1,0:T(8,128)S(1)}, f32[3,32,32]{2,1,0:T(8,128)S(1)}, u32[]{:S(2)}, u32[]{:S(2)}) collective-permute-start(f32[3,32,32]{2,1,0:T(8,128)S(1)} %add.157), channel_id=1, source_target_pairs={{0,12},{1,13},{2,14},{3,15},{4,8},{5,9},{6,10},{7,11},{8,4},{9,5},... | collective-permute-start | bytes 36872 | tf_op jit(solution)/shard_map/ppermute | solution.py:59

commit v12 on v10

--- a/solution.py
+++ b/solution.py
@@ -71,7 +71,7 @@
     nb = tiles_ref.shape[0]
     bs = tiles_ref.shape[2]
     win_ref[...] = jnp.zeros(win_ref.shape, win_ref.dtype)
-    f = f_ref[...]
+    f = f_ref[2]
     for r in range(nb):
         rows = [
             jnp.dot(f, cot_ref[m, :, r * bs : (r + 1) * bs], preferred_element_type=jnp.float32)
@@ -84,7 +84,7 @@
 
 def first_window(flags, cot, f2, tiles):
     nb, bs = tiles.shape[0], tiles.shape[2]
-    rows = cot.shape[0] * f2.shape[0]
+    rows = cot.shape[0] * f2.shape[1]
     return pl.pallas_call(
         window_kernel,
         out_shape=jax.ShapeDtypeStruct((nb + 4, rows, bs), jnp.float32),
@@ -147,7 +147,7 @@
     grad_two = grads[2].astype(jnp.bfloat16)
 
     flags = jnp.stack([back_one[:, 0, 0], next_one[:, 0, 0]], axis=1).astype(jnp.int32)
-    win1 = first_window(flags, cotangent, filters[2], tiles)
+    win1 = first_window(flags, cotangent, filters, tiles)
     x0f = x_zero.astype(jnp.float32)
     send_left = jnp.stack([x0f[0:2], win1[0:2]])
     send_right = jnp.stack([x0f[nb - 2 : nb], win1[nb + 2 : nb + 4]])

time: 109 us -> 108 us (level)
  local copies, waits for them, and re-layouts: 6.85 us -> 5.56 us
    squeeze x1 -> x0, local copies, waits for them, and re-layouts: 1.29 us -> none  [per_device(): win1 = first_window(flags, cotangent, filters[2], tiles)]
where the time goes in v12:
time: 108 us; the launch traced here: 107 us
  starting transfers between devices  55.9 us (52%)
  waiting for transfers between devices  34.6 us (32%)
  local copies, waits for them, and re-layouts  5.56 us (5%)
  Pallas kernels  3.73 us (3%)
  matrix products  3.2 us (3%)
  other arithmetic  2.49 us (2%)
    ppermute x9, starting transfers between devices, butterfly_sum(): x = x + lax.ppermute(x, axes, pairs)  39.1 us
    ppermute x9, waiting for transfers between devices, butterfly_sum(): x = x + lax.ppermute(x, axes, pairs)  27.7 us
    ppermute x2, starting transfers between devices, exchange(): from_left = lax.ppermute(edge_right, 'patch', to_right)  8.84 us
    ppermute x2, starting transfers between devices, exchange(): from_right = lax.ppermute(edge_left, 'patch', to_left)  7.97 us
    ppermute x2, waiting for transfers between devices, exchange(): from_right = lax.ppermute(edge_left, 'patch', to_left)  4.37 us
    pallas_call x1, Pallas kernels, first_window(): pl.pallas_call(window_kernel, out_shape=jax.ShapeDtypeStruct((nb + 4, row...  3.73 us
    ppermute x2, waiting for transfers between devices, exchange(): from_left = lax.ppermute(edge_right, 'patch', to_right)  2.49 us
  transfers between devices with their start and end apart: 13, of which 12 were waited for; matrix products, arithmetic and copies ran while one was open for 3% of the time, Pallas kernels for 0%

profile of v12, /device:TPU:24, one launch (start us, length us, event | category | flops | bytes accessed | tf_op | source)
XLA Modules:
  0.0 106.6 jit_solution(8849435535227205314)
XLA Ops:
  3.5 3.7 %shard_map.76 = f32[10,64,256]{2,1,0:T(8,128)} custom-call(s32[6,2]{1,0:T(8,128)} %add_convert_fusion.flags_ref, bf16[2,32,1536]{2,1,0:T(8,128)(2,1)} %cot_ref.1, bf16[3,32,32]{2,1,0:T(8,128)(2,1)} %f_ref.1, bf16[6,3,256,256]{3,2,1,0:T(8,128)(2,1)} %tiles_ref.1), custom_call_target="tpu_custom_call" | custom-call | tf_op jit(solution)/shard_map/pallas_call | solution.py:88
  8.3 1.9 %collective-permute-start = (f32[2,2,64,256]{3,2,1,0:T(8,128)S(1)}, f32[2,2,64,256]{3,2,1,0:T(8,128)S(1)}, u32[]{:S(2)}, u32[]{:S(2)}) collective-permute-start(f32[2,2,64,256]{3,2,1,0:T(8,128)S(1)} %pad_maximum_fusion.6), channel_id=1, source_target_pairs={{0,32},{32,64},{64,96},{96,128},{128,160},{160,192},{192,224},{224... | collective-permute-start | bytes 786440 | tf_op jit(solution)/shard_map/ppermute | solution.py:114
  10.2 6.0 %collective-permute-start.1 = (f32[2,2,64,256]{3,2,1,0:T(8,128)S(1)}, f32[2,2,64,256]{3,2,1,0:T(8,128)S(1)}, u32[]{:S(2)}, u32[]{:S(2)}) collective-permute-start(f32[2,2,64,256]{3,2,1,0:T(8,128)S(1)} %pad_maximum_fusion.5), channel_id=1, source_target_pairs={{32,0},{64,32},{96,64},{128,96},{160,128},{192,160},{224,192},{256... | collective-permute-start | bytes 786440 | tf_op jit(solution)/shard_map/ppermute | solution.py:113
  17.1 1.3 %collective-permute-done = f32[2,2,64,256]{3,2,1,0:T(8,128)S(1)} collective-permute-done((f32[2,2,64,256]{3,2,1,0:T(8,128)S(1)}, f32[2,2,64,256]{3,2,1,0:T(8,128)S(1)}, u32[]{:S(2)}, u32[]{:S(2)}) %collective-permute-start) | collective-permute-done | bytes 262176 | tf_op jit(solution)/shard_map/ppermute | solution.py:114
  18.4 1.7 %collective-permute-done.1 = f32[2,2,64,256]{3,2,1,0:T(8,128)S(1)} collective-permute-done((f32[2,2,64,256]{3,2,1,0:T(8,128)S(1)}, f32[2,2,64,256]{3,2,1,0:T(8,128)S(1)}, u32[]{:S(2)}, u32[]{:S(2)}) %collective-permute-start.1) | collective-permute-done | bytes 262176 | tf_op jit(solution)/shard_map/ppermute | solution.py:113
  22.2 6.9 %collective-permute-start.2 = (f32[2,2,64,256]{3,2,1,0:T(8,128)S(1)}, f32[2,2,64,256]{3,2,1,0:T(8,128)S(1)}, u32[]{:S(2)}, u32[]{:S(2)}) collective-permute-start(f32[2,2,64,256]{3,2,1,0:T(8,128)S(1)} %pad_maximum_fusion.8), channel_id=1, source_target_pairs={{0,32},{32,64},{64,96},{96,128},{128,160},{160,192},{192,224},{224... | collective-permute-start | bytes 786440 | tf_op jit(solution)/shard_map/ppermute | solution.py:114
  29.1 1.9 %collective-permute-start.3 = (f32[2,2,64,256]{3,2,1,0:T(8,128)S(1)}, f32[2,2,64,256]{3,2,1,0:T(8,128)S(1)}, u32[]{:S(2)}, u32[]{:S(2)}) collective-permute-start(f32[2,2,64,256]{3,2,1,0:T(8,128)S(1)} %pad_maximum_fusion.7), channel_id=1, source_target_pairs={{32,0},{64,32},{96,64},{128,96},{160,128},{192,160},{224,192},{256... | collective-permute-start | bytes 786440 | tf_op jit(solution)/shard_map/ppermute | solution.py:113
  32.5 2.6 %collective-permute-done.3 = f32[2,2,64,256]{3,2,1,0:T(8,128)S(1)} collective-permute-done((f32[2,2,64,256]{3,2,1,0:T(8,128)S(1)}, f32[2,2,64,256]{3,2,1,0:T(8,128)S(1)}, u32[]{:S(2)}, u32[]{:S(2)}) %collective-permute-start.3) | collective-permute-done | bytes 262176 | tf_op jit(solution)/shard_map/ppermute | solution.py:113
  36.3 7.9 %collective-permute-start.4 = (f32[3,32,32]{2,1,0:T(8,128)S(1)}, f32[3,32,32]{2,1,0:T(8,128)S(1)}, u32[]{:S(2)}, u32[]{:S(2)}) collective-permute-start(f32[3,32,32]{2,1,0:T(8,128)S(1)} %pad_maximum_fusion.9), channel_id=1, source_target_pairs={{0,32},{1,33},{2,34},{3,35},{4,36},{5,37},{6,38},{7,39},{8,40},{9,... | collective-permute-start | bytes 36872 | tf_op jit(solution)/shard_map/ppermute | solution.py:59
  45.1 1.9 %collective-permute-start.5 = (f32[3,32,32]{2,1,0:T(8,128)S(1)}, f32[3,32,32]{2,1,0:T(8,128)S(1)}, u32[]{:S(2)}, u32[]{:S(2)}) collective-permute-start(f32[3,32,32]{2,1,0:T(8,128)S(1)} %fusion.89), channel_id=1, source_target_pairs={{0,16},{1,17},{2,18},{3,19},{4,20},{5,21},{6,22},{7,23},{8,24},{9,... | collective-permute-start | bytes 36872 | tf_op jit(solution)/shard_map/ppermute | solution.py:59
  47.0 4.1 %collective-permute-done.5 = f32[3,32,32]{2,1,0:T(8,128)S(1)} collective-permute-done((f32[3,32,32]{2,1,0:T(8,128)S(1)}, f32[3,32,32]{2,1,0:T(8,128)S(1)}, u32[]{:S(2)}, u32[]{:S(2)}) %collective-permute-start.5) | collective-permute-done | bytes 12320 | tf_op jit(solution)/shard_map/ppermute | solution.py:59
  51.1 5.7 %collective-permute-start.6 = (f32[3,32,32]{2,1,0:T(8,128)S(1)}, f32[3,32,32]{2,1,0:T(8,128)S(1)}, u32[]{:S(2)}, u32[]{:S(2)}) collective-permute-start(f32[3,32,32]{2,1,0:T(8,128)S(1)} %add.151), channel_id=1, source_target_pairs={{0,80},{1,81},{2,82},{3,83},{4,84},{5,85},{6,86},{7,87},{8,88},{9,... | collective-permute-start | bytes 36872 | tf_op jit(solution)/shard_map/ppermute | solution.py:59
  56.8 2.1 %collective-permute-done.6 = f32[3,32,32]{2,1,0:T(8,128)S(1)} collective-permute-done((f32[3,32,32]{2,1,0:T(8,128)S(1)}, f32[3,32,32]{2,1,0:T(8,128)S(1)}, u32[]{:S(2)}, u32[]{:S(2)}) %collective-permute-start.6) | collective-permute-done | bytes 12320 | tf_op jit(solution)/shard_map/ppermute | solution.py:59
  58.9 1.9 %collective-permute-start.7 = (f32[3,32,32]{2,1,0:T(8,128)S(1)}, f32[3,32,32]{2,1,0:T(8,128)S(1)}, u32[]{:S(2)}, u32[]{:S(2)}) collective-permute-start(f32[3,32,32]{2,1,0:T(8,128)S(1)} %add.152), channel_id=1, source_target_pairs={{0,128},{1,129},{2,130},{3,131},{4,132},{5,133},{6,134},{7,135},{8... | collective-permute-start | bytes 36872 | tf_op jit(solution)/shard_map/ppermute | solution.py:59
  60.8 4.1 %collective-permute-done.7 = f32[3,32,32]{2,1,0:T(8,128)S(1)} collective-permute-done((f32[3,32,32]{2,1,0:T(8,128)S(1)}, f32[3,32,32]{2,1,0:T(8,128)S(1)}, u32[]{:S(2)}, u32[]{:S(2)}) %collective-permute-start.7) | collective-permute-done | bytes 12320 | tf_op jit(solution)/shard_map/ppermute | solution.py:59
  64.8 3.5 %collective-permute-start.8 = (f32[3,32,32]{2,1,0:T(8,128)S(1)}, f32[3,32,32]{2,1,0:T(8,128)S(1)}, u32[]{:S(2)}, u32[]{:S(2)}) collective-permute-start(f32[3,32,32]{2,1,0:T(8,128)S(1)} %add.153), channel_id=1, source_target_pairs={{0,384},{1,385},{2,386},{3,387},{4,388},{5,389},{6,390},{7,391},{8... | collective-permute-start | bytes 36872 | tf_op jit(solution)/shard_map/ppermute | solution.py:59
  68.5 3.5 %collective-permute-done.8 = f32[3,32,32]{2,1,0:T(8,128)S(1)} collective-permute-done((f32[3,32,32]{2,1,0:T(8,128)S(1)}, f32[3,32,32]{2,1,0:T(8,128)S(1)}, u32[]{:S(2)}, u32[]{:S(2)}) %collective-permute-start.8) | collective-permute-done | bytes 12320 | tf_op jit(solution)/shard_map/ppermute | solution.py:59
  72.1 1.9 %collective-permute-start.9 = (f32[3,32,32]{2,1,0:T(8,128)S(1)}, f32[3,32,32]{2,1,0:T(8,128)S(1)}, u32[]{:S(2)}, u32[]{:S(2)}) collective-permute-start(f32[3,32,32]{2,1,0:T(8,128)S(1)} %add.154), channel_id=1, source_target_pairs={{0,1},{1,0},{2,3},{3,2},{4,5},{5,4},{6,7},{7,6},{8,9},{9,8},{10,11... | collective-permute-start | bytes 36872 | tf_op jit(solution)/shard_map/ppermute | solution.py:59
  74.0 4.0 %collective-permute-done.9 = f32[3,32,32]{2,1,0:T(8,128)S(1)} collective-permute-done((f32[3,32,32]{2,1,0:T(8,128)S(1)}, f32[3,32,32]{2,1,0:T(8,128)S(1)}, u32[]{:S(2)}, u32[]{:S(2)}) %collective-permute-start.9) | collective-permute-done | bytes 12320 | tf_op jit(solution)/shard_map/ppermute | solution.py:59
  78.0 1.9 %collective-permute-start.10 = (f32[3,32,32]{2,1,0:T(8,128)S(1)}, f32[3,32,32]{2,1,0:T(8,128)S(1)}, u32[]{:S(2)}, u32[]{:S(2)}) collective-permute-start(f32[3,32,32]{2,1,0:T(8,128)S(1)} %add.155), channel_id=1, source_target_pairs={{0,2},{1,3},{2,0},{3,1},{4,6},{5,7},{6,4},{7,5},{8,10},{9,11},{10,... | collective-permute-start | bytes 36872 | tf_op jit(solution)/shard_map/ppermute | solution.py:59
  80.0 4.9 %collective-permute-done.10 = f32[3,32,32]{2,1,0:T(8,128)S(1)} collective-permute-done((f32[3,32,32]{2,1,0:T(8,128)S(1)}, f32[3,32,32]{2,1,0:T(8,128)S(1)}, u32[]{:S(2)}, u32[]{:S(2)}) %collective-permute-start.10) | collective-permute-done | bytes 12320 | tf_op jit(solution)/shard_map/ppermute | solution.py:59
  84.9 6.1 %collective-permute-start.11 = (f32[3,32,32]{2,1,0:T(8,128)S(1)}, f32[3,32,32]{2,1,0:T(8,128)S(1)}, u32[]{:S(2)}, u32[]{:S(2)}) collective-permute-start(f32[3,32,32]{2,1,0:T(8,128)S(1)} %add.156), channel_id=1, source_target_pairs={{0,4},{1,5},{2,6},{3,7},{4,0},{5,1},{6,2},{7,3},{8,12},{9,13},{10,... | collective-permute-start | bytes 36872 | tf_op jit(solution)/shard_map/ppermute | solution.py:59
  91.1 4.3 %collective-permute-done.11 = f32[3,32,32]{2,1,0:T(8,128)S(1)} collective-permute-done((f32[3,32,32]{2,1,0:T(8,128)S(1)}, f32[3,32,32]{2,1,0:T(8,128)S(1)}, u32[]{:S(2)}, u32[]{:S(2)}) %collective-permute-start.11) | collective-permute-done | bytes 12320 | tf_op jit(solution)/shard_map/ppermute | solution.py:59
  95.4 8.2 %collective-permute-start.12 = (f32[3,32,32]{2,1,0:T(8,128)S(1)}, f32[3,32,32]{2,1,0:T(8,128)S(1)}, u32[]{:S(2)}, u32[]{:S(2)}) collective-permute-start(f32[3,32,32]{2,1,0:T(8,128)S(1)} %add.157), channel_id=1, source_target_pairs={{0,12},{1,13},{2,14},{3,15},{4,8},{5,9},{6,10},{7,11},{8,4},{9,5},... | collective-permute-start | bytes 36872 | tf_op jit(solution)/shard_map/ppermute | solution.py:59
  (71 shorter events, 13.3 us)
Async XLA Ops:
  3.5 12.8 %copy-start.2 = (bf16[2,32,1536]{2,1,0:T(8,128)(2,1)S(1)}, bf16[2,32,1536]{2,1,0:T(8,128)(2,1)}, u32[]{:S(2)}) copy-start(bf16[2,32,1536]{2,1,0:T(8,128)(2,1)} %cot_ref.1) | copy-start | bytes 589828
  3.5 13.1 %copy-start.3 = (bf16[3,32,32]{2,1,0:T(8,128)(2,1)S(1)}, bf16[3,32,32]{2,1,0:T(8,128)(2,1)}, u32[]{:S(2)}) copy-start(bf16[3,32,32]{2,1,0:T(8,128)(2,1)} %f_ref.1) | copy-start | bytes 18436
  8.3 8.8 %copy-start.4 = (s32[6,3]{0,1:T(4,128)S(1)}, s32[6,3]{0,1:T(4,128)}, u32[]{:S(2)}) copy-start(s32[6,3]{0,1:T(4,128)} %param.16) | copy-start | bytes 220
  8.3 10.1 %collective-permute-start = (f32[2,2,64,256]{3,2,1,0:T(8,128)S(1)}, f32[2,2,64,256]{3,2,1,0:T(8,128)S(1)}, u32[]{:S(2)}, u32[]{:S(2)}) collective-permute-start(f32[2,2,64,256]{3,2,1,0:T(8,128)S(1)} %pad_maximum_fusion.6), channel_id=1, source_target_pairs={{0,32},{32,64},{64,96},{96,128},{128,160},{160,192},{192,224},{224... | collective-permute-start | bytes 786440 | tf_op jit(solution)/shard_map/ppermute | solution.py:114
  10.2 9.9 %collective-permute-start.1 = (f32[2,2,64,256]{3,2,1,0:T(8,128)S(1)}, f32[2,2,64,256]{3,2,1,0:T(8,128)S(1)}, u32[]{:S(2)}, u32[]{:S(2)}) collective-permute-start(f32[2,2,64,256]{3,2,1,0:T(8,128)S(1)} %pad_maximum_fusion.5), channel_id=1, source_target_pairs={{32,0},{64,32},{96,64},{128,96},{160,128},{192,160},{224,192},{256... | collective-permute-start | bytes 786440 | tf_op jit(solution)/shard_map/ppermute | solution.py:113
  16.5 1.9 %copy-start.1 = (f32[10,64,256]{2,1,0:T(8,128)S(1)}, f32[10,64,256]{2,1,0:T(8,128)}, u32[]{:S(2)}) copy-start(f32[10,64,256]{2,1,0:T(8,128)} %shard_map.76) | copy-start | bytes 1966084
  16.6 1.9 %slice-start = ((f32[10,64,256]{2,1,0:T(8,128)}), f32[6,64,256]{2,1,0:T(8,128)S(1)}, s32[]{:S(2)}) async-start(f32[10,64,256]{2,1,0:T(8,128)} %shard_map.76), calls=%async_computation | async-start | bytes 786432 | tf_op jit(solution)/shard_map/slice | solution.py:157
  16.9 3.3 %copy-start = (bf16[6,3,256,256]{3,2,1,0:T(8,128)(2,1)S(1)}, bf16[6,3,256,256]{3,2,1,0:T(8,128)(2,1)}, u32[]{:S(2)}) copy-start(bf16[6,3,256,256]{3,2,1,0:T(8,128)(2,1)} %tiles_ref.1) | copy-start | bytes 7077892
  22.2 10.3 %collective-permute-start.2 = (f32[2,2,64,256]{3,2,1,0:T(8,128)S(1)}, f32[2,2,64,256]{3,2,1,0:T(8,128)S(1)}, u32[]{:S(2)}, u32[]{:S(2)}) collective-permute-start(f32[2,2,64,256]{3,2,1,0:T(8,128)S(1)} %pad_maximum_fusion.8), channel_id=1, source_target_pairs={{0,32},{32,64},{64,96},{96,128},{128,160},{160,192},{192,224},{224... | collective-permute-start | bytes 786440 | tf_op jit(solution)/shard_map/ppermute | solution.py:114
  29.1 6.0 %collective-permute-start.3 = (f32[2,2,64,256]{3,2,1,0:T(8,128)S(1)}, f32[2,2,64,256]{3,2,1,0:T(8,128)S(1)}, u32[]{:S(2)}, u32[]{:S(2)}) collective-permute-start(f32[2,2,64,256]{3,2,1,0:T(8,128)S(1)} %pad_maximum_fusion.7), channel_id=1, source_target_pairs={{32,0},{64,32},{96,64},{128,96},{160,128},{192,160},{224,192},{256... | collective-permute-start | bytes 786440 | tf_op jit(solution)/shard_map/ppermute | solution.py:113
  36.3 8.8 %collective-permute-start.4 = (f32[3,32,32]{2,1,0:T(8,128)S(1)}, f32[3,32,32]{2,1,0:T(8,128)S(1)}, u32[]{:S(2)}, u32[]{:S(2)}) collective-permute-start(f32[3,32,32]{2,1,0:T(8,128)S(1)} %pad_maximum_fusion.9), channel_id=1, source_target_pairs={{0,32},{1,33},{2,34},{3,35},{4,36},{5,37},{6,38},{7,39},{8,40},{9,... | collective-permute-start | bytes 36872 | tf_op jit(solution)/shard_map/ppermute | solution.py:59
  45.1 6.0 %collective-permute-start.5 = (f32[3,32,32]{2,1,0:T(8,128)S(1)}, f32[3,32,32]{2,1,0:T(8,128)S(1)}, u32[]{:S(2)}, u32[]{:S(2)}) collective-permute-start(f32[3,32,32]{2,1,0:T(8,128)S(1)} %fusion.89), channel_id=1, source_target_pairs={{0,16},{1,17},{2,18},{3,19},{4,20},{5,21},{6,22},{7,23},{8,24},{9,... | collective-permute-start | bytes 36872 | tf_op jit(solution)/shard_map/ppermute | solution.py:59
  51.1 7.7 %collective-permute-start.6 = (f32[3,32,32]{2,1,0:T(8,128)S(1)}, f32[3,32,32]{2,1,0:T(8,128)S(1)}, u32[]{:S(2)}, u32[]{:S(2)}) collective-permute-start(f32[3,32,32]{2,1,0:T(8,128)S(1)} %add.151), channel_id=1, source_target_pairs={{0,80},{1,81},{2,82},{3,83},{4,84},{5,85},{6,86},{7,87},{8,88},{9,... | collective-permute-start | bytes 36872 | tf_op jit(solution)/shard_map/ppermute | solution.py:59
  58.9 6.0 %collective-permute-start.7 = (f32[3,32,32]{2,1,0:T(8,128)S(1)}, f32[3,32,32]{2,1,0:T(8,128)S(1)}, u32[]{:S(2)}, u32[]{:S(2)}) collective-permute-start(f32[3,32,32]{2,1,0:T(8,128)S(1)} %add.152), channel_id=1, source_target_pairs={{0,128},{1,129},{2,130},{3,131},{4,132},{5,133},{6,134},{7,135},{8... | collective-permute-start | bytes 36872 | tf_op jit(solution)/shard_map/ppermute | solution.py:59
  64.8 7.2 %collective-permute-start.8 = (f32[3,32,32]{2,1,0:T(8,128)S(1)}, f32[3,32,32]{2,1,0:T(8,128)S(1)}, u32[]{:S(2)}, u32[]{:S(2)}) collective-permute-start(f32[3,32,32]{2,1,0:T(8,128)S(1)} %add.153), channel_id=1, source_target_pairs={{0,384},{1,385},{2,386},{3,387},{4,388},{5,389},{6,390},{7,391},{8... | collective-permute-start | bytes 36872 | tf_op jit(solution)/shard_map/ppermute | solution.py:59
  72.1 6.0 %collective-permute-start.9 = (f32[3,32,32]{2,1,0:T(8,128)S(1)}, f32[3,32,32]{2,1,0:T(8,128)S(1)}, u32[]{:S(2)}, u32[]{:S(2)}) collective-permute-start(f32[3,32,32]{2,1,0:T(8,128)S(1)} %add.154), channel_id=1, source_target_pairs={{0,1},{1,0},{2,3},{3,2},{4,5},{5,4},{6,7},{7,6},{8,9},{9,8},{10,11... | collective-permute-start | bytes 36872 | tf_op jit(solution)/shard_map/ppermute | solution.py:59
  78.0 6.9 %collective-permute-start.10 = (f32[3,32,32]{2,1,0:T(8,128)S(1)}, f32[3,32,32]{2,1,0:T(8,128)S(1)}, u32[]{:S(2)}, u32[]{:S(2)}) collective-permute-start(f32[3,32,32]{2,1,0:T(8,128)S(1)} %add.155), channel_id=1, source_target_pairs={{0,2},{1,3},{2,0},{3,1},{4,6},{5,7},{6,4},{7,5},{8,10},{9,11},{10,... | collective-permute-start | bytes 36872 | tf_op jit(solution)/shard_map/ppermute | solution.py:59
  84.9 10.4 %collective-permute-start.11 = (f32[3,32,32]{2,1,0:T(8,128)S(1)}, f32[3,32,32]{2,1,0:T(8,128)S(1)}, u32[]{:S(2)}, u32[]{:S(2)}) collective-permute-start(f32[3,32,32]{2,1,0:T(8,128)S(1)} %add.156), channel_id=1, source_target_pairs={{0,4},{1,5},{2,6},{3,7},{4,0},{5,1},{6,2},{7,3},{8,12},{9,13},{10,... | collective-permute-start | bytes 36872 | tf_op jit(solution)/shard_map/ppermute | solution.py:59
  95.4 10.6 %collective-permute-start.12 = (f32[3,32,32]{2,1,0:T(8,128)S(1)}, f32[3,32,32]{2,1,0:T(8,128)S(1)}, u32[]{:S(2)}, u32[]{:S(2)}) collective-permute-start(f32[3,32,32]{2,1,0:T(8,128)S(1)} %add.157), channel_id=1, source_target_pairs={{0,12},{1,13},{2,14},{3,15},{4,8},{5,9},{6,10},{7,11},{8,4},{9,5},... | collective-permute-start | bytes 36872 | tf_op jit(solution)/shard_map/ppermute | solution.py:59

commit v13 on v12

--- a/solution.py
+++ b/solution.py
@@ -1,3 +1,4 @@
+import functools
 import math
 
 import jax
@@ -67,7 +68,7 @@
     return x
 
 
-def window_kernel(flags_ref, cot_ref, f_ref, tiles_ref, win_ref):
+def window_kernel(total_blocks, cols_ref, cot_ref, f_ref, tiles_ref, win_ref):
     nb = tiles_ref.shape[0]
     bs = tiles_ref.shape[2]
     win_ref[...] = jnp.zeros(win_ref.shape, win_ref.dtype)
@@ -79,18 +80,26 @@
         ]
         g = jnp.concatenate(rows, axis=0).astype(jnp.bfloat16)
         win_ref[r + 2] += jnp.dot(g, tiles_ref[r, 0], preferred_element_type=jnp.float32)
-        win_ref[r + flags_ref[r, 0]] += jnp.dot(g, tiles_ref[r, 1], preferred_element_type=jnp.float32)
-        win_ref[r + 4 - flags_ref[r, 1]] += jnp.dot(g, tiles_ref[r, 2], preferred_element_type=jnp.float32)
-
-def first_window(flags, cot, f2, tiles):
+        row = lax.axis_index("patch") * nb + r
+        back = row - cols_ref[r, 1]
+        back = jnp.where(back < 0, back + total_blocks, back)
+        ahead = cols_ref[r, 2] - row
+        ahead = jnp.where(ahead < 0, ahead + total_blocks, ahead)
+        back_one = (back == 1).astype(jnp.int32)
+        next_one = (ahead == 1).astype(jnp.int32)
+        win_ref[r + back_one] += jnp.dot(g, tiles_ref[r, 1], preferred_element_type=jnp.float32)
+        win_ref[r + 4 - next_one] += jnp.dot(g, tiles_ref[r, 2], preferred_element_type=jnp.float32)
+
+def first_window(columns, cot, f2, tiles):
     nb, bs = tiles.shape[0], tiles.shape[2]
     rows = cot.shape[0] * f2.shape[1]
+    total_blocks = nb * lax.axis_size("patch")
     return pl.pallas_call(
-        window_kernel,
+        functools.partial(window_kernel, total_blocks),
         out_shape=jax.ShapeDtypeStruct((nb + 4, rows, bs), jnp.float32),
         in_specs=[pl.BlockSpec(memory_space=pltpu.SMEM)] + [pl.BlockSpec(memory_space=pltpu.VMEM)] * 3,
         out_specs=pl.BlockSpec(memory_space=pltpu.VMEM),
-    )(flags, cot, f2, tiles)
+    )(columns, cot, f2, tiles)
 
 
 def per_device(maps, cotangent, tiles, columns, filters):
@@ -146,8 +155,7 @@
     grads = grads.reshape(3, nb, row_count, block_size)
     grad_two = grads[2].astype(jnp.bfloat16)
 
-    flags = jnp.stack([back_one[:, 0, 0], next_one[:, 0, 0]], axis=1).astype(jnp.int32)
-    win1 = first_window(flags, cotangent, filters, tiles)
+    win1 = first_window(columns, cotangent, filters, tiles)
     x0f = x_zero.astype(jnp.float32)
     send_left = jnp.stack([x0f[0:2], win1[0:2]])
     send_right = jnp.stack([x0f[nb - 2 : nb], win1[nb + 2 : nb + 4]])

time: 108 us -> 115 us (1.065)
  other arithmetic: 2.49 us -> 6.99 us
  local copies, waits for them, and re-layouts: 5.56 us -> 9.17 us
  starting transfers between devices: 55.9 us -> 54.3 us
    unnamed x12 -> x23, local copies, waits for them, and re-layouts: 0.21 us -> 2.78 us
    ppermute x9, waiting for transfers between devices: 27.7 us -> 30.1 us  [butterfly_sum(): x = x + lax.ppermute(x, axes, pairs)]
    squeeze x2, local copies, waits for them, and re-layouts: 0.02 us -> 1.83 us  [per_device(): ext0 = jnp.concatenate([got_left[0], x0f, got_right[0]], axis=0)]
    ppermute x9, starting transfers between devices: 39.1 us -> 37.4 us  [butterfly_sum(): x = x + lax.ppermute(x, axes, pairs)]
    ppermute x2, waiting for transfers between devices: 2.49 us -> 1.31 us  [exchange(): from_left = lax.ppermute(edge_right, 'patch', to_right)]
  transfers between devices with their start and end apart: 13 -> 13, of which waited for: 12 -> 13; matrix products, arithmetic and copies ran while one was open for 3% -> 5% of each run, Pallas kernels for 0% -> 0%
where the time goes in v13:
time: 115 us; the launch traced here: 113 us
  starting transfers between devices  54.3 us (47%)
  waiting for transfers between devices  34.9 us (30%)
  local copies, waits for them, and re-layouts  9.17 us (8%)
  other arithmetic  6.99 us (6%)
  Pallas kernels  3.75 us (3%)
  matrix products  3.19 us (3%)
    ppermute x9, starting transfers between devices, butterfly_sum(): x = x + lax.ppermute(x, axes, pairs)  37.4 us
    ppermute x9, waiting for transfers between devices, butterfly_sum(): x = x + lax.ppermute(x, axes, pairs)  30.1 us
    ppermute x2, starting transfers between devices, exchange(): from_left = lax.ppermute(edge_right, 'patch', to_right)  8.96 us
    ppermute x2, starting transfers between devices, exchange(): from_right = lax.ppermute(edge_left, 'patch', to_left)  7.97 us
    pallas_call x1, Pallas kernels, first_window(): pl.pallas_call(functools.partial(window_kernel, total_blocks), out_shape=...  3.75 us
    ppermute x2, waiting for transfers between devices, exchange(): from_right = lax.ppermute(edge_left, 'patch', to_left)  3.47 us
    unnamed x23, local copies, waits for them, and re-layouts  2.78 us
  transfers between devices with their start and end apart: 13, of which 13 were waited for; matrix products, arithmetic and copies ran while one was open for 5% of the time, Pallas kernels for 0%

profile of v13, /device:TPU:24, one launch (start us, length us, event | category | flops | bytes accessed | tf_op | source)
XLA Modules:
  0.0 113.4 jit_solution(441362587732631483)
XLA Ops:
  0.6 1.4 %copy.22.cols_ref = s32[6,3]{1,0:T(8,128)} copy(s32[6,3]{0,1:T(4,128)} %param.16) | data formatting | bytes 144 | tf_op args[3]
  2.0 1.2 %reshape.188 = bf16[64,6,256]{2,1,0:T(8,128)(2,1)S(1)} reshape(bf16[2,32,1536]{2,1,0:T(8,128)(2,1)} %param.13) | data formatting | bytes 393216 | tf_op jit(solution)/shard_map/reshape | solution.py:127
  4.7 3.8 %shard_map.76 = f32[10,64,256]{2,1,0:T(8,128)} custom-call(s32[6,3]{1,0:T(8,128)} %copy.22.cols_ref, bf16[2,32,1536]{2,1,0:T(8,128)(2,1)} %cot_ref.1, bf16[3,32,32]{2,1,0:T(8,128)(2,1)} %f_ref.1, bf16[6,3,256,256]{3,2,1,0:T(8,128)(2,1)} %tiles_ref.1), custom_call_target="tpu_custom_call" | custom-call | tf_op jit(solution)/shard_map/pallas_call | solution.py:97
  10.3 2.0 %collective-permute-start = (f32[2,2,64,256]{3,2,1,0:T(8,128)}, f32[2,2,64,256]{3,2,1,0:T(8,128)}, u32[]{:S(2)}, u32[]{:S(2)}) collective-permute-start(f32[2,2,64,256]{3,2,1,0:T(8,128)} %get-tuple-element.55), channel_id=1, source_target_pairs={{0,32},{32,64},{64,96},{96,128},{128,160},{160,192},{192,224},{224... | collective-permute-start | bytes 786440 | tf_op jit(solution)/shard_map/ppermute | solution.py:123
  12.3 6.0 %collective-permute-start.1 = (f32[2,2,64,256]{3,2,1,0:T(8,128)}, f32[2,2,64,256]{3,2,1,0:T(8,128)}, u32[]{:S(2)}, u32[]{:S(2)}) collective-permute-start(f32[2,2,64,256]{3,2,1,0:T(8,128)} %get-tuple-element.56), channel_id=1, source_target_pairs={{32,0},{64,32},{96,64},{128,96},{160,128},{192,160},{224,192},{256... | collective-permute-start | bytes 786440 | tf_op jit(solution)/shard_map/ppermute | solution.py:122
  28.3 6.9 %collective-permute-start.2 = (f32[2,2,64,256]{3,2,1,0:T(8,128)S(1)}, f32[2,2,64,256]{3,2,1,0:T(8,128)S(1)}, u32[]{:S(2)}, u32[]{:S(2)}) collective-permute-start(f32[2,2,64,256]{3,2,1,0:T(8,128)S(1)} %pad_maximum_fusion.8), channel_id=1, source_target_pairs={{0,32},{32,64},{64,96},{96,128},{128,160},{160,192},{192,224},{224... | collective-permute-start | bytes 786440 | tf_op jit(solution)/shard_map/ppermute | solution.py:123
  35.2 1.9 %collective-permute-start.3 = (f32[2,2,64,256]{3,2,1,0:T(8,128)S(1)}, f32[2,2,64,256]{3,2,1,0:T(8,128)S(1)}, u32[]{:S(2)}, u32[]{:S(2)}) collective-permute-start(f32[2,2,64,256]{3,2,1,0:T(8,128)S(1)} %pad_maximum_fusion.7), channel_id=1, source_target_pairs={{32,0},{64,32},{96,64},{128,96},{160,128},{192,160},{224,192},{256... | collective-permute-start | bytes 786440 | tf_op jit(solution)/shard_map/ppermute | solution.py:122
  38.6 2.6 %collective-permute-done.3 = f32[2,2,64,256]{3,2,1,0:T(8,128)S(1)} collective-permute-done((f32[2,2,64,256]{3,2,1,0:T(8,128)S(1)}, f32[2,2,64,256]{3,2,1,0:T(8,128)S(1)}, u32[]{:S(2)}, u32[]{:S(2)}) %collective-permute-start.3) | collective-permute-done | bytes 262176 | tf_op jit(solution)/shard_map/ppermute | solution.py:122
  42.4 8.8 %collective-permute-start.4 = (f32[3,32,32]{2,1,0:T(8,128)S(1)}, f32[3,32,32]{2,1,0:T(8,128)S(1)}, u32[]{:S(2)}, u32[]{:S(2)}) collective-permute-start(f32[3,32,32]{2,1,0:T(8,128)S(1)} %pad_maximum_fusion.9), channel_id=1, source_target_pairs={{0,32},{1,33},{2,34},{3,35},{4,36},{5,37},{6,38},{7,39},{8,40},{9,... | collective-permute-start | bytes 36872 | tf_op jit(solution)/shard_map/ppermute | solution.py:60
  52.1 1.9 %collective-permute-start.5 = (f32[3,32,32]{2,1,0:T(8,128)S(1)}, f32[3,32,32]{2,1,0:T(8,128)S(1)}, u32[]{:S(2)}, u32[]{:S(2)}) collective-permute-start(f32[3,32,32]{2,1,0:T(8,128)S(1)} %fusion.87), channel_id=1, source_target_pairs={{0,16},{1,17},{2,18},{3,19},{4,20},{5,21},{6,22},{7,23},{8,24},{9,... | collective-permute-start | bytes 36872 | tf_op jit(solution)/shard_map/ppermute | solution.py:60
  54.0 4.1 %collective-permute-done.5 = f32[3,32,32]{2,1,0:T(8,128)S(1)} collective-permute-done((f32[3,32,32]{2,1,0:T(8,128)S(1)}, f32[3,32,32]{2,1,0:T(8,128)S(1)}, u32[]{:S(2)}, u32[]{:S(2)}) %collective-permute-start.5) | collective-permute-done | bytes 12320 | tf_op jit(solution)/shard_map/ppermute | solution.py:60
  58.1 5.7 %collective-permute-start.6 = (f32[3,32,32]{2,1,0:T(8,128)S(1)}, f32[3,32,32]{2,1,0:T(8,128)S(1)}, u32[]{:S(2)}, u32[]{:S(2)}) collective-permute-start(f32[3,32,32]{2,1,0:T(8,128)S(1)} %add.129), channel_id=1, source_target_pairs={{0,80},{1,81},{2,82},{3,83},{4,84},{5,85},{6,86},{7,87},{8,88},{9,... | collective-permute-start | bytes 36872 | tf_op jit(solution)/shard_map/ppermute | solution.py:60
  63.8 2.1 %collective-permute-done.6 = f32[3,32,32]{2,1,0:T(8,128)S(1)} collective-permute-done((f32[3,32,32]{2,1,0:T(8,128)S(1)}, f32[3,32,32]{2,1,0:T(8,128)S(1)}, u32[]{:S(2)}, u32[]{:S(2)}) %collective-permute-start.6) | collective-permute-done | bytes 12320 | tf_op jit(solution)/shard_map/ppermute | solution.py:60
  65.8 1.9 %collective-permute-start.7 = (f32[3,32,32]{2,1,0:T(8,128)S(1)}, f32[3,32,32]{2,1,0:T(8,128)S(1)}, u32[]{:S(2)}, u32[]{:S(2)}) collective-permute-start(f32[3,32,32]{2,1,0:T(8,128)S(1)} %add.130), channel_id=1, source_target_pairs={{0,128},{1,129},{2,130},{3,131},{4,132},{5,133},{6,134},{7,135},{8... | collective-permute-start | bytes 36872 | tf_op jit(solution)/shard_map/ppermute | solution.py:60
  67.8 4.1 %collective-permute-done.7 = f32[3,32,32]{2,1,0:T(8,128)S(1)} collective-permute-done((f32[3,32,32]{2,1,0:T(8,128)S(1)}, f32[3,32,32]{2,1,0:T(8,128)S(1)}, u32[]{:S(2)}, u32[]{:S(2)}) %collective-permute-start.7) | collective-permute-done | bytes 12320 | tf_op jit(solution)/shard_map/ppermute | solution.py:60
  71.8 3.6 %collective-permute-start.8 = (f32[3,32,32]{2,1,0:T(8,128)S(1)}, f32[3,32,32]{2,1,0:T(8,128)S(1)}, u32[]{:S(2)}, u32[]{:S(2)}) collective-permute-start(f32[3,32,32]{2,1,0:T(8,128)S(1)} %add.131), channel_id=1, source_target_pairs={{0,384},{1,385},{2,386},{3,387},{4,388},{5,389},{6,390},{7,391},{8... | collective-permute-start | bytes 36872 | tf_op jit(solution)/shard_map/ppermute | solution.py:60
  75.6 3.4 %collective-permute-done.8 = f32[3,32,32]{2,1,0:T(8,128)S(1)} collective-permute-done((f32[3,32,32]{2,1,0:T(8,128)S(1)}, f32[3,32,32]{2,1,0:T(8,128)S(1)}, u32[]{:S(2)}, u32[]{:S(2)}) %collective-permute-start.8) | collective-permute-done | bytes 12320 | tf_op jit(solution)/shard_map/ppermute | solution.py:60
  79.0 1.9 %collective-permute-start.9 = (f32[3,32,32]{2,1,0:T(8,128)S(1)}, f32[3,32,32]{2,1,0:T(8,128)S(1)}, u32[]{:S(2)}, u32[]{:S(2)}) collective-permute-start(f32[3,32,32]{2,1,0:T(8,128)S(1)} %add.132), channel_id=1, source_target_pairs={{0,1},{1,0},{2,3},{3,2},{4,5},{5,4},{6,7},{7,6},{8,9},{9,8},{10,11... | collective-permute-start | bytes 36872 | tf_op jit(solution)/shard_map/ppermute | solution.py:60
  81.0 4.0 %collective-permute-done.9 = f32[3,32,32]{2,1,0:T(8,128)S(1)} collective-permute-done((f32[3,32,32]{2,1,0:T(8,128)S(1)}, f32[3,32,32]{2,1,0:T(8,128)S(1)}, u32[]{:S(2)}, u32[]{:S(2)}) %collective-permute-start.9) | collective-permute-done | bytes 12320 | tf_op jit(solution)/shard_map/ppermute | solution.py:60
  85.0 1.9 %collective-permute-start.10 = (f32[3,32,32]{2,1,0:T(8,128)S(1)}, f32[3,32,32]{2,1,0:T(8,128)S(1)}, u32[]{:S(2)}, u32[]{:S(2)}) collective-permute-start(f32[3,32,32]{2,1,0:T(8,128)S(1)} %add.133), channel_id=1, source_target_pairs={{0,2},{1,3},{2,0},{3,1},{4,6},{5,7},{6,4},{7,5},{8,10},{9,11},{10,... | collective-permute-start | bytes 36872 | tf_op jit(solution)/shard_map/ppermute | solution.py:60
  87.0 4.9 %collective-permute-done.10 = f32[3,32,32]{2,1,0:T(8,128)S(1)} collective-permute-done((f32[3,32,32]{2,1,0:T(8,128)S(1)}, f32[3,32,32]{2,1,0:T(8,128)S(1)}, u32[]{:S(2)}, u32[]{:S(2)}) %collective-permute-start.10) | collective-permute-done | bytes 12320 | tf_op jit(solution)/shard_map/ppermute | solution.py:60
  91.9 4.8 %collective-permute-start.11 = (f32[3,32,32]{2,1,0:T(8,128)S(1)}, f32[3,32,32]{2,1,0:T(8,128)S(1)}, u32[]{:S(2)}, u32[]{:S(2)}) collective-permute-start(f32[3,32,32]{2,1,0:T(8,128)S(1)} %add.134), channel_id=1, source_target_pairs={{0,4},{1,5},{2,6},{3,7},{4,0},{5,1},{6,2},{7,3},{8,12},{9,13},{10,... | collective-permute-start | bytes 36872 | tf_op jit(solution)/shard_map/ppermute | solution.py:60
  96.8 6.0 %collective-permute-done.11 = f32[3,32,32]{2,1,0:T(8,128)S(1)} collective-permute-done((f32[3,32,32]{2,1,0:T(8,128)S(1)}, f32[3,32,32]{2,1,0:T(8,128)S(1)}, u32[]{:S(2)}, u32[]{:S(2)}) %collective-permute-start.11) | collective-permute-done | bytes 12320 | tf_op jit(solution)/shard_map/ppermute | solution.py:60
  102.9 6.8 %collective-permute-start.12 = (f32[3,32,32]{2,1,0:T(8,128)S(1)}, f32[3,32,32]{2,1,0:T(8,128)S(1)}, u32[]{:S(2)}, u32[]{:S(2)}) collective-permute-start(f32[3,32,32]{2,1,0:T(8,128)S(1)} %add.135), channel_id=1, source_target_pairs={{0,12},{1,13},{2,14},{3,15},{4,8},{5,9},{6,10},{7,11},{8,4},{9,5},... | collective-permute-start | bytes 36872 | tf_op jit(solution)/shard_map/ppermute | solution.py:60
  (78 shorter events, 20.6 us)
Async XLA Ops:
  3.9 0.8 copy-start.2
  4.7 13.7 %copy-start.7 = (bf16[2,32,1536]{2,1,0:T(8,128)(2,1)S(1)}, bf16[2,32,1536]{2,1,0:T(8,128)(2,1)}, u32[]{:S(2)}) copy-start(bf16[2,32,1536]{2,1,0:T(8,128)(2,1)} %cot_ref.1) | copy-start | bytes 589828
  4.7 14.6 %copy-start.9 = (bf16[3,32,32]{2,1,0:T(8,128)(2,1)S(1)}, bf16[3,32,32]{2,1,0:T(8,128)(2,1)}, u32[]{:S(2)}) copy-start(bf16[3,32,32]{2,1,0:T(8,128)(2,1)} %f_ref.1) | copy-start | bytes 18436
  10.3 10.4 %copy-start.10 = (s32[6,3]{0,1:T(4,128)S(1)}, s32[6,3]{0,1:T(4,128)}, u32[]{:S(2)}) copy-start(s32[6,3]{0,1:T(4,128)} %param.16) | copy-start | bytes 220
  10.3 10.5 %collective-permute-start = (f32[2,2,64,256]{3,2,1,0:T(8,128)}, f32[2,2,64,256]{3,2,1,0:T(8,128)}, u32[]{:S(2)}, u32[]{:S(2)}) collective-permute-start(f32[2,2,64,256]{3,2,1,0:T(8,128)} %get-tuple-element.55), channel_id=1, source_target_pairs={{0,32},{32,64},{64,96},{96,128},{128,160},{160,192},{192,224},{224... | collective-permute-start | bytes 786440 | tf_op jit(solution)/shard_map/ppermute | solution.py:123
  12.3 10.2 %collective-permute-start.1 = (f32[2,2,64,256]{3,2,1,0:T(8,128)}, f32[2,2,64,256]{3,2,1,0:T(8,128)}, u32[]{:S(2)}, u32[]{:S(2)}) collective-permute-start(f32[2,2,64,256]{3,2,1,0:T(8,128)} %get-tuple-element.56), channel_id=1, source_target_pairs={{32,0},{64,32},{96,64},{128,96},{160,128},{192,160},{224,192},{256... | collective-permute-start | bytes 786440 | tf_op jit(solution)/shard_map/ppermute | solution.py:122
  18.6 2.2 %copy-start.1 = (f32[10,64,256]{2,1,0:T(8,128)S(1)}, f32[10,64,256]{2,1,0:T(8,128)}, u32[]{:S(2)}) copy-start(f32[10,64,256]{2,1,0:T(8,128)} %shard_map.76) | copy-start | bytes 1966084
  18.6 2.2 %slice-start = ((f32[10,64,256]{2,1,0:T(8,128)}), f32[6,64,256]{2,1,0:T(8,128)S(1)}, s32[]{:S(2)}) async-start(f32[10,64,256]{2,1,0:T(8,128)} %shard_map.76), calls=%async_computation | async-start | bytes 786432 | tf_op jit(solution)/shard_map/slice | solution.py:165
  19.6 4.9 %copy-start = (bf16[6,3,256,256]{3,2,1,0:T(8,128)(2,1)S(1)}, bf16[6,3,256,256]{3,2,1,0:T(8,128)(2,1)}, u32[]{:S(2)}) copy-start(bf16[6,3,256,256]{3,2,1,0:T(8,128)(2,1)} %tiles_ref.1) | copy-start | bytes 7077892
  25.1 2.1 %copy-start.3 = (f32[6,64,256]{2,1,0:T(8,128)S(1)}, f32[6,64,256]{2,1,0:T(8,128)}, u32[]{:S(2)}) copy-start(f32[6,64,256]{2,1,0:T(8,128)} %copy-done.2) | copy-start | bytes 1179652
  25.1 2.2 %copy-start.8 = (bf16[64,6,256]{2,0,1:T(8,128)(2,1)S(1)}, bf16[64,6,256]{2,0,1:T(8,128)(2,1)}, u32[]{:S(2)}) copy-start(bf16[64,6,256]{2,0,1:T(8,128)(2,1)} %get-tuple-element.60) | copy-start | bytes 589828
  28.1 9.0 %copy-start.6 = (bf16[64,6,256]{2,1,0:T(8,128)(2,1)S(1)}, bf16[64,6,256]{2,1,0:T(8,128)(2,1)}, u32[]{:S(2)}) copy-start(bf16[64,6,256]{2,1,0:T(8,128)(2,1)} %copy-done.5) | copy-start | bytes 589828
  28.3 10.3 %collective-permute-start.2 = (f32[2,2,64,256]{3,2,1,0:T(8,128)S(1)}, f32[2,2,64,256]{3,2,1,0:T(8,128)S(1)}, u32[]{:S(2)}, u32[]{:S(2)}) collective-permute-start(f32[2,2,64,256]{3,2,1,0:T(8,128)S(1)} %pad_maximum_fusion.8), channel_id=1, source_target_pairs={{0,32},{32,64},{64,96},{96,128},{128,160},{160,192},{192,224},{224... | collective-permute-start | bytes 786440 | tf_op jit(solution)/shard_map/ppermute | solution.py:123
  35.2 6.0 %collective-permute-start.3 = (f32[2,2,64,256]{3,2,1,0:T(8,128)S(1)}, f32[2,2,64,256]{3,2,1,0:T(8,128)S(1)}, u32[]{:S(2)}, u32[]{:S(2)}) collective-permute-start(f32[2,2,64,256]{3,2,1,0:T(8,128)S(1)} %pad_maximum_fusion.7), channel_id=1, source_target_pairs={{32,0},{64,32},{96,64},{128,96},{160,128},{192,160},{224,192},{256... | collective-permute-start | bytes 786440 | tf_op jit(solution)/shard_map/ppermute | solution.py:122
  42.4 9.7 %collective-permute-start.4 = (f32[3,32,32]{2,1,0:T(8,128)S(1)}, f32[3,32,32]{2,1,0:T(8,128)S(1)}, u32[]{:S(2)}, u32[]{:S(2)}) collective-permute-start(f32[3,32,32]{2,1,0:T(8,128)S(1)} %pad_maximum_fusion.9), channel_id=1, source_target_pairs={{0,32},{1,33},{2,34},{3,35},{4,36},{5,37},{6,38},{7,39},{8,40},{9,... | collective-permute-start | bytes 36872 | tf_op jit(solution)/shard_map/ppermute | solution.py:60
  52.1 6.0 %collective-permute-start.5 = (f32[3,32,32]{2,1,0:T(8,128)S(1)}, f32[3,32,32]{2,1,0:T(8,128)S(1)}, u32[]{:S(2)}, u32[]{:S(2)}) collective-permute-start(f32[3,32,32]{2,1,0:T(8,128)S(1)} %fusion.87), channel_id=1, source_target_pairs={{0,16},{1,17},{2,18},{3,19},{4,20},{5,21},{6,22},{7,23},{8,24},{9,... | collective-permute-start | bytes 36872 | tf_op jit(solution)/shard_map/ppermute | solution.py:60
  58.1 7.8 %collective-permute-start.6 = (f32[3,32,32]{2,1,0:T(8,128)S(1)}, f32[3,32,32]{2,1,0:T(8,128)S(1)}, u32[]{:S(2)}, u32[]{:S(2)}) collective-permute-start(f32[3,32,32]{2,1,0:T(8,128)S(1)} %add.129), channel_id=1, source_target_pairs={{0,80},{1,81},{2,82},{3,83},{4,84},{5,85},{6,86},{7,87},{8,88},{9,... | collective-permute-start | bytes 36872 | tf_op jit(solution)/shard_map/ppermute | solution.py:60
  65.8 6.0 %collective-permute-start.7 = (f32[3,32,32]{2,1,0:T(8,128)S(1)}, f32[3,32,32]{2,1,0:T(8,128)S(1)}, u32[]{:S(2)}, u32[]{:S(2)}) collective-permute-start(f32[3,32,32]{2,1,0:T(8,128)S(1)} %add.130), channel_id=1, source_target_pairs={{0,128},{1,129},{2,130},{3,131},{4,132},{5,133},{6,134},{7,135},{8... | collective-permute-start | bytes 36872 | tf_op jit(solution)/shard_map/ppermute | solution.py:60
  71.8 7.2 %collective-permute-start.8 = (f32[3,32,32]{2,1,0:T(8,128)S(1)}, f32[3,32,32]{2,1,0:T(8,128)S(1)}, u32[]{:S(2)}, u32[]{:S(2)}) collective-permute-start(f32[3,32,32]{2,1,0:T(8,128)S(1)} %add.131), channel_id=1, source_target_pairs={{0,384},{1,385},{2,386},{3,387},{4,388},{5,389},{6,390},{7,391},{8... | collective-permute-start | bytes 36872 | tf_op jit(solution)/shard_map/ppermute | solution.py:60
  75.6 21.2 %copy-start.4 = (f32[1,6,2,32,256]{4,3,0,2,1:T(8,128)S(1)}, f32[1,6,2,32,256]{4,3,0,2,1:T(8,128)}, u32[]{:S(2)}) copy-start(f32[1,6,2,32,256]{4,3,0,2,1:T(8,128)} %get-tuple-element.67) | copy-start | bytes 1179652
  79.0 6.0 %collective-permute-start.9 = (f32[3,32,32]{2,1,0:T(8,128)S(1)}, f32[3,32,32]{2,1,0:T(8,128)S(1)}, u32[]{:S(2)}, u32[]{:S(2)}) collective-permute-start(f32[3,32,32]{2,1,0:T(8,128)S(1)} %add.132), channel_id=1, source_target_pairs={{0,1},{1,0},{2,3},{3,2},{4,5},{5,4},{6,7},{7,6},{8,9},{9,8},{10,11... | collective-permute-start | bytes 36872 | tf_op jit(solution)/shard_map/ppermute | solution.py:60
  85.0 6.9 %collective-permute-start.10 = (f32[3,32,32]{2,1,0:T(8,128)S(1)}, f32[3,32,32]{2,1,0:T(8,128)S(1)}, u32[]{:S(2)}, u32[]{:S(2)}) collective-permute-start(f32[3,32,32]{2,1,0:T(8,128)S(1)} %add.133), channel_id=1, source_target_pairs={{0,2},{1,3},{2,0},{3,1},{4,6},{5,7},{6,4},{7,5},{8,10},{9,11},{10,... | collective-permute-start | bytes 36872 | tf_op jit(solution)/shard_map/ppermute | solution.py:60
  91.9 10.9 %collective-permute-start.11 = (f32[3,32,32]{2,1,0:T(8,128)S(1)}, f32[3,32,32]{2,1,0:T(8,128)S(1)}, u32[]{:S(2)}, u32[]{:S(2)}) collective-permute-start(f32[3,32,32]{2,1,0:T(8,128)S(1)} %add.134), channel_id=1, source_target_pairs={{0,4},{1,5},{2,6},{3,7},{4,0},{5,1},{6,2},{7,3},{8,12},{9,13},{10,... | collective-permute-start | bytes 36872 | tf_op jit(solution)/shard_map/ppermute | solution.py:60
  102.9 9.9 %collective-permute-start.12 = (f32[3,32,32]{2,1,0:T(8,128)S(1)}, f32[3,32,32]{2,1,0:T(8,128)S(1)}, u32[]{:S(2)}, u32[]{:S(2)}) collective-permute-start(f32[3,32,32]{2,1,0:T(8,128)S(1)} %add.135), channel_id=1, source_target_pairs={{0,12},{1,13},{2,14},{3,15},{4,8},{5,9},{6,10},{7,11},{8,4},{9,5},... | collective-permute-start | bytes 36872 | tf_op jit(solution)/shard_map/ppermute | solution.py:60
  (1 other events, 0.7 us)

commit v14 on v12

--- a/solution.py
+++ b/solution.py
@@ -68,28 +68,40 @@
 
 
 def window_kernel(flags_ref, cot_ref, f_ref, tiles_ref, win_ref):
-    nb = tiles_ref.shape[0]
+    r = pl.program_id(0)
     bs = tiles_ref.shape[2]
-    win_ref[...] = jnp.zeros(win_ref.shape, win_ref.dtype)
+
+    @pl.when(r == 0)
+    def _():
+        win_ref[...] = jnp.zeros(win_ref.shape, win_ref.dtype)
+
     f = f_ref[2]
-    for r in range(nb):
-        rows = [
-            jnp.dot(f, cot_ref[m, :, r * bs : (r + 1) * bs], preferred_element_type=jnp.float32)
-            for m in range(cot_ref.shape[0])
-        ]
-        g = jnp.concatenate(rows, axis=0).astype(jnp.bfloat16)
-        win_ref[r + 2] += jnp.dot(g, tiles_ref[r, 0], preferred_element_type=jnp.float32)
-        win_ref[r + flags_ref[r, 0]] += jnp.dot(g, tiles_ref[r, 1], preferred_element_type=jnp.float32)
-        win_ref[r + 4 - flags_ref[r, 1]] += jnp.dot(g, tiles_ref[r, 2], preferred_element_type=jnp.float32)
+    cols = pl.ds(pl.multiple_of(r * bs, bs), bs)
+    rows = [
+        jnp.dot(f, cot_ref[m, :, cols], preferred_element_type=jnp.float32)
+        for m in range(cot_ref.shape[0])
+    ]
+    g = jnp.concatenate(rows, axis=0).astype(jnp.bfloat16)
+    win_ref[r + 2] += jnp.dot(g, tiles_ref[0, 0], preferred_element_type=jnp.float32)
+    win_ref[r + flags_ref[r, 0]] += jnp.dot(g, tiles_ref[0, 1], preferred_element_type=jnp.float32)
+    win_ref[r + 4 - flags_ref[r, 1]] += jnp.dot(g, tiles_ref[0, 2], preferred_element_type=jnp.float32)
+
 
 def first_window(flags, cot, f2, tiles):
-    nb, bs = tiles.shape[0], tiles.shape[2]
+    nb, slots, bs = tiles.shape[0], tiles.shape[1], tiles.shape[2]
     rows = cot.shape[0] * f2.shape[1]
+    whole = lambda shape: pl.BlockSpec(shape, lambda r: (0,) * len(shape))
     return pl.pallas_call(
         window_kernel,
+        grid=(nb,),
         out_shape=jax.ShapeDtypeStruct((nb + 4, rows, bs), jnp.float32),
-        in_specs=[pl.BlockSpec(memory_space=pltpu.SMEM)] + [pl.BlockSpec(memory_space=pltpu.VMEM)] * 3,
-        out_specs=pl.BlockSpec(memory_space=pltpu.VMEM),
+        in_specs=[
+            pl.BlockSpec(memory_space=pltpu.SMEM),
+            whole(cot.shape),
+            whole(f2.shape),
+            pl.BlockSpec((1, slots, bs, bs), lambda r: (r, 0, 0, 0)),
+        ],
+        out_specs=whole((nb + 4, rows, bs)),
     )(flags, cot, f2, tiles)
 
 

time: 108 us -> 109 us (level)
  Pallas kernels: 3.73 us -> 5.24 us
    pallas_call x1, Pallas kernels: 3.73 us -> 5.24 us  [first_window(): pl.pallas_call(window_kernel, grid=(nb,), out_shape=jax.ShapeDtypeStruct(...]
where the time goes in v14:
time: 109 us; the launch traced here: 108 us
  starting transfers between devices  55.9 us (51%)
  waiting for transfers between devices  34.6 us (32%)
  local copies, waits for them, and re-layouts  5.56 us (5%)
  Pallas kernels  5.24 us (5%)
  matrix products  3.2 us (3%)
  other arithmetic  2.49 us (2%)
    ppermute x9, starting transfers between devices, butterfly_sum(): x = x + lax.ppermute(x, axes, pairs)  39.1 us
    ppermute x9, waiting for transfers between devices, butterfly_sum(): x = x + lax.ppermute(x, axes, pairs)  27.7 us
    ppermute x2, starting transfers between devices, exchange(): from_left = lax.ppermute(edge_right, 'patch', to_right)  8.84 us
    ppermute x2, starting transfers between devices, exchange(): from_right = lax.ppermute(edge_left, 'patch', to_left)  7.97 us
    pallas_call x1, Pallas kernels, first_window(): pl.pallas_call(window_kernel, grid=(nb,), out_shape=jax.ShapeDtypeStruct(...  5.24 us
    ppermute x2, waiting for transfers between devices, exchange(): from_right = lax.ppermute(edge_left, 'patch', to_left)  4.37 us
    ppermute x2, waiting for transfers between devices, exchange(): from_left = lax.ppermute(edge_right, 'patch', to_right)  2.5 us
  transfers between devices with their start and end apart: 13, of which 12 were waited for; matrix products, arithmetic and copies ran while one was open for 3% of the time, Pallas kernels for 0%

profile of v14, /device:TPU:24, one launch (start us, length us, event | category | flops | bytes accessed | tf_op | source)
XLA Modules:
  0.0 108.1 jit_solution(14886470120407864084)
XLA Ops:
  3.5 5.2 %shard_map.76 = f32[10,64,256]{2,1,0:T(8,128)} custom-call(s32[6,2]{1,0:T(8,128)} %add_convert_fusion.flags_ref, bf16[2,32,1536]{2,1,0:T(8,128)(2,1)} %cot_ref.1, bf16[3,32,32]{2,1,0:T(8,128)(2,1)} %f_ref.1, bf16[6,3,256,256]{3,2,1,0:T(8,128)(2,1)} %tiles_ref.1), custom_call_target="tpu_custom_call" | custom-call | tf_op jit(solution)/shard_map/pallas_call | solution.py:94
  9.8 1.9 %collective-permute-start = (f32[2,2,64,256]{3,2,1,0:T(8,128)S(1)}, f32[2,2,64,256]{3,2,1,0:T(8,128)S(1)}, u32[]{:S(2)}, u32[]{:S(2)}) collective-permute-start(f32[2,2,64,256]{3,2,1,0:T(8,128)S(1)} %pad_maximum_fusion.6), channel_id=1, source_target_pairs={{0,32},{32,64},{64,96},{96,128},{128,160},{160,192},{192,224},{224... | collective-permute-start | bytes 786440 | tf_op jit(solution)/shard_map/ppermute | solution.py:126
  11.8 6.0 %collective-permute-start.1 = (f32[2,2,64,256]{3,2,1,0:T(8,128)S(1)}, f32[2,2,64,256]{3,2,1,0:T(8,128)S(1)}, u32[]{:S(2)}, u32[]{:S(2)}) collective-permute-start(f32[2,2,64,256]{3,2,1,0:T(8,128)S(1)} %pad_maximum_fusion.5), channel_id=1, source_target_pairs={{32,0},{64,32},{96,64},{128,96},{160,128},{192,160},{224,192},{256... | collective-permute-start | bytes 786440 | tf_op jit(solution)/shard_map/ppermute | solution.py:125
  18.6 1.3 %collective-permute-done = f32[2,2,64,256]{3,2,1,0:T(8,128)S(1)} collective-permute-done((f32[2,2,64,256]{3,2,1,0:T(8,128)S(1)}, f32[2,2,64,256]{3,2,1,0:T(8,128)S(1)}, u32[]{:S(2)}, u32[]{:S(2)}) %collective-permute-start) | collective-permute-done | bytes 262176 | tf_op jit(solution)/shard_map/ppermute | solution.py:126
  19.9 1.7 %collective-permute-done.1 = f32[2,2,64,256]{3,2,1,0:T(8,128)S(1)} collective-permute-done((f32[2,2,64,256]{3,2,1,0:T(8,128)S(1)}, f32[2,2,64,256]{3,2,1,0:T(8,128)S(1)}, u32[]{:S(2)}, u32[]{:S(2)}) %collective-permute-start.1) | collective-permute-done | bytes 262176 | tf_op jit(solution)/shard_map/ppermute | solution.py:125
  23.7 6.9 %collective-permute-start.2 = (f32[2,2,64,256]{3,2,1,0:T(8,128)S(1)}, f32[2,2,64,256]{3,2,1,0:T(8,128)S(1)}, u32[]{:S(2)}, u32[]{:S(2)}) collective-permute-start(f32[2,2,64,256]{3,2,1,0:T(8,128)S(1)} %pad_maximum_fusion.8), channel_id=1, source_target_pairs={{0,32},{32,64},{64,96},{96,128},{128,160},{160,192},{192,224},{224... | collective-permute-start | bytes 786440 | tf_op jit(solution)/shard_map/ppermute | solution.py:126
  30.6 1.9 %collective-permute-start.3 = (f32[2,2,64,256]{3,2,1,0:T(8,128)S(1)}, f32[2,2,64,256]{3,2,1,0:T(8,128)S(1)}, u32[]{:S(2)}, u32[]{:S(2)}) collective-permute-start(f32[2,2,64,256]{3,2,1,0:T(8,128)S(1)} %pad_maximum_fusion.7), channel_id=1, source_target_pairs={{32,0},{64,32},{96,64},{128,96},{160,128},{192,160},{224,192},{256... | collective-permute-start | bytes 786440 | tf_op jit(solution)/shard_map/ppermute | solution.py:125
  34.0 2.6 %collective-permute-done.3 = f32[2,2,64,256]{3,2,1,0:T(8,128)S(1)} collective-permute-done((f32[2,2,64,256]{3,2,1,0:T(8,128)S(1)}, f32[2,2,64,256]{3,2,1,0:T(8,128)S(1)}, u32[]{:S(2)}, u32[]{:S(2)}) %collective-permute-start.3) | collective-permute-done | bytes 262176 | tf_op jit(solution)/shard_map/ppermute | solution.py:125
  37.8 7.9 %collective-permute-start.4 = (f32[3,32,32]{2,1,0:T(8,128)S(1)}, f32[3,32,32]{2,1,0:T(8,128)S(1)}, u32[]{:S(2)}, u32[]{:S(2)}) collective-permute-start(f32[3,32,32]{2,1,0:T(8,128)S(1)} %pad_maximum_fusion.9), channel_id=1, source_target_pairs={{0,32},{1,33},{2,34},{3,35},{4,36},{5,37},{6,38},{7,39},{8,40},{9,... | collective-permute-start | bytes 36872 | tf_op jit(solution)/shard_map/ppermute | solution.py:59
  46.6 1.9 %collective-permute-start.5 = (f32[3,32,32]{2,1,0:T(8,128)S(1)}, f32[3,32,32]{2,1,0:T(8,128)S(1)}, u32[]{:S(2)}, u32[]{:S(2)}) collective-permute-start(f32[3,32,32]{2,1,0:T(8,128)S(1)} %fusion.89), channel_id=1, source_target_pairs={{0,16},{1,17},{2,18},{3,19},{4,20},{5,21},{6,22},{7,23},{8,24},{9,... | collective-permute-start | bytes 36872 | tf_op jit(solution)/shard_map/ppermute | solution.py:59
  48.5 4.1 %collective-permute-done.5 = f32[3,32,32]{2,1,0:T(8,128)S(1)} collective-permute-done((f32[3,32,32]{2,1,0:T(8,128)S(1)}, f32[3,32,32]{2,1,0:T(8,128)S(1)}, u32[]{:S(2)}, u32[]{:S(2)}) %collective-permute-start.5) | collective-permute-done | bytes 12320 | tf_op jit(solution)/shard_map/ppermute | solution.py:59
  52.6 5.7 %collective-permute-start.6 = (f32[3,32,32]{2,1,0:T(8,128)S(1)}, f32[3,32,32]{2,1,0:T(8,128)S(1)}, u32[]{:S(2)}, u32[]{:S(2)}) collective-permute-start(f32[3,32,32]{2,1,0:T(8,128)S(1)} %add.151), channel_id=1, source_target_pairs={{0,80},{1,81},{2,82},{3,83},{4,84},{5,85},{6,86},{7,87},{8,88},{9,... | collective-permute-start | bytes 36872 | tf_op jit(solution)/shard_map/ppermute | solution.py:59
  58.3 2.1 %collective-permute-done.6 = f32[3,32,32]{2,1,0:T(8,128)S(1)} collective-permute-done((f32[3,32,32]{2,1,0:T(8,128)S(1)}, f32[3,32,32]{2,1,0:T(8,128)S(1)}, u32[]{:S(2)}, u32[]{:S(2)}) %collective-permute-start.6) | collective-permute-done | bytes 12320 | tf_op jit(solution)/shard_map/ppermute | solution.py:59
  60.4 1.9 %collective-permute-start.7 = (f32[3,32,32]{2,1,0:T(8,128)S(1)}, f32[3,32,32]{2,1,0:T(8,128)S(1)}, u32[]{:S(2)}, u32[]{:S(2)}) collective-permute-start(f32[3,32,32]{2,1,0:T(8,128)S(1)} %add.152), channel_id=1, source_target_pairs={{0,128},{1,129},{2,130},{3,131},{4,132},{5,133},{6,134},{7,135},{8... | collective-permute-start | bytes 36872 | tf_op jit(solution)/shard_map/ppermute | solution.py:59
  62.3 4.1 %collective-permute-done.7 = f32[3,32,32]{2,1,0:T(8,128)S(1)} collective-permute-done((f32[3,32,32]{2,1,0:T(8,128)S(1)}, f32[3,32,32]{2,1,0:T(8,128)S(1)}, u32[]{:S(2)}, u32[]{:S(2)}) %collective-permute-start.7) | collective-permute-done | bytes 12320 | tf_op jit(solution)/shard_map/ppermute | solution.py:59
  66.4 3.5 %collective-permute-start.8 = (f32[3,32,32]{2,1,0:T(8,128)S(1)}, f32[3,32,32]{2,1,0:T(8,128)S(1)}, u32[]{:S(2)}, u32[]{:S(2)}) collective-permute-start(f32[3,32,32]{2,1,0:T(8,128)S(1)} %add.153), channel_id=1, source_target_pairs={{0,384},{1,385},{2,386},{3,387},{4,388},{5,389},{6,390},{7,391},{8... | collective-permute-start | bytes 36872 | tf_op jit(solution)/shard_map/ppermute | solution.py:59
  70.0 3.5 %collective-permute-done.8 = f32[3,32,32]{2,1,0:T(8,128)S(1)} collective-permute-done((f32[3,32,32]{2,1,0:T(8,128)S(1)}, f32[3,32,32]{2,1,0:T(8,128)S(1)}, u32[]{:S(2)}, u32[]{:S(2)}) %collective-permute-start.8) | collective-permute-done | bytes 12320 | tf_op jit(solution)/shard_map/ppermute | solution.py:59
  73.6 1.9 %collective-permute-start.9 = (f32[3,32,32]{2,1,0:T(8,128)S(1)}, f32[3,32,32]{2,1,0:T(8,128)S(1)}, u32[]{:S(2)}, u32[]{:S(2)}) collective-permute-start(f32[3,32,32]{2,1,0:T(8,128)S(1)} %add.154), channel_id=1, source_target_pairs={{0,1},{1,0},{2,3},{3,2},{4,5},{5,4},{6,7},{7,6},{8,9},{9,8},{10,11... | collective-permute-start | bytes 36872 | tf_op jit(solution)/shard_map/ppermute | solution.py:59
  75.5 4.0 %collective-permute-done.9 = f32[3,32,32]{2,1,0:T(8,128)S(1)} collective-permute-done((f32[3,32,32]{2,1,0:T(8,128)S(1)}, f32[3,32,32]{2,1,0:T(8,128)S(1)}, u32[]{:S(2)}, u32[]{:S(2)}) %collective-permute-start.9) | collective-permute-done | bytes 12320 | tf_op jit(solution)/shard_map/ppermute | solution.py:59
  79.6 1.9 %collective-permute-start.10 = (f32[3,32,32]{2,1,0:T(8,128)S(1)}, f32[3,32,32]{2,1,0:T(8,128)S(1)}, u32[]{:S(2)}, u32[]{:S(2)}) collective-permute-start(f32[3,32,32]{2,1,0:T(8,128)S(1)} %add.155), channel_id=1, source_target_pairs={{0,2},{1,3},{2,0},{3,1},{4,6},{5,7},{6,4},{7,5},{8,10},{9,11},{10,... | collective-permute-start | bytes 36872 | tf_op jit(solution)/shard_map/ppermute | solution.py:59
  81.5 4.9 %collective-permute-done.10 = f32[3,32,32]{2,1,0:T(8,128)S(1)} collective-permute-done((f32[3,32,32]{2,1,0:T(8,128)S(1)}, f32[3,32,32]{2,1,0:T(8,128)S(1)}, u32[]{:S(2)}, u32[]{:S(2)}) %collective-permute-start.10) | collective-permute-done | bytes 12320 | tf_op jit(solution)/shard_map/ppermute | solution.py:59
  86.4 6.1 %collective-permute-start.11 = (f32[3,32,32]{2,1,0:T(8,128)S(1)}, f32[3,32,32]{2,1,0:T(8,128)S(1)}, u32[]{:S(2)}, u32[]{:S(2)}) collective-permute-start(f32[3,32,32]{2,1,0:T(8,128)S(1)} %add.156), channel_id=1, source_target_pairs={{0,4},{1,5},{2,6},{3,7},{4,0},{5,1},{6,2},{7,3},{8,12},{9,13},{10,... | collective-permute-start | bytes 36872 | tf_op jit(solution)/shard_map/ppermute | solution.py:59
  92.6 4.3 %collective-permute-done.11 = f32[3,32,32]{2,1,0:T(8,128)S(1)} collective-permute-done((f32[3,32,32]{2,1,0:T(8,128)S(1)}, f32[3,32,32]{2,1,0:T(8,128)S(1)}, u32[]{:S(2)}, u32[]{:S(2)}) %collective-permute-start.11) | collective-permute-done | bytes 12320 | tf_op jit(solution)/shard_map/ppermute | solution.py:59
  96.9 8.2 %collective-permute-start.12 = (f32[3,32,32]{2,1,0:T(8,128)S(1)}, f32[3,32,32]{2,1,0:T(8,128)S(1)}, u32[]{:S(2)}, u32[]{:S(2)}) collective-permute-start(f32[3,32,32]{2,1,0:T(8,128)S(1)} %add.157), channel_id=1, source_target_pairs={{0,12},{1,13},{2,14},{3,15},{4,8},{5,9},{6,10},{7,11},{8,4},{9,5},... | collective-permute-start | bytes 36872 | tf_op jit(solution)/shard_map/ppermute | solution.py:59
  (71 shorter events, 13.3 us)
Async XLA Ops:
  3.5 14.3 %copy-start.2 = (bf16[2,32,1536]{2,1,0:T(8,128)(2,1)S(1)}, bf16[2,32,1536]{2,1,0:T(8,128)(2,1)}, u32[]{:S(2)}) copy-start(bf16[2,32,1536]{2,1,0:T(8,128)(2,1)} %cot_ref.1) | copy-start | bytes 589828
  3.5 14.6 %copy-start.3 = (bf16[3,32,32]{2,1,0:T(8,128)(2,1)S(1)}, bf16[3,32,32]{2,1,0:T(8,128)(2,1)}, u32[]{:S(2)}) copy-start(bf16[3,32,32]{2,1,0:T(8,128)(2,1)} %f_ref.1) | copy-start | bytes 18436
  9.8 8.8 %copy-start.4 = (s32[6,3]{0,1:T(4,128)S(1)}, s32[6,3]{0,1:T(4,128)}, u32[]{:S(2)}) copy-start(s32[6,3]{0,1:T(4,128)} %param.16) | copy-start | bytes 220
  9.8 10.1 %collective-permute-start = (f32[2,2,64,256]{3,2,1,0:T(8,128)S(1)}, f32[2,2,64,256]{3,2,1,0:T(8,128)S(1)}, u32[]{:S(2)}, u32[]{:S(2)}) collective-permute-start(f32[2,2,64,256]{3,2,1,0:T(8,128)S(1)} %pad_maximum_fusion.6), channel_id=1, source_target_pairs={{0,32},{32,64},{64,96},{96,128},{128,160},{160,192},{192,224},{224... | collective-permute-start | bytes 786440 | tf_op jit(solution)/shard_map/ppermute | solution.py:126
  11.8 9.9 %collective-permute-start.1 = (f32[2,2,64,256]{3,2,1,0:T(8,128)S(1)}, f32[2,2,64,256]{3,2,1,0:T(8,128)S(1)}, u32[]{:S(2)}, u32[]{:S(2)}) collective-permute-start(f32[2,2,64,256]{3,2,1,0:T(8,128)S(1)} %pad_maximum_fusion.5), channel_id=1, source_target_pairs={{32,0},{64,32},{96,64},{128,96},{160,128},{192,160},{224,192},{256... | collective-permute-start | bytes 786440 | tf_op jit(solution)/shard_map/ppermute | solution.py:125
  18.0 1.9 %copy-start.1 = (f32[10,64,256]{2,1,0:T(8,128)S(1)}, f32[10,64,256]{2,1,0:T(8,128)}, u32[]{:S(2)}) copy-start(f32[10,64,256]{2,1,0:T(8,128)} %shard_map.76) | copy-start | bytes 1966084
  18.1 1.9 %slice-start = ((f32[10,64,256]{2,1,0:T(8,128)}), f32[6,64,256]{2,1,0:T(8,128)S(1)}, s32[]{:S(2)}) async-start(f32[10,64,256]{2,1,0:T(8,128)} %shard_map.76), calls=%async_computation | async-start | bytes 786432 | tf_op jit(solution)/shard_map/slice | solution.py:169
  18.4 3.3 %copy-start = (bf16[6,3,256,256]{3,2,1,0:T(8,128)(2,1)S(1)}, bf16[6,3,256,256]{3,2,1,0:T(8,128)(2,1)}, u32[]{:S(2)}) copy-start(bf16[6,3,256,256]{3,2,1,0:T(8,128)(2,1)} %tiles_ref.1) | copy-start | bytes 7077892
  23.7 10.3 %collective-permute-start.2 = (f32[2,2,64,256]{3,2,1,0:T(8,128)S(1)}, f32[2,2,64,256]{3,2,1,0:T(8,128)S(1)}, u32[]{:S(2)}, u32[]{:S(2)}) collective-permute-start(f32[2,2,64,256]{3,2,1,0:T(8,128)S(1)} %pad_maximum_fusion.8), channel_id=1, source_target_pairs={{0,32},{32,64},{64,96},{96,128},{128,160},{160,192},{192,224},{224... | collective-permute-start | bytes 786440 | tf_op jit(solution)/shard_map/ppermute | solution.py:126
  30.6 6.0 %collective-permute-start.3 = (f32[2,2,64,256]{3,2,1,0:T(8,128)S(1)}, f32[2,2,64,256]{3,2,1,0:T(8,128)S(1)}, u32[]{:S(2)}, u32[]{:S(2)}) collective-permute-start(f32[2,2,64,256]{3,2,1,0:T(8,128)S(1)} %pad_maximum_fusion.7), channel_id=1, source_target_pairs={{32,0},{64,32},{96,64},{128,96},{160,128},{192,160},{224,192},{256... | collective-permute-start | bytes 786440 | tf_op jit(solution)/shard_map/ppermute | solution.py:125
  37.8 8.8 %collective-permute-start.4 = (f32[3,32,32]{2,1,0:T(8,128)S(1)}, f32[3,32,32]{2,1,0:T(8,128)S(1)}, u32[]{:S(2)}, u32[]{:S(2)}) collective-permute-start(f32[3,32,32]{2,1,0:T(8,128)S(1)} %pad_maximum_fusion.9), channel_id=1, source_target_pairs={{0,32},{1,33},{2,34},{3,35},{4,36},{5,37},{6,38},{7,39},{8,40},{9,... | collective-permute-start | bytes 36872 | tf_op jit(solution)/shard_map/ppermute | solution.py:59
  46.6 6.0 %collective-permute-start.5 = (f32[3,32,32]{2,1,0:T(8,128)S(1)}, f32[3,32,32]{2,1,0:T(8,128)S(1)}, u32[]{:S(2)}, u32[]{:S(2)}) collective-permute-start(f32[3,32,32]{2,1,0:T(8,128)S(1)} %fusion.89), channel_id=1, source_target_pairs={{0,16},{1,17},{2,18},{3,19},{4,20},{5,21},{6,22},{7,23},{8,24},{9,... | collective-permute-start | bytes 36872 | tf_op jit(solution)/shard_map/ppermute | solution.py:59
  52.6 7.8 %collective-permute-start.6 = (f32[3,32,32]{2,1,0:T(8,128)S(1)}, f32[3,32,32]{2,1,0:T(8,128)S(1)}, u32[]{:S(2)}, u32[]{:S(2)}) collective-permute-start(f32[3,32,32]{2,1,0:T(8,128)S(1)} %add.151), channel_id=1, source_target_pairs={{0,80},{1,81},{2,82},{3,83},{4,84},{5,85},{6,86},{7,87},{8,88},{9,... | collective-permute-start | bytes 36872 | tf_op jit(solution)/shard_map/ppermute | solution.py:59
  60.4 6.0 %collective-permute-start.7 = (f32[3,32,32]{2,1,0:T(8,128)S(1)}, f32[3,32,32]{2,1,0:T(8,128)S(1)}, u32[]{:S(2)}, u32[]{:S(2)}) collective-permute-start(f32[3,32,32]{2,1,0:T(8,128)S(1)} %add.152), channel_id=1, source_target_pairs={{0,128},{1,129},{2,130},{3,131},{4,132},{5,133},{6,134},{7,135},{8... | collective-permute-start | bytes 36872 | tf_op jit(solution)/shard_map/ppermute | solution.py:59
  66.4 7.2 %collective-permute-start.8 = (f32[3,32,32]{2,1,0:T(8,128)S(1)}, f32[3,32,32]{2,1,0:T(8,128)S(1)}, u32[]{:S(2)}, u32[]{:S(2)}) collective-permute-start(f32[3,32,32]{2,1,0:T(8,128)S(1)} %add.153), channel_id=1, source_target_pairs={{0,384},{1,385},{2,386},{3,387},{4,388},{5,389},{6,390},{7,391},{8... | collective-permute-start | bytes 36872 | tf_op jit(solution)/shard_map/ppermute | solution.py:59
  73.6 6.0 %collective-permute-start.9 = (f32[3,32,32]{2,1,0:T(8,128)S(1)}, f32[3,32,32]{2,1,0:T(8,128)S(1)}, u32[]{:S(2)}, u32[]{:S(2)}) collective-permute-start(f32[3,32,32]{2,1,0:T(8,128)S(1)} %add.154), channel_id=1, source_target_pairs={{0,1},{1,0},{2,3},{3,2},{4,5},{5,4},{6,7},{7,6},{8,9},{9,8},{10,11... | collective-permute-start | bytes 36872 | tf_op jit(solution)/shard_map/ppermute | solution.py:59
  79.6 6.9 %collective-permute-start.10 = (f32[3,32,32]{2,1,0:T(8,128)S(1)}, f32[3,32,32]{2,1,0:T(8,128)S(1)}, u32[]{:S(2)}, u32[]{:S(2)}) collective-permute-start(f32[3,32,32]{2,1,0:T(8,128)S(1)} %add.155), channel_id=1, source_target_pairs={{0,2},{1,3},{2,0},{3,1},{4,6},{5,7},{6,4},{7,5},{8,10},{9,11},{10,... | collective-permute-start | bytes 36872 | tf_op jit(solution)/shard_map/ppermute | solution.py:59
  86.4 10.4 %collective-permute-start.11 = (f32[3,32,32]{2,1,0:T(8,128)S(1)}, f32[3,32,32]{2,1,0:T(8,128)S(1)}, u32[]{:S(2)}, u32[]{:S(2)}) collective-permute-start(f32[3,32,32]{2,1,0:T(8,128)S(1)} %add.156), channel_id=1, source_target_pairs={{0,4},{1,5},{2,6},{3,7},{4,0},{5,1},{6,2},{7,3},{8,12},{9,13},{10,... | collective-permute-start | bytes 36872 | tf_op jit(solution)/shard_map/ppermute | solution.py:59
  96.9 10.6 %collective-permute-start.12 = (f32[3,32,32]{2,1,0:T(8,128)S(1)}, f32[3,32,32]{2,1,0:T(8,128)S(1)}, u32[]{:S(2)}, u32[]{:S(2)}) collective-permute-start(f32[3,32,32]{2,1,0:T(8,128)S(1)} %add.157), channel_id=1, source_target_pairs={{0,12},{1,13},{2,14},{3,15},{4,8},{5,9},{6,10},{7,11},{8,4},{9,5},... | collective-permute-start | bytes 36872 | tf_op jit(solution)/shard_map/ppermute | solution.py:59

commit v15 on v13

--- a/solution.py
+++ b/solution.py
@@ -81,9 +81,9 @@
         g = jnp.concatenate(rows, axis=0).astype(jnp.bfloat16)
         win_ref[r + 2] += jnp.dot(g, tiles_ref[r, 0], preferred_element_type=jnp.float32)
         row = lax.axis_index("patch") * nb + r
-        back = row - cols_ref[r, 1]
+        back = row - cols_ref[1, r]
         back = jnp.where(back < 0, back + total_blocks, back)
-        ahead = cols_ref[r, 2] - row
+        ahead = cols_ref[2, r] - row
         ahead = jnp.where(ahead < 0, ahead + total_blocks, ahead)
         back_one = (back == 1).astype(jnp.int32)
         next_one = (ahead == 1).astype(jnp.int32)
@@ -155,7 +155,7 @@
     grads = grads.reshape(3, nb, row_count, block_size)
     grad_two = grads[2].astype(jnp.bfloat16)
 
-    win1 = first_window(columns, cotangent, filters, tiles)
+    win1 = first_window(columns.T, cotangent, filters, tiles)
     x0f = x_zero.astype(jnp.float32)
     send_left = jnp.stack([x0f[0:2], win1[0:2]])
     send_right = jnp.stack([x0f[nb - 2 : nb], win1[nb + 2 : nb + 4]])

time: 115 us -> 113 us (0.983)
  local copies, waits for them, and re-layouts: 9.17 us -> 7.82 us
    unnamed x23 -> x22, local copies, waits for them, and re-layouts: 2.78 us -> 1.43 us
where the time goes in v15:
time: 113 us; the launch traced here: 112 us
  starting transfers between devices  54.3 us (48%)
  waiting for transfers between devices  34.9 us (31%)
  local copies, waits for them, and re-layouts  7.82 us (7%)
  other arithmetic  6.99 us (6%)
  Pallas kernels  3.75 us (3%)
  matrix products  3.2 us (3%)
    ppermute x9, starting transfers between devices, butterfly_sum(): x = x + lax.ppermute(x, axes, pairs)  37.4 us
    ppermute x9, waiting for transfers between devices, butterfly_sum(): x = x + lax.ppermute(x, axes, pairs)  30.1 us
    ppermute x2, starting transfers between devices, exchange(): from_left = lax.ppermute(edge_right, 'patch', to_right)  8.96 us
    ppermute x2, starting transfers between devices, exchange(): from_right = lax.ppermute(edge_left, 'patch', to_left)  7.97 us
    pallas_call x1, Pallas kernels, first_window(): pl.pallas_call(functools.partial(window_kernel, total_blocks), out_shape=...  3.75 us
    ppermute x2, waiting for transfers between devices, exchange(): from_right = lax.ppermute(edge_left, 'patch', to_left)  3.47 us
  transfers between devices with their start and end apart: 13, of which 13 were waited for; matrix products, arithmetic and copies ran while one was open for 5% of the time, Pallas kernels for 0%

profile of v15, /device:TPU:24, one launch (start us, length us, event | category | flops | bytes accessed | tf_op | source)
XLA Modules:
  0.0 112.0 jit_solution(14121509964033967814)
XLA Ops:
  0.6 1.2 %reshape.188 = bf16[64,6,256]{2,1,0:T(8,128)(2,1)S(1)} reshape(bf16[2,32,1536]{2,1,0:T(8,128)(2,1)} %param.13) | data formatting | bytes 393216 | tf_op jit(solution)/shard_map/reshape | solution.py:127
  3.3 3.8 %shard_map.76 = f32[10,64,256]{2,1,0:T(8,128)} custom-call(s32[3,6]{1,0:T(4,128)} %bitcast.180, bf16[2,32,1536]{2,1,0:T(8,128)(2,1)} %cot_ref.1, bf16[3,32,32]{2,1,0:T(8,128)(2,1)} %f_ref.1, bf16[6,3,256,256]{3,2,1,0:T(8,128)(2,1)} %tiles_ref.1), custom_call_target="tpu_custom_call" | custom-call | tf_op jit(solution)/shard_map/pallas_call | solution.py:97
  8.9 2.0 %collective-permute-start = (f32[2,2,64,256]{3,2,1,0:T(8,128)}, f32[2,2,64,256]{3,2,1,0:T(8,128)}, u32[]{:S(2)}, u32[]{:S(2)}) collective-permute-start(f32[2,2,64,256]{3,2,1,0:T(8,128)} %get-tuple-element.55), channel_id=1, source_target_pairs={{0,32},{32,64},{64,96},{96,128},{128,160},{160,192},{192,224},{224... | collective-permute-start | bytes 786440 | tf_op jit(solution)/shard_map/ppermute | solution.py:123
  11.0 6.0 %collective-permute-start.1 = (f32[2,2,64,256]{3,2,1,0:T(8,128)}, f32[2,2,64,256]{3,2,1,0:T(8,128)}, u32[]{:S(2)}, u32[]{:S(2)}) collective-permute-start(f32[2,2,64,256]{3,2,1,0:T(8,128)} %get-tuple-element.56), channel_id=1, source_target_pairs={{32,0},{64,32},{96,64},{128,96},{160,128},{192,160},{224,192},{256... | collective-permute-start | bytes 786440 | tf_op jit(solution)/shard_map/ppermute | solution.py:122
  26.9 6.9 %collective-permute-start.2 = (f32[2,2,64,256]{3,2,1,0:T(8,128)S(1)}, f32[2,2,64,256]{3,2,1,0:T(8,128)S(1)}, u32[]{:S(2)}, u32[]{:S(2)}) collective-permute-start(f32[2,2,64,256]{3,2,1,0:T(8,128)S(1)} %pad_maximum_fusion.8), channel_id=1, source_target_pairs={{0,32},{32,64},{64,96},{96,128},{128,160},{160,192},{192,224},{224... | collective-permute-start | bytes 786440 | tf_op jit(solution)/shard_map/ppermute | solution.py:123
  33.8 1.9 %collective-permute-start.3 = (f32[2,2,64,256]{3,2,1,0:T(8,128)S(1)}, f32[2,2,64,256]{3,2,1,0:T(8,128)S(1)}, u32[]{:S(2)}, u32[]{:S(2)}) collective-permute-start(f32[2,2,64,256]{3,2,1,0:T(8,128)S(1)} %pad_maximum_fusion.7), channel_id=1, source_target_pairs={{32,0},{64,32},{96,64},{128,96},{160,128},{192,160},{224,192},{256... | collective-permute-start | bytes 786440 | tf_op jit(solution)/shard_map/ppermute | solution.py:122
  36.0 1.1 %collective-permute-done.2 = f32[2,2,64,256]{3,2,1,0:T(8,128)S(1)} collective-permute-done((f32[2,2,64,256]{3,2,1,0:T(8,128)S(1)}, f32[2,2,64,256]{3,2,1,0:T(8,128)S(1)}, u32[]{:S(2)}, u32[]{:S(2)}) %collective-permute-start.2) | collective-permute-done | bytes 262176 | tf_op jit(solution)/shard_map/ppermute | solution.py:123
  37.2 2.6 %collective-permute-done.3 = f32[2,2,64,256]{3,2,1,0:T(8,128)S(1)} collective-permute-done((f32[2,2,64,256]{3,2,1,0:T(8,128)S(1)}, f32[2,2,64,256]{3,2,1,0:T(8,128)S(1)}, u32[]{:S(2)}, u32[]{:S(2)}) %collective-permute-start.3) | collective-permute-done | bytes 262176 | tf_op jit(solution)/shard_map/ppermute | solution.py:122
  41.0 8.8 %collective-permute-start.4 = (f32[3,32,32]{2,1,0:T(8,128)S(1)}, f32[3,32,32]{2,1,0:T(8,128)S(1)}, u32[]{:S(2)}, u32[]{:S(2)}) collective-permute-start(f32[3,32,32]{2,1,0:T(8,128)S(1)} %pad_maximum_fusion.9), channel_id=1, source_target_pairs={{0,32},{1,33},{2,34},{3,35},{4,36},{5,37},{6,38},{7,39},{8,40},{9,... | collective-permute-start | bytes 36872 | tf_op jit(solution)/shard_map/ppermute | solution.py:60
  50.7 1.9 %collective-permute-start.5 = (f32[3,32,32]{2,1,0:T(8,128)S(1)}, f32[3,32,32]{2,1,0:T(8,128)S(1)}, u32[]{:S(2)}, u32[]{:S(2)}) collective-permute-start(f32[3,32,32]{2,1,0:T(8,128)S(1)} %fusion.87), channel_id=1, source_target_pairs={{0,16},{1,17},{2,18},{3,19},{4,20},{5,21},{6,22},{7,23},{8,24},{9,... | collective-permute-start | bytes 36872 | tf_op jit(solution)/shard_map/ppermute | solution.py:60
  52.7 4.1 %collective-permute-done.5 = f32[3,32,32]{2,1,0:T(8,128)S(1)} collective-permute-done((f32[3,32,32]{2,1,0:T(8,128)S(1)}, f32[3,32,32]{2,1,0:T(8,128)S(1)}, u32[]{:S(2)}, u32[]{:S(2)}) %collective-permute-start.5) | collective-permute-done | bytes 12320 | tf_op jit(solution)/shard_map/ppermute | solution.py:60
  56.7 5.7 %collective-permute-start.6 = (f32[3,32,32]{2,1,0:T(8,128)S(1)}, f32[3,32,32]{2,1,0:T(8,128)S(1)}, u32[]{:S(2)}, u32[]{:S(2)}) collective-permute-start(f32[3,32,32]{2,1,0:T(8,128)S(1)} %add.129), channel_id=1, source_target_pairs={{0,80},{1,81},{2,82},{3,83},{4,84},{5,85},{6,86},{7,87},{8,88},{9,... | collective-permute-start | bytes 36872 | tf_op jit(solution)/shard_map/ppermute | solution.py:60
  62.4 2.1 %collective-permute-done.6 = f32[3,32,32]{2,1,0:T(8,128)S(1)} collective-permute-done((f32[3,32,32]{2,1,0:T(8,128)S(1)}, f32[3,32,32]{2,1,0:T(8,128)S(1)}, u32[]{:S(2)}, u32[]{:S(2)}) %collective-permute-start.6) | collective-permute-done | bytes 12320 | tf_op jit(solution)/shard_map/ppermute | solution.py:60
  64.5 1.9 %collective-permute-start.7 = (f32[3,32,32]{2,1,0:T(8,128)S(1)}, f32[3,32,32]{2,1,0:T(8,128)S(1)}, u32[]{:S(2)}, u32[]{:S(2)}) collective-permute-start(f32[3,32,32]{2,1,0:T(8,128)S(1)} %add.130), channel_id=1, source_target_pairs={{0,128},{1,129},{2,130},{3,131},{4,132},{5,133},{6,134},{7,135},{8... | collective-permute-start | bytes 36872 | tf_op jit(solution)/shard_map/ppermute | solution.py:60
  66.4 4.1 %collective-permute-done.7 = f32[3,32,32]{2,1,0:T(8,128)S(1)} collective-permute-done((f32[3,32,32]{2,1,0:T(8,128)S(1)}, f32[3,32,32]{2,1,0:T(8,128)S(1)}, u32[]{:S(2)}, u32[]{:S(2)}) %collective-permute-start.7) | collective-permute-done | bytes 12320 | tf_op jit(solution)/shard_map/ppermute | solution.py:60
  70.5 3.6 %collective-permute-start.8 = (f32[3,32,32]{2,1,0:T(8,128)S(1)}, f32[3,32,32]{2,1,0:T(8,128)S(1)}, u32[]{:S(2)}, u32[]{:S(2)}) collective-permute-start(f32[3,32,32]{2,1,0:T(8,128)S(1)} %add.131), channel_id=1, source_target_pairs={{0,384},{1,385},{2,386},{3,387},{4,388},{5,389},{6,390},{7,391},{8... | collective-permute-start | bytes 36872 | tf_op jit(solution)/shard_map/ppermute | solution.py:60
  74.3 3.4 %collective-permute-done.8 = f32[3,32,32]{2,1,0:T(8,128)S(1)} collective-permute-done((f32[3,32,32]{2,1,0:T(8,128)S(1)}, f32[3,32,32]{2,1,0:T(8,128)S(1)}, u32[]{:S(2)}, u32[]{:S(2)}) %collective-permute-start.8) | collective-permute-done | bytes 12320 | tf_op jit(solution)/shard_map/ppermute | solution.py:60
  77.7 1.9 %collective-permute-start.9 = (f32[3,32,32]{2,1,0:T(8,128)S(1)}, f32[3,32,32]{2,1,0:T(8,128)S(1)}, u32[]{:S(2)}, u32[]{:S(2)}) collective-permute-start(f32[3,32,32]{2,1,0:T(8,128)S(1)} %add.132), channel_id=1, source_target_pairs={{0,1},{1,0},{2,3},{3,2},{4,5},{5,4},{6,7},{7,6},{8,9},{9,8},{10,11... | collective-permute-start | bytes 36872 | tf_op jit(solution)/shard_map/ppermute | solution.py:60
  79.7 4.0 %collective-permute-done.9 = f32[3,32,32]{2,1,0:T(8,128)S(1)} collective-permute-done((f32[3,32,32]{2,1,0:T(8,128)S(1)}, f32[3,32,32]{2,1,0:T(8,128)S(1)}, u32[]{:S(2)}, u32[]{:S(2)}) %collective-permute-start.9) | collective-permute-done | bytes 12320 | tf_op jit(solution)/shard_map/ppermute | solution.py:60
  83.7 1.9 %collective-permute-start.10 = (f32[3,32,32]{2,1,0:T(8,128)S(1)}, f32[3,32,32]{2,1,0:T(8,128)S(1)}, u32[]{:S(2)}, u32[]{:S(2)}) collective-permute-start(f32[3,32,32]{2,1,0:T(8,128)S(1)} %add.133), channel_id=1, source_target_pairs={{0,2},{1,3},{2,0},{3,1},{4,6},{5,7},{6,4},{7,5},{8,10},{9,11},{10,... | collective-permute-start | bytes 36872 | tf_op jit(solution)/shard_map/ppermute | solution.py:60
  85.7 4.9 %collective-permute-done.10 = f32[3,32,32]{2,1,0:T(8,128)S(1)} collective-permute-done((f32[3,32,32]{2,1,0:T(8,128)S(1)}, f32[3,32,32]{2,1,0:T(8,128)S(1)}, u32[]{:S(2)}, u32[]{:S(2)}) %collective-permute-start.10) | collective-permute-done | bytes 12320 | tf_op jit(solution)/shard_map/ppermute | solution.py:60
  90.6 4.8 %collective-permute-start.11 = (f32[3,32,32]{2,1,0:T(8,128)S(1)}, f32[3,32,32]{2,1,0:T(8,128)S(1)}, u32[]{:S(2)}, u32[]{:S(2)}) collective-permute-start(f32[3,32,32]{2,1,0:T(8,128)S(1)} %add.134), channel_id=1, source_target_pairs={{0,4},{1,5},{2,6},{3,7},{4,0},{5,1},{6,2},{7,3},{8,12},{9,13},{10,... | collective-permute-start | bytes 36872 | tf_op jit(solution)/shard_map/ppermute | solution.py:60
  95.5 6.0 %collective-permute-done.11 = f32[3,32,32]{2,1,0:T(8,128)S(1)} collective-permute-done((f32[3,32,32]{2,1,0:T(8,128)S(1)}, f32[3,32,32]{2,1,0:T(8,128)S(1)}, u32[]{:S(2)}, u32[]{:S(2)}) %collective-permute-start.11) | collective-permute-done | bytes 12320 | tf_op jit(solution)/shard_map/ppermute | solution.py:60
  101.5 6.8 %collective-permute-start.12 = (f32[3,32,32]{2,1,0:T(8,128)S(1)}, f32[3,32,32]{2,1,0:T(8,128)S(1)}, u32[]{:S(2)}, u32[]{:S(2)}) collective-permute-start(f32[3,32,32]{2,1,0:T(8,128)S(1)} %add.135), channel_id=1, source_target_pairs={{0,12},{1,13},{2,14},{3,15},{4,8},{5,9},{6,10},{7,11},{8,4},{9,5},... | collective-permute-start | bytes 36872 | tf_op jit(solution)/shard_map/ppermute | solution.py:60
  (77 shorter events, 19.4 us)
Async XLA Ops:
  2.5 0.8 copy-start.2
  3.3 13.7 %copy-start.7 = (bf16[2,32,1536]{2,1,0:T(8,128)(2,1)S(1)}, bf16[2,32,1536]{2,1,0:T(8,128)(2,1)}, u32[]{:S(2)}) copy-start(bf16[2,32,1536]{2,1,0:T(8,128)(2,1)} %cot_ref.1) | copy-start | bytes 589828
  3.3 14.6 %copy-start.9 = (bf16[3,32,32]{2,1,0:T(8,128)(2,1)S(1)}, bf16[3,32,32]{2,1,0:T(8,128)(2,1)}, u32[]{:S(2)}) copy-start(bf16[3,32,32]{2,1,0:T(8,128)(2,1)} %f_ref.1) | copy-start | bytes 18436
  8.9 10.4 %copy-start.10 = (s32[6,3]{0,1:T(4,128)S(1)}, s32[6,3]{0,1:T(4,128)}, u32[]{:S(2)}) copy-start(s32[6,3]{0,1:T(4,128)} %param.16) | copy-start | bytes 220
  8.9 10.5 %collective-permute-start = (f32[2,2,64,256]{3,2,1,0:T(8,128)}, f32[2,2,64,256]{3,2,1,0:T(8,128)}, u32[]{:S(2)}, u32[]{:S(2)}) collective-permute-start(f32[2,2,64,256]{3,2,1,0:T(8,128)} %get-tuple-element.55), channel_id=1, source_target_pairs={{0,32},{32,64},{64,96},{96,128},{128,160},{160,192},{192,224},{224... | collective-permute-start | bytes 786440 | tf_op jit(solution)/shard_map/ppermute | solution.py:123
  11.0 10.2 %collective-permute-start.1 = (f32[2,2,64,256]{3,2,1,0:T(8,128)}, f32[2,2,64,256]{3,2,1,0:T(8,128)}, u32[]{:S(2)}, u32[]{:S(2)}) collective-permute-start(f32[2,2,64,256]{3,2,1,0:T(8,128)} %get-tuple-element.56), channel_id=1, source_target_pairs={{32,0},{64,32},{96,64},{128,96},{160,128},{192,160},{224,192},{256... | collective-permute-start | bytes 786440 | tf_op jit(solution)/shard_map/ppermute | solution.py:122
  17.3 2.2 %copy-start.1 = (f32[10,64,256]{2,1,0:T(8,128)S(1)}, f32[10,64,256]{2,1,0:T(8,128)}, u32[]{:S(2)}) copy-start(f32[10,64,256]{2,1,0:T(8,128)} %shard_map.76) | copy-start | bytes 1966084
  17.3 2.2 %slice-start = ((f32[10,64,256]{2,1,0:T(8,128)}), f32[6,64,256]{2,1,0:T(8,128)S(1)}, s32[]{:S(2)}) async-start(f32[10,64,256]{2,1,0:T(8,128)} %shard_map.76), calls=%async_computation | async-start | bytes 786432 | tf_op jit(solution)/shard_map/slice | solution.py:165
  18.3 4.9 %copy-start = (bf16[6,3,256,256]{3,2,1,0:T(8,128)(2,1)S(1)}, bf16[6,3,256,256]{3,2,1,0:T(8,128)(2,1)}, u32[]{:S(2)}) copy-start(bf16[6,3,256,256]{3,2,1,0:T(8,128)(2,1)} %tiles_ref.1) | copy-start | bytes 7077892
  23.7 2.1 %copy-start.3 = (f32[6,64,256]{2,1,0:T(8,128)S(1)}, f32[6,64,256]{2,1,0:T(8,128)}, u32[]{:S(2)}) copy-start(f32[6,64,256]{2,1,0:T(8,128)} %copy-done.2) | copy-start | bytes 1179652
  23.7 2.2 %copy-start.8 = (bf16[64,6,256]{2,0,1:T(8,128)(2,1)S(1)}, bf16[64,6,256]{2,0,1:T(8,128)(2,1)}, u32[]{:S(2)}) copy-start(bf16[64,6,256]{2,0,1:T(8,128)(2,1)} %get-tuple-element.60) | copy-start | bytes 589828
  26.8 9.0 %copy-start.6 = (bf16[64,6,256]{2,1,0:T(8,128)(2,1)S(1)}, bf16[64,6,256]{2,1,0:T(8,128)(2,1)}, u32[]{:S(2)}) copy-start(bf16[64,6,256]{2,1,0:T(8,128)(2,1)} %copy-done.5) | copy-start | bytes 589828
  26.9 10.3 %collective-permute-start.2 = (f32[2,2,64,256]{3,2,1,0:T(8,128)S(1)}, f32[2,2,64,256]{3,2,1,0:T(8,128)S(1)}, u32[]{:S(2)}, u32[]{:S(2)}) collective-permute-start(f32[2,2,64,256]{3,2,1,0:T(8,128)S(1)} %pad_maximum_fusion.8), channel_id=1, source_target_pairs={{0,32},{32,64},{64,96},{96,128},{128,160},{160,192},{192,224},{224... | collective-permute-start | bytes 786440 | tf_op jit(solution)/shard_map/ppermute | solution.py:123
  33.8 6.0 %collective-permute-start.3 = (f32[2,2,64,256]{3,2,1,0:T(8,128)S(1)}, f32[2,2,64,256]{3,2,1,0:T(8,128)S(1)}, u32[]{:S(2)}, u32[]{:S(2)}) collective-permute-start(f32[2,2,64,256]{3,2,1,0:T(8,128)S(1)} %pad_maximum_fusion.7), channel_id=1, source_target_pairs={{32,0},{64,32},{96,64},{128,96},{160,128},{192,160},{224,192},{256... | collective-permute-start | bytes 786440 | tf_op jit(solution)/shard_map/ppermute | solution.py:122
  41.0 9.7 %collective-permute-start.4 = (f32[3,32,32]{2,1,0:T(8,128)S(1)}, f32[3,32,32]{2,1,0:T(8,128)S(1)}, u32[]{:S(2)}, u32[]{:S(2)}) collective-permute-start(f32[3,32,32]{2,1,0:T(8,128)S(1)} %pad_maximum_fusion.9), channel_id=1, source_target_pairs={{0,32},{1,33},{2,34},{3,35},{4,36},{5,37},{6,38},{7,39},{8,40},{9,... | collective-permute-start | bytes 36872 | tf_op jit(solution)/shard_map/ppermute | solution.py:60
  50.7 6.0 %collective-permute-start.5 = (f32[3,32,32]{2,1,0:T(8,128)S(1)}, f32[3,32,32]{2,1,0:T(8,128)S(1)}, u32[]{:S(2)}, u32[]{:S(2)}) collective-permute-start(f32[3,32,32]{2,1,0:T(8,128)S(1)} %fusion.87), channel_id=1, source_target_pairs={{0,16},{1,17},{2,18},{3,19},{4,20},{5,21},{6,22},{7,23},{8,24},{9,... | collective-permute-start | bytes 36872 | tf_op jit(solution)/shard_map/ppermute | solution.py:60
  56.7 7.8 %collective-permute-start.6 = (f32[3,32,32]{2,1,0:T(8,128)S(1)}, f32[3,32,32]{2,1,0:T(8,128)S(1)}, u32[]{:S(2)}, u32[]{:S(2)}) collective-permute-start(f32[3,32,32]{2,1,0:T(8,128)S(1)} %add.129), channel_id=1, source_target_pairs={{0,80},{1,81},{2,82},{3,83},{4,84},{5,85},{6,86},{7,87},{8,88},{9,... | collective-permute-start | bytes 36872 | tf_op jit(solution)/shard_map/ppermute | solution.py:60
  64.5 6.0 %collective-permute-start.7 = (f32[3,32,32]{2,1,0:T(8,128)S(1)}, f32[3,32,32]{2,1,0:T(8,128)S(1)}, u32[]{:S(2)}, u32[]{:S(2)}) collective-permute-start(f32[3,32,32]{2,1,0:T(8,128)S(1)} %add.130), channel_id=1, source_target_pairs={{0,128},{1,129},{2,130},{3,131},{4,132},{5,133},{6,134},{7,135},{8... | collective-permute-start | bytes 36872 | tf_op jit(solution)/shard_map/ppermute | solution.py:60
  70.5 7.2 %collective-permute-start.8 = (f32[3,32,32]{2,1,0:T(8,128)S(1)}, f32[3,32,32]{2,1,0:T(8,128)S(1)}, u32[]{:S(2)}, u32[]{:S(2)}) collective-permute-start(f32[3,32,32]{2,1,0:T(8,128)S(1)} %add.131), channel_id=1, source_target_pairs={{0,384},{1,385},{2,386},{3,387},{4,388},{5,389},{6,390},{7,391},{8... | collective-permute-start | bytes 36872 | tf_op jit(solution)/shard_map/ppermute | solution.py:60
  74.2 21.2 %copy-start.4 = (f32[1,6,2,32,256]{4,3,0,2,1:T(8,128)S(1)}, f32[1,6,2,32,256]{4,3,0,2,1:T(8,128)}, u32[]{:S(2)}) copy-start(f32[1,6,2,32,256]{4,3,0,2,1:T(8,128)} %get-tuple-element.67) | copy-start | bytes 1179652
  77.7 6.0 %collective-permute-start.9 = (f32[3,32,32]{2,1,0:T(8,128)S(1)}, f32[3,32,32]{2,1,0:T(8,128)S(1)}, u32[]{:S(2)}, u32[]{:S(2)}) collective-permute-start(f32[3,32,32]{2,1,0:T(8,128)S(1)} %add.132), channel_id=1, source_target_pairs={{0,1},{1,0},{2,3},{3,2},{4,5},{5,4},{6,7},{7,6},{8,9},{9,8},{10,11... | collective-permute-start | bytes 36872 | tf_op jit(solution)/shard_map/ppermute | solution.py:60
  83.7 6.9 %collective-permute-start.10 = (f32[3,32,32]{2,1,0:T(8,128)S(1)}, f32[3,32,32]{2,1,0:T(8,128)S(1)}, u32[]{:S(2)}, u32[]{:S(2)}) collective-permute-start(f32[3,32,32]{2,1,0:T(8,128)S(1)} %add.133), channel_id=1, source_target_pairs={{0,2},{1,3},{2,0},{3,1},{4,6},{5,7},{6,4},{7,5},{8,10},{9,11},{10,... | collective-permute-start | bytes 36872 | tf_op jit(solution)/shard_map/ppermute | solution.py:60
  90.6 10.9 %collective-permute-start.11 = (f32[3,32,32]{2,1,0:T(8,128)S(1)}, f32[3,32,32]{2,1,0:T(8,128)S(1)}, u32[]{:S(2)}, u32[]{:S(2)}) collective-permute-start(f32[3,32,32]{2,1,0:T(8,128)S(1)} %add.134), channel_id=1, source_target_pairs={{0,4},{1,5},{2,6},{3,7},{4,0},{5,1},{6,2},{7,3},{8,12},{9,13},{10,... | collective-permute-start | bytes 36872 | tf_op jit(solution)/shard_map/ppermute | solution.py:60
  101.5 9.9 %collective-permute-start.12 = (f32[3,32,32]{2,1,0:T(8,128)S(1)}, f32[3,32,32]{2,1,0:T(8,128)S(1)}, u32[]{:S(2)}, u32[]{:S(2)}) collective-permute-start(f32[3,32,32]{2,1,0:T(8,128)S(1)} %add.135), channel_id=1, source_target_pairs={{0,12},{1,13},{2,14},{3,15},{4,8},{5,9},{6,10},{7,11},{8,4},{9,5},... | collective-permute-start | bytes 36872 | tf_op jit(solution)/shard_map/ppermute | solution.py:60
  (1 other events, 0.7 us)

commit v16 on v12

--- a/solution.py
+++ b/solution.py
@@ -67,9 +67,12 @@
     return x
 
 
-def window_kernel(flags_ref, cot_ref, f_ref, tiles_ref, win_ref):
-    nb = tiles_ref.shape[0]
-    bs = tiles_ref.shape[2]
+def window_kernel(flags_ref, cot_ref, f_ref, tiles_hbm, win_ref, tiles_vmem, sems):
+    nb = tiles_vmem.shape[0]
+    bs = tiles_vmem.shape[2]
+    copies = [pltpu.make_async_copy(tiles_hbm.at[r], tiles_vmem.at[r], sems.at[r]) for r in range(nb)]
+    for copy in copies:
+        copy.start()
     win_ref[...] = jnp.zeros(win_ref.shape, win_ref.dtype)
     f = f_ref[2]
     for r in range(nb):
@@ -78,18 +81,22 @@
             for m in range(cot_ref.shape[0])
         ]
         g = jnp.concatenate(rows, axis=0).astype(jnp.bfloat16)
-        win_ref[r + 2] += jnp.dot(g, tiles_ref[r, 0], preferred_element_type=jnp.float32)
-        win_ref[r + flags_ref[r, 0]] += jnp.dot(g, tiles_ref[r, 1], preferred_element_type=jnp.float32)
-        win_ref[r + 4 - flags_ref[r, 1]] += jnp.dot(g, tiles_ref[r, 2], preferred_element_type=jnp.float32)
+        copies[r].wait()
+        win_ref[r + 2] += jnp.dot(g, tiles_vmem[r, 0], preferred_element_type=jnp.float32)
+        win_ref[r + flags_ref[r, 0]] += jnp.dot(g, tiles_vmem[r, 1], preferred_element_type=jnp.float32)
+        win_ref[r + 4 - flags_ref[r, 1]] += jnp.dot(g, tiles_vmem[r, 2], preferred_element_type=jnp.float32)
+
 
 def first_window(flags, cot, f2, tiles):
     nb, bs = tiles.shape[0], tiles.shape[2]
     rows = cot.shape[0] * f2.shape[1]
+    vmem = pl.BlockSpec(memory_space=pltpu.VMEM)
     return pl.pallas_call(
         window_kernel,
         out_shape=jax.ShapeDtypeStruct((nb + 4, rows, bs), jnp.float32),
-        in_specs=[pl.BlockSpec(memory_space=pltpu.SMEM)] + [pl.BlockSpec(memory_space=pltpu.VMEM)] * 3,
-        out_specs=pl.BlockSpec(memory_space=pltpu.VMEM),
+        in_specs=[pl.BlockSpec(memory_space=pltpu.SMEM), vmem, vmem, pl.BlockSpec(memory_space=pl.ANY)],
+        out_specs=vmem,
+        scratch_shapes=[pltpu.VMEM(tiles.shape, tiles.dtype), pltpu.SemaphoreType.DMA((nb,))],
     )(flags, cot, f2, tiles)
 
 

time: 108 us -> 108 us (level)
  no operation moved by 1% of the time
where the time goes in v16:
time: 108 us; the launch traced here: 107 us
  starting transfers between devices  55.9 us (52%)
  waiting for transfers between devices  34.6 us (32%)
  local copies, waits for them, and re-layouts  5.56 us (5%)
  Pallas kernels  4.16 us (4%)
  matrix products  3.21 us (3%)
  other arithmetic  2.49 us (2%)
    ppermute x9, starting transfers between devices, butterfly_sum(): x = x + lax.ppermute(x, axes, pairs)  39.1 us
    ppermute x9, waiting for transfers between devices, butterfly_sum(): x = x + lax.ppermute(x, axes, pairs)  27.7 us
    ppermute x2, starting transfers between devices, exchange(): from_left = lax.ppermute(edge_right, 'patch', to_right)  8.84 us
    ppermute x2, starting transfers between devices, exchange(): from_right = lax.ppermute(edge_left, 'patch', to_left)  7.97 us
    ppermute x2, waiting for transfers between devices, exchange(): from_right = lax.ppermute(edge_left, 'patch', to_left)  4.37 us
    pallas_call x1, Pallas kernels, first_window(): pl.pallas_call(window_kernel, out_shape=jax.ShapeDtypeStruct((nb + 4, row...  4.16 us
    ppermute x2, waiting for transfers between devices, exchange(): from_left = lax.ppermute(edge_right, 'patch', to_right)  2.5 us
  transfers between devices with their start and end apart: 13, of which 12 were waited for; matrix products, arithmetic and copies ran while one was open for 3% of the time, Pallas kernels for 0%

profile of v16, /device:TPU:24, one launch (start us, length us, event | category | flops | bytes accessed | tf_op | source)
XLA Modules:
  0.0 107.0 jit_solution(5966153599443386637)
XLA Ops:
  3.5 4.2 %shard_map.76 = f32[10,64,256]{2,1,0:T(8,128)} custom-call(s32[6,2]{1,0:T(8,128)} %add_convert_fusion.flags_ref, bf16[2,32,1536]{2,1,0:T(8,128)(2,1)} %cot_ref.1, bf16[3,32,32]{2,1,0:T(8,128)(2,1)} %f_ref.1, bf16[6,3,256,256]{3,2,1,0:T(8,128)(2,1)} %tiles_hbm.1), custom_call_target="tpu_custom_call" | custom-call | tf_op jit(solution)/shard_map/pallas_call | solution.py:94
  8.8 1.9 %collective-permute-start = (f32[2,2,64,256]{3,2,1,0:T(8,128)S(1)}, f32[2,2,64,256]{3,2,1,0:T(8,128)S(1)}, u32[]{:S(2)}, u32[]{:S(2)}) collective-permute-start(f32[2,2,64,256]{3,2,1,0:T(8,128)S(1)} %pad_maximum_fusion.6), channel_id=1, source_target_pairs={{0,32},{32,64},{64,96},{96,128},{128,160},{160,192},{192,224},{224... | collective-permute-start | bytes 786440 | tf_op jit(solution)/shard_map/ppermute | solution.py:121
  10.7 6.0 %collective-permute-start.1 = (f32[2,2,64,256]{3,2,1,0:T(8,128)S(1)}, f32[2,2,64,256]{3,2,1,0:T(8,128)S(1)}, u32[]{:S(2)}, u32[]{:S(2)}) collective-permute-start(f32[2,2,64,256]{3,2,1,0:T(8,128)S(1)} %pad_maximum_fusion.5), channel_id=1, source_target_pairs={{32,0},{64,32},{96,64},{128,96},{160,128},{192,160},{224,192},{256... | collective-permute-start | bytes 786440 | tf_op jit(solution)/shard_map/ppermute | solution.py:120
  17.5 1.3 %collective-permute-done = f32[2,2,64,256]{3,2,1,0:T(8,128)S(1)} collective-permute-done((f32[2,2,64,256]{3,2,1,0:T(8,128)S(1)}, f32[2,2,64,256]{3,2,1,0:T(8,128)S(1)}, u32[]{:S(2)}, u32[]{:S(2)}) %collective-permute-start) | collective-permute-done | bytes 262176 | tf_op jit(solution)/shard_map/ppermute | solution.py:121
  18.9 1.7 %collective-permute-done.1 = f32[2,2,64,256]{3,2,1,0:T(8,128)S(1)} collective-permute-done((f32[2,2,64,256]{3,2,1,0:T(8,128)S(1)}, f32[2,2,64,256]{3,2,1,0:T(8,128)S(1)}, u32[]{:S(2)}, u32[]{:S(2)}) %collective-permute-start.1) | collective-permute-done | bytes 262176 | tf_op jit(solution)/shard_map/ppermute | solution.py:120
  22.6 6.9 %collective-permute-start.2 = (f32[2,2,64,256]{3,2,1,0:T(8,128)S(1)}, f32[2,2,64,256]{3,2,1,0:T(8,128)S(1)}, u32[]{:S(2)}, u32[]{:S(2)}) collective-permute-start(f32[2,2,64,256]{3,2,1,0:T(8,128)S(1)} %pad_maximum_fusion.8), channel_id=1, source_target_pairs={{0,32},{32,64},{64,96},{96,128},{128,160},{160,192},{192,224},{224... | collective-permute-start | bytes 786440 | tf_op jit(solution)/shard_map/ppermute | solution.py:121
  29.5 1.9 %collective-permute-start.3 = (f32[2,2,64,256]{3,2,1,0:T(8,128)S(1)}, f32[2,2,64,256]{3,2,1,0:T(8,128)S(1)}, u32[]{:S(2)}, u32[]{:S(2)}) collective-permute-start(f32[2,2,64,256]{3,2,1,0:T(8,128)S(1)} %pad_maximum_fusion.7), channel_id=1, source_target_pairs={{32,0},{64,32},{96,64},{128,96},{160,128},{192,160},{224,192},{256... | collective-permute-start | bytes 786440 | tf_op jit(solution)/shard_map/ppermute | solution.py:120
  32.9 2.6 %collective-permute-done.3 = f32[2,2,64,256]{3,2,1,0:T(8,128)S(1)} collective-permute-done((f32[2,2,64,256]{3,2,1,0:T(8,128)S(1)}, f32[2,2,64,256]{3,2,1,0:T(8,128)S(1)}, u32[]{:S(2)}, u32[]{:S(2)}) %collective-permute-start.3) | collective-permute-done | bytes 262176 | tf_op jit(solution)/shard_map/ppermute | solution.py:120
  36.7 7.9 %collective-permute-start.4 = (f32[3,32,32]{2,1,0:T(8,128)S(1)}, f32[3,32,32]{2,1,0:T(8,128)S(1)}, u32[]{:S(2)}, u32[]{:S(2)}) collective-permute-start(f32[3,32,32]{2,1,0:T(8,128)S(1)} %pad_maximum_fusion.9), channel_id=1, source_target_pairs={{0,32},{1,33},{2,34},{3,35},{4,36},{5,37},{6,38},{7,39},{8,40},{9,... | collective-permute-start | bytes 36872 | tf_op jit(solution)/shard_map/ppermute | solution.py:59
  45.5 1.9 %collective-permute-start.5 = (f32[3,32,32]{2,1,0:T(8,128)S(1)}, f32[3,32,32]{2,1,0:T(8,128)S(1)}, u32[]{:S(2)}, u32[]{:S(2)}) collective-permute-start(f32[3,32,32]{2,1,0:T(8,128)S(1)} %fusion.89), channel_id=1, source_target_pairs={{0,16},{1,17},{2,18},{3,19},{4,20},{5,21},{6,22},{7,23},{8,24},{9,... | collective-permute-start | bytes 36872 | tf_op jit(solution)/shard_map/ppermute | solution.py:59
  47.5 4.1 %collective-permute-done.5 = f32[3,32,32]{2,1,0:T(8,128)S(1)} collective-permute-done((f32[3,32,32]{2,1,0:T(8,128)S(1)}, f32[3,32,32]{2,1,0:T(8,128)S(1)}, u32[]{:S(2)}, u32[]{:S(2)}) %collective-permute-start.5) | collective-permute-done | bytes 12320 | tf_op jit(solution)/shard_map/ppermute | solution.py:59
  51.5 5.7 %collective-permute-start.6 = (f32[3,32,32]{2,1,0:T(8,128)S(1)}, f32[3,32,32]{2,1,0:T(8,128)S(1)}, u32[]{:S(2)}, u32[]{:S(2)}) collective-permute-start(f32[3,32,32]{2,1,0:T(8,128)S(1)} %add.151), channel_id=1, source_target_pairs={{0,80},{1,81},{2,82},{3,83},{4,84},{5,85},{6,86},{7,87},{8,88},{9,... | collective-permute-start | bytes 36872 | tf_op jit(solution)/shard_map/ppermute | solution.py:59
  57.2 2.1 %collective-permute-done.6 = f32[3,32,32]{2,1,0:T(8,128)S(1)} collective-permute-done((f32[3,32,32]{2,1,0:T(8,128)S(1)}, f32[3,32,32]{2,1,0:T(8,128)S(1)}, u32[]{:S(2)}, u32[]{:S(2)}) %collective-permute-start.6) | collective-permute-done | bytes 12320 | tf_op jit(solution)/shard_map/ppermute | solution.py:59
  59.3 1.9 %collective-permute-start.7 = (f32[3,32,32]{2,1,0:T(8,128)S(1)}, f32[3,32,32]{2,1,0:T(8,128)S(1)}, u32[]{:S(2)}, u32[]{:S(2)}) collective-permute-start(f32[3,32,32]{2,1,0:T(8,128)S(1)} %add.152), channel_id=1, source_target_pairs={{0,128},{1,129},{2,130},{3,131},{4,132},{5,133},{6,134},{7,135},{8... | collective-permute-start | bytes 36872 | tf_op jit(solution)/shard_map/ppermute | solution.py:59
  61.2 4.1 %collective-permute-done.7 = f32[3,32,32]{2,1,0:T(8,128)S(1)} collective-permute-done((f32[3,32,32]{2,1,0:T(8,128)S(1)}, f32[3,32,32]{2,1,0:T(8,128)S(1)}, u32[]{:S(2)}, u32[]{:S(2)}) %collective-permute-start.7) | collective-permute-done | bytes 12320 | tf_op jit(solution)/shard_map/ppermute | solution.py:59
  65.3 3.5 %collective-permute-start.8 = (f32[3,32,32]{2,1,0:T(8,128)S(1)}, f32[3,32,32]{2,1,0:T(8,128)S(1)}, u32[]{:S(2)}, u32[]{:S(2)}) collective-permute-start(f32[3,32,32]{2,1,0:T(8,128)S(1)} %add.153), channel_id=1, source_target_pairs={{0,384},{1,385},{2,386},{3,387},{4,388},{5,389},{6,390},{7,391},{8... | collective-permute-start | bytes 36872 | tf_op jit(solution)/shard_map/ppermute | solution.py:59
  69.0 3.5 %collective-permute-done.8 = f32[3,32,32]{2,1,0:T(8,128)S(1)} collective-permute-done((f32[3,32,32]{2,1,0:T(8,128)S(1)}, f32[3,32,32]{2,1,0:T(8,128)S(1)}, u32[]{:S(2)}, u32[]{:S(2)}) %collective-permute-start.8) | collective-permute-done | bytes 12320 | tf_op jit(solution)/shard_map/ppermute | solution.py:59
  72.5 1.9 %collective-permute-start.9 = (f32[3,32,32]{2,1,0:T(8,128)S(1)}, f32[3,32,32]{2,1,0:T(8,128)S(1)}, u32[]{:S(2)}, u32[]{:S(2)}) collective-permute-start(f32[3,32,32]{2,1,0:T(8,128)S(1)} %add.154), channel_id=1, source_target_pairs={{0,1},{1,0},{2,3},{3,2},{4,5},{5,4},{6,7},{7,6},{8,9},{9,8},{10,11... | collective-permute-start | bytes 36872 | tf_op jit(solution)/shard_map/ppermute | solution.py:59
  74.5 4.0 %collective-permute-done.9 = f32[3,32,32]{2,1,0:T(8,128)S(1)} collective-permute-done((f32[3,32,32]{2,1,0:T(8,128)S(1)}, f32[3,32,32]{2,1,0:T(8,128)S(1)}, u32[]{:S(2)}, u32[]{:S(2)}) %collective-permute-start.9) | collective-permute-done | bytes 12320 | tf_op jit(solution)/shard_map/ppermute | solution.py:59
  78.5 1.9 %collective-permute-start.10 = (f32[3,32,32]{2,1,0:T(8,128)S(1)}, f32[3,32,32]{2,1,0:T(8,128)S(1)}, u32[]{:S(2)}, u32[]{:S(2)}) collective-permute-start(f32[3,32,32]{2,1,0:T(8,128)S(1)} %add.155), channel_id=1, source_target_pairs={{0,2},{1,3},{2,0},{3,1},{4,6},{5,7},{6,4},{7,5},{8,10},{9,11},{10,... | collective-permute-start | bytes 36872 | tf_op jit(solution)/shard_map/ppermute | solution.py:59
  80.4 4.9 %collective-permute-done.10 = f32[3,32,32]{2,1,0:T(8,128)S(1)} collective-permute-done((f32[3,32,32]{2,1,0:T(8,128)S(1)}, f32[3,32,32]{2,1,0:T(8,128)S(1)}, u32[]{:S(2)}, u32[]{:S(2)}) %collective-permute-start.10) | collective-permute-done | bytes 12320 | tf_op jit(solution)/shard_map/ppermute | solution.py:59
  85.4 6.1 %collective-permute-start.11 = (f32[3,32,32]{2,1,0:T(8,128)S(1)}, f32[3,32,32]{2,1,0:T(8,128)S(1)}, u32[]{:S(2)}, u32[]{:S(2)}) collective-permute-start(f32[3,32,32]{2,1,0:T(8,128)S(1)} %add.156), channel_id=1, source_target_pairs={{0,4},{1,5},{2,6},{3,7},{4,0},{5,1},{6,2},{7,3},{8,12},{9,13},{10,... | collective-permute-start | bytes 36872 | tf_op jit(solution)/shard_map/ppermute | solution.py:59
  91.5 4.3 %collective-permute-done.11 = f32[3,32,32]{2,1,0:T(8,128)S(1)} collective-permute-done((f32[3,32,32]{2,1,0:T(8,128)S(1)}, f32[3,32,32]{2,1,0:T(8,128)S(1)}, u32[]{:S(2)}, u32[]{:S(2)}) %collective-permute-start.11) | collective-permute-done | bytes 12320 | tf_op jit(solution)/shard_map/ppermute | solution.py:59
  95.8 8.2 %collective-permute-start.12 = (f32[3,32,32]{2,1,0:T(8,128)S(1)}, f32[3,32,32]{2,1,0:T(8,128)S(1)}, u32[]{:S(2)}, u32[]{:S(2)}) collective-permute-start(f32[3,32,32]{2,1,0:T(8,128)S(1)} %add.157), channel_id=1, source_target_pairs={{0,12},{1,13},{2,14},{3,15},{4,8},{5,9},{6,10},{7,11},{8,4},{9,5},... | collective-permute-start | bytes 36872 | tf_op jit(solution)/shard_map/ppermute | solution.py:59
  (71 shorter events, 13.3 us)
Async XLA Ops:
  3.5 13.2 %copy-start.2 = (bf16[2,32,1536]{2,1,0:T(8,128)(2,1)S(1)}, bf16[2,32,1536]{2,1,0:T(8,128)(2,1)}, u32[]{:S(2)}) copy-start(bf16[2,32,1536]{2,1,0:T(8,128)(2,1)} %cot_ref.1) | copy-start | bytes 589828
  3.5 13.5 %copy-start.3 = (bf16[3,32,32]{2,1,0:T(8,128)(2,1)S(1)}, bf16[3,32,32]{2,1,0:T(8,128)(2,1)}, u32[]{:S(2)}) copy-start(bf16[3,32,32]{2,1,0:T(8,128)(2,1)} %f_ref.1) | copy-start | bytes 18436
  8.7 8.8 %copy-start.4 = (s32[6,3]{0,1:T(4,128)S(1)}, s32[6,3]{0,1:T(4,128)}, u32[]{:S(2)}) copy-start(s32[6,3]{0,1:T(4,128)} %param.16) | copy-start | bytes 220
  8.8 10.1 %collective-permute-start = (f32[2,2,64,256]{3,2,1,0:T(8,128)S(1)}, f32[2,2,64,256]{3,2,1,0:T(8,128)S(1)}, u32[]{:S(2)}, u32[]{:S(2)}) collective-permute-start(f32[2,2,64,256]{3,2,1,0:T(8,128)S(1)} %pad_maximum_fusion.6), channel_id=1, source_target_pairs={{0,32},{32,64},{64,96},{96,128},{128,160},{160,192},{192,224},{224... | collective-permute-start | bytes 786440 | tf_op jit(solution)/shard_map/ppermute | solution.py:121
  10.7 9.9 %collective-permute-start.1 = (f32[2,2,64,256]{3,2,1,0:T(8,128)S(1)}, f32[2,2,64,256]{3,2,1,0:T(8,128)S(1)}, u32[]{:S(2)}, u32[]{:S(2)}) collective-permute-start(f32[2,2,64,256]{3,2,1,0:T(8,128)S(1)} %pad_maximum_fusion.5), channel_id=1, source_target_pairs={{32,0},{64,32},{96,64},{128,96},{160,128},{192,160},{224,192},{256... | collective-permute-start | bytes 786440 | tf_op jit(solution)/shard_map/ppermute | solution.py:120
  17.0 1.9 %copy-start.1 = (f32[10,64,256]{2,1,0:T(8,128)S(1)}, f32[10,64,256]{2,1,0:T(8,128)}, u32[]{:S(2)}) copy-start(f32[10,64,256]{2,1,0:T(8,128)} %shard_map.76) | copy-start | bytes 1966084
  17.0 1.9 %slice-start = ((f32[10,64,256]{2,1,0:T(8,128)}), f32[6,64,256]{2,1,0:T(8,128)S(1)}, s32[]{:S(2)}) async-start(f32[10,64,256]{2,1,0:T(8,128)} %shard_map.76), calls=%async_computation | async-start | bytes 786432 | tf_op jit(solution)/shard_map/slice | solution.py:164
  17.4 3.3 %copy-start = (bf16[6,3,256,256]{3,2,1,0:T(8,128)(2,1)S(1)}, bf16[6,3,256,256]{3,2,1,0:T(8,128)(2,1)}, u32[]{:S(2)}) copy-start(bf16[6,3,256,256]{3,2,1,0:T(8,128)(2,1)} %tiles_hbm.1) | copy-start | bytes 7077892
  22.6 10.3 %collective-permute-start.2 = (f32[2,2,64,256]{3,2,1,0:T(8,128)S(1)}, f32[2,2,64,256]{3,2,1,0:T(8,128)S(1)}, u32[]{:S(2)}, u32[]{:S(2)}) collective-permute-start(f32[2,2,64,256]{3,2,1,0:T(8,128)S(1)} %pad_maximum_fusion.8), channel_id=1, source_target_pairs={{0,32},{32,64},{64,96},{96,128},{128,160},{160,192},{192,224},{224... | collective-permute-start | bytes 786440 | tf_op jit(solution)/shard_map/ppermute | solution.py:121
  29.5 6.0 %collective-permute-start.3 = (f32[2,2,64,256]{3,2,1,0:T(8,128)S(1)}, f32[2,2,64,256]{3,2,1,0:T(8,128)S(1)}, u32[]{:S(2)}, u32[]{:S(2)}) collective-permute-start(f32[2,2,64,256]{3,2,1,0:T(8,128)S(1)} %pad_maximum_fusion.7), channel_id=1, source_target_pairs={{32,0},{64,32},{96,64},{128,96},{160,128},{192,160},{224,192},{256... | collective-permute-start | bytes 786440 | tf_op jit(solution)/shard_map/ppermute | solution.py:120
  36.7 8.8 %collective-permute-start.4 = (f32[3,32,32]{2,1,0:T(8,128)S(1)}, f32[3,32,32]{2,1,0:T(8,128)S(1)}, u32[]{:S(2)}, u32[]{:S(2)}) collective-permute-start(f32[3,32,32]{2,1,0:T(8,128)S(1)} %pad_maximum_fusion.9), channel_id=1, source_target_pairs={{0,32},{1,33},{2,34},{3,35},{4,36},{5,37},{6,38},{7,39},{8,40},{9,... | collective-permute-start | bytes 36872 | tf_op jit(solution)/shard_map/ppermute | solution.py:59
  45.5 6.0 %collective-permute-start.5 = (f32[3,32,32]{2,1,0:T(8,128)S(1)}, f32[3,32,32]{2,1,0:T(8,128)S(1)}, u32[]{:S(2)}, u32[]{:S(2)}) collective-permute-start(f32[3,32,32]{2,1,0:T(8,128)S(1)} %fusion.89), channel_id=1, source_target_pairs={{0,16},{1,17},{2,18},{3,19},{4,20},{5,21},{6,22},{7,23},{8,24},{9,... | collective-permute-start | bytes 36872 | tf_op jit(solution)/shard_map/ppermute | solution.py:59
  51.5 7.7 %collective-permute-start.6 = (f32[3,32,32]{2,1,0:T(8,128)S(1)}, f32[3,32,32]{2,1,0:T(8,128)S(1)}, u32[]{:S(2)}, u32[]{:S(2)}) collective-permute-start(f32[3,32,32]{2,1,0:T(8,128)S(1)} %add.151), channel_id=1, source_target_pairs={{0,80},{1,81},{2,82},{3,83},{4,84},{5,85},{6,86},{7,87},{8,88},{9,... | collective-permute-start | bytes 36872 | tf_op jit(solution)/shard_map/ppermute | solution.py:59
  59.3 6.0 %collective-permute-start.7 = (f32[3,32,32]{2,1,0:T(8,128)S(1)}, f32[3,32,32]{2,1,0:T(8,128)S(1)}, u32[]{:S(2)}, u32[]{:S(2)}) collective-permute-start(f32[3,32,32]{2,1,0:T(8,128)S(1)} %add.152), channel_id=1, source_target_pairs={{0,128},{1,129},{2,130},{3,131},{4,132},{5,133},{6,134},{7,135},{8... | collective-permute-start | bytes 36872 | tf_op jit(solution)/shard_map/ppermute | solution.py:59
  65.3 7.2 %collective-permute-start.8 = (f32[3,32,32]{2,1,0:T(8,128)S(1)}, f32[3,32,32]{2,1,0:T(8,128)S(1)}, u32[]{:S(2)}, u32[]{:S(2)}) collective-permute-start(f32[3,32,32]{2,1,0:T(8,128)S(1)} %add.153), channel_id=1, source_target_pairs={{0,384},{1,385},{2,386},{3,387},{4,388},{5,389},{6,390},{7,391},{8... | collective-permute-start | bytes 36872 | tf_op jit(solution)/shard_map/ppermute | solution.py:59
  72.5 6.0 %collective-permute-start.9 = (f32[3,32,32]{2,1,0:T(8,128)S(1)}, f32[3,32,32]{2,1,0:T(8,128)S(1)}, u32[]{:S(2)}, u32[]{:S(2)}) collective-permute-start(f32[3,32,32]{2,1,0:T(8,128)S(1)} %add.154), channel_id=1, source_target_pairs={{0,1},{1,0},{2,3},{3,2},{4,5},{5,4},{6,7},{7,6},{8,9},{9,8},{10,11... | collective-permute-start | bytes 36872 | tf_op jit(solution)/shard_map/ppermute | solution.py:59
  78.5 6.9 %collective-permute-start.10 = (f32[3,32,32]{2,1,0:T(8,128)S(1)}, f32[3,32,32]{2,1,0:T(8,128)S(1)}, u32[]{:S(2)}, u32[]{:S(2)}) collective-permute-start(f32[3,32,32]{2,1,0:T(8,128)S(1)} %add.155), channel_id=1, source_target_pairs={{0,2},{1,3},{2,0},{3,1},{4,6},{5,7},{6,4},{7,5},{8,10},{9,11},{10,... | collective-permute-start | bytes 36872 | tf_op jit(solution)/shard_map/ppermute | solution.py:59
  85.4 10.4 %collective-permute-start.11 = (f32[3,32,32]{2,1,0:T(8,128)S(1)}, f32[3,32,32]{2,1,0:T(8,128)S(1)}, u32[]{:S(2)}, u32[]{:S(2)}) collective-permute-start(f32[3,32,32]{2,1,0:T(8,128)S(1)} %add.156), channel_id=1, source_target_pairs={{0,4},{1,5},{2,6},{3,7},{4,0},{5,1},{6,2},{7,3},{8,12},{9,13},{10,... | collective-permute-start | bytes 36872 | tf_op jit(solution)/shard_map/ppermute | solution.py:59
  95.8 10.6 %collective-permute-start.12 = (f32[3,32,32]{2,1,0:T(8,128)S(1)}, f32[3,32,32]{2,1,0:T(8,128)S(1)}, u32[]{:S(2)}, u32[]{:S(2)}) collective-permute-start(f32[3,32,32]{2,1,0:T(8,128)S(1)} %add.157), channel_id=1, source_target_pairs={{0,12},{1,13},{2,14},{3,15},{4,8},{5,9},{6,10},{7,11},{8,4},{9,5},... | collective-permute-start | bytes 36872 | tf_op jit(solution)/shard_map/ppermute | solution.py:59

commit v17 on v12

--- a/solution.py
+++ b/solution.py
@@ -49,7 +49,7 @@
                     d["z"] = (c["z"] + 4) % 16 if g % 2 else (c["z"] - 4) % 16
                 pairs.append((linear(c), linear(d)))
         steps.append(pairs)
-    return steps
+    return steps[-2:] + steps[:-2]
 
 
 def butterfly_sum(x, axes):

time: 108 us -> 107 us (level)
  waiting for transfers between devices: 34.6 us -> 26.3 us
  starting transfers between devices: 55.9 us -> 63.7 us
    ppermute x9, waiting for transfers between devices: 27.7 us -> 19.4 us  [butterfly_sum(): x = x + lax.ppermute(x, axes, pairs)]
    ppermute x9, starting transfers between devices: 39.1 us -> 46.9 us  [butterfly_sum(): x = x + lax.ppermute(x, axes, pairs)]
where the time goes in v17:
time: 107 us; the launch traced here: 106 us
  starting transfers between devices  63.7 us (60%)
  waiting for transfers between devices  26.3 us (25%)
  local copies, waits for them, and re-layouts  5.56 us (5%)
  Pallas kernels  3.73 us (3%)
  matrix products  3.2 us (3%)
  other arithmetic  2.49 us (2%)
    ppermute x9, starting transfers between devices, butterfly_sum(): x = x + lax.ppermute(x, axes, pairs)  46.9 us
    ppermute x9, waiting for transfers between devices, butterfly_sum(): x = x + lax.ppermute(x, axes, pairs)  19.4 us
    ppermute x2, starting transfers between devices, exchange(): from_left = lax.ppermute(edge_right, 'patch', to_right)  8.84 us
    ppermute x2, starting transfers between devices, exchange(): from_right = lax.ppermute(edge_left, 'patch', to_left)  7.97 us
    ppermute x2, waiting for transfers between devices, exchange(): from_right = lax.ppermute(edge_left, 'patch', to_left)  4.37 us
    pallas_call x1, Pallas kernels, first_window(): pl.pallas_call(window_kernel, out_shape=jax.ShapeDtypeStruct((nb + 4, row...  3.73 us
    ppermute x2, waiting for transfers between devices, exchange(): from_left = lax.ppermute(edge_right, 'patch', to_right)  2.49 us
  transfers between devices with their start and end apart: 13, of which 12 were waited for; matrix products, arithmetic and copies ran while one was open for 3% of the time, Pallas kernels for 0%

profile of v17, /device:TPU:24, one launch (start us, length us, event | category | flops | bytes accessed | tf_op | source)
XLA Modules:
  0.0 106.0 jit_solution(10759762452621929326)
XLA Ops:
  3.5 3.7 %shard_map.76 = f32[10,64,256]{2,1,0:T(8,128)} custom-call(s32[6,2]{1,0:T(8,128)} %add_convert_fusion.flags_ref, bf16[2,32,1536]{2,1,0:T(8,128)(2,1)} %cot_ref.1, bf16[3,32,32]{2,1,0:T(8,128)(2,1)} %f_ref.1, bf16[6,3,256,256]{3,2,1,0:T(8,128)(2,1)} %tiles_ref.1), custom_call_target="tpu_custom_call" | custom-call | tf_op jit(solution)/shard_map/pallas_call | solution.py:88
  8.3 1.9 %collective-permute-start = (f32[2,2,64,256]{3,2,1,0:T(8,128)S(1)}, f32[2,2,64,256]{3,2,1,0:T(8,128)S(1)}, u32[]{:S(2)}, u32[]{:S(2)}) collective-permute-start(f32[2,2,64,256]{3,2,1,0:T(8,128)S(1)} %pad_maximum_fusion.6), channel_id=1, source_target_pairs={{0,32},{32,64},{64,96},{96,128},{128,160},{160,192},{192,224},{224... | collective-permute-start | bytes 786440 | tf_op jit(solution)/shard_map/ppermute | solution.py:114
  10.2 6.0 %collective-permute-start.1 = (f32[2,2,64,256]{3,2,1,0:T(8,128)S(1)}, f32[2,2,64,256]{3,2,1,0:T(8,128)S(1)}, u32[]{:S(2)}, u32[]{:S(2)}) collective-permute-start(f32[2,2,64,256]{3,2,1,0:T(8,128)S(1)} %pad_maximum_fusion.5), channel_id=1, source_target_pairs={{32,0},{64,32},{96,64},{128,96},{160,128},{192,160},{224,192},{256... | collective-permute-start | bytes 786440 | tf_op jit(solution)/shard_map/ppermute | solution.py:113
  17.1 1.3 %collective-permute-done = f32[2,2,64,256]{3,2,1,0:T(8,128)S(1)} collective-permute-done((f32[2,2,64,256]{3,2,1,0:T(8,128)S(1)}, f32[2,2,64,256]{3,2,1,0:T(8,128)S(1)}, u32[]{:S(2)}, u32[]{:S(2)}) %collective-permute-start) | collective-permute-done | bytes 262176 | tf_op jit(solution)/shard_map/ppermute | solution.py:114
  18.4 1.7 %collective-permute-done.1 = f32[2,2,64,256]{3,2,1,0:T(8,128)S(1)} collective-permute-done((f32[2,2,64,256]{3,2,1,0:T(8,128)S(1)}, f32[2,2,64,256]{3,2,1,0:T(8,128)S(1)}, u32[]{:S(2)}, u32[]{:S(2)}) %collective-permute-start.1) | collective-permute-done | bytes 262176 | tf_op jit(solution)/shard_map/ppermute | solution.py:113
  22.2 6.9 %collective-permute-start.2 = (f32[2,2,64,256]{3,2,1,0:T(8,128)S(1)}, f32[2,2,64,256]{3,2,1,0:T(8,128)S(1)}, u32[]{:S(2)}, u32[]{:S(2)}) collective-permute-start(f32[2,2,64,256]{3,2,1,0:T(8,128)S(1)} %pad_maximum_fusion.8), channel_id=1, source_target_pairs={{0,32},{32,64},{64,96},{96,128},{128,160},{160,192},{192,224},{224... | collective-permute-start | bytes 786440 | tf_op jit(solution)/shard_map/ppermute | solution.py:114
  29.1 1.9 %collective-permute-start.3 = (f32[2,2,64,256]{3,2,1,0:T(8,128)S(1)}, f32[2,2,64,256]{3,2,1,0:T(8,128)S(1)}, u32[]{:S(2)}, u32[]{:S(2)}) collective-permute-start(f32[2,2,64,256]{3,2,1,0:T(8,128)S(1)} %pad_maximum_fusion.7), channel_id=1, source_target_pairs={{32,0},{64,32},{96,64},{128,96},{160,128},{192,160},{224,192},{256... | collective-permute-start | bytes 786440 | tf_op jit(solution)/shard_map/ppermute | solution.py:113
  32.5 2.6 %collective-permute-done.3 = f32[2,2,64,256]{3,2,1,0:T(8,128)S(1)} collective-permute-done((f32[2,2,64,256]{3,2,1,0:T(8,128)S(1)}, f32[2,2,64,256]{3,2,1,0:T(8,128)S(1)}, u32[]{:S(2)}, u32[]{:S(2)}) %collective-permute-start.3) | collective-permute-done | bytes 262176 | tf_op jit(solution)/shard_map/ppermute | solution.py:113
  36.3 8.2 %collective-permute-start.4 = (f32[3,32,32]{2,1,0:T(8,128)S(1)}, f32[3,32,32]{2,1,0:T(8,128)S(1)}, u32[]{:S(2)}, u32[]{:S(2)}) collective-permute-start(f32[3,32,32]{2,1,0:T(8,128)S(1)} %pad_maximum_fusion.9), channel_id=1, source_target_pairs={{0,4},{1,5},{2,6},{3,7},{4,0},{5,1},{6,2},{7,3},{8,12},{9,13},{10,... | collective-permute-start | bytes 36872 | tf_op jit(solution)/shard_map/ppermute | solution.py:59
  44.5 2.1 %collective-permute-done.4 = f32[3,32,32]{2,1,0:T(8,128)S(1)} collective-permute-done((f32[3,32,32]{2,1,0:T(8,128)S(1)}, f32[3,32,32]{2,1,0:T(8,128)S(1)}, u32[]{:S(2)}, u32[]{:S(2)}) %collective-permute-start.4) | collective-permute-done | bytes 12320 | tf_op jit(solution)/shard_map/ppermute | solution.py:59
  46.5 11.8 %collective-permute-start.5 = (f32[3,32,32]{2,1,0:T(8,128)S(1)}, f32[3,32,32]{2,1,0:T(8,128)S(1)}, u32[]{:S(2)}, u32[]{:S(2)}) collective-permute-start(f32[3,32,32]{2,1,0:T(8,128)S(1)} %fusion.89), channel_id=1, source_target_pairs={{0,12},{1,13},{2,14},{3,15},{4,8},{5,9},{6,10},{7,11},{8,4},{9,5},... | collective-permute-start | bytes 36872 | tf_op jit(solution)/shard_map/ppermute | solution.py:59
  58.3 2.9 %collective-permute-done.5 = f32[3,32,32]{2,1,0:T(8,128)S(1)} collective-permute-done((f32[3,32,32]{2,1,0:T(8,128)S(1)}, f32[3,32,32]{2,1,0:T(8,128)S(1)}, u32[]{:S(2)}, u32[]{:S(2)}) %collective-permute-start.5) | collective-permute-done | bytes 12320 | tf_op jit(solution)/shard_map/ppermute | solution.py:59
  61.2 1.9 %collective-permute-start.6 = (f32[3,32,32]{2,1,0:T(8,128)S(1)}, f32[3,32,32]{2,1,0:T(8,128)S(1)}, u32[]{:S(2)}, u32[]{:S(2)}) collective-permute-start(f32[3,32,32]{2,1,0:T(8,128)S(1)} %add.151), channel_id=1, source_target_pairs={{0,32},{1,33},{2,34},{3,35},{4,36},{5,37},{6,38},{7,39},{8,40},{9,... | collective-permute-start | bytes 36872 | tf_op jit(solution)/shard_map/ppermute | solution.py:59
  64.4 3.2 %collective-permute-start.7 = (f32[3,32,32]{2,1,0:T(8,128)S(1)}, f32[3,32,32]{2,1,0:T(8,128)S(1)}, u32[]{:S(2)}, u32[]{:S(2)}) collective-permute-start(f32[3,32,32]{2,1,0:T(8,128)S(1)} %add.152), channel_id=1, source_target_pairs={{0,16},{1,17},{2,18},{3,19},{4,20},{5,21},{6,22},{7,23},{8,24},{9,... | collective-permute-start | bytes 36872 | tf_op jit(solution)/shard_map/ppermute | solution.py:59
  67.5 2.8 %collective-permute-done.7 = f32[3,32,32]{2,1,0:T(8,128)S(1)} collective-permute-done((f32[3,32,32]{2,1,0:T(8,128)S(1)}, f32[3,32,32]{2,1,0:T(8,128)S(1)}, u32[]{:S(2)}, u32[]{:S(2)}) %collective-permute-start.7) | collective-permute-done | bytes 12320 | tf_op jit(solution)/shard_map/ppermute | solution.py:59
  70.3 5.2 %collective-permute-start.8 = (f32[3,32,32]{2,1,0:T(8,128)S(1)}, f32[3,32,32]{2,1,0:T(8,128)S(1)}, u32[]{:S(2)}, u32[]{:S(2)}) collective-permute-start(f32[3,32,32]{2,1,0:T(8,128)S(1)} %add.153), channel_id=1, source_target_pairs={{0,80},{1,81},{2,82},{3,83},{4,84},{5,85},{6,86},{7,87},{8,88},{9,... | collective-permute-start | bytes 36872 | tf_op jit(solution)/shard_map/ppermute | solution.py:59
  75.7 1.9 %collective-permute-done.8 = f32[3,32,32]{2,1,0:T(8,128)S(1)} collective-permute-done((f32[3,32,32]{2,1,0:T(8,128)S(1)}, f32[3,32,32]{2,1,0:T(8,128)S(1)}, u32[]{:S(2)}, u32[]{:S(2)}) %collective-permute-start.8) | collective-permute-done | bytes 12320 | tf_op jit(solution)/shard_map/ppermute | solution.py:59
  77.6 2.6 %collective-permute-start.9 = (f32[3,32,32]{2,1,0:T(8,128)S(1)}, f32[3,32,32]{2,1,0:T(8,128)S(1)}, u32[]{:S(2)}, u32[]{:S(2)}) collective-permute-start(f32[3,32,32]{2,1,0:T(8,128)S(1)} %add.154), channel_id=1, source_target_pairs={{0,128},{1,129},{2,130},{3,131},{4,132},{5,133},{6,134},{7,135},{8... | collective-permute-start | bytes 36872 | tf_op jit(solution)/shard_map/ppermute | solution.py:59
  80.3 3.3 %collective-permute-done.9 = f32[3,32,32]{2,1,0:T(8,128)S(1)} collective-permute-done((f32[3,32,32]{2,1,0:T(8,128)S(1)}, f32[3,32,32]{2,1,0:T(8,128)S(1)}, u32[]{:S(2)}, u32[]{:S(2)}) %collective-permute-start.9) | collective-permute-done | bytes 12320 | tf_op jit(solution)/shard_map/ppermute | solution.py:59
  83.6 4.6 %collective-permute-start.10 = (f32[3,32,32]{2,1,0:T(8,128)S(1)}, f32[3,32,32]{2,1,0:T(8,128)S(1)}, u32[]{:S(2)}, u32[]{:S(2)}) collective-permute-start(f32[3,32,32]{2,1,0:T(8,128)S(1)} %add.155), channel_id=1, source_target_pairs={{0,384},{1,385},{2,386},{3,387},{4,388},{5,389},{6,390},{7,391},{8... | collective-permute-start | bytes 36872 | tf_op jit(solution)/shard_map/ppermute | solution.py:59
  88.2 2.6 %collective-permute-done.10 = f32[3,32,32]{2,1,0:T(8,128)S(1)} collective-permute-done((f32[3,32,32]{2,1,0:T(8,128)S(1)}, f32[3,32,32]{2,1,0:T(8,128)S(1)}, u32[]{:S(2)}, u32[]{:S(2)}) %collective-permute-start.10) | collective-permute-done | bytes 12320 | tf_op jit(solution)/shard_map/ppermute | solution.py:59
  90.8 3.3 %collective-permute-start.11 = (f32[3,32,32]{2,1,0:T(8,128)S(1)}, f32[3,32,32]{2,1,0:T(8,128)S(1)}, u32[]{:S(2)}, u32[]{:S(2)}) collective-permute-start(f32[3,32,32]{2,1,0:T(8,128)S(1)} %add.156), channel_id=1, source_target_pairs={{0,1},{1,0},{2,3},{3,2},{4,5},{5,4},{6,7},{7,6},{8,9},{9,8},{10,11... | collective-permute-start | bytes 36872 | tf_op jit(solution)/shard_map/ppermute | solution.py:59
  94.2 2.6 %collective-permute-done.11 = f32[3,32,32]{2,1,0:T(8,128)S(1)} collective-permute-done((f32[3,32,32]{2,1,0:T(8,128)S(1)}, f32[3,32,32]{2,1,0:T(8,128)S(1)}, u32[]{:S(2)}, u32[]{:S(2)}) %collective-permute-start.11) | collective-permute-done | bytes 12320 | tf_op jit(solution)/shard_map/ppermute | solution.py:59
  96.8 6.2 %collective-permute-start.12 = (f32[3,32,32]{2,1,0:T(8,128)S(1)}, f32[3,32,32]{2,1,0:T(8,128)S(1)}, u32[]{:S(2)}, u32[]{:S(2)}) collective-permute-start(f32[3,32,32]{2,1,0:T(8,128)S(1)} %add.157), channel_id=1, source_target_pairs={{0,2},{1,3},{2,0},{3,1},{4,6},{5,7},{6,4},{7,5},{8,10},{9,11},{10,... | collective-permute-start | bytes 36872 | tf_op jit(solution)/shard_map/ppermute | solution.py:59
  (71 shorter events, 13.6 us)
Async XLA Ops:
  3.5 12.8 %copy-start.2 = (bf16[2,32,1536]{2,1,0:T(8,128)(2,1)S(1)}, bf16[2,32,1536]{2,1,0:T(8,128)(2,1)}, u32[]{:S(2)}) copy-start(bf16[2,32,1536]{2,1,0:T(8,128)(2,1)} %cot_ref.1) | copy-start | bytes 589828
  3.5 13.1 %copy-start.3 = (bf16[3,32,32]{2,1,0:T(8,128)(2,1)S(1)}, bf16[3,32,32]{2,1,0:T(8,128)(2,1)}, u32[]{:S(2)}) copy-start(bf16[3,32,32]{2,1,0:T(8,128)(2,1)} %f_ref.1) | copy-start | bytes 18436
  8.3 8.8 %copy-start.4 = (s32[6,3]{0,1:T(4,128)S(1)}, s32[6,3]{0,1:T(4,128)}, u32[]{:S(2)}) copy-start(s32[6,3]{0,1:T(4,128)} %param.16) | copy-start | bytes 220
  8.3 10.1 %collective-permute-start = (f32[2,2,64,256]{3,2,1,0:T(8,128)S(1)}, f32[2,2,64,256]{3,2,1,0:T(8,128)S(1)}, u32[]{:S(2)}, u32[]{:S(2)}) collective-permute-start(f32[2,2,64,256]{3,2,1,0:T(8,128)S(1)} %pad_maximum_fusion.6), channel_id=1, source_target_pairs={{0,32},{32,64},{64,96},{96,128},{128,160},{160,192},{192,224},{224... | collective-permute-start | bytes 786440 | tf_op jit(solution)/shard_map/ppermute | solution.py:114
  10.2 9.9 %collective-permute-start.1 = (f32[2,2,64,256]{3,2,1,0:T(8,128)S(1)}, f32[2,2,64,256]{3,2,1,0:T(8,128)S(1)}, u32[]{:S(2)}, u32[]{:S(2)}) collective-permute-start(f32[2,2,64,256]{3,2,1,0:T(8,128)S(1)} %pad_maximum_fusion.5), channel_id=1, source_target_pairs={{32,0},{64,32},{96,64},{128,96},{160,128},{192,160},{224,192},{256... | collective-permute-start | bytes 786440 | tf_op jit(solution)/shard_map/ppermute | solution.py:113
  16.5 1.9 %copy-start.1 = (f32[10,64,256]{2,1,0:T(8,128)S(1)}, f32[10,64,256]{2,1,0:T(8,128)}, u32[]{:S(2)}) copy-start(f32[10,64,256]{2,1,0:T(8,128)} %shard_map.76) | copy-start | bytes 1966084
  16.6 1.9 %slice-start = ((f32[10,64,256]{2,1,0:T(8,128)}), f32[6,64,256]{2,1,0:T(8,128)S(1)}, s32[]{:S(2)}) async-start(f32[10,64,256]{2,1,0:T(8,128)} %shard_map.76), calls=%async_computation | async-start | bytes 786432 | tf_op jit(solution)/shard_map/slice | solution.py:157
  16.9 3.3 %copy-start = (bf16[6,3,256,256]{3,2,1,0:T(8,128)(2,1)S(1)}, bf16[6,3,256,256]{3,2,1,0:T(8,128)(2,1)}, u32[]{:S(2)}) copy-start(bf16[6,3,256,256]{3,2,1,0:T(8,128)(2,1)} %tiles_ref.1) | copy-start | bytes 7077892
  22.2 10.3 %collective-permute-start.2 = (f32[2,2,64,256]{3,2,1,0:T(8,128)S(1)}, f32[2,2,64,256]{3,2,1,0:T(8,128)S(1)}, u32[]{:S(2)}, u32[]{:S(2)}) collective-permute-start(f32[2,2,64,256]{3,2,1,0:T(8,128)S(1)} %pad_maximum_fusion.8), channel_id=1, source_target_pairs={{0,32},{32,64},{64,96},{96,128},{128,160},{160,192},{192,224},{224... | collective-permute-start | bytes 786440 | tf_op jit(solution)/shard_map/ppermute | solution.py:114
  29.1 6.0 %collective-permute-start.3 = (f32[2,2,64,256]{3,2,1,0:T(8,128)S(1)}, f32[2,2,64,256]{3,2,1,0:T(8,128)S(1)}, u32[]{:S(2)}, u32[]{:S(2)}) collective-permute-start(f32[2,2,64,256]{3,2,1,0:T(8,128)S(1)} %pad_maximum_fusion.7), channel_id=1, source_target_pairs={{32,0},{64,32},{96,64},{128,96},{160,128},{192,160},{224,192},{256... | collective-permute-start | bytes 786440 | tf_op jit(solution)/shard_map/ppermute | solution.py:113
  36.3 10.3 %collective-permute-start.4 = (f32[3,32,32]{2,1,0:T(8,128)S(1)}, f32[3,32,32]{2,1,0:T(8,128)S(1)}, u32[]{:S(2)}, u32[]{:S(2)}) collective-permute-start(f32[3,32,32]{2,1,0:T(8,128)S(1)} %pad_maximum_fusion.9), channel_id=1, source_target_pairs={{0,4},{1,5},{2,6},{3,7},{4,0},{5,1},{6,2},{7,3},{8,12},{9,13},{10,... | collective-permute-start | bytes 36872 | tf_op jit(solution)/shard_map/ppermute | solution.py:59
  46.5 14.7 %collective-permute-start.5 = (f32[3,32,32]{2,1,0:T(8,128)S(1)}, f32[3,32,32]{2,1,0:T(8,128)S(1)}, u32[]{:S(2)}, u32[]{:S(2)}) collective-permute-start(f32[3,32,32]{2,1,0:T(8,128)S(1)} %fusion.89), channel_id=1, source_target_pairs={{0,12},{1,13},{2,14},{3,15},{4,8},{5,9},{6,10},{7,11},{8,4},{9,5},... | collective-permute-start | bytes 36872 | tf_op jit(solution)/shard_map/ppermute | solution.py:59
  61.2 3.1 %collective-permute-start.6 = (f32[3,32,32]{2,1,0:T(8,128)S(1)}, f32[3,32,32]{2,1,0:T(8,128)S(1)}, u32[]{:S(2)}, u32[]{:S(2)}) collective-permute-start(f32[3,32,32]{2,1,0:T(8,128)S(1)} %add.151), channel_id=1, source_target_pairs={{0,32},{1,33},{2,34},{3,35},{4,36},{5,37},{6,38},{7,39},{8,40},{9,... | collective-permute-start | bytes 36872 | tf_op jit(solution)/shard_map/ppermute | solution.py:59
  64.4 6.0 %collective-permute-start.7 = (f32[3,32,32]{2,1,0:T(8,128)S(1)}, f32[3,32,32]{2,1,0:T(8,128)S(1)}, u32[]{:S(2)}, u32[]{:S(2)}) collective-permute-start(f32[3,32,32]{2,1,0:T(8,128)S(1)} %add.152), channel_id=1, source_target_pairs={{0,16},{1,17},{2,18},{3,19},{4,20},{5,21},{6,22},{7,23},{8,24},{9,... | collective-permute-start | bytes 36872 | tf_op jit(solution)/shard_map/ppermute | solution.py:59
  70.3 7.2 %collective-permute-start.8 = (f32[3,32,32]{2,1,0:T(8,128)S(1)}, f32[3,32,32]{2,1,0:T(8,128)S(1)}, u32[]{:S(2)}, u32[]{:S(2)}) collective-permute-start(f32[3,32,32]{2,1,0:T(8,128)S(1)} %add.153), channel_id=1, source_target_pairs={{0,80},{1,81},{2,82},{3,83},{4,84},{5,85},{6,86},{7,87},{8,88},{9,... | collective-permute-start | bytes 36872 | tf_op jit(solution)/shard_map/ppermute | solution.py:59
  77.6 6.0 %collective-permute-start.9 = (f32[3,32,32]{2,1,0:T(8,128)S(1)}, f32[3,32,32]{2,1,0:T(8,128)S(1)}, u32[]{:S(2)}, u32[]{:S(2)}) collective-permute-start(f32[3,32,32]{2,1,0:T(8,128)S(1)} %add.154), channel_id=1, source_target_pairs={{0,128},{1,129},{2,130},{3,131},{4,132},{5,133},{6,134},{7,135},{8... | collective-permute-start | bytes 36872 | tf_op jit(solution)/shard_map/ppermute | solution.py:59
  83.6 7.2 %collective-permute-start.10 = (f32[3,32,32]{2,1,0:T(8,128)S(1)}, f32[3,32,32]{2,1,0:T(8,128)S(1)}, u32[]{:S(2)}, u32[]{:S(2)}) collective-permute-start(f32[3,32,32]{2,1,0:T(8,128)S(1)} %add.155), channel_id=1, source_target_pairs={{0,384},{1,385},{2,386},{3,387},{4,388},{5,389},{6,390},{7,391},{8... | collective-permute-start | bytes 36872 | tf_op jit(solution)/shard_map/ppermute | solution.py:59
  90.8 6.0 %collective-permute-start.11 = (f32[3,32,32]{2,1,0:T(8,128)S(1)}, f32[3,32,32]{2,1,0:T(8,128)S(1)}, u32[]{:S(2)}, u32[]{:S(2)}) collective-permute-start(f32[3,32,32]{2,1,0:T(8,128)S(1)} %add.156), channel_id=1, source_target_pairs={{0,1},{1,0},{2,3},{3,2},{4,5},{5,4},{6,7},{7,6},{8,9},{9,8},{10,11... | collective-permute-start | bytes 36872 | tf_op jit(solution)/shard_map/ppermute | solution.py:59
  96.8 8.6 %collective-permute-start.12 = (f32[3,32,32]{2,1,0:T(8,128)S(1)}, f32[3,32,32]{2,1,0:T(8,128)S(1)}, u32[]{:S(2)}, u32[]{:S(2)}) collective-permute-start(f32[3,32,32]{2,1,0:T(8,128)S(1)} %add.157), channel_id=1, source_target_pairs={{0,2},{1,3},{2,0},{3,1},{4,6},{5,7},{6,4},{7,5},{8,10},{9,11},{10,... | collective-permute-start | bytes 36872 | tf_op jit(solution)/shard_map/ppermute | solution.py:59

commit v18 on v17

--- a/solution.py
+++ b/solution.py
@@ -49,7 +49,7 @@
                     d["z"] = (c["z"] + 4) % 16 if g % 2 else (c["z"] - 4) % 16
                 pairs.append((linear(c), linear(d)))
         steps.append(pairs)
-    return steps[-2:] + steps[:-2]
+    return [steps[i] for i in (7, 8, 6, 2, 4, 1, 3, 5, 0)]
 
 
 def butterfly_sum(x, axes):

time: 107 us -> 110 us (1.028)
  the two profiles are of different devices: /device:TPU:24 before, /device:TPU:1 now
where the time goes in v18:
time: 110 us
  starting transfers between devices  70.9 us (64%)
  waiting for transfers between devices  21.9 us (20%)
  local copies, waits for them, and re-layouts  6.22 us (6%)
  Pallas kernels  3.74 us (3%)
  matrix products  3.2 us (3%)
  other arithmetic  2.49 us (2%)
    ppermute x9, starting transfers between devices, butterfly_sum(): x = x + lax.ppermute(x, axes, pairs)  51.1 us
    ppermute x9, waiting for transfers between devices, butterfly_sum(): x = x + lax.ppermute(x, axes, pairs)  16.8 us
    ppermute x2, starting transfers between devices, exchange(): from_right = lax.ppermute(edge_left, 'patch', to_left)  11.9 us
    ppermute x2, starting transfers between devices, exchange(): from_left = lax.ppermute(edge_right, 'patch', to_right)  7.96 us
    ppermute x2, waiting for transfers between devices, exchange(): from_right = lax.ppermute(edge_left, 'patch', to_left)  5.05 us
    pallas_call x1, Pallas kernels, first_window(): pl.pallas_call(window_kernel, out_shape=jax.ShapeDtypeStruct((nb + 4, row...  3.74 us
  transfers between devices with their start and end apart: 13, of which 10 were waited for; matrix products, arithmetic and copies ran while one was open for 3% of the time, Pallas kernels for 0%

profile of v18, /device:TPU:1, one launch (start us, length us, event | category | flops | bytes accessed | tf_op | source)
XLA Modules:
  0.0 109.5 jit_solution(4643781075458227918)
XLA Ops:
  3.5 3.7 %shard_map.76 = f32[10,64,256]{2,1,0:T(8,128)} custom-call(s32[6,2]{1,0:T(8,128)} %add_convert_fusion.flags_ref, bf16[2,32,1536]{2,1,0:T(8,128)(2,1)} %cot_ref.1, bf16[3,32,32]{2,1,0:T(8,128)(2,1)} %f_ref.1, bf16[6,3,256,256]{3,2,1,0:T(8,128)(2,1)} %tiles_ref.1), custom_call_target="tpu_custom_call" | custom-call | tf_op jit(solution)/shard_map/pallas_call | solution.py:88
  8.3 6.0 %collective-permute-start = (f32[2,2,64,256]{3,2,1,0:T(8,128)S(1)}, f32[2,2,64,256]{3,2,1,0:T(8,128)S(1)}, u32[]{:S(2)}, u32[]{:S(2)}) collective-permute-start(f32[2,2,64,256]{3,2,1,0:T(8,128)S(1)} %pad_maximum_fusion.6), channel_id=1, source_target_pairs={{0,32},{32,64},{64,96},{96,128},{128,160},{160,192},{192,224},{224... | collective-permute-start | bytes 786440 | tf_op jit(solution)/shard_map/ppermute | solution.py:114
  14.4 4.7 %collective-permute-start.1 = (f32[2,2,64,256]{3,2,1,0:T(8,128)S(1)}, f32[2,2,64,256]{3,2,1,0:T(8,128)S(1)}, u32[]{:S(2)}, u32[]{:S(2)}) collective-permute-start(f32[2,2,64,256]{3,2,1,0:T(8,128)S(1)} %pad_maximum_fusion.5), channel_id=1, source_target_pairs={{32,0},{64,32},{96,64},{128,96},{160,128},{192,160},{224,192},{256... | collective-permute-start | bytes 786440 | tf_op jit(solution)/shard_map/ppermute | solution.py:113
  20.5 3.4 %collective-permute-done.1 = f32[2,2,64,256]{3,2,1,0:T(8,128)S(1)} collective-permute-done((f32[2,2,64,256]{3,2,1,0:T(8,128)S(1)}, f32[2,2,64,256]{3,2,1,0:T(8,128)S(1)}, u32[]{:S(2)}, u32[]{:S(2)}) %collective-permute-start.1) | collective-permute-done | bytes 262176 | tf_op jit(solution)/shard_map/ppermute | solution.py:113
  25.9 1.9 %collective-permute-start.2 = (f32[2,2,64,256]{3,2,1,0:T(8,128)S(1)}, f32[2,2,64,256]{3,2,1,0:T(8,128)S(1)}, u32[]{:S(2)}, u32[]{:S(2)}) collective-permute-start(f32[2,2,64,256]{3,2,1,0:T(8,128)S(1)} %pad_maximum_fusion.8), channel_id=1, source_target_pairs={{0,32},{32,64},{64,96},{96,128},{128,160},{160,192},{192,224},{224... | collective-permute-start | bytes 786440 | tf_op jit(solution)/shard_map/ppermute | solution.py:114
  27.8 7.2 %collective-permute-start.3 = (f32[2,2,64,256]{3,2,1,0:T(8,128)S(1)}, f32[2,2,64,256]{3,2,1,0:T(8,128)S(1)}, u32[]{:S(2)}, u32[]{:S(2)}) collective-permute-start(f32[2,2,64,256]{3,2,1,0:T(8,128)S(1)} %pad_maximum_fusion.7), channel_id=1, source_target_pairs={{32,0},{64,32},{96,64},{128,96},{160,128},{192,160},{224,192},{256... | collective-permute-start | bytes 786440 | tf_op jit(solution)/shard_map/ppermute | solution.py:113
  35.3 1.7 %collective-permute-done.3 = f32[2,2,64,256]{3,2,1,0:T(8,128)S(1)} collective-permute-done((f32[2,2,64,256]{3,2,1,0:T(8,128)S(1)}, f32[2,2,64,256]{3,2,1,0:T(8,128)S(1)}, u32[]{:S(2)}, u32[]{:S(2)}) %collective-permute-start.3) | collective-permute-done | bytes 262176 | tf_op jit(solution)/shard_map/ppermute | solution.py:113
  38.2 8.5 %collective-permute-start.4 = (f32[3,32,32]{2,1,0:T(8,128)S(1)}, f32[3,32,32]{2,1,0:T(8,128)S(1)}, u32[]{:S(2)}, u32[]{:S(2)}) collective-permute-start(f32[3,32,32]{2,1,0:T(8,128)S(1)} %pad_maximum_fusion.9), channel_id=1, source_target_pairs={{0,4},{1,5},{2,6},{3,7},{4,0},{5,1},{6,2},{7,3},{8,12},{9,13},{10,... | collective-permute-start | bytes 36872 | tf_op jit(solution)/shard_map/ppermute | solution.py:59
  46.7 1.5 %collective-permute-done.4 = f32[3,32,32]{2,1,0:T(8,128)S(1)} collective-permute-done((f32[3,32,32]{2,1,0:T(8,128)S(1)}, f32[3,32,32]{2,1,0:T(8,128)S(1)}, u32[]{:S(2)}, u32[]{:S(2)}) %collective-permute-start.4) | collective-permute-done | bytes 12320 | tf_op jit(solution)/shard_map/ppermute | solution.py:59
  48.2 11.2 %collective-permute-start.5 = (f32[3,32,32]{2,1,0:T(8,128)S(1)}, f32[3,32,32]{2,1,0:T(8,128)S(1)}, u32[]{:S(2)}, u32[]{:S(2)}) collective-permute-start(f32[3,32,32]{2,1,0:T(8,128)S(1)} %fusion.89), channel_id=1, source_target_pairs={{0,12},{1,13},{2,14},{3,15},{4,8},{5,9},{6,10},{7,11},{8,4},{9,5},... | collective-permute-start | bytes 36872 | tf_op jit(solution)/shard_map/ppermute | solution.py:59
  59.3 1.6 %collective-permute-done.5 = f32[3,32,32]{2,1,0:T(8,128)S(1)} collective-permute-done((f32[3,32,32]{2,1,0:T(8,128)S(1)}, f32[3,32,32]{2,1,0:T(8,128)S(1)}, u32[]{:S(2)}, u32[]{:S(2)}) %collective-permute-start.5) | collective-permute-done | bytes 12320 | tf_op jit(solution)/shard_map/ppermute | solution.py:59
  60.9 2.9 %collective-permute-start.6 = (f32[3,32,32]{2,1,0:T(8,128)S(1)}, f32[3,32,32]{2,1,0:T(8,128)S(1)}, u32[]{:S(2)}, u32[]{:S(2)}) collective-permute-start(f32[3,32,32]{2,1,0:T(8,128)S(1)} %add.151), channel_id=1, source_target_pairs={{0,2},{1,3},{2,0},{3,1},{4,6},{5,7},{6,4},{7,5},{8,10},{9,11},{10,... | collective-permute-start | bytes 36872 | tf_op jit(solution)/shard_map/ppermute | solution.py:59
  63.9 3.8 %collective-permute-done.6 = f32[3,32,32]{2,1,0:T(8,128)S(1)} collective-permute-done((f32[3,32,32]{2,1,0:T(8,128)S(1)}, f32[3,32,32]{2,1,0:T(8,128)S(1)}, u32[]{:S(2)}, u32[]{:S(2)}) %collective-permute-start.6) | collective-permute-done | bytes 12320 | tf_op jit(solution)/shard_map/ppermute | solution.py:59
  67.7 5.7 %collective-permute-start.7 = (f32[3,32,32]{2,1,0:T(8,128)S(1)}, f32[3,32,32]{2,1,0:T(8,128)S(1)}, u32[]{:S(2)}, u32[]{:S(2)}) collective-permute-start(f32[3,32,32]{2,1,0:T(8,128)S(1)} %add.152), channel_id=1, source_target_pairs={{0,80},{1,81},{2,82},{3,83},{4,84},{5,85},{6,86},{7,87},{8,88},{9,... | collective-permute-start | bytes 36872 | tf_op jit(solution)/shard_map/ppermute | solution.py:59
  73.4 1.5 %collective-permute-done.7 = f32[3,32,32]{2,1,0:T(8,128)S(1)} collective-permute-done((f32[3,32,32]{2,1,0:T(8,128)S(1)}, f32[3,32,32]{2,1,0:T(8,128)S(1)}, u32[]{:S(2)}, u32[]{:S(2)}) %collective-permute-start.7) | collective-permute-done | bytes 12320 | tf_op jit(solution)/shard_map/ppermute | solution.py:59
  74.9 5.0 %collective-permute-start.8 = (f32[3,32,32]{2,1,0:T(8,128)S(1)}, f32[3,32,32]{2,1,0:T(8,128)S(1)}, u32[]{:S(2)}, u32[]{:S(2)}) collective-permute-start(f32[3,32,32]{2,1,0:T(8,128)S(1)} %add.153), channel_id=1, source_target_pairs={{0,384},{1,385},{2,386},{3,387},{4,388},{5,389},{6,390},{7,391},{8... | collective-permute-start | bytes 36872 | tf_op jit(solution)/shard_map/ppermute | solution.py:59
  80.0 1.3 %collective-permute-done.8 = f32[3,32,32]{2,1,0:T(8,128)S(1)} collective-permute-done((f32[3,32,32]{2,1,0:T(8,128)S(1)}, f32[3,32,32]{2,1,0:T(8,128)S(1)}, u32[]{:S(2)}, u32[]{:S(2)}) %collective-permute-start.8) | collective-permute-done | bytes 12320 | tf_op jit(solution)/shard_map/ppermute | solution.py:59
  81.3 1.9 %collective-permute-start.9 = (f32[3,32,32]{2,1,0:T(8,128)S(1)}, f32[3,32,32]{2,1,0:T(8,128)S(1)}, u32[]{:S(2)}, u32[]{:S(2)}) collective-permute-start(f32[3,32,32]{2,1,0:T(8,128)S(1)} %add.154), channel_id=1, source_target_pairs={{0,16},{1,17},{2,18},{3,19},{4,20},{5,21},{6,22},{7,23},{8,24},{9,... | collective-permute-start | bytes 36872 | tf_op jit(solution)/shard_map/ppermute | solution.py:59
  83.3 2.9 %collective-permute-done.9 = f32[3,32,32]{2,1,0:T(8,128)S(1)} collective-permute-done((f32[3,32,32]{2,1,0:T(8,128)S(1)}, f32[3,32,32]{2,1,0:T(8,128)S(1)}, u32[]{:S(2)}, u32[]{:S(2)}) %collective-permute-start.9) | collective-permute-done | bytes 12320 | tf_op jit(solution)/shard_map/ppermute | solution.py:59
  86.3 1.9 %collective-permute-start.10 = (f32[3,32,32]{2,1,0:T(8,128)S(1)}, f32[3,32,32]{2,1,0:T(8,128)S(1)}, u32[]{:S(2)}, u32[]{:S(2)}) collective-permute-start(f32[3,32,32]{2,1,0:T(8,128)S(1)} %add.155), channel_id=1, source_target_pairs={{0,128},{1,129},{2,130},{3,131},{4,132},{5,133},{6,134},{7,135},{8... | collective-permute-start | bytes 36872 | tf_op jit(solution)/shard_map/ppermute | solution.py:59
  88.2 2.9 %collective-permute-done.10 = f32[3,32,32]{2,1,0:T(8,128)S(1)} collective-permute-done((f32[3,32,32]{2,1,0:T(8,128)S(1)}, f32[3,32,32]{2,1,0:T(8,128)S(1)}, u32[]{:S(2)}, u32[]{:S(2)}) %collective-permute-start.10) | collective-permute-done | bytes 12320 | tf_op jit(solution)/shard_map/ppermute | solution.py:59
  91.1 4.0 %collective-permute-start.11 = (f32[3,32,32]{2,1,0:T(8,128)S(1)}, f32[3,32,32]{2,1,0:T(8,128)S(1)}, u32[]{:S(2)}, u32[]{:S(2)}) collective-permute-start(f32[3,32,32]{2,1,0:T(8,128)S(1)} %add.156), channel_id=1, source_target_pairs={{0,1},{1,0},{2,3},{3,2},{4,5},{5,4},{6,7},{7,6},{8,9},{9,8},{10,11... | collective-permute-start | bytes 36872 | tf_op jit(solution)/shard_map/ppermute | solution.py:59
  95.1 1.4 %collective-permute-done.11 = f32[3,32,32]{2,1,0:T(8,128)S(1)} collective-permute-done((f32[3,32,32]{2,1,0:T(8,128)S(1)}, f32[3,32,32]{2,1,0:T(8,128)S(1)}, u32[]{:S(2)}, u32[]{:S(2)}) %collective-permute-start.11) | collective-permute-done | bytes 12320 | tf_op jit(solution)/shard_map/ppermute | solution.py:59
  96.5 10.0 %collective-permute-start.12 = (f32[3,32,32]{2,1,0:T(8,128)S(1)}, f32[3,32,32]{2,1,0:T(8,128)S(1)}, u32[]{:S(2)}, u32[]{:S(2)}) collective-permute-start(f32[3,32,32]{2,1,0:T(8,128)S(1)} %add.157), channel_id=1, source_target_pairs={{0,32},{1,33},{2,34},{3,35},{4,36},{5,37},{6,38},{7,39},{8,40},{9,... | collective-permute-start | bytes 36872 | tf_op jit(solution)/shard_map/ppermute | solution.py:59
  (71 shorter events, 11.9 us)
Async XLA Ops:
  3.5 15.5 %copy-start.2 = (bf16[2,32,1536]{2,1,0:T(8,128)(2,1)S(1)}, bf16[2,32,1536]{2,1,0:T(8,128)(2,1)}, u32[]{:S(2)}) copy-start(bf16[2,32,1536]{2,1,0:T(8,128)(2,1)} %cot_ref.1) | copy-start | bytes 589828
  3.5 15.8 %copy-start.3 = (bf16[3,32,32]{2,1,0:T(8,128)(2,1)S(1)}, bf16[3,32,32]{2,1,0:T(8,128)(2,1)}, u32[]{:S(2)}) copy-start(bf16[3,32,32]{2,1,0:T(8,128)(2,1)} %f_ref.1) | copy-start | bytes 18436
  8.3 11.5 %copy-start.4 = (s32[6,3]{0,1:T(4,128)S(1)}, s32[6,3]{0,1:T(4,128)}, u32[]{:S(2)}) copy-start(s32[6,3]{0,1:T(4,128)} %param.16) | copy-start | bytes 220
  8.3 11.5 %collective-permute-start = (f32[2,2,64,256]{3,2,1,0:T(8,128)S(1)}, f32[2,2,64,256]{3,2,1,0:T(8,128)S(1)}, u32[]{:S(2)}, u32[]{:S(2)}) collective-permute-start(f32[2,2,64,256]{3,2,1,0:T(8,128)S(1)} %pad_maximum_fusion.6), channel_id=1, source_target_pairs={{0,32},{32,64},{64,96},{96,128},{128,160},{160,192},{192,224},{224... | collective-permute-start | bytes 786440 | tf_op jit(solution)/shard_map/ppermute | solution.py:114
  14.4 9.5 %collective-permute-start.1 = (f32[2,2,64,256]{3,2,1,0:T(8,128)S(1)}, f32[2,2,64,256]{3,2,1,0:T(8,128)S(1)}, u32[]{:S(2)}, u32[]{:S(2)}) collective-permute-start(f32[2,2,64,256]{3,2,1,0:T(8,128)S(1)} %pad_maximum_fusion.5), channel_id=1, source_target_pairs={{32,0},{64,32},{96,64},{128,96},{160,128},{192,160},{224,192},{256... | collective-permute-start | bytes 786440 | tf_op jit(solution)/shard_map/ppermute | solution.py:113
  19.3 1.1 copy-start.1
  19.3 1.2 %slice-start = ((f32[10,64,256]{2,1,0:T(8,128)}), f32[6,64,256]{2,1,0:T(8,128)S(1)}, s32[]{:S(2)}) async-start(f32[10,64,256]{2,1,0:T(8,128)} %shard_map.76), calls=%async_computation | async-start | bytes 786432 | tf_op jit(solution)/shard_map/slice | solution.py:157
  19.7 4.3 %copy-start = (bf16[6,3,256,256]{3,2,1,0:T(8,128)(2,1)S(1)}, bf16[6,3,256,256]{3,2,1,0:T(8,128)(2,1)}, u32[]{:S(2)}) copy-start(bf16[6,3,256,256]{3,2,1,0:T(8,128)(2,1)} %tiles_ref.1) | copy-start | bytes 7077892
  25.9 9.4 %collective-permute-start.2 = (f32[2,2,64,256]{3,2,1,0:T(8,128)S(1)}, f32[2,2,64,256]{3,2,1,0:T(8,128)S(1)}, u32[]{:S(2)}, u32[]{:S(2)}) collective-permute-start(f32[2,2,64,256]{3,2,1,0:T(8,128)S(1)} %pad_maximum_fusion.8), channel_id=1, source_target_pairs={{0,32},{32,64},{64,96},{96,128},{128,160},{160,192},{192,224},{224... | collective-permute-start | bytes 786440 | tf_op jit(solution)/shard_map/ppermute | solution.py:114
  27.8 9.2 %collective-permute-start.3 = (f32[2,2,64,256]{3,2,1,0:T(8,128)S(1)}, f32[2,2,64,256]{3,2,1,0:T(8,128)S(1)}, u32[]{:S(2)}, u32[]{:S(2)}) collective-permute-start(f32[2,2,64,256]{3,2,1,0:T(8,128)S(1)} %pad_maximum_fusion.7), channel_id=1, source_target_pairs={{32,0},{64,32},{96,64},{128,96},{160,128},{192,160},{224,192},{256... | collective-permute-start | bytes 786440 | tf_op jit(solution)/shard_map/ppermute | solution.py:113
  38.2 10.0 %collective-permute-start.4 = (f32[3,32,32]{2,1,0:T(8,128)S(1)}, f32[3,32,32]{2,1,0:T(8,128)S(1)}, u32[]{:S(2)}, u32[]{:S(2)}) collective-permute-start(f32[3,32,32]{2,1,0:T(8,128)S(1)} %pad_maximum_fusion.9), channel_id=1, source_target_pairs={{0,4},{1,5},{2,6},{3,7},{4,0},{5,1},{6,2},{7,3},{8,12},{9,13},{10,... | collective-permute-start | bytes 36872 | tf_op jit(solution)/shard_map/ppermute | solution.py:59
  48.2 12.7 %collective-permute-start.5 = (f32[3,32,32]{2,1,0:T(8,128)S(1)}, f32[3,32,32]{2,1,0:T(8,128)S(1)}, u32[]{:S(2)}, u32[]{:S(2)}) collective-permute-start(f32[3,32,32]{2,1,0:T(8,128)S(1)} %fusion.89), channel_id=1, source_target_pairs={{0,12},{1,13},{2,14},{3,15},{4,8},{5,9},{6,10},{7,11},{8,4},{9,5},... | collective-permute-start | bytes 36872 | tf_op jit(solution)/shard_map/ppermute | solution.py:59
  60.9 6.8 %collective-permute-start.6 = (f32[3,32,32]{2,1,0:T(8,128)S(1)}, f32[3,32,32]{2,1,0:T(8,128)S(1)}, u32[]{:S(2)}, u32[]{:S(2)}) collective-permute-start(f32[3,32,32]{2,1,0:T(8,128)S(1)} %add.151), channel_id=1, source_target_pairs={{0,2},{1,3},{2,0},{3,1},{4,6},{5,7},{6,4},{7,5},{8,10},{9,11},{10,... | collective-permute-start | bytes 36872 | tf_op jit(solution)/shard_map/ppermute | solution.py:59
  67.7 7.1 %collective-permute-start.7 = (f32[3,32,32]{2,1,0:T(8,128)S(1)}, f32[3,32,32]{2,1,0:T(8,128)S(1)}, u32[]{:S(2)}, u32[]{:S(2)}) collective-permute-start(f32[3,32,32]{2,1,0:T(8,128)S(1)} %add.152), channel_id=1, source_target_pairs={{0,80},{1,81},{2,82},{3,83},{4,84},{5,85},{6,86},{7,87},{8,88},{9,... | collective-permute-start | bytes 36872 | tf_op jit(solution)/shard_map/ppermute | solution.py:59
  74.9 6.5 %collective-permute-start.8 = (f32[3,32,32]{2,1,0:T(8,128)S(1)}, f32[3,32,32]{2,1,0:T(8,128)S(1)}, u32[]{:S(2)}, u32[]{:S(2)}) collective-permute-start(f32[3,32,32]{2,1,0:T(8,128)S(1)} %add.153), channel_id=1, source_target_pairs={{0,384},{1,385},{2,386},{3,387},{4,388},{5,389},{6,390},{7,391},{8... | collective-permute-start | bytes 36872 | tf_op jit(solution)/shard_map/ppermute | solution.py:59
  81.3 4.9 %collective-permute-start.9 = (f32[3,32,32]{2,1,0:T(8,128)S(1)}, f32[3,32,32]{2,1,0:T(8,128)S(1)}, u32[]{:S(2)}, u32[]{:S(2)}) collective-permute-start(f32[3,32,32]{2,1,0:T(8,128)S(1)} %add.154), channel_id=1, source_target_pairs={{0,16},{1,17},{2,18},{3,19},{4,20},{5,21},{6,22},{7,23},{8,24},{9,... | collective-permute-start | bytes 36872 | tf_op jit(solution)/shard_map/ppermute | solution.py:59
  86.3 4.8 %collective-permute-start.10 = (f32[3,32,32]{2,1,0:T(8,128)S(1)}, f32[3,32,32]{2,1,0:T(8,128)S(1)}, u32[]{:S(2)}, u32[]{:S(2)}) collective-permute-start(f32[3,32,32]{2,1,0:T(8,128)S(1)} %add.155), channel_id=1, source_target_pairs={{0,128},{1,129},{2,130},{3,131},{4,132},{5,133},{6,134},{7,135},{8... | collective-permute-start | bytes 36872 | tf_op jit(solution)/shard_map/ppermute | solution.py:59
  91.1 5.4 %collective-permute-start.11 = (f32[3,32,32]{2,1,0:T(8,128)S(1)}, f32[3,32,32]{2,1,0:T(8,128)S(1)}, u32[]{:S(2)}, u32[]{:S(2)}) collective-permute-start(f32[3,32,32]{2,1,0:T(8,128)S(1)} %add.156), channel_id=1, source_target_pairs={{0,1},{1,0},{2,3},{3,2},{4,5},{5,4},{6,7},{7,6},{8,9},{9,8},{10,11... | collective-permute-start | bytes 36872 | tf_op jit(solution)/shard_map/ppermute | solution.py:59
  96.5 12.3 %collective-permute-start.12 = (f32[3,32,32]{2,1,0:T(8,128)S(1)}, f32[3,32,32]{2,1,0:T(8,128)S(1)}, u32[]{:S(2)}, u32[]{:S(2)}) collective-permute-start(f32[3,32,32]{2,1,0:T(8,128)S(1)} %add.157), channel_id=1, source_target_pairs={{0,32},{1,33},{2,34},{3,35},{4,36},{5,37},{6,38},{7,39},{8,40},{9,... | collective-permute-start | bytes 36872 | tf_op jit(solution)/shard_map/ppermute | solution.py:59

commit v19 on v18

--- a/solution.py
+++ b/solution.py
@@ -49,7 +49,7 @@
                     d["z"] = (c["z"] + 4) % 16 if g % 2 else (c["z"] - 4) % 16
                 pairs.append((linear(c), linear(d)))
         steps.append(pairs)
-    return [steps[i] for i in (7, 8, 6, 2, 4, 1, 3, 5, 0)]
+    return [steps[i] for i in (7, 8, 6, 0, 1, 2, 3, 4, 5)]
 
 
 def butterfly_sum(x, axes):

time: 110 us -> 106 us (0.964)
  the two profiles are of different devices: /device:TPU:1 before, /device:TPU:24 now
where the time goes in v19:
time: 106 us
  starting transfers between devices  62.5 us (59%)
  waiting for transfers between devices  27.3 us (26%)
  local copies, waits for them, and re-layouts  5.56 us (5%)
  Pallas kernels  3.73 us (4%)
  matrix products  3.2 us (3%)
  other arithmetic  2.49 us (2%)
  between operations  1.06 us (1%)
    ppermute x9, starting transfers between devices, butterfly_sum(): x = x + lax.ppermute(x, axes, pairs)  45.7 us
    ppermute x9, waiting for transfers between devices, butterfly_sum(): x = x + lax.ppermute(x, axes, pairs)  20.4 us
    ppermute x2, starting transfers between devices, exchange(): from_left = lax.ppermute(edge_right, 'patch', to_right)  8.84 us
    ppermute x2, starting transfers between devices, exchange(): from_right = lax.ppermute(edge_left, 'patch', to_left)  7.97 us
    ppermute x2, waiting for transfers between devices, exchange(): from_right = lax.ppermute(edge_left, 'patch', to_left)  4.37 us
    pallas_call x1, Pallas kernels, first_window(): pl.pallas_call(window_kernel, out_shape=jax.ShapeDtypeStruct((nb + 4, row...  3.73 us
    ppermute x2, waiting for transfers between devices, exchange(): from_left = lax.ppermute(edge_right, 'patch', to_right)  2.49 us
  transfers between devices with their start and end apart: 13, of which 12 were waited for; matrix products, arithmetic and copies ran while one was open for 3% of the time, Pallas kernels for 0%

profile of v19, /device:TPU:24, one launch (start us, length us, event | category | flops | bytes accessed | tf_op | source)
XLA Modules:
  0.0 105.8 jit_solution(12684653537234949002)
XLA Ops:
  3.5 3.7 %shard_map.76 = f32[10,64,256]{2,1,0:T(8,128)} custom-call(s32[6,2]{1,0:T(8,128)} %add_convert_fusion.flags_ref, bf16[2,32,1536]{2,1,0:T(8,128)(2,1)} %cot_ref.1, bf16[3,32,32]{2,1,0:T(8,128)(2,1)} %f_ref.1, bf16[6,3,256,256]{3,2,1,0:T(8,128)(2,1)} %tiles_ref.1), custom_call_target="tpu_custom_call" | custom-call | tf_op jit(solution)/shard_map/pallas_call | solution.py:88
  8.3 1.9 %collective-permute-start = (f32[2,2,64,256]{3,2,1,0:T(8,128)S(1)}, f32[2,2,64,256]{3,2,1,0:T(8,128)S(1)}, u32[]{:S(2)}, u32[]{:S(2)}) collective-permute-start(f32[2,2,64,256]{3,2,1,0:T(8,128)S(1)} %pad_maximum_fusion.6), channel_id=1, source_target_pairs={{0,32},{32,64},{64,96},{96,128},{128,160},{160,192},{192,224},{224... | collective-permute-start | bytes 786440 | tf_op jit(solution)/shard_map/ppermute | solution.py:114
  10.2 6.0 %collective-permute-start.1 = (f32[2,2,64,256]{3,2,1,0:T(8,128)S(1)}, f32[2,2,64,256]{3,2,1,0:T(8,128)S(1)}, u32[]{:S(2)}, u32[]{:S(2)}) collective-permute-start(f32[2,2,64,256]{3,2,1,0:T(8,128)S(1)} %pad_maximum_fusion.5), channel_id=1, source_target_pairs={{32,0},{64,32},{96,64},{128,96},{160,128},{192,160},{224,192},{256... | collective-permute-start | bytes 786440 | tf_op jit(solution)/shard_map/ppermute | solution.py:113
  17.1 1.3 %collective-permute-done = f32[2,2,64,256]{3,2,1,0:T(8,128)S(1)} collective-permute-done((f32[2,2,64,256]{3,2,1,0:T(8,128)S(1)}, f32[2,2,64,256]{3,2,1,0:T(8,128)S(1)}, u32[]{:S(2)}, u32[]{:S(2)}) %collective-permute-start) | collective-permute-done | bytes 262176 | tf_op jit(solution)/shard_map/ppermute | solution.py:114
  18.4 1.7 %collective-permute-done.1 = f32[2,2,64,256]{3,2,1,0:T(8,128)S(1)} collective-permute-done((f32[2,2,64,256]{3,2,1,0:T(8,128)S(1)}, f32[2,2,64,256]{3,2,1,0:T(8,128)S(1)}, u32[]{:S(2)}, u32[]{:S(2)}) %collective-permute-start.1) | collective-permute-done | bytes 262176 | tf_op jit(solution)/shard_map/ppermute | solution.py:113
  22.2 6.9 %collective-permute-start.2 = (f32[2,2,64,256]{3,2,1,0:T(8,128)S(1)}, f32[2,2,64,256]{3,2,1,0:T(8,128)S(1)}, u32[]{:S(2)}, u32[]{:S(2)}) collective-permute-start(f32[2,2,64,256]{3,2,1,0:T(8,128)S(1)} %pad_maximum_fusion.8), channel_id=1, source_target_pairs={{0,32},{32,64},{64,96},{96,128},{128,160},{160,192},{192,224},{224... | collective-permute-start | bytes 786440 | tf_op jit(solution)/shard_map/ppermute | solution.py:114
  29.1 1.9 %collective-permute-start.3 = (f32[2,2,64,256]{3,2,1,0:T(8,128)S(1)}, f32[2,2,64,256]{3,2,1,0:T(8,128)S(1)}, u32[]{:S(2)}, u32[]{:S(2)}) collective-permute-start(f32[2,2,64,256]{3,2,1,0:T(8,128)S(1)} %pad_maximum_fusion.7), channel_id=1, source_target_pairs={{32,0},{64,32},{96,64},{128,96},{160,128},{192,160},{224,192},{256... | collective-permute-start | bytes 786440 | tf_op jit(solution)/shard_map/ppermute | solution.py:113
  32.5 2.6 %collective-permute-done.3 = f32[2,2,64,256]{3,2,1,0:T(8,128)S(1)} collective-permute-done((f32[2,2,64,256]{3,2,1,0:T(8,128)S(1)}, f32[2,2,64,256]{3,2,1,0:T(8,128)S(1)}, u32[]{:S(2)}, u32[]{:S(2)}) %collective-permute-start.3) | collective-permute-done | bytes 262176 | tf_op jit(solution)/shard_map/ppermute | solution.py:113
  36.3 8.2 %collective-permute-start.4 = (f32[3,32,32]{2,1,0:T(8,128)S(1)}, f32[3,32,32]{2,1,0:T(8,128)S(1)}, u32[]{:S(2)}, u32[]{:S(2)}) collective-permute-start(f32[3,32,32]{2,1,0:T(8,128)S(1)} %pad_maximum_fusion.9), channel_id=1, source_target_pairs={{0,4},{1,5},{2,6},{3,7},{4,0},{5,1},{6,2},{7,3},{8,12},{9,13},{10,... | collective-permute-start | bytes 36872 | tf_op jit(solution)/shard_map/ppermute | solution.py:59
  44.5 2.1 %collective-permute-done.4 = f32[3,32,32]{2,1,0:T(8,128)S(1)} collective-permute-done((f32[3,32,32]{2,1,0:T(8,128)S(1)}, f32[3,32,32]{2,1,0:T(8,128)S(1)}, u32[]{:S(2)}, u32[]{:S(2)}) %collective-permute-start.4) | collective-permute-done | bytes 12320 | tf_op jit(solution)/shard_map/ppermute | solution.py:59
  46.5 11.8 %collective-permute-start.5 = (f32[3,32,32]{2,1,0:T(8,128)S(1)}, f32[3,32,32]{2,1,0:T(8,128)S(1)}, u32[]{:S(2)}, u32[]{:S(2)}) collective-permute-start(f32[3,32,32]{2,1,0:T(8,128)S(1)} %fusion.89), channel_id=1, source_target_pairs={{0,12},{1,13},{2,14},{3,15},{4,8},{5,9},{6,10},{7,11},{8,4},{9,5},... | collective-permute-start | bytes 36872 | tf_op jit(solution)/shard_map/ppermute | solution.py:59
  58.3 2.9 %collective-permute-done.5 = f32[3,32,32]{2,1,0:T(8,128)S(1)} collective-permute-done((f32[3,32,32]{2,1,0:T(8,128)S(1)}, f32[3,32,32]{2,1,0:T(8,128)S(1)}, u32[]{:S(2)}, u32[]{:S(2)}) %collective-permute-start.5) | collective-permute-done | bytes 12320 | tf_op jit(solution)/shard_map/ppermute | solution.py:59
  61.2 5.6 %collective-permute-start.6 = (f32[3,32,32]{2,1,0:T(8,128)S(1)}, f32[3,32,32]{2,1,0:T(8,128)S(1)}, u32[]{:S(2)}, u32[]{:S(2)}) collective-permute-start(f32[3,32,32]{2,1,0:T(8,128)S(1)} %add.151), channel_id=1, source_target_pairs={{0,2},{1,3},{2,0},{3,1},{4,6},{5,7},{6,4},{7,5},{8,10},{9,11},{10,... | collective-permute-start | bytes 36872 | tf_op jit(solution)/shard_map/ppermute | solution.py:59
  66.9 2.1 %collective-permute-done.6 = f32[3,32,32]{2,1,0:T(8,128)S(1)} collective-permute-done((f32[3,32,32]{2,1,0:T(8,128)S(1)}, f32[3,32,32]{2,1,0:T(8,128)S(1)}, u32[]{:S(2)}, u32[]{:S(2)}) %collective-permute-start.6) | collective-permute-done | bytes 12320 | tf_op jit(solution)/shard_map/ppermute | solution.py:59
  68.9 1.9 %collective-permute-start.7 = (f32[3,32,32]{2,1,0:T(8,128)S(1)}, f32[3,32,32]{2,1,0:T(8,128)S(1)}, u32[]{:S(2)}, u32[]{:S(2)}) collective-permute-start(f32[3,32,32]{2,1,0:T(8,128)S(1)} %add.152), channel_id=1, source_target_pairs={{0,32},{1,33},{2,34},{3,35},{4,36},{5,37},{6,38},{7,39},{8,40},{9,... | collective-permute-start | bytes 36872 | tf_op jit(solution)/shard_map/ppermute | solution.py:59
  72.1 3.5 %collective-permute-start.8 = (f32[3,32,32]{2,1,0:T(8,128)S(1)}, f32[3,32,32]{2,1,0:T(8,128)S(1)}, u32[]{:S(2)}, u32[]{:S(2)}) collective-permute-start(f32[3,32,32]{2,1,0:T(8,128)S(1)} %add.153), channel_id=1, source_target_pairs={{0,16},{1,17},{2,18},{3,19},{4,20},{5,21},{6,22},{7,23},{8,24},{9,... | collective-permute-start | bytes 36872 | tf_op jit(solution)/shard_map/ppermute | solution.py:59
  75.8 2.3 %collective-permute-done.8 = f32[3,32,32]{2,1,0:T(8,128)S(1)} collective-permute-done((f32[3,32,32]{2,1,0:T(8,128)S(1)}, f32[3,32,32]{2,1,0:T(8,128)S(1)}, u32[]{:S(2)}, u32[]{:S(2)}) %collective-permute-start.8) | collective-permute-done | bytes 12320 | tf_op jit(solution)/shard_map/ppermute | solution.py:59
  78.1 3.7 %collective-permute-start.9 = (f32[3,32,32]{2,1,0:T(8,128)S(1)}, f32[3,32,32]{2,1,0:T(8,128)S(1)}, u32[]{:S(2)}, u32[]{:S(2)}) collective-permute-start(f32[3,32,32]{2,1,0:T(8,128)S(1)} %add.154), channel_id=1, source_target_pairs={{0,80},{1,81},{2,82},{3,83},{4,84},{5,85},{6,86},{7,87},{8,88},{9,... | collective-permute-start | bytes 36872 | tf_op jit(solution)/shard_map/ppermute | solution.py:59
  81.9 3.4 %collective-permute-done.9 = f32[3,32,32]{2,1,0:T(8,128)S(1)} collective-permute-done((f32[3,32,32]{2,1,0:T(8,128)S(1)}, f32[3,32,32]{2,1,0:T(8,128)S(1)}, u32[]{:S(2)}, u32[]{:S(2)}) %collective-permute-start.9) | collective-permute-done | bytes 12320 | tf_op jit(solution)/shard_map/ppermute | solution.py:59
  85.3 2.6 %collective-permute-start.10 = (f32[3,32,32]{2,1,0:T(8,128)S(1)}, f32[3,32,32]{2,1,0:T(8,128)S(1)}, u32[]{:S(2)}, u32[]{:S(2)}) collective-permute-start(f32[3,32,32]{2,1,0:T(8,128)S(1)} %add.155), channel_id=1, source_target_pairs={{0,128},{1,129},{2,130},{3,131},{4,132},{5,133},{6,134},{7,135},{8... | collective-permute-start | bytes 36872 | tf_op jit(solution)/shard_map/ppermute | solution.py:59
  88.0 3.3 %collective-permute-done.10 = f32[3,32,32]{2,1,0:T(8,128)S(1)} collective-permute-done((f32[3,32,32]{2,1,0:T(8,128)S(1)}, f32[3,32,32]{2,1,0:T(8,128)S(1)}, u32[]{:S(2)}, u32[]{:S(2)}) %collective-permute-start.10) | collective-permute-done | bytes 12320 | tf_op jit(solution)/shard_map/ppermute | solution.py:59
  91.3 3.9 %collective-permute-start.11 = (f32[3,32,32]{2,1,0:T(8,128)S(1)}, f32[3,32,32]{2,1,0:T(8,128)S(1)}, u32[]{:S(2)}, u32[]{:S(2)}) collective-permute-start(f32[3,32,32]{2,1,0:T(8,128)S(1)} %add.156), channel_id=1, source_target_pairs={{0,384},{1,385},{2,386},{3,387},{4,388},{5,389},{6,390},{7,391},{8... | collective-permute-start | bytes 36872 | tf_op jit(solution)/shard_map/ppermute | solution.py:59
  95.3 3.2 %collective-permute-done.11 = f32[3,32,32]{2,1,0:T(8,128)S(1)} collective-permute-done((f32[3,32,32]{2,1,0:T(8,128)S(1)}, f32[3,32,32]{2,1,0:T(8,128)S(1)}, u32[]{:S(2)}, u32[]{:S(2)}) %collective-permute-start.11) | collective-permute-done | bytes 12320 | tf_op jit(solution)/shard_map/ppermute | solution.py:59
  98.5 4.3 %collective-permute-start.12 = (f32[3,32,32]{2,1,0:T(8,128)S(1)}, f32[3,32,32]{2,1,0:T(8,128)S(1)}, u32[]{:S(2)}, u32[]{:S(2)}) collective-permute-start(f32[3,32,32]{2,1,0:T(8,128)S(1)} %add.157), channel_id=1, source_target_pairs={{0,1},{1,0},{2,3},{3,2},{4,5},{5,4},{6,7},{7,6},{8,9},{9,8},{10,11... | collective-permute-start | bytes 36872 | tf_op jit(solution)/shard_map/ppermute | solution.py:59
  (71 shorter events, 13.6 us)
Async XLA Ops:
  3.5 12.8 %copy-start.2 = (bf16[2,32,1536]{2,1,0:T(8,128)(2,1)S(1)}, bf16[2,32,1536]{2,1,0:T(8,128)(2,1)}, u32[]{:S(2)}) copy-start(bf16[2,32,1536]{2,1,0:T(8,128)(2,1)} %cot_ref.1) | copy-start | bytes 589828
  3.5 13.1 %copy-start.3 = (bf16[3,32,32]{2,1,0:T(8,128)(2,1)S(1)}, bf16[3,32,32]{2,1,0:T(8,128)(2,1)}, u32[]{:S(2)}) copy-start(bf16[3,32,32]{2,1,0:T(8,128)(2,1)} %f_ref.1) | copy-start | bytes 18436
  8.3 8.8 %copy-start.4 = (s32[6,3]{0,1:T(4,128)S(1)}, s32[6,3]{0,1:T(4,128)}, u32[]{:S(2)}) copy-start(s32[6,3]{0,1:T(4,128)} %param.16) | copy-start | bytes 220
  8.3 10.1 %collective-permute-start = (f32[2,2,64,256]{3,2,1,0:T(8,128)S(1)}, f32[2,2,64,256]{3,2,1,0:T(8,128)S(1)}, u32[]{:S(2)}, u32[]{:S(2)}) collective-permute-start(f32[2,2,64,256]{3,2,1,0:T(8,128)S(1)} %pad_maximum_fusion.6), channel_id=1, source_target_pairs={{0,32},{32,64},{64,96},{96,128},{128,160},{160,192},{192,224},{224... | collective-permute-start | bytes 786440 | tf_op jit(solution)/shard_map/ppermute | solution.py:114
  10.2 9.9 %collective-permute-start.1 = (f32[2,2,64,256]{3,2,1,0:T(8,128)S(1)}, f32[2,2,64,256]{3,2,1,0:T(8,128)S(1)}, u32[]{:S(2)}, u32[]{:S(2)}) collective-permute-start(f32[2,2,64,256]{3,2,1,0:T(8,128)S(1)} %pad_maximum_fusion.5), channel_id=1, source_target_pairs={{32,0},{64,32},{96,64},{128,96},{160,128},{192,160},{224,192},{256... | collective-permute-start | bytes 786440 | tf_op jit(solution)/shard_map/ppermute | solution.py:113
  16.5 1.9 %copy-start.1 = (f32[10,64,256]{2,1,0:T(8,128)S(1)}, f32[10,64,256]{2,1,0:T(8,128)}, u32[]{:S(2)}) copy-start(f32[10,64,256]{2,1,0:T(8,128)} %shard_map.76) | copy-start | bytes 1966084
  16.6 1.9 %slice-start = ((f32[10,64,256]{2,1,0:T(8,128)}), f32[6,64,256]{2,1,0:T(8,128)S(1)}, s32[]{:S(2)}) async-start(f32[10,64,256]{2,1,0:T(8,128)} %shard_map.76), calls=%async_computation | async-start | bytes 786432 | tf_op jit(solution)/shard_map/slice | solution.py:157
  16.9 3.3 %copy-start = (bf16[6,3,256,256]{3,2,1,0:T(8,128)(2,1)S(1)}, bf16[6,3,256,256]{3,2,1,0:T(8,128)(2,1)}, u32[]{:S(2)}) copy-start(bf16[6,3,256,256]{3,2,1,0:T(8,128)(2,1)} %tiles_ref.1) | copy-start | bytes 7077892
  22.2 10.3 %collective-permute-start.2 = (f32[2,2,64,256]{3,2,1,0:T(8,128)S(1)}, f32[2,2,64,256]{3,2,1,0:T(8,128)S(1)}, u32[]{:S(2)}, u32[]{:S(2)}) collective-permute-start(f32[2,2,64,256]{3,2,1,0:T(8,128)S(1)} %pad_maximum_fusion.8), channel_id=1, source_target_pairs={{0,32},{32,64},{64,96},{96,128},{128,160},{160,192},{192,224},{224... | collective-permute-start | bytes 786440 | tf_op jit(solution)/shard_map/ppermute | solution.py:114
  29.1 6.0 %collective-permute-start.3 = (f32[2,2,64,256]{3,2,1,0:T(8,128)S(1)}, f32[2,2,64,256]{3,2,1,0:T(8,128)S(1)}, u32[]{:S(2)}, u32[]{:S(2)}) collective-permute-start(f32[2,2,64,256]{3,2,1,0:T(8,128)S(1)} %pad_maximum_fusion.7), channel_id=1, source_target_pairs={{32,0},{64,32},{96,64},{128,96},{160,128},{192,160},{224,192},{256... | collective-permute-start | bytes 786440 | tf_op jit(solution)/shard_map/ppermute | solution.py:113
  36.3 10.3 %collective-permute-start.4 = (f32[3,32,32]{2,1,0:T(8,128)S(1)}, f32[3,32,32]{2,1,0:T(8,128)S(1)}, u32[]{:S(2)}, u32[]{:S(2)}) collective-permute-start(f32[3,32,32]{2,1,0:T(8,128)S(1)} %pad_maximum_fusion.9), channel_id=1, source_target_pairs={{0,4},{1,5},{2,6},{3,7},{4,0},{5,1},{6,2},{7,3},{8,12},{9,13},{10,... | collective-permute-start | bytes 36872 | tf_op jit(solution)/shard_map/ppermute | solution.py:59
  46.5 14.7 %collective-permute-start.5 = (f32[3,32,32]{2,1,0:T(8,128)S(1)}, f32[3,32,32]{2,1,0:T(8,128)S(1)}, u32[]{:S(2)}, u32[]{:S(2)}) collective-permute-start(f32[3,32,32]{2,1,0:T(8,128)S(1)} %fusion.89), channel_id=1, source_target_pairs={{0,12},{1,13},{2,14},{3,15},{4,8},{5,9},{6,10},{7,11},{8,4},{9,5},... | collective-permute-start | bytes 36872 | tf_op jit(solution)/shard_map/ppermute | solution.py:59
  61.2 7.7 %collective-permute-start.6 = (f32[3,32,32]{2,1,0:T(8,128)S(1)}, f32[3,32,32]{2,1,0:T(8,128)S(1)}, u32[]{:S(2)}, u32[]{:S(2)}) collective-permute-start(f32[3,32,32]{2,1,0:T(8,128)S(1)} %add.151), channel_id=1, source_target_pairs={{0,2},{1,3},{2,0},{3,1},{4,6},{5,7},{6,4},{7,5},{8,10},{9,11},{10,... | collective-permute-start | bytes 36872 | tf_op jit(solution)/shard_map/ppermute | solution.py:59
  68.9 3.1 %collective-permute-start.7 = (f32[3,32,32]{2,1,0:T(8,128)S(1)}, f32[3,32,32]{2,1,0:T(8,128)S(1)}, u32[]{:S(2)}, u32[]{:S(2)}) collective-permute-start(f32[3,32,32]{2,1,0:T(8,128)S(1)} %add.152), channel_id=1, source_target_pairs={{0,32},{1,33},{2,34},{3,35},{4,36},{5,37},{6,38},{7,39},{8,40},{9,... | collective-permute-start | bytes 36872 | tf_op jit(solution)/shard_map/ppermute | solution.py:59
  72.1 6.0 %collective-permute-start.8 = (f32[3,32,32]{2,1,0:T(8,128)S(1)}, f32[3,32,32]{2,1,0:T(8,128)S(1)}, u32[]{:S(2)}, u32[]{:S(2)}) collective-permute-start(f32[3,32,32]{2,1,0:T(8,128)S(1)} %add.153), channel_id=1, source_target_pairs={{0,16},{1,17},{2,18},{3,19},{4,20},{5,21},{6,22},{7,23},{8,24},{9,... | collective-permute-start | bytes 36872 | tf_op jit(solution)/shard_map/ppermute | solution.py:59
  78.1 7.2 %collective-permute-start.9 = (f32[3,32,32]{2,1,0:T(8,128)S(1)}, f32[3,32,32]{2,1,0:T(8,128)S(1)}, u32[]{:S(2)}, u32[]{:S(2)}) collective-permute-start(f32[3,32,32]{2,1,0:T(8,128)S(1)} %add.154), channel_id=1, source_target_pairs={{0,80},{1,81},{2,82},{3,83},{4,84},{5,85},{6,86},{7,87},{8,88},{9,... | collective-permute-start | bytes 36872 | tf_op jit(solution)/shard_map/ppermute | solution.py:59
  85.3 6.0 %collective-permute-start.10 = (f32[3,32,32]{2,1,0:T(8,128)S(1)}, f32[3,32,32]{2,1,0:T(8,128)S(1)}, u32[]{:S(2)}, u32[]{:S(2)}) collective-permute-start(f32[3,32,32]{2,1,0:T(8,128)S(1)} %add.155), channel_id=1, source_target_pairs={{0,128},{1,129},{2,130},{3,131},{4,132},{5,133},{6,134},{7,135},{8... | collective-permute-start | bytes 36872 | tf_op jit(solution)/shard_map/ppermute | solution.py:59
  91.3 7.2 %collective-permute-start.11 = (f32[3,32,32]{2,1,0:T(8,128)S(1)}, f32[3,32,32]{2,1,0:T(8,128)S(1)}, u32[]{:S(2)}, u32[]{:S(2)}) collective-permute-start(f32[3,32,32]{2,1,0:T(8,128)S(1)} %add.156), channel_id=1, source_target_pairs={{0,384},{1,385},{2,386},{3,387},{4,388},{5,389},{6,390},{7,391},{8... | collective-permute-start | bytes 36872 | tf_op jit(solution)/shard_map/ppermute | solution.py:59
  98.5 6.7 %collective-permute-start.12 = (f32[3,32,32]{2,1,0:T(8,128)S(1)}, f32[3,32,32]{2,1,0:T(8,128)S(1)}, u32[]{:S(2)}, u32[]{:S(2)}) collective-permute-start(f32[3,32,32]{2,1,0:T(8,128)S(1)} %add.157), channel_id=1, source_target_pairs={{0,1},{1,0},{2,3},{3,2},{4,5},{5,4},{6,7},{7,6},{8,9},{9,8},{10,11... | collective-permute-start | bytes 36872 | tf_op jit(solution)/shard_map/ppermute | solution.py:59
